TPU v7x, 32 devices: a whole 2x2x4 slice. The times are simulated.
32 devices in a mesh: groups: 2 (over y), ctx: 4 (over z), eg: 4 (over x, core), rep: 1.
Axes of the slice: x: 2, y: 2, z: 4, core: 2. Of those that a mesh axis runs over, the one named last changes fastest.
Arguments:
- queries: bfloat16 [4096, 2048], P(('groups', 'ctx', 'eg'), 'rep'), parts along dimension 0, may hold values from -12 to 12
- keys: bfloat16 [8, 512, 256], P(('groups', 'ctx'), 'eg', 'rep'), parts along dimension 0, may hold values from -4 to 4
- values: bfloat16 [8, 512, 256], P(('groups', 'ctx'), 'eg', 'rep'), parts along dimension 0, may hold values from -12 to 12
- selected: int32 [8, 2], P('groups'), parts along dimension 0, may hold values from 0 to 3, as said below
- out_weight: bfloat16 [2048, 2048], P('rep', 'eg'), may hold values from -0.125 to 0.125
- residual: bfloat16 [4096, 2048], P(('groups', 'ctx', 'eg', 'rep')), parts along dimension 0, may hold values from -27 to 27
- norm_gain: float32 [2048], replicated, may hold values from 0.5 to 1.5
- expert_ids: int32 [4096, 8], P(('groups', 'ctx', 'eg', 'rep')), parts along dimension 0, may hold values from 0 to 15, all different within a row; in each aligned block of 128 rows (0 to 127, 128 to 255, ...) at most 64 rows name the same one
- gate_weights: float32 [4096, 8], P(('groups', 'ctx', 'eg', 'rep')), parts along dimension 0, may hold values from 0.05 to 0.5
- expert_home: int32 [16], replicated, may hold values from 0 to 15, each once
- w_gate: bfloat16 [16, 2048, 384], P(('ctx', 'eg'), None, 'rep'), may hold values from -0.125 to 0.125
- w_up: bfloat16 [16, 2048, 384], P(('ctx', 'eg'), None, 'rep'), may hold values from -0.125 to 0.125
- w_down: bfloat16 [16, 384, 2048], P(('ctx', 'eg'), 'rep'), may hold values from -0.3125 to 0.3125
Outputs:
- attn_out: bfloat16 [4096, 2048], P(('groups', 'ctx', 'eg', 'rep')), parts along dimension 0
- moe_out: bfloat16 [4096, 2048], P(('groups', 'ctx', 'eg', 'rep')), parts along dimension 0
There are 2 independent parts, one for each index of `groups`. A program takes and returns all parts, laid end to end along the dimension named above; an argument that names none is the same for every part. Nothing has to cross between parts.
Inputs may be any that keep to these rules, and one draw needn't show every extreme that they name: `selected`: block c lies in context shard c; query block b lies in shard b. The 2 blocks listed by the query blocks of one shard lie in distinct shards, and no query block lists itself. `expert_ids`: each aligned block of 128 rows (the rows of one device) names every expert exactly 64 times. Expert e's weights are entry expert_home[e] of w_gate, w_up and w_down.
All inputs are finite; a program needn't handle non-finite values.
Results may differ from a plain program's by a relative error of at most 0.0085.
Values may be sent and summed in bfloat16 or wider, within the bound.
No kernel may reach another device: no remote copies, remote signals or barrier semaphores. Data moves between devices by JAX's collectives and lax.ppermute only.
A program may use at most 64 MiB of HBM per device.

v0:
```python
import math

import jax
import jax.numpy as jnp
from jax import lax
from jax.sharding import PartitionSpec as P

HD = 128


def swapped(value, axis, bit):
    mask = 2**bit
    pairs = [(source, source ^ mask) for source in range(lax.axis_size(axis))]
    return lax.ppermute(value, axis, pairs)


def attend_pair(query_pair, key_rows, value_rows, inverse_root):
    logits = (
        jnp.einsum("rkgd,nkd->krgn", query_pair, key_rows, preferred_element_type=jnp.float32)
        * inverse_root
    )
    largest = jnp.max(logits, axis=-1, keepdims=True)
    raised = jnp.exp(logits - largest)
    denominator = jnp.sum(raised, axis=-1, keepdims=True)
    weights_low = (raised / denominator).astype(jnp.bfloat16)
    blended = jnp.einsum(
        "krgn,nkd->rkgd", weights_low, value_rows, preferred_element_type=jnp.float32
    )
    return blended.astype(jnp.bfloat16)


def attend_rows(queries_flat, key_rows, value_rows):
    row_count = queries_flat.shape[0]
    kv_heads = key_rows.shape[1]
    per_group = queries_flat.shape[1] // (kv_heads * HD)
    arranged = queries_flat.reshape(row_count, kv_heads, per_group // 2, 2, HD)
    inverse_root = 1.0 / math.sqrt(HD)

    def one_pair(pair_index):
        query_pair = lax.dynamic_index_in_dim(arranged, pair_index, 2, keepdims=False)
        return attend_pair(query_pair, key_rows, value_rows, inverse_root)

    stacked = lax.map(one_pair, jnp.arange(per_group // 2, dtype=jnp.int32))
    return jnp.moveaxis(stacked, 0, 2).reshape(row_count, kv_heads * per_group * HD)


def expert_apply(rows_in, gate_full, up_full, down_full):
    gate_act = jnp.dot(rows_in, gate_full, preferred_element_type=jnp.float32)
    up_act = jnp.dot(rows_in, up_full, preferred_element_type=jnp.float32)
    activation = (jax.nn.silu(gate_act) * up_act).astype(jnp.bfloat16)
    return jnp.dot(activation, down_full, preferred_element_type=jnp.float32).astype(jnp.bfloat16)


def local(
    queries,
    keys,
    values,
    selected,
    out_weight,
    residual,
    norm_gain,
    expert_ids,
    gate_weights,
    expert_home,
    w_gate,
    w_up,
    w_down,
):
    n_ctx = lax.axis_size("ctx")
    n_eg = lax.axis_size("eg")
    n_rep = lax.axis_size("rep")
    my_ctx = lax.axis_index("ctx")

    def fetch_panels():
        if n_rep == 1:
            return (w_gate[0], w_up[0], w_down[0])
        other_gate, other_up, other_down = swapped((w_gate, w_up, w_down), "rep", 0)
        first = lax.axis_index("rep") == 0
        gate_full = jnp.where(
            first,
            jnp.concatenate([w_gate[0], other_gate[0]], axis=1),
            jnp.concatenate([other_gate[0], w_gate[0]], axis=1),
        )
        up_full = jnp.where(
            first,
            jnp.concatenate([w_up[0], other_up[0]], axis=1),
            jnp.concatenate([other_up[0], w_up[0]], axis=1),
        )
        down_full = jnp.where(
            first,
            jnp.concatenate([w_down[0], other_down[0]], axis=0),
            jnp.concatenate([other_down[0], w_down[0]], axis=0),
        )
        return (gate_full, up_full, down_full)

    shard_blocks, slice_rows, kv_width = keys.shape
    pick_count = selected.shape[1]
    block_rows = slice_rows * n_eg
    listed = selected.reshape(n_ctx, shard_blocks * pick_count)
    owned_here = listed // shard_blocks == my_ctx
    block_match = (listed % shard_blocks)[:, :, None] == jnp.arange(shard_blocks, dtype=jnp.int32)[
        None, None, :
    ]
    request = jnp.max(
        jnp.logical_and(owned_here[:, :, None], block_match).astype(jnp.int32), axis=1
    ).astype(jnp.bfloat16)
    outgoing_keys = jnp.einsum(
        "cb,btw->ctw", request, keys, preferred_element_type=jnp.float32
    ).astype(jnp.bfloat16)
    outgoing_values = jnp.einsum(
        "cb,btw->ctw", request, values, preferred_element_type=jnp.float32
    ).astype(jnp.bfloat16)
    far_keys, far_values = (
        lax.all_to_all(outgoing_keys, "ctx", split_axis=0, concat_axis=0, tiled=True),
        lax.all_to_all(outgoing_values, "ctx", split_axis=0, concat_axis=0, tiled=True),
    )
    query_rows = queries.shape[0]
    peer_ids = jnp.arange(n_eg, dtype=jnp.int32)
    own_block = peer_ids * query_rows // block_rows
    peer_lists = jnp.take(selected, my_ctx * shard_blocks + own_block, axis=0) // shard_blocks

    def assemble(local_part, fetched):
        own_rows = jnp.take(local_part, own_block, axis=0)[:, None]
        far_rows = jnp.take(fetched, peer_lists.reshape(-1), axis=0).reshape(
            n_eg, pick_count, slice_rows, kv_width
        )
        return jnp.concatenate([own_rows, far_rows], axis=1)

    context_keys, context_values = (
        lax.all_to_all(assemble(keys, far_keys), "eg", split_axis=0, concat_axis=2, tiled=True),
        lax.all_to_all(assemble(values, far_values), "eg", split_axis=0, concat_axis=2, tiled=True),
    )
    span = (1 + pick_count) * block_rows
    kv_heads = kv_width // HD
    attended = attend_rows(
        queries,
        context_keys.reshape(span, kv_heads, HD),
        context_values.reshape(span, kv_heads, HD),
    )
    tok_dev = residual.shape[0]
    partial_out = jnp.dot(
        attended,
        lax.all_gather(out_weight, "eg", axis=1, tiled=True),
        preferred_element_type=jnp.float32,
    )
    attn_out = lax.psum_scatter(
        partial_out.astype(jnp.bfloat16), "rep", scatter_dimension=0, tiled=True
    )
    stream = residual.astype(jnp.float32) + attn_out.astype(jnp.float32)
    meansq = jnp.mean(stream * stream, axis=1, keepdims=True)
    normed = (stream * lax.rsqrt(meansq + 1e-06) * norm_gain).astype(jnp.bfloat16)
    top_count = expert_ids.shape[1]
    slot_count = n_ctx * n_eg
    pair_count = tok_dev * top_count
    per_slot = pair_count // slot_count
    home_slot = jnp.take(expert_home, expert_ids.reshape(-1), axis=0)
    indicator = (home_slot[:, None] == jnp.arange(slot_count, dtype=jnp.int32)[None, :]).astype(
        jnp.int32
    )
    rank_in_slot = jnp.sum((jnp.cumsum(indicator, axis=0) - 1) * indicator, axis=1)
    position = home_slot * per_slot + rank_in_slot
    source_pair = (
        jnp.zeros((pair_count,), jnp.int32)
        .at[position]
        .set(jnp.arange(pair_count, dtype=jnp.int32))
    )
    outbound = jnp.take(normed, source_pair // top_count, axis=0).reshape(slot_count, per_slot, -1)
    partner = fetch_panels()
    arrived = lax.all_to_all(outbound, ("ctx", "eg"), split_axis=0, concat_axis=0, tiled=True)
    flat_rows = arrived.reshape(-1, arrived.shape[2])
    produced = expert_apply(flat_rows, partner[0], partner[1], partner[2])
    returned = lax.all_to_all(
        produced.reshape(arrived.shape), ("ctx", "eg"), split_axis=0, concat_axis=0, tiled=True
    )
    answers = jnp.take(returned.reshape(pair_count, -1), position, axis=0).reshape(
        tok_dev, top_count, -1
    )
    combined = gate_weights[:, 0:1] * answers[:, 0].astype(jnp.float32)
    for choice_slot in range(1, top_count):
        combined = combined + gate_weights[:, choice_slot : choice_slot + 1] * answers[
            :, choice_slot
        ].astype(jnp.float32)
    moe_out = combined.astype(jnp.bfloat16)
    return (attn_out, moe_out)


def solution(mesh):
    return jax.shard_map(
        local,
        mesh=mesh,
        in_specs=(
            P(("groups", "ctx", "eg"), "rep"),
            P(("groups", "ctx"), "eg", "rep"),
            P(("groups", "ctx"), "eg", "rep"),
            P("groups", None),
            P("rep", "eg"),
            P(("groups", "ctx", "eg", "rep"), None),
            P(),
            P(("groups", "ctx", "eg", "rep"), None),
            P(("groups", "ctx", "eg", "rep"), None),
            P(),
            P(("ctx", "eg"), None, "rep"),
            P(("ctx", "eg"), None, "rep"),
            P(("ctx", "eg"), "rep", None),
        ),
        out_specs=(
            P(("groups", "ctx", "eg", "rep"), None),
            P(("groups", "ctx", "eg", "rep"), None),
        ),
        check_vma=False,
    )
```

profile of v0, /device:TPU:11, one launch (start us, length us, event | category | flops | bytes accessed | tf_op | source)
XLA Modules:
  0.0 375.9 jit_solution(7449543417492950134)
XLA Ops:
  10.5 4.8 %all-to-all-start = ((bf16[4,128,256]{2,1,0:T(8,128)(2,1)}), bf16[4,128,256]{2,1,0:T(8,128)(2,1)S(1)}, u32[]{:S(2)}, u32[]{:S(2)}) async-start(bf16[4,128,256]{2,1,0:T(8,128)(2,1)} %get-tuple-element.111), calls=%async_computation | async-start | bytes 524288 | tf_op jit(solution)/shard_map/all_to_all | solution.py:114
  17.3 4.5 %compare_select_fusion.2 = (s32[1024,1]{0,1:T(1,128)S(1)}, s32[1024,1]{0,1:T(1,128)S(1)}) fusion(s32[]{:T(128)} %bitcast.34, s32[]{:T(128)} %bitcast.35, s32[]{:T(128)} %bitcast.36, s32[]{:T(128)} %bitcast.37, s32[]{:T(128)} %bitcast.38, s32[]{:T(128)} %bitcast.40, s32[]{:T(128)} %bitcast.39, s32[1024,1]{0,1:T(1,128)S(1)} %reshape.322), kind=kLoop, calls=%fused_computation.88 | loop fusion | flops 15360 | bytes 12316 | tf_op jit(solution)/shard_map/jit(_take)/gather | solution.py:156
  21.9 5.4 %and_select_fusion.1 = (s32[1024]{0:T(1024)S(1)}, s32[1024]{0:T(1024)S(1)}) fusion(s32[1024]{0:T(1024)S(1)} %reshape.323, pred[1024]{0:T(1024)(128)(4,1)S(1)} %get-tuple-element.63, pred[1024]{0:T(1024)(128)(4,1)S(1)} %get-tuple-element.61, pred[1024]{0:T(1024)(128)(4,1)S(1)} %get-tuple-element.62, pred[1024]{0:T(1024)(128)(4,1)S(1)} %get-tuple-element.60, ...), kind=kLoop, calls=%fused_computation.113 | loop fusion | flops 16384 | bytes 25636 | tf_op jit(solution)/shard_map/jit(_take)/select_n | solution.py:156
  27.4 4.5 %all-to-all-start.2 = ((bf16[4,128,256]{2,1,0:T(8,128)(2,1)}), bf16[4,128,256]{2,1,0:T(8,128)(2,1)S(1)}, u32[]{:S(2)}, u32[]{:S(2)}) async-start(bf16[4,128,256]{2,1,0:T(8,128)(2,1)} %get-tuple-element.110), calls=%async_computation.2 | async-start | bytes 524288 | tf_op jit(solution)/shard_map/all_to_all | solution.py:115
  33.4 4.2 %all-to-all-done.2 = bf16[4,128,256]{2,1,0:T(8,128)(2,1)S(1)} async-done(((bf16[4,128,256]{2,1,0:T(8,128)(2,1)}), bf16[4,128,256]{2,1,0:T(8,128)(2,1)S(1)}, u32[]{:S(2)}, u32[]{:S(2)}) %all-to-all-start.2) | async-done | bytes 262176 | tf_op jit(solution)/shard_map/all_to_all | solution.py:115
  41.2 6.2 %all-to-all-start.1 = ((bf16[4,3,128,256]{3,2,1,0:T(8,128)(2,1)}), bf16[4,3,128,256]{3,2,1,0:T(8,128)(2,1)S(1)}, u32[]{:S(2)}, u32[]{:S(2)}) async-start(bf16[4,3,128,256]{3,2,1,0:T(8,128)(2,1)} %pad_maximum_fusion), calls=%async_computation.1 | async-start | bytes 1572864 | tf_op jit(solution)/shard_map/all_to_all | solution.py:130
  47.4 4.5 %reduce-window.6 = s32[16,8,128]{2,1,0:T(8,128)S(1)} reduce-window(s32[16,8,128]{2,1,0:T(8,128)S(1)} %fusion.44, s32[]{:T(128)} %constant.159.clone.1), window={size=1x1x128 pad=0_0x0_0x127_0}, to_apply=%region_5.8 | reduce-window | flops 2080768 | bytes 131076 | tf_op jit(solution)/shard_map/reduce-window
  55.4 10.4 %all-to-all-done.1 = bf16[4,3,128,256]{3,2,1,0:T(8,128)(2,1)S(1)} async-done(((bf16[4,3,128,256]{3,2,1,0:T(8,128)(2,1)}), bf16[4,3,128,256]{3,2,1,0:T(8,128)(2,1)S(1)}, u32[]{:S(2)}, u32[]{:S(2)}) %all-to-all-start.1) | async-done | bytes 786464 | tf_op jit(solution)/shard_map/all_to_all | solution.py:130
  65.8 5.5 %all-to-all-start.3 = ((bf16[4,3,128,256]{3,2,1,0:T(8,128)(2,1)}), bf16[4,3,128,256]{3,2,1,0:T(8,128)(2,1)S(1)}, u32[]{:S(2)}, u32[]{:S(2)}) async-start(bf16[4,3,128,256]{3,2,1,0:T(8,128)(2,1)} %pad_maximum_fusion.1), calls=%async_computation.3 | async-start | bytes 1572864 | tf_op jit(solution)/shard_map/all_to_all | solution.py:131
  71.3 4.3 %scatter_custom_fusion = s32[1024]{0:T(1024)S(1)} fusion(s32[1024]{0:T(1024)S(1)} %bitcast.203, s32[1024]{0:T(1024)S(1)} %iota.27, s32[]{:T(128)} %constant.159.clone.1), kind=kCustom, calls=%fused_computation.120 | custom fusion | bytes 4100 | tf_op jit(solution)/shard_map/scatter | solution.py:165
  79.7 3.8 %all-to-all-done.3 = bf16[4,3,128,256]{3,2,1,0:T(8,128)(2,1)S(1)} async-done(((bf16[4,3,128,256]{3,2,1,0:T(8,128)(2,1)}), bf16[4,3,128,256]{3,2,1,0:T(8,128)(2,1)S(1)}, u32[]{:S(2)}, u32[]{:S(2)}) %all-to-all-start.3) | async-done | bytes 786464 | tf_op jit(solution)/shard_map/all_to_all | solution.py:131
  84.7 38.8 %while.10 = (s32[]{:T(128)}, bf16[4,128,2,2,128]{1,4,3,0,2:T(8,128)(2,1)}, s32[4]{0:T(128)S(1)}, bf16[128,2,4,2,128]{0,4,3,2,1:T(8,128)(2,1)}, bf16[1536,2,128]{...) while((s32[]{:T(128)}, bf16[4,128,2,2,128]{1,4,3,0,2:T(8,128)(2,1)}, ...), condition=%wide.region_4.7_spmd, body=%wide.region_1.6_spmd.sunk | while | flops 406652416 | bytes 11801259 | solution.py:43
  87.0 4.1 %fusion.70 = (f32[2,128,2]{1,2,0:T(2,128)S(1)}, f32[2,128,2,1536]{3,1,2,0:T(8,128)}) fusion(bf16[1536,2,128]{2,0,1:T(8,128)(2,1)} %get-tuple-element.179, bf16[128,2,4,2,128]{0,4,3,2,1:T(8,128)(2,1)} %get-tuple-element.178, s32[]{:T(128)S(6)} %select_n.268), kind=kOutput, calls=%fused_computation.150.clone.1 | convolution fusion | flops 203687424 | bytes 4065284 | tf_op jit(solution)/shard_map/while/body/eval_jaxpr/sub | solution.py:23
  96.7 4.1 %fusion.70 = (f32[2,128,2]{1,2,0:T(2,128)S(1)}, f32[2,128,2,1536]{3,1,2,0:T(8,128)}) fusion(bf16[1536,2,128]{2,0,1:T(8,128)(2,1)} %get-tuple-element.179, bf16[128,2,4,2,128]{0,4,3,2,1:T(8,128)(2,1)} %get-tuple-element.178, s32[]{:T(128)S(6)} %select_n.268), kind=kOutput, calls=%fused_computation.150.clone.1 | convolution fusion | flops 203687424 | bytes 4065284 | tf_op jit(solution)/shard_map/while/body/eval_jaxpr/sub | solution.py:23
  106.4 4.1 %fusion.70 = (f32[2,128,2]{1,2,0:T(2,128)S(1)}, f32[2,128,2,1536]{3,1,2,0:T(8,128)}) fusion(bf16[1536,2,128]{2,0,1:T(8,128)(2,1)} %get-tuple-element.179, bf16[128,2,4,2,128]{0,4,3,2,1:T(8,128)(2,1)} %get-tuple-element.178, s32[]{:T(128)S(6)} %select_n.268), kind=kOutput, calls=%fused_computation.150.clone.1 | convolution fusion | flops 203687424 | bytes 4065284 | tf_op jit(solution)/shard_map/while/body/eval_jaxpr/sub | solution.py:23
  116.1 4.1 %fusion.70 = (f32[2,128,2]{1,2,0:T(2,128)S(1)}, f32[2,128,2,1536]{3,1,2,0:T(8,128)}) fusion(bf16[1536,2,128]{2,0,1:T(8,128)(2,1)} %get-tuple-element.179, bf16[128,2,4,2,128]{0,4,3,2,1:T(8,128)(2,1)} %get-tuple-element.178, s32[]{:T(128)S(6)} %select_n.268), kind=kOutput, calls=%fused_computation.150.clone.1 | convolution fusion | flops 203687424 | bytes 4065284 | tf_op jit(solution)/shard_map/while/body/eval_jaxpr/sub | solution.py:23
  123.5 5.0 %multiply_reduce_fusion = (f32[128]{0:T(128)S(1)}, bf16[128,2048]{1,0:T(8,128)(2,1)S(1)}) fusion(bf16[128,2048]{1,0:T(8,128)(2,1)S(1)} %copy-done.2, bf16[128,2048]{0,1:T(8,128)(2,1)} %bitcast.195, bf16[2048,2048]{1,0:T(8,128)(2,1)} %all-gather.2.cloned.1.call-done), kind=kOutput, calls=%fused_computation.52 | convolution fusion | flops 1075314560 | bytes 9961984 | tf_op jit(solution)/shard_map/dot_general | solution.py:141
  128.8 6.0 %gather_fusion.1 = bf16[1024,2048]{1,0:T(8,128)(2,1)} fusion(bf16[128,2048]{1,0:T(8,128)(2,1)S(1)} %multiply_convert_fusion.1, s32[1024]{0:T(1024)S(1)} %broadcast_clamp_fusion.1), kind=kCustom, calls=%fused_computation.3 | custom fusion | bytes 8392704 | tf_op jit(solution)/shard_map/jit(_take)/gather | solution.py:167
  137.4 98.3 %all_to_all.50 = bf16[16,64,2048]{2,1,0:T(8,128)(2,1)S(1)} all-to-all(bf16[16,64,2048]{2,1,0:T(8,128)(2,1)S(1)} %broadcast_select_fusion), channel_id=1, replica_groups=mesh['groups'=2,'ctx'=4,'eg'=4,'rep'=1] {'ctx','eg'}, dimensions={0} | all-to-all | bytes 8388608 | tf_op jit(solution)/shard_map/all_to_all | solution.py:169
  241.3 7.8 %convolution_convert_fusion = bf16[1024,2048]{1,0:T(8,128)(2,1)} fusion(bf16[1,384,2048]{2,1,0:T(8,128)(2,1)S(1)} %copy-done, f32[1024,384]{1,0:T(8,128)} %fusion.28, bf16[1024,2048]{1,0:T(8,128)(2,1)} %bitcast.190, bf16[1,2048,384]{2,1,0:T(8,128)(2,1)S(1)} %copy-done.14), kind=kOutput, calls=%fused_computation.27 | convolution fusion | flops 3225681920 | bytes 13107200 | tf_op jit(solution)/shard_map/dot_general | solution.py:51
  249.0 5.4 %all-to-all-start.5 = ((bf16[16,64,2048]{2,1,0:T(8,128)(2,1)}), bf16[16,64,2048]{2,1,0:T(8,128)(2,1)}, u32[]{:S(2)}, u32[]{:S(2)}) async-start(bf16[16,64,2048]{2,1,0:T(8,128)(2,1)} %bitcast.188), calls=%async_computation.5 | async-start | bytes 8388608 | tf_op jit(solution)/shard_map/all_to_all | solution.py:172
  254.8 92.1 %all-to-all-done.5 = bf16[16,64,2048]{2,1,0:T(8,128)(2,1)} async-done(((bf16[16,64,2048]{2,1,0:T(8,128)(2,1)}), bf16[16,64,2048]{2,1,0:T(8,128)(2,1)}, u32[]{:S(2)}, u32[]{:S(2)}) %all-to-all-start.5) | async-done | bytes 4194336 | tf_op jit(solution)/shard_map/all_to_all | solution.py:172
  347.0 11.6 %gather_fusion.2 = bf16[1024,2048]{1,0:T(8,128)(2,1)} fusion(bf16[1024,2048]{1,0:T(8,128)(2,1)} %bitcast.54, s32[1024]{0:T(1024)S(1)} %broadcast_clamp_fusion), kind=kCustom, calls=%fused_computation.4 | custom fusion | bytes 8392704 | tf_op jit(solution)/shard_map/jit(_take)/gather | solution.py:175
  358.5 8.8 %copy_select_fusion = bf16[128,8,2048]{2,0,1:T(8,128)(2,1)S(1)} fusion(bf16[128,8,2048]{2,1,0:T(8,128)(2,1)} %bitcast.187, pred[128,8]{0,1:T(8,128)(4,1)S(1)} %compare_and_fusion.1), kind=kLoop, calls=%fused_computation.25 | loop fusion | flops 2097152 | bytes 8389632 | tf_op jit(solution)/shard_map/jit(_take)/select_n | solution.py:175
  (118 shorter events, 45.2 us)
Async XLA Ops:
  7.2 234.1 %copy-start = (bf16[1,384,2048]{2,1,0:T(8,128)(2,1)S(1)}, bf16[1,384,2048]{2,1,0:T(8,128)(2,1)}, u32[]{:S(2)}) copy-start(bf16[1,384,2048]{2,1,0:T(8,128)(2,1)} %param.31) | copy-start | bytes 4718596
  7.2 8.5 %copy-start.11 = (s32[4,2]{0,1:T(2,128)S(1)}, s32[4,2]{0,1:T(2,128)}, u32[]{:S(2)}) copy-start(s32[4,2]{0,1:T(2,128)} %param.22) | copy-start | bytes 100
  7.2 24.8 %copy-start.7 = (bf16[1,128,256]{2,1,0:T(8,128)(2,1)S(1)}, bf16[1,128,256]{2,1,0:T(8,128)(2,1)}, u32[]{:S(2)}) copy-start(bf16[1,128,256]{2,1,0:T(8,128)(2,1)} %param.20) | copy-start | bytes 196612
  7.2 24.8 %copy-start.6 = (bf16[1,128,256]{2,1,0:T(8,128)(2,1)S(1)}, bf16[1,128,256]{2,1,0:T(8,128)(2,1)}, u32[]{:S(2)}) copy-start(bf16[1,128,256]{2,1,0:T(8,128)(2,1)} %param.21) | copy-start | bytes 196612
  7.2 8.1 %copy-start.9 = (s32[128,8]{0,1:T(8,128)S(1)}, s32[128,8]{0,1:T(8,128)}, u32[]{:S(2)}) copy-start(s32[128,8]{0,1:T(8,128)} %param.26) | copy-start | bytes 12292
  7.2 9.3 %copy-start.8 = (s32[16]{0:T(128)S(1)}, s32[16]{0:T(128)}, u32[]{:S(2)}) copy-start(s32[16]{0:T(128)} %param.28) | copy-start | bytes 196
  7.2 116.3 %all-gather.2.cloned.1.call-start = ((), (), s32[]{:S(2)}) async-start(), calls=%async_computation.6 | async-start | bytes 10485760 | tf_op jit(solution)/shard_map/all_gather | solution.py:143
  10.5 16.8 %all-to-all-start = ((bf16[4,128,256]{2,1,0:T(8,128)(2,1)}), bf16[4,128,256]{2,1,0:T(8,128)(2,1)S(1)}, u32[]{:S(2)}, u32[]{:S(2)}) async-start(bf16[4,128,256]{2,1,0:T(8,128)(2,1)} %get-tuple-element.111), calls=%async_computation | async-start | bytes 524288 | tf_op jit(solution)/shard_map/all_to_all | solution.py:114
  27.4 10.2 %all-to-all-start.2 = ((bf16[4,128,256]{2,1,0:T(8,128)(2,1)}), bf16[4,128,256]{2,1,0:T(8,128)(2,1)S(1)}, u32[]{:S(2)}, u32[]{:S(2)}) async-start(bf16[4,128,256]{2,1,0:T(8,128)(2,1)} %get-tuple-element.110), calls=%async_computation.2 | async-start | bytes 524288 | tf_op jit(solution)/shard_map/all_to_all | solution.py:115
  40.2 14.2 %copy-start.4 = (bf16[4,1,128,256]{3,2,1,0:T(8,128)(2,1)S(1)}, bf16[4,1,128,256]{3,2,1,0:T(8,128)(2,1)}, u32[]{:S(2)}) copy-start(bf16[4,1,128,256]{3,2,1,0:T(8,128)(2,1)} %get-tuple-element.106) | copy-start | bytes 786436
  41.2 24.6 %all-to-all-start.1 = ((bf16[4,3,128,256]{3,2,1,0:T(8,128)(2,1)}), bf16[4,3,128,256]{3,2,1,0:T(8,128)(2,1)S(1)}, u32[]{:S(2)}, u32[]{:S(2)}) async-start(bf16[4,3,128,256]{3,2,1,0:T(8,128)(2,1)} %pad_maximum_fusion), calls=%async_computation.1 | async-start | bytes 1572864 | tf_op jit(solution)/shard_map/all_to_all | solution.py:130
  65.8 17.7 %all-to-all-start.3 = ((bf16[4,3,128,256]{3,2,1,0:T(8,128)(2,1)}), bf16[4,3,128,256]{3,2,1,0:T(8,128)(2,1)S(1)}, u32[]{:S(2)}, u32[]{:S(2)}) async-start(bf16[4,3,128,256]{3,2,1,0:T(8,128)(2,1)} %pad_maximum_fusion.1), calls=%async_computation.3 | async-start | bytes 1572864 | tf_op jit(solution)/shard_map/all_to_all | solution.py:131
  84.7 38.8 %copy-start.2 = (bf16[128,2048]{1,0:T(8,128)(2,1)S(1)}, bf16[128,2048]{1,0:T(8,128)(2,1)}, u32[]{:S(2)}) copy-start(bf16[128,2048]{1,0:T(8,128)(2,1)} %param.24) | copy-start | bytes 1572868
  84.7 6.3 %copy-start.5 = (bf16[1536,2,128]{2,0,1:T(8,128)(2,1)S(1)}, bf16[1536,2,128]{2,0,1:T(8,128)(2,1)}, u32[]{:S(2)}) copy-start(bf16[1536,2,128]{2,0,1:T(8,128)(2,1)} %get-tuple-element.180) | copy-start | bytes 2359300 | tf_op jit(solution)/shard_map/while
  94.4 6.3 %copy-start.5 = (bf16[1536,2,128]{2,0,1:T(8,128)(2,1)S(1)}, bf16[1536,2,128]{2,0,1:T(8,128)(2,1)}, u32[]{:S(2)}) copy-start(bf16[1536,2,128]{2,0,1:T(8,128)(2,1)} %get-tuple-element.180) | copy-start | bytes 2359300 | tf_op jit(solution)/shard_map/while
  104.1 6.3 %copy-start.5 = (bf16[1536,2,128]{2,0,1:T(8,128)(2,1)S(1)}, bf16[1536,2,128]{2,0,1:T(8,128)(2,1)}, u32[]{:S(2)}) copy-start(bf16[1536,2,128]{2,0,1:T(8,128)(2,1)} %get-tuple-element.180) | copy-start | bytes 2359300 | tf_op jit(solution)/shard_map/while
  113.8 6.3 %copy-start.5 = (bf16[1536,2,128]{2,0,1:T(8,128)(2,1)S(1)}, bf16[1536,2,128]{2,0,1:T(8,128)(2,1)}, u32[]{:S(2)}) copy-start(bf16[1536,2,128]{2,0,1:T(8,128)(2,1)} %get-tuple-element.180) | copy-start | bytes 2359300 | tf_op jit(solution)/shard_map/while
  123.5 5.0 %copy-start.10 = (f32[2048]{0:T(1024)S(1)}, f32[2048]{0:T(1024)}, u32[]{:S(2)}) copy-start(f32[2048]{0:T(1024)} %param.25) | copy-start | bytes 24580
  128.5 6.3 %copy-start.3 = (bf16[128,2048]{1,0:T(8,128)(2,1)}, bf16[128,2048]{1,0:T(8,128)(2,1)S(1)}, u32[]{:S(2)}) copy-start(bf16[128,2048]{1,0:T(8,128)(2,1)S(1)} %get-tuple-element.113) | copy-start | bytes 1572868
  137.4 100.3 %copy-start.13 = (bf16[1,2048,384]{2,1,0:T(8,128)(2,1)S(1)}, bf16[1,2048,384]{2,1,0:T(8,128)(2,1)}, u32[]{:S(2)}) copy-start(bf16[1,2048,384]{2,1,0:T(8,128)(2,1)} %param.29) | copy-start | bytes 4718596
  235.7 2.0 copy-start.1
  237.7 3.6 copy-start.14
  249.0 5.7 %copy-start.12 = (f32[128,8]{0,1:T(8,128)S(1)}, f32[128,8]{0,1:T(8,128)}, u32[]{:S(2)}) copy-start(f32[128,8]{0,1:T(8,128)} %param.27) | copy-start | bytes 12292
  249.0 97.9 %all-to-all-start.5 = ((bf16[16,64,2048]{2,1,0:T(8,128)(2,1)}), bf16[16,64,2048]{2,1,0:T(8,128)(2,1)}, u32[]{:S(2)}, u32[]{:S(2)}) async-start(bf16[16,64,2048]{2,1,0:T(8,128)(2,1)} %bitcast.188), calls=%async_computation.5 | async-start | bytes 8388608 | tf_op jit(solution)/shard_map/all_to_all | solution.py:172
Sparse Core Ops, SparseCore 0:
  9.6 69.9 all-gather.1
where the time goes:
time: 377 us; the launch traced here: 376 us
  waiting for transfers between devices  111 us (29%)
  blocking collectives  98.3 us (26%)
  matrix products  42.7 us (11%)
  local copies, waits for them, and re-layouts  41.1 us (11%)
  other arithmetic  34.9 us (9%)
  starting transfers between devices  26.5 us (7%)
  between operations  14.4 us (4%)
  loops' own time  6.89 us (2%)
    all_to_all x1, blocking collectives, local(): lax.all_to_all(outbound, ('ctx', 'eg'), split_axis=0, concat_axis=0, tile...  98.3 us
    all_to_all x1, waiting for transfers between devices, local(): lax.all_to_all(produced.reshape(arrived.shape), ('ctx', 'eg'), split_axis...  92.1 us
    sub x4, matrix products, attend_pair(): raised = jnp.exp(logits - largest)  16.3 us
    gather x1, local copies, waits for them, and re-layouts, local(): jnp.take(returned.reshape(pair_count, -1), position, axis=0)  11.6 us
    all_to_all x1, waiting for transfers between devices, local(): lax.all_to_all(assemble(keys, far_keys), 'eg', split_axis=0, concat_axis=...  10.4 us
    dot_general x4, matrix products, attend_pair(): jnp.einsum('krgn,nkd->rkgd', weights_low, value_rows, preferred_element_t...  10.1 us
    select_n x2, other arithmetic, local(): jnp.take(returned.reshape(pair_count, -1), position, axis=0)  8.84 us
    dot_general x1, matrix products, expert_apply(): jnp.dot(activation, down_full, preferred_element_type=jnp.float32)  7.77 us
  transfers between devices with their start and end apart: 6, of which 4 were waited for; matrix products, arithmetic and copies ran while one was open for 18% of the time, Pallas kernels for 0%

commit v1 on v0

--- a/solution.py
+++ b/solution.py
@@ -164,13 +164,36 @@
         .at[position]
         .set(jnp.arange(pair_count, dtype=jnp.int32))
     )
-    outbound = jnp.take(normed, source_pair // top_count, axis=0).reshape(slot_count, per_slot, -1)
     partner = fetch_panels()
-    arrived = lax.all_to_all(outbound, ("ctx", "eg"), split_axis=0, concat_axis=0, tiled=True)
-    flat_rows = arrived.reshape(-1, arrived.shape[2])
+    if slot_count <= 4 * top_count:
+        my_slot = my_ctx * n_eg + lax.axis_index("eg")
+        all_normed = lax.all_gather(normed, ("ctx", "eg"), axis=0, tiled=True)
+        all_ids = lax.all_gather(expert_ids, ("ctx", "eg"), axis=0, tiled=True)
+        hits = jnp.any(jnp.take(expert_home, all_ids, axis=0) == my_slot, axis=1)
+        hits = hits.reshape(slot_count, tok_dev).astype(jnp.int32)
+        rank = jnp.cumsum(hits, axis=1) - 1
+        chosen = jnp.logical_and(
+            hits[:, None, :] == 1,
+            rank[:, None, :] == jnp.arange(per_slot, dtype=jnp.int32)[None, :, None],
+        )
+        local_row = jnp.sum(
+            chosen.astype(jnp.int32) * jnp.arange(tok_dev, dtype=jnp.int32)[None, None, :], axis=2
+        )
+        src_rows = local_row + jnp.arange(slot_count, dtype=jnp.int32)[:, None] * tok_dev
+        flat_rows = jnp.take(all_normed, src_rows.reshape(-1), axis=0)
+    else:
+        outbound = jnp.take(normed, source_pair // top_count, axis=0).reshape(
+            slot_count, per_slot, -1
+        )
+        arrived = lax.all_to_all(outbound, ("ctx", "eg"), split_axis=0, concat_axis=0, tiled=True)
+        flat_rows = arrived.reshape(-1, arrived.shape[2])
     produced = expert_apply(flat_rows, partner[0], partner[1], partner[2])
     returned = lax.all_to_all(
-        produced.reshape(arrived.shape), ("ctx", "eg"), split_axis=0, concat_axis=0, tiled=True
+        produced.reshape(slot_count, per_slot, -1),
+        ("ctx", "eg"),
+        split_axis=0,
+        concat_axis=0,
+        tiled=True,
     )
     answers = jnp.take(returned.reshape(pair_count, -1), position, axis=0).reshape(
         tok_dev, top_count, -1

time: 377 us -> 363 us (0.963)
  blocking collectives: 98.3 us -> 16.7 us
  waiting for transfers between devices: 111 us -> 161 us
  other arithmetic: 34.9 us -> 44.7 us
  matrix products: 42.7 us -> 47.2 us
    all_to_all x1 -> x0, blocking collectives: 98.3 us -> none  [local(): lax.all_to_all(outbound, ('ctx', 'eg'), split_axis=0, concat_axis=0, tile...]
    all_gather x0 -> x1, waiting for transfers between devices: none -> 46.5 us  [local(): all_normed = lax.all_gather(normed, ('ctx', 'eg'), axis=0, tiled=True)]
    all_gather x0 -> x1, blocking collectives: none -> 16.7 us  [local(): all_ids = lax.all_gather(expert_ids, ('ctx', 'eg'), axis=0, tiled=True)]
    all_to_all x1, waiting for transfers between devices: 92.1 us -> 76.7 us  [local(): lax.all_to_all(produced.reshape(slot_count, per_slot, -1), ('ctx', 'eg'),...]
    reduce_or x0 -> x1, other arithmetic: none -> 9.99 us  [local(): hits = jnp.any(jnp.take(expert_home, all_ids, axis=0) == my_slot, axis=1)]
    all_to_all x1, waiting for transfers between devices: 3.81 us -> 11.3 us  [local(): lax.all_to_all(assemble(values, far_values), 'eg', split_axis=0, concat_a...]
    gather x1, local copies, waits for them, and re-layouts: 6.02 us -> 13.3 us  [local(): flat_rows = jnp.take(all_normed, src_rows.reshape(-1), axis=0)]
    all_to_all x1, waiting for transfers between devices: 10.4 us -> 16.4 us  [local(): lax.all_to_all(assemble(keys, far_keys), 'eg', split_axis=0, concat_axis=...]
  transfers between devices with their start and end apart: 6 -> 7, of which waited for: 4 -> 6; matrix products, arithmetic and copies ran while one was open for 18% -> 21% of each run, Pallas kernels for 0% -> 0%
where the time goes in v1:
time: 363 us; the launch traced here: 361 us
  waiting for transfers between devices  161 us (44%)
  matrix products  47.2 us (13%)
  other arithmetic  44.7 us (12%)
  local copies, waits for them, and re-layouts  42.1 us (12%)
  starting transfers between devices  28.6 us (8%)
  blocking collectives  16.7 us (5%)
  between operations  14.4 us (4%)
  loops' own time  6.89 us (2%)
    all_to_all x1, waiting for transfers between devices, local(): lax.all_to_all(produced.reshape(slot_count, per_slot, -1), ('ctx', 'eg'),...  76.7 us
    all_gather x1, waiting for transfers between devices, local(): all_normed = lax.all_gather(normed, ('ctx', 'eg'), axis=0, tiled=True)  46.5 us
    all_gather x1, blocking collectives, local(): all_ids = lax.all_gather(expert_ids, ('ctx', 'eg'), axis=0, tiled=True)  16.7 us
    all_to_all x1, waiting for transfers between devices, local(): lax.all_to_all(assemble(keys, far_keys), 'eg', split_axis=0, concat_axis=...  16.4 us
    sub x4, matrix products, attend_pair(): raised = jnp.exp(logits - largest)  16.3 us
    gather x1, local copies, waits for them, and re-layouts, local(): flat_rows = jnp.take(all_normed, src_rows.reshape(-1), axis=0)  13.3 us
    gather x1, local copies, waits for them, and re-layouts, local(): jnp.take(returned.reshape(pair_count, -1), position, axis=0)  11.6 us
    all_to_all x1, waiting for transfers between devices, local(): lax.all_to_all(assemble(values, far_values), 'eg', split_axis=0, concat_a...  11.3 us
  transfers between devices with their start and end apart: 7, of which 6 were waited for; matrix products, arithmetic and copies ran while one was open for 21% of the time, Pallas kernels for 0%

profile of v1, /device:TPU:11, one launch (start us, length us, event | category | flops | bytes accessed | tf_op | source)
XLA Modules:
  0.0 361.3 jit_solution(17848309234385541498)
XLA Ops:
  10.5 4.8 %all-to-all-start = ((bf16[4,128,256]{2,1,0:T(8,128)(2,1)}), bf16[4,128,256]{2,1,0:T(8,128)(2,1)S(1)}, u32[]{:S(2)}, u32[]{:S(2)}) async-start(bf16[4,128,256]{2,1,0:T(8,128)(2,1)} %get-tuple-element.117), calls=%async_computation | async-start | bytes 524288 | tf_op jit(solution)/shard_map/all_to_all | solution.py:114
  16.2 5.2 %all-to-all-done = bf16[4,128,256]{2,1,0:T(8,128)(2,1)S(1)} async-done(((bf16[4,128,256]{2,1,0:T(8,128)(2,1)}), bf16[4,128,256]{2,1,0:T(8,128)(2,1)S(1)}, u32[]{:S(2)}, u32[]{:S(2)}) %all-to-all-start) | async-done | bytes 262176 | tf_op jit(solution)/shard_map/all_to_all | solution.py:114
  21.4 4.9 %all-to-all-start.2 = ((bf16[4,128,256]{2,1,0:T(8,128)(2,1)}), bf16[4,128,256]{2,1,0:T(8,128)(2,1)S(1)}, u32[]{:S(2)}, u32[]{:S(2)}) async-start(bf16[4,128,256]{2,1,0:T(8,128)(2,1)} %get-tuple-element.116), calls=%async_computation.2 | async-start | bytes 524288 | tf_op jit(solution)/shard_map/all_to_all | solution.py:115
  35.2 7.1 %all-to-all-start.1 = ((bf16[4,3,128,256]{3,2,1,0:T(8,128)(2,1)}), bf16[4,3,128,256]{3,2,1,0:T(8,128)(2,1)S(1)}, u32[]{:S(2)}, u32[]{:S(2)}) async-start(bf16[4,3,128,256]{3,2,1,0:T(8,128)(2,1)} %pad_maximum_fusion), calls=%async_computation.1 | async-start | bytes 1572864 | tf_op jit(solution)/shard_map/all_to_all | solution.py:130
  44.2 16.4 %all-to-all-done.1 = bf16[4,3,128,256]{3,2,1,0:T(8,128)(2,1)S(1)} async-done(((bf16[4,3,128,256]{3,2,1,0:T(8,128)(2,1)}), bf16[4,3,128,256]{3,2,1,0:T(8,128)(2,1)S(1)}, u32[]{:S(2)}, u32[]{:S(2)}) %all-to-all-start.1) | async-done | bytes 786464 | tf_op jit(solution)/shard_map/all_to_all | solution.py:130
  60.7 5.5 %all-to-all-start.3 = ((bf16[4,3,128,256]{3,2,1,0:T(8,128)(2,1)}), bf16[4,3,128,256]{3,2,1,0:T(8,128)(2,1)S(1)}, u32[]{:S(2)}, u32[]{:S(2)}) async-start(bf16[4,3,128,256]{3,2,1,0:T(8,128)(2,1)} %pad_maximum_fusion.1), calls=%async_computation.3 | async-start | bytes 1572864 | tf_op jit(solution)/shard_map/all_to_all | solution.py:131
  72.1 11.3 %all-to-all-done.3 = bf16[4,3,128,256]{3,2,1,0:T(8,128)(2,1)S(1)} async-done(((bf16[4,3,128,256]{3,2,1,0:T(8,128)(2,1)}), bf16[4,3,128,256]{3,2,1,0:T(8,128)(2,1)S(1)}, u32[]{:S(2)}, u32[]{:S(2)}) %all-to-all-start.3) | async-done | bytes 786464 | tf_op jit(solution)/shard_map/all_to_all | solution.py:131
  84.7 38.8 %while.10 = (s32[]{:T(128)}, bf16[4,128,2,2,128]{1,4,3,0,2:T(8,128)(2,1)}, s32[4]{0:T(128)S(1)}, bf16[128,2,4,2,128]{0,4,3,2,1:T(8,128)(2,1)}, bf16[1536,2,128]{...) while((s32[]{:T(128)}, bf16[4,128,2,2,128]{1,4,3,0,2:T(8,128)(2,1)}, ...), condition=%wide.region_4.7_spmd, body=%wide.region_1.6_spmd.sunk | while | flops 406652416 | bytes 11801259 | solution.py:43
  87.0 4.1 %fusion.71 = (f32[2,128,2]{1,2,0:T(2,128)S(1)}, f32[2,128,2,1536]{3,1,2,0:T(8,128)}) fusion(bf16[1536,2,128]{2,0,1:T(8,128)(2,1)} %get-tuple-element.185, bf16[128,2,4,2,128]{0,4,3,2,1:T(8,128)(2,1)} %get-tuple-element.184, s32[]{:T(128)S(6)} %select_n.288), kind=kOutput, calls=%fused_computation.156.clone.1 | convolution fusion | flops 203687424 | bytes 4065284 | tf_op jit(solution)/shard_map/while/body/eval_jaxpr/sub | solution.py:23
  116.0 4.1 %fusion.71 = (f32[2,128,2]{1,2,0:T(2,128)S(1)}, f32[2,128,2,1536]{3,1,2,0:T(8,128)}) fusion(bf16[1536,2,128]{2,0,1:T(8,128)(2,1)} %get-tuple-element.185, bf16[128,2,4,2,128]{0,4,3,2,1:T(8,128)(2,1)} %get-tuple-element.184, s32[]{:T(128)S(6)} %select_n.288), kind=kOutput, calls=%fused_computation.156.clone.1 | convolution fusion | flops 203687424 | bytes 4065284 | tf_op jit(solution)/shard_map/while/body/eval_jaxpr/sub | solution.py:23
  123.5 5.0 %multiply_reduce_fusion = (f32[128]{0:T(128)S(1)}, bf16[128,2048]{1,0:T(8,128)(2,1)S(1)}) fusion(bf16[128,2048]{1,0:T(8,128)(2,1)S(1)} %copy-done.1, bf16[128,2048]{0,1:T(8,128)(2,1)} %bitcast.193, bf16[2048,2048]{1,0:T(8,128)(2,1)} %all-gather.3.cloned.1.call-done), kind=kOutput, calls=%fused_computation.51 | convolution fusion | flops 1075314560 | bytes 9961984 | tf_op jit(solution)/shard_map/dot_general | solution.py:141
  129.5 16.7 %all_gather.10 = s32[2048,8]{0,1:T(8,128)S(1)} all-gather(s32[128,8]{0,1:T(8,128)S(1)} %copy-done.7), channel_id=1, replica_groups=mesh['groups'=2,'ctx'=4,'eg'=4,'rep'=1] {'ctx','eg'}, dimensions={0}, use_global_device_ids=true | all-gather | bytes 69632 | tf_op jit(solution)/shard_map/all_gather | solution.py:171
  147.0 10.0 %fusion.48 = pred[2048]{0:T(1024)(128)(4,1)S(1)} fusion(s32[2048,8]{0,1:T(8,128)S(1)} %all_gather.10, s32[]{:T(128)} %bitcast.25, s32[]{:T(128)} %bitcast.26, s32[]{:T(128)} %bitcast.27, s32[]{:T(128)} %bitcast.28, s32[]{:T(128)} %bitcast.29, s32[]{:T(128)} %bitcast.30, s32[]{:T(128)} %bitcast.31, s32[]{:T(128)} %bitcast.32, s32[]{:T(128)} %bitcast.33, ...), kind=kLoop, calls=%fused_computation.83 | loop fusion | flops 636928 | bytes 67652 | tf_op jit(solution)/shard_map/reduce_or | solution.py:172
  157.9 46.5 %all-gather.5.cloned.1.call-done = bf16[2048,2048]{1,0:T(8,128)(2,1)} async-done(((bf16[128,2048]{1,0:T(8,128)(2,1)}), bf16[2048,2048]{1,0:T(8,128)(2,1)}) %all-gather.5.cloned.1.call-update) | async-done | bytes 8388624 | tf_op jit(solution)/shard_map/all_gather | solution.py:170
  204.4 13.3 %gather_fusion.1 = bf16[1024,2048]{1,0:T(8,128)(2,1)} fusion(bf16[2048,2048]{1,0:T(8,128)(2,1)} %all-gather.5.cloned.1.call-done, s32[1024]{0:T(1024)S(1)} %broadcast_clamp_fusion.1), kind=kCustom, calls=%fused_computation.3 | custom fusion | bytes 8392704 | tf_op jit(solution)/shard_map/jit(_take)/gather | solution.py:183
  217.7 6.2 %fusion.26 = f32[1024,384]{1,0:T(8,128)} fusion(bf16[1024,2048]{1,0:T(8,128)(2,1)} %gather_fusion.1, pred[1024]{0:T(1024)(128)(4,1)S(1)} %compare_and_fusion, bf16[1,2048,384]{2,1,0:T(8,128)(2,1)} %param.29), kind=kOutput, calls=%fused_computation.29 | convolution fusion | flops 1612709888 | bytes 7341056 | tf_op jit(solution)/shard_map/dot_general | solution.py:48
  223.9 9.6 %convolution_convert_fusion = bf16[1024,2048]{1,0:T(8,128)(2,1)} fusion(bf16[1,384,2048]{2,1,0:T(8,128)(2,1)S(1)} %copy-done, f32[1024,384]{1,0:T(8,128)} %fusion.26, bf16[1,2048,384]{2,1,0:T(8,128)(2,1)} %param.30, bf16[1024,2048]{1,0:T(8,128)(2,1)} %gather_fusion.1, pred[1024]{0:T(1024)(128)(4,1)S(1)} %compare_and_fusion), kind=kOutput, calls=%fused_computation.26 | convolution fusion | flops 3227779072 | bytes 13108224 | tf_op jit(solution)/shard_map/dot_general | solution.py:51
  233.5 6.4 %all-to-all-start.4 = ((bf16[16,64,2048]{2,1,0:T(8,128)(2,1)}), bf16[16,64,2048]{2,1,0:T(8,128)(2,1)}, u32[]{:S(2)}, u32[]{:S(2)}) async-start(bf16[16,64,2048]{2,1,0:T(8,128)(2,1)} %bitcast.188), calls=%async_computation.4 | async-start | bytes 8388608 | tf_op jit(solution)/shard_map/all_to_all | solution.py:191
  240.3 4.3 %compare_select_fusion.4 = (s32[1024,1]{0,1:T(1,128)S(1)}, s32[1024,1]{0,1:T(1,128)S(1)}) fusion(s32[]{:T(128)} %bitcast.34, s32[]{:T(128)} %bitcast.35, s32[]{:T(128)} %bitcast.36, s32[]{:T(128)} %bitcast.37, s32[]{:T(128)} %bitcast.38, s32[]{:T(128)} %bitcast.40, s32[]{:T(128)} %bitcast.39, s32[1024,1]{0,1:T(1,128)S(1)} %reshape.377), kind=kLoop, calls=%fused_computation.96 | loop fusion | flops 15360 | bytes 12316 | tf_op jit(solution)/shard_map/jit(_take)/gather | solution.py:156
  244.7 5.6 %and_select_fusion.1 = (s32[1024]{0:T(1024)S(1)}, s32[1024]{0:T(1024)S(1)}) fusion(s32[1024]{0:T(1024)S(1)} %reshape.378, pred[1024]{0:T(1024)(128)(4,1)S(1)} %get-tuple-element.69, pred[1024]{0:T(1024)(128)(4,1)S(1)} %get-tuple-element.67, pred[1024]{0:T(1024)(128)(4,1)S(1)} %get-tuple-element.68, pred[1024]{0:T(1024)(128)(4,1)S(1)} %get-tuple-element.66, ...), kind=kLoop, calls=%fused_computation.118 | loop fusion | flops 16384 | bytes 25636 | tf_op jit(solution)/shard_map/jit(_take)/select_n | solution.py:156
  250.4 4.5 %reduce-window.6 = s32[16,8,128]{2,1,0:T(8,128)S(1)} reduce-window(s32[16,8,128]{2,1,0:T(8,128)S(1)} %fusion.47, s32[]{:T(128)} %constant.170.clone.1), window={size=1x1x128 pad=0_0x0_0x127_0}, to_apply=%region_5.8 | reduce-window | flops 2080768 | bytes 131076 | tf_op jit(solution)/shard_map/reduce-window
  255.7 76.7 %all-to-all-done.4 = bf16[16,64,2048]{2,1,0:T(8,128)(2,1)} async-done(((bf16[16,64,2048]{2,1,0:T(8,128)(2,1)}), bf16[16,64,2048]{2,1,0:T(8,128)(2,1)}, u32[]{:S(2)}, u32[]{:S(2)}) %all-to-all-start.4) | async-done | bytes 4194336 | tf_op jit(solution)/shard_map/all_to_all | solution.py:191
  332.4 11.6 %gather_fusion.2 = bf16[1024,2048]{1,0:T(8,128)(2,1)} fusion(bf16[1024,2048]{1,0:T(8,128)(2,1)} %bitcast.51, s32[1024]{0:T(1024)S(1)} %broadcast_clamp_fusion), kind=kCustom, calls=%fused_computation.4 | custom fusion | bytes 8392704 | tf_op jit(solution)/shard_map/jit(_take)/gather | solution.py:198
  343.9 8.8 %copy_select_fusion = bf16[128,8,2048]{2,0,1:T(8,128)(2,1)S(1)} fusion(bf16[128,8,2048]{2,1,0:T(8,128)(2,1)} %bitcast.187, pred[128,8]{0,1:T(8,128)(4,1)S(1)} %compare_and_fusion.1), kind=kLoop, calls=%fused_computation.24 | loop fusion | flops 2097152 | bytes 8389632 | tf_op jit(solution)/shard_map/jit(_take)/select_n | solution.py:198
  (120 shorter events, 51.6 us)
Async XLA Ops:
  7.2 216.7 %copy-start = (bf16[1,384,2048]{2,1,0:T(8,128)(2,1)S(1)}, bf16[1,384,2048]{2,1,0:T(8,128)(2,1)}, u32[]{:S(2)}) copy-start(bf16[1,384,2048]{2,1,0:T(8,128)(2,1)} %param.31) | copy-start | bytes 4718596
  7.2 8.1 %copy-start.9 = (s32[4,2]{0,1:T(2,128)S(1)}, s32[4,2]{0,1:T(2,128)}, u32[]{:S(2)}) copy-start(s32[4,2]{0,1:T(2,128)} %param.22) | copy-start | bytes 100
  7.2 19.1 %copy-start.5 = (bf16[1,128,256]{2,1,0:T(8,128)(2,1)S(1)}, bf16[1,128,256]{2,1,0:T(8,128)(2,1)}, u32[]{:S(2)}) copy-start(bf16[1,128,256]{2,1,0:T(8,128)(2,1)} %param.20) | copy-start | bytes 196612
  7.2 19.1 %copy-start.4 = (bf16[1,128,256]{2,1,0:T(8,128)(2,1)S(1)}, bf16[1,128,256]{2,1,0:T(8,128)(2,1)}, u32[]{:S(2)}) copy-start(bf16[1,128,256]{2,1,0:T(8,128)(2,1)} %param.21) | copy-start | bytes 196612
  7.2 116.3 %all-gather.3.cloned.1.call-start = ((), (), s32[]{:S(2)}) async-start(), calls=%async_computation.5 | async-start | bytes 10485760 | tf_op jit(solution)/shard_map/all_gather | solution.py:143
  10.5 10.8 %all-to-all-start = ((bf16[4,128,256]{2,1,0:T(8,128)(2,1)}), bf16[4,128,256]{2,1,0:T(8,128)(2,1)S(1)}, u32[]{:S(2)}, u32[]{:S(2)}) async-start(bf16[4,128,256]{2,1,0:T(8,128)(2,1)} %get-tuple-element.117), calls=%async_computation | async-start | bytes 524288 | tf_op jit(solution)/shard_map/all_to_all | solution.py:114
  21.4 10.2 %all-to-all-start.2 = ((bf16[4,128,256]{2,1,0:T(8,128)(2,1)}), bf16[4,128,256]{2,1,0:T(8,128)(2,1)S(1)}, u32[]{:S(2)}, u32[]{:S(2)}) async-start(bf16[4,128,256]{2,1,0:T(8,128)(2,1)} %get-tuple-element.116), calls=%async_computation.2 | async-start | bytes 524288 | tf_op jit(solution)/shard_map/all_to_all | solution.py:115
  35.2 25.5 %all-to-all-start.1 = ((bf16[4,3,128,256]{3,2,1,0:T(8,128)(2,1)}), bf16[4,3,128,256]{3,2,1,0:T(8,128)(2,1)S(1)}, u32[]{:S(2)}, u32[]{:S(2)}) async-start(bf16[4,3,128,256]{3,2,1,0:T(8,128)(2,1)} %pad_maximum_fusion), calls=%async_computation.1 | async-start | bytes 1572864 | tf_op jit(solution)/shard_map/all_to_all | solution.py:130
  60.7 22.8 %all-to-all-start.3 = ((bf16[4,3,128,256]{3,2,1,0:T(8,128)(2,1)}), bf16[4,3,128,256]{3,2,1,0:T(8,128)(2,1)S(1)}, u32[]{:S(2)}, u32[]{:S(2)}) async-start(bf16[4,3,128,256]{3,2,1,0:T(8,128)(2,1)} %pad_maximum_fusion.1), calls=%async_computation.3 | async-start | bytes 1572864 | tf_op jit(solution)/shard_map/all_to_all | solution.py:131
  66.1 138.2 %all-gather.5.cloned.1.call-start = ((), (), s32[]{:S(2)}) async-start(), calls=%async_computation.6 | async-start | bytes 8912896 | tf_op jit(solution)/shard_map/all_gather | solution.py:170
  84.7 38.8 %copy-start.1 = (bf16[128,2048]{1,0:T(8,128)(2,1)S(1)}, bf16[128,2048]{1,0:T(8,128)(2,1)}, u32[]{:S(2)}) copy-start(bf16[128,2048]{1,0:T(8,128)(2,1)} %param.24) | copy-start | bytes 1572868
  84.7 6.3 %copy-start.3 = (bf16[1536,2,128]{2,0,1:T(8,128)(2,1)S(1)}, bf16[1536,2,128]{2,0,1:T(8,128)(2,1)}, u32[]{:S(2)}) copy-start(bf16[1536,2,128]{2,0,1:T(8,128)(2,1)} %get-tuple-element.186) | copy-start | bytes 2359300 | tf_op jit(solution)/shard_map/while
  94.4 6.3 %copy-start.3 = (bf16[1536,2,128]{2,0,1:T(8,128)(2,1)S(1)}, bf16[1536,2,128]{2,0,1:T(8,128)(2,1)}, u32[]{:S(2)}) copy-start(bf16[1536,2,128]{2,0,1:T(8,128)(2,1)} %get-tuple-element.186) | copy-start | bytes 2359300 | tf_op jit(solution)/shard_map/while
  104.1 6.3 %copy-start.3 = (bf16[1536,2,128]{2,0,1:T(8,128)(2,1)S(1)}, bf16[1536,2,128]{2,0,1:T(8,128)(2,1)}, u32[]{:S(2)}) copy-start(bf16[1536,2,128]{2,0,1:T(8,128)(2,1)} %get-tuple-element.186) | copy-start | bytes 2359300 | tf_op jit(solution)/shard_map/while
  113.8 6.3 %copy-start.3 = (bf16[1536,2,128]{2,0,1:T(8,128)(2,1)S(1)}, bf16[1536,2,128]{2,0,1:T(8,128)(2,1)}, u32[]{:S(2)}) copy-start(bf16[1536,2,128]{2,0,1:T(8,128)(2,1)} %get-tuple-element.186) | copy-start | bytes 2359300 | tf_op jit(solution)/shard_map/while
  123.5 5.0 %copy-start.8 = (f32[2048]{0:T(1024)S(1)}, f32[2048]{0:T(1024)}, u32[]{:S(2)}) copy-start(f32[2048]{0:T(1024)} %param.25) | copy-start | bytes 24580
  123.5 6.1 %copy-start.7 = (s32[128,8]{0,1:T(8,128)S(1)}, s32[128,8]{0,1:T(8,128)}, u32[]{:S(2)}) copy-start(s32[128,8]{0,1:T(8,128)} %param.26) | copy-start | bytes 12292
  123.5 22.8 %copy-start.6 = (s32[16]{0:T(128)S(1)}, s32[16]{0:T(128)}, u32[]{:S(2)}) copy-start(s32[16]{0:T(128)} %param.28) | copy-start | bytes 196
  128.5 89.2 %copy-start.2 = (bf16[128,2048]{1,0:T(8,128)(2,1)}, bf16[128,2048]{1,0:T(8,128)(2,1)S(1)}, u32[]{:S(2)}) copy-start(bf16[128,2048]{1,0:T(8,128)(2,1)S(1)} %get-tuple-element.119) | copy-start | bytes 1572868
  233.5 22.1 %copy-start.10 = (f32[128,8]{0,1:T(8,128)S(1)}, f32[128,8]{0,1:T(8,128)}, u32[]{:S(2)}) copy-start(f32[128,8]{0,1:T(8,128)} %param.27) | copy-start | bytes 12292
  233.5 98.9 %all-to-all-start.4 = ((bf16[16,64,2048]{2,1,0:T(8,128)(2,1)}), bf16[16,64,2048]{2,1,0:T(8,128)(2,1)}, u32[]{:S(2)}, u32[]{:S(2)}) async-start(bf16[16,64,2048]{2,1,0:T(8,128)(2,1)} %bitcast.188), calls=%async_computation.4 | async-start | bytes 8388608 | tf_op jit(solution)/shard_map/all_to_all | solution.py:191
Sparse Core Ops, SparseCore 0:
  9.6 74.9 all-gather.2
  129.7 74.6 all-gather.4

commit v2 on v1

--- a/solution.py
+++ b/solution.py
@@ -96,40 +96,22 @@
     shard_blocks, slice_rows, kv_width = keys.shape
     pick_count = selected.shape[1]
     block_rows = slice_rows * n_eg
-    listed = selected.reshape(n_ctx, shard_blocks * pick_count)
-    owned_here = listed // shard_blocks == my_ctx
-    block_match = (listed % shard_blocks)[:, :, None] == jnp.arange(shard_blocks, dtype=jnp.int32)[
-        None, None, :
-    ]
-    request = jnp.max(
-        jnp.logical_and(owned_here[:, :, None], block_match).astype(jnp.int32), axis=1
-    ).astype(jnp.bfloat16)
-    outgoing_keys = jnp.einsum(
-        "cb,btw->ctw", request, keys, preferred_element_type=jnp.float32
-    ).astype(jnp.bfloat16)
-    outgoing_values = jnp.einsum(
-        "cb,btw->ctw", request, values, preferred_element_type=jnp.float32
-    ).astype(jnp.bfloat16)
-    far_keys, far_values = (
-        lax.all_to_all(outgoing_keys, "ctx", split_axis=0, concat_axis=0, tiled=True),
-        lax.all_to_all(outgoing_values, "ctx", split_axis=0, concat_axis=0, tiled=True),
+    my_eg = lax.axis_index("eg")
+    both = jnp.concatenate([keys, values], axis=2)
+    gathered = lax.all_gather(both[None], ("ctx", "eg"), axis=0, tiled=True)
+    every_block = (
+        gathered.reshape(n_ctx, n_eg, shard_blocks, slice_rows, 2 * kv_width)
+        .transpose(0, 2, 1, 3, 4)
+        .reshape(n_ctx * shard_blocks, block_rows, 2 * kv_width)
     )
     query_rows = queries.shape[0]
-    peer_ids = jnp.arange(n_eg, dtype=jnp.int32)
-    own_block = peer_ids * query_rows // block_rows
-    peer_lists = jnp.take(selected, my_ctx * shard_blocks + own_block, axis=0) // shard_blocks
-
-    def assemble(local_part, fetched):
-        own_rows = jnp.take(local_part, own_block, axis=0)[:, None]
-        far_rows = jnp.take(fetched, peer_lists.reshape(-1), axis=0).reshape(
-            n_eg, pick_count, slice_rows, kv_width
-        )
-        return jnp.concatenate([own_rows, far_rows], axis=1)
-
-    context_keys, context_values = (
-        lax.all_to_all(assemble(keys, far_keys), "eg", split_axis=0, concat_axis=2, tiled=True),
-        lax.all_to_all(assemble(values, far_values), "eg", split_axis=0, concat_axis=2, tiled=True),
-    )
+    my_block = (my_ctx * n_eg + my_eg) * query_rows // block_rows
+    chosen_blocks = jnp.concatenate(
+        [my_block[None].astype(jnp.int32), jnp.take(selected, my_block, axis=0)]
+    )
+    context = jnp.take(every_block, chosen_blocks, axis=0)
+    context_keys = context[:, :, :kv_width]
+    context_values = context[:, :, kv_width:]
     span = (1 + pick_count) * block_rows
     kv_heads = kv_width // HD
     attended = attend_rows(
@@ -138,11 +120,19 @@
         context_values.reshape(span, kv_heads, HD),
     )
     tok_dev = residual.shape[0]
-    partial_out = jnp.dot(
-        attended,
-        lax.all_gather(out_weight, "eg", axis=1, tiled=True),
-        preferred_element_type=jnp.float32,
-    )
+    pieces = {0: out_weight}
+    for bit in reversed(range(n_eg.bit_length() - 1)):
+        stride = 2**bit
+        held = sorted(pieces)
+        fetched = swapped(tuple(pieces[m] for m in held), "eg", bit)
+        for m, piece in zip(held, fetched):
+            pieces[m + stride] = piece
+    weight_cols = jnp.concatenate([pieces[m] for m in range(n_eg)], axis=1)
+    out_by_piece = jnp.dot(attended, weight_cols, preferred_element_type=jnp.float32).reshape(
+        query_rows, n_eg, -1
+    )
+    piece_of_col = jnp.arange(n_eg, dtype=jnp.int32) ^ my_eg
+    partial_out = jnp.take(out_by_piece, piece_of_col, axis=1).reshape(query_rows, -1)
     attn_out = lax.psum_scatter(
         partial_out.astype(jnp.bfloat16), "rep", scatter_dimension=0, tiled=True
     )
@@ -166,10 +156,19 @@
     )
     partner = fetch_panels()
     if slot_count <= 4 * top_count:
-        my_slot = my_ctx * n_eg + lax.axis_index("eg")
-        all_normed = lax.all_gather(normed, ("ctx", "eg"), axis=0, tiled=True)
-        all_ids = lax.all_gather(expert_ids, ("ctx", "eg"), axis=0, tiled=True)
-        hits = jnp.any(jnp.take(expert_home, all_ids, axis=0) == my_slot, axis=1)
+        my_slot = my_ctx * n_eg + my_eg
+        width = normed.shape[1]
+        id_cols = jnp.full((tok_dev, 128), -1.0, jnp.bfloat16)
+        id_cols = id_cols.at[:, :top_count].set(expert_ids.astype(jnp.bfloat16))
+        packed = jnp.concatenate([normed, id_cols], axis=1)
+        all_packed = lax.all_gather(packed, ("ctx", "eg"), axis=0, tiled=True)
+        all_normed = all_packed[:, :width]
+        all_ids = all_packed[:, width : width + top_count].astype(jnp.int32)
+        expert_count = expert_home.shape[0]
+        my_expert = jnp.sum(
+            jnp.where(expert_home == my_slot, jnp.arange(expert_count, dtype=jnp.int32), 0)
+        )
+        hits = jnp.any(all_ids == my_expert, axis=1)
         hits = hits.reshape(slot_count, tok_dev).astype(jnp.int32)
         rank = jnp.cumsum(hits, axis=1) - 1
         chosen = jnp.logical_and(

time: 363 us -> 386 us (1.063)
  waiting for transfers between devices: 161 us -> 200 us
  local copies, waits for them, and re-layouts: 42.1 us -> 63.1 us
  starting transfers between devices: 28.6 us -> 9.43 us
  blocking collectives: 16.7 us -> 0 us
    ppermute x0 -> x3, waiting for transfers between devices: none -> 47.3 us  [swapped(): return lax.ppermute(value, axis, pairs)]
    all_to_all x4 -> x0, waiting for transfers between devices: 36.9 us -> none  [the longest x1 16.4 us: local(): lax.all_to_all(assemble(keys, far_keys), 'eg', split_axis=0, concat_axis=...]
    all_gather x2, waiting for transfers between devices: 46.5 us -> 77.1 us  [the longest x1 77.1 us: local(): all_packed = lax.all_gather(packed, ('ctx', 'eg'), axis=0, tiled=True)]
    all_to_all x4 -> x0, starting transfers between devices: 22.2 us -> none  [the longest x1 7.11 us: local(): lax.all_to_all(assemble(keys, far_keys), 'eg', split_axis=0, concat_axis=...]
    all_gather x1 -> x0, blocking collectives: 16.7 us -> none  [local(): all_ids = lax.all_gather(expert_ids, ('ctx', 'eg'), axis=0, tiled=True)]
    dot_general x0 -> x1, local copies, waits for them, and re-layouts: none -> 12.4 us  [local(): jnp.dot(attended, weight_cols, preferred_element_type=jnp.float32)]
    slice x2, local copies, waits for them, and re-layouts: 0.21 us -> 9.26 us  [the longest x1 8.27 us: local(): all_normed = all_packed[:, :width]]
    reduce_or x1, other arithmetic: 9.99 us -> 2.04 us  [local(): hits = jnp.any(all_ids == my_expert, axis=1)]
  transfers between devices with their start and end apart: 7 -> 6, of which waited for: 6 -> 3; matrix products, arithmetic and copies ran while one was open for 21% -> 16% of each run, Pallas kernels for 0% -> 0%
where the time goes in v2:
time: 386 us; the launch traced here: 385 us
  waiting for transfers between devices  200 us (52%)
  local copies, waits for them, and re-layouts  63.1 us (16%)
  matrix products  46.8 us (12%)
  other arithmetic  42.3 us (11%)
  between operations  14.4 us (4%)
  starting transfers between devices  9.43 us (2%)
  loops' own time  8.35 us (2%)
    all_gather x1, waiting for transfers between devices, local(): all_packed = lax.all_gather(packed, ('ctx', 'eg'), axis=0, tiled=True)  77.1 us
    all_to_all x1, waiting for transfers between devices, local(): lax.all_to_all(produced.reshape(slot_count, per_slot, -1), ('ctx', 'eg'),...  75.9 us
    ppermute x3, waiting for transfers between devices, swapped(): return lax.ppermute(value, axis, pairs)  47.3 us
    sub x4, matrix products, attend_pair(): raised = jnp.exp(logits - largest)  15.9 us
    gather x1, local copies, waits for them, and re-layouts, local(): flat_rows = jnp.take(all_normed, src_rows.reshape(-1), axis=0)  13.3 us
    dot_general x1, local copies, waits for them, and re-layouts, local(): jnp.dot(attended, weight_cols, preferred_element_type=jnp.float32)  12.4 us
    gather x1, local copies, waits for them, and re-layouts, local(): jnp.take(returned.reshape(pair_count, -1), position, axis=0)  11.6 us
    dot_general x4, matrix products, attend_pair(): jnp.einsum('krgn,nkd->rkgd', weights_low, value_rows, preferred_element_t...  10.1 us
  transfers between devices with their start and end apart: 6, of which 3 were waited for; matrix products, arithmetic and copies ran while one was open for 16% of the time, Pallas kernels for 0%

profile of v2, /device:TPU:11, one launch (start us, length us, event | category | flops | bytes accessed | tf_op | source)
XLA Modules:
  0.0 384.6 jit_solution(16186856635313429402)
XLA Ops:
  15.6 47.3 %collective-permute-done.1 = bf16[2048,512]{1,0:T(8,128)(2,1)} collective-permute-done((bf16[2048,512]{1,0:T(8,128)(2,1)}, bf16[2048,512]{1,0:T(8,128)(2,1)}, u32[]{:S(2)}, u32[]{:S(2)}) %collective-permute-start.1) | collective-permute-done | bytes 2097184 | tf_op jit(solution)/shard_map/ppermute | solution.py:14
  71.2 40.3 %while.12 = (s32[]{:T(128)}, bf16[4,128,2,2,128]{1,4,3,0,2:T(8,128)(2,1)}, s32[4]{0:T(128)S(1)}, bf16[128,2,4,2,128]{0,4,3,2,1:T(8,128)(2,1)}, bf16[1536,2,128]{...) while((s32[]{:T(128)}, ...), condition=%wide.region_3.4_spmd, body=%wide.region_0.0_spmd.sunk | while | flops 406652416 | bytes 8655003 | solution.py:43
  73.9 4.0 %fusion.75 = (f32[2,128,2]{1,2,0:T(2,128)S(1)}, f32[2,128,2,1536]{3,1,2,0:T(8,128)}) fusion(bf16[1536,2,128]{2,0,1:T(8,128)(2,1)} %get-tuple-element.200, bf16[128,2,4,2,128]{0,4,3,2,1:T(8,128)(2,1)} %get-tuple-element.199, s32[]{:T(128)S(6)} %select_n.249), kind=kOutput, calls=%fused_computation.143.clone.1 | convolution fusion | flops 203687424 | bytes 4065284 | tf_op jit(solution)/shard_map/while/body/eval_jaxpr/sub | solution.py:23
  84.0 4.0 %fusion.75 = (f32[2,128,2]{1,2,0:T(2,128)S(1)}, f32[2,128,2,1536]{3,1,2,0:T(8,128)}) fusion(bf16[1536,2,128]{2,0,1:T(8,128)(2,1)} %get-tuple-element.200, bf16[128,2,4,2,128]{0,4,3,2,1:T(8,128)(2,1)} %get-tuple-element.199, s32[]{:T(128)S(6)} %select_n.249), kind=kOutput, calls=%fused_computation.143.clone.1 | convolution fusion | flops 203687424 | bytes 4065284 | tf_op jit(solution)/shard_map/while/body/eval_jaxpr/sub | solution.py:23
  88.0 2.5 fusion.76
  94.0 4.0 %fusion.75 = (f32[2,128,2]{1,2,0:T(2,128)S(1)}, f32[2,128,2,1536]{3,1,2,0:T(8,128)}) fusion(bf16[1536,2,128]{2,0,1:T(8,128)(2,1)} %get-tuple-element.200, bf16[128,2,4,2,128]{0,4,3,2,1:T(8,128)(2,1)} %get-tuple-element.199, s32[]{:T(128)S(6)} %select_n.249), kind=kOutput, calls=%fused_computation.143.clone.1 | convolution fusion | flops 203687424 | bytes 4065284 | tf_op jit(solution)/shard_map/while/body/eval_jaxpr/sub | solution.py:23
  98.0 2.5 fusion.76
  104.1 4.0 %fusion.75 = (f32[2,128,2]{1,2,0:T(2,128)S(1)}, f32[2,128,2,1536]{3,1,2,0:T(8,128)}) fusion(bf16[1536,2,128]{2,0,1:T(8,128)(2,1)} %get-tuple-element.200, bf16[128,2,4,2,128]{0,4,3,2,1:T(8,128)(2,1)} %get-tuple-element.199, s32[]{:T(128)S(6)} %select_n.249), kind=kOutput, calls=%fused_computation.143.clone.1 | convolution fusion | flops 203687424 | bytes 4065284 | tf_op jit(solution)/shard_map/while/body/eval_jaxpr/sub | solution.py:23
  108.1 2.5 fusion.76
  111.5 7.1 %maximum_bitcast_fusion = bf16[2048,2048]{0,1:T(8,128)(2,1)} fusion(bf16[2048,512]{1,0:T(8,128)(2,1)} %collective-permute-done.2, bf16[2048,512]{1,0:T(8,128)(2,1)} %collective-permute-done.1, bf16[2048,512]{1,0:T(8,128)(2,1)} %collective-permute-done, bf16[2048,512]{1,0:T(8,128)(2,1)} %param.21), kind=kLoop, calls=%fused_computation.23 | loop fusion | flops 33554432 | bytes 16777216 | tf_op jit(solution)/shard_map/dot_general | solution.py:131
  118.6 12.4 %copy.91 = bf16[2048,2048]{1,0:T(8,128)(2,1)} copy(bf16[2048,2048]{0,1:T(8,128)(2,1)} %maximum_bitcast_fusion) | data formatting | bytes 16777216 | tf_op jit(solution)/shard_map/dot_general | solution.py:131
  131.0 6.3 %fusion.64 = bf16[128,4,512]{2,0,1:T(8,128)(2,1)S(1)} fusion(bf16[128,2048,1]{0,1,2:T(8,128)(2,1)S(1)} %bitcast.185, bf16[4,512,2048]{2,1,0:T(8,128)(2,1)} %bitcast.179), kind=kOutput, calls=%fused_computation.146 | convolution fusion | flops 1073741824 | bytes 9437184 | tf_op jit(solution)/shard_map/dot_general | solution.py:131
  140.6 77.1 %all-gather.4.cloned.1.call-done = bf16[2048,2176]{1,0:T(8,128)(2,1)} async-done(((bf16[128,2176]{1,0:T(8,128)(2,1)}), bf16[2048,2176]{1,0:T(8,128)(2,1)}) %all-gather.4.cloned.1.call-update) | async-done | bytes 8912912 | tf_op jit(solution)/shard_map/all_gather | solution.py:164
  220.6 8.3 %slice.141 = bf16[2048,2048]{1,0:T(8,128)(2,1)} slice(bf16[2048,2176]{1,0:T(8,128)(2,1)} %all-gather.4.cloned.1.call-done), slice={[0:2048], [0:2048]} | slice | bytes 16777216 | tf_op jit(solution)/shard_map/slice | solution.py:165
  228.9 13.3 %gather_fusion.2 = bf16[1024,2048]{1,0:T(8,128)(2,1)} fusion(bf16[2048,2048]{1,0:T(8,128)(2,1)} %slice.141, s32[1024]{0:T(1024)S(1)} %broadcast_clamp_fusion.1), kind=kCustom, calls=%fused_computation.2 | custom fusion | bytes 8392704 | tf_op jit(solution)/shard_map/jit(_take)/gather | solution.py:182
  242.2 6.4 %fusion.26 = f32[1024,384]{1,0:T(8,128)} fusion(bf16[1024,2048]{1,0:T(8,128)(2,1)} %gather_fusion.2, pred[1024]{0:T(1024)(128)(4,1)S(1)} %compare_and_fusion, bf16[1,2048,384]{2,1,0:T(8,128)(2,1)} %param.27), kind=kOutput, calls=%fused_computation.28 | convolution fusion | flops 1612709888 | bytes 7341056 | tf_op jit(solution)/shard_map/dot_general | solution.py:48
  248.6 8.1 %convolution_convert_fusion = bf16[1024,2048]{1,0:T(8,128)(2,1)} fusion(bf16[1,384,2048]{2,1,0:T(8,128)(2,1)S(1)} %copy-done, f32[1024,384]{1,0:T(8,128)} %fusion.26, bf16[1,2048,384]{2,1,0:T(8,128)(2,1)S(1)} %copy-done.8, bf16[1024,2048]{1,0:T(8,128)(2,1)} %gather_fusion.2, pred[1024]{0:T(1024)(128)(4,1)S(1)} %compare_and_fusion), kind=kOutput, calls=%fused_computation.26 | convolution fusion | flops 3227779072 | bytes 13108224 | tf_op jit(solution)/shard_map/dot_general | solution.py:51
  256.7 6.5 %all-to-all-start = ((bf16[16,64,2048]{2,1,0:T(8,128)(2,1)}), bf16[16,64,2048]{2,1,0:T(8,128)(2,1)}, u32[]{:S(2)}, u32[]{:S(2)}) async-start(bf16[16,64,2048]{2,1,0:T(8,128)(2,1)} %bitcast.181), calls=%async_computation | async-start | bytes 8388608 | tf_op jit(solution)/shard_map/all_to_all | solution.py:190
  264.3 4.5 %compare_select_fusion.3 = (s32[1024,1]{0,1:T(1,128)S(1)}, s32[1024,1]{0,1:T(1,128)S(1)}) fusion(s32[]{:T(128)} %bitcast.31, s32[]{:T(128)} %bitcast.32, s32[]{:T(128)} %bitcast.33, s32[]{:T(128)} %bitcast.34, s32[]{:T(128)} %bitcast.35, s32[]{:T(128)} %bitcast.37, s32[]{:T(128)} %bitcast.36, s32[1024,1]{0,1:T(1,128)S(1)} %reshape.384), kind=kLoop, calls=%fused_computation.92 | loop fusion | flops 15360 | bytes 12316 | tf_op jit(solution)/shard_map/jit(_take)/gather | solution.py:146
  268.9 5.5 %and_select_fusion.1 = (s32[1024]{0:T(1024)S(1)}, s32[1024]{0:T(1024)S(1)}) fusion(s32[1024]{0:T(1024)S(1)} %reshape.385, pred[1024]{0:T(1024)(128)(4,1)S(1)} %get-tuple-element.90, pred[1024]{0:T(1024)(128)(4,1)S(1)} %get-tuple-element.88, pred[1024]{0:T(1024)(128)(4,1)S(1)} %get-tuple-element.89, pred[1024]{0:T(1024)(128)(4,1)S(1)} %get-tuple-element.87, ...), kind=kLoop, calls=%fused_computation.114 | loop fusion | flops 16384 | bytes 25636 | tf_op jit(solution)/shard_map/jit(_take)/select_n | solution.py:146
  274.6 4.5 %reduce-window.6 = s32[16,8,128]{2,1,0:T(8,128)S(1)} reduce-window(s32[16,8,128]{2,1,0:T(8,128)S(1)} %fusion.49, s32[]{:T(128)} %constant.160.clone.1), window={size=1x1x128 pad=0_0x0_0x127_0}, to_apply=%region_4.5 | reduce-window | flops 2080768 | bytes 131076 | tf_op jit(solution)/shard_map/reduce-window
  279.8 75.9 %all-to-all-done = bf16[16,64,2048]{2,1,0:T(8,128)(2,1)} async-done(((bf16[16,64,2048]{2,1,0:T(8,128)(2,1)}), bf16[16,64,2048]{2,1,0:T(8,128)(2,1)}, u32[]{:S(2)}, u32[]{:S(2)}) %all-to-all-start) | async-done | bytes 4194336 | tf_op jit(solution)/shard_map/all_to_all | solution.py:190
  355.7 11.6 %gather_fusion.3 = bf16[1024,2048]{1,0:T(8,128)(2,1)} fusion(bf16[1024,2048]{1,0:T(8,128)(2,1)} %bitcast.48, s32[1024]{0:T(1024)S(1)} %broadcast_clamp_fusion), kind=kCustom, calls=%fused_computation.3 | custom fusion | bytes 8392704 | tf_op jit(solution)/shard_map/jit(_take)/gather | solution.py:197
  367.3 8.8 %copy_select_fusion = bf16[128,8,2048]{2,0,1:T(8,128)(2,1)S(1)} fusion(bf16[128,8,2048]{2,1,0:T(8,128)(2,1)} %bitcast.180, pred[128,8]{0,1:T(8,128)(4,1)S(1)} %compare_and_fusion.1), kind=kLoop, calls=%fused_computation.24 | loop fusion | flops 2097152 | bytes 8389632 | tf_op jit(solution)/shard_map/jit(_take)/select_n | solution.py:197
  (110 shorter events, 34.9 us)
Async XLA Ops:
  7.2 241.4 %copy-start = (bf16[1,384,2048]{2,1,0:T(8,128)(2,1)S(1)}, bf16[1,384,2048]{2,1,0:T(8,128)(2,1)}, u32[]{:S(2)}) copy-start(bf16[1,384,2048]{2,1,0:T(8,128)(2,1)} %param.29) | copy-start | bytes 4718596
  7.2 57.2 %all-gather.6.cloned.1.call-start = ((), (), s32[]{:S(2)}) async-start(), calls=%async_computation.2 | async-start | bytes 2228224 | tf_op jit(solution)/shard_map/all_gather | solution.py:101
  8.9 208.8 %all-gather.4.cloned.1.call-start = ((), (), s32[]{:S(2)}) async-start(), calls=%async_computation.1 | async-start | bytes 9469952 | tf_op jit(solution)/shard_map/all_gather | solution.py:164
  8.9 53.9 %collective-permute-start.1 = (bf16[2048,512]{1,0:T(8,128)(2,1)}, bf16[2048,512]{1,0:T(8,128)(2,1)}, u32[]{:S(2)}, u32[]{:S(2)}) collective-permute-start(bf16[2048,512]{1,0:T(8,128)(2,1)} %param.21), channel_id=1, source_target_pairs={{0,2},{1,3},{2,0},{3,1},{4,6},{5,7},{6,4},{7,5},{8,10},{9,11},{10,... | collective-permute-start | bytes 6291464 | tf_op jit(solution)/shard_map/ppermute | solution.py:14
  9.3 102.2 %collective-permute-start = (bf16[2048,512]{1,0:T(8,128)(2,1)}, bf16[2048,512]{1,0:T(8,128)(2,1)}, u32[]{:S(2)}, u32[]{:S(2)}) collective-permute-start(bf16[2048,512]{1,0:T(8,128)(2,1)} %param.21), channel_id=1, source_target_pairs={{0,1},{1,0},{2,3},{3,2},{4,5},{5,4},{6,7},{7,6},{8,9},{9,8},{10,11... | collective-permute-start | bytes 6291464 | tf_op jit(solution)/shard_map/ppermute | solution.py:14
  62.8 48.6 %collective-permute-start.2 = (bf16[2048,512]{1,0:T(8,128)(2,1)}, bf16[2048,512]{1,0:T(8,128)(2,1)}, u32[]{:S(2)}, u32[]{:S(2)}) collective-permute-start(bf16[2048,512]{1,0:T(8,128)(2,1)} %collective-permute-done.1), channel_id=1, source_target_pairs={{0,1},{1,0},{2,3},{3,2},{4,5},{5,4},{6,7},{7,6},{8,9},{9,8},{10,11... | collective-permute-start | bytes 6291464 | tf_op jit(solution)/shard_map/ppermute | solution.py:14
  118.6 12.4 %copy-start.3 = (bf16[4,128,2,2,128]{1,4,3,0,2:T(8,128)(2,1)S(1)}, bf16[4,128,2,2,128]{1,4,3,0,2:T(8,128)(2,1)}, u32[]{:S(2)}) copy-start(bf16[4,128,2,2,128]{1,4,3,0,2:T(8,128)(2,1)} %get-tuple-element.46) | copy-start | bytes 1572868
  137.3 1.1 copy-start.1
  137.3 1.5 copy-start.6
  138.2 1.8 copy-start.4
  138.8 90.2 %copy-start.2 = (bf16[128,2048]{1,0:T(8,128)(2,1)}, bf16[128,2048]{1,0:T(8,128)(2,1)S(1)}, u32[]{:S(2)}) copy-start(bf16[128,2048]{1,0:T(8,128)(2,1)S(1)} %get-tuple-element.108) | copy-start | bytes 1572868
  242.2 6.4 %copy-start.8 = (bf16[1,2048,384]{2,1,0:T(8,128)(2,1)S(1)}, bf16[1,2048,384]{2,1,0:T(8,128)(2,1)}, u32[]{:S(2)}) copy-start(bf16[1,2048,384]{2,1,0:T(8,128)(2,1)} %param.28) | copy-start | bytes 4718596
  256.7 6.5 %copy-start.5 = (s32[128,8]{0,1:T(8,128)S(1)}, s32[128,8]{0,1:T(8,128)}, u32[]{:S(2)}) copy-start(s32[128,8]{0,1:T(8,128)} %param.24) | copy-start | bytes 12292
  256.7 23.1 %copy-start.7 = (f32[128,8]{0,1:T(8,128)S(1)}, f32[128,8]{0,1:T(8,128)}, u32[]{:S(2)}) copy-start(f32[128,8]{0,1:T(8,128)} %param.25) | copy-start | bytes 12292
  256.7 99.0 %all-to-all-start = ((bf16[16,64,2048]{2,1,0:T(8,128)(2,1)}), bf16[16,64,2048]{2,1,0:T(8,128)(2,1)}, u32[]{:S(2)}, u32[]{:S(2)}) async-start(bf16[16,64,2048]{2,1,0:T(8,128)(2,1)} %bitcast.181), calls=%async_computation | async-start | bytes 8388608 | tf_op jit(solution)/shard_map/all_to_all | solution.py:190
Sparse Core Ops, SparseCore 0:
  10.2 48.3 all-gather.5
  140.1 77.5 all-gather.3

commit v3 on v2

--- a/solution.py
+++ b/solution.py
@@ -124,6 +124,10 @@
     for bit in reversed(range(n_eg.bit_length() - 1)):
         stride = 2**bit
         held = sorted(pieces)
+        if len(held) > 1:
+            barrier_out = lax.optimization_barrier((tuple(pieces[m] for m in held), attended))
+            pieces = dict(zip(held, barrier_out[0]))
+            attended = barrier_out[1]
         fetched = swapped(tuple(pieces[m] for m in held), "eg", bit)
         for m, piece in zip(held, fetched):
             pieces[m + stride] = piece
@@ -179,14 +183,25 @@
             chosen.astype(jnp.int32) * jnp.arange(tok_dev, dtype=jnp.int32)[None, None, :], axis=2
         )
         src_rows = local_row + jnp.arange(slot_count, dtype=jnp.int32)[:, None] * tok_dev
-        flat_rows = jnp.take(all_normed, src_rows.reshape(-1), axis=0)
+        pad_rows = ((0, all_packed.shape[1] - width), (0, 0))
+        gate_act = jnp.dot(
+            all_packed, jnp.pad(partner[0], pad_rows), preferred_element_type=jnp.float32
+        )
+        up_act = jnp.dot(
+            all_packed, jnp.pad(partner[1], pad_rows), preferred_element_type=jnp.float32
+        )
+        activation = (jax.nn.silu(gate_act) * up_act).astype(jnp.bfloat16)
+        picked = jnp.take(activation, src_rows.reshape(-1), axis=0)
+        produced = jnp.dot(picked, partner[2], preferred_element_type=jnp.float32).astype(
+            jnp.bfloat16
+        )
     else:
         outbound = jnp.take(normed, source_pair // top_count, axis=0).reshape(
             slot_count, per_slot, -1
         )
         arrived = lax.all_to_all(outbound, ("ctx", "eg"), split_axis=0, concat_axis=0, tiled=True)
         flat_rows = arrived.reshape(-1, arrived.shape[2])
-    produced = expert_apply(flat_rows, partner[0], partner[1], partner[2])
+        produced = expert_apply(flat_rows, partner[0], partner[1], partner[2])
     returned = lax.all_to_all(
         produced.reshape(slot_count, per_slot, -1),
         ("ctx", "eg"),
@@ -194,14 +209,17 @@
         concat_axis=0,
         tiled=True,
     )
-    answers = jnp.take(returned.reshape(pair_count, -1), position, axis=0).reshape(
-        tok_dev, top_count, -1
-    )
-    combined = gate_weights[:, 0:1] * answers[:, 0].astype(jnp.float32)
-    for choice_slot in range(1, top_count):
-        combined = combined + gate_weights[:, choice_slot : choice_slot + 1] * answers[
-            :, choice_slot
-        ].astype(jnp.float32)
+    returned_rows = returned.reshape(pair_count, -1)
+    placed = position.reshape(tok_dev, top_count)[:, :, None] == jnp.arange(
+        pair_count, dtype=jnp.int32
+    )[None, None, :]
+    mixing = jnp.sum(jnp.where(placed, gate_weights[:, :, None], 0.0), axis=1)
+    combined = jnp.zeros((tok_dev, returned_rows.shape[1]), jnp.float32)
+    remainder = mixing
+    for _ in range(3):
+        part = remainder.astype(jnp.bfloat16)
+        remainder = remainder - part.astype(jnp.float32)
+        combined = combined + jnp.dot(part, returned_rows, preferred_element_type=jnp.float32)
     moe_out = combined.astype(jnp.bfloat16)
     return (attn_out, moe_out)
 

time: 386 us -> 344 us (0.89)
  local copies, waits for them, and re-layouts: 63.1 us -> 25.5 us
  other arithmetic: 42.3 us -> 24.9 us
  matrix products: 46.8 us -> 59.3 us
    all_gather x1, waiting for transfers between devices: 0.01 us -> 46.2 us  [local(): gathered = lax.all_gather(both[None], ('ctx', 'eg'), axis=0, tiled=True)]
    ppermute x3, waiting for transfers between devices: 47.3 us -> 5.29 us  [swapped(): return lax.ppermute(value, axis, pairs)]
    gather x2 -> x1, local copies, waits for them, and re-layouts: 24.8 us -> 4.99 us  [local(): picked = jnp.take(activation, src_rows.reshape(-1), axis=0)]
    dot_general x2 -> x6, matrix products: 14.5 us -> 28.9 us  [the longest x3 9.6 us: local(): jnp.dot(part, returned_rows, preferred_element_type=jnp.float32)]
    dot_general x1 -> x0, local copies, waits for them, and re-layouts: 12.4 us -> none  [local(): jnp.dot(attended, weight_cols, preferred_element_type=jnp.float32)]
    select_n x3 -> x1, other arithmetic: 8.87 us -> 0.01 us  [local(): picked = jnp.take(activation, src_rows.reshape(-1), axis=0)]
    slice x1 -> x0, local copies, waits for them, and re-layouts: 8.27 us -> none  [local(): all_normed = all_packed[:, :width]]
    dot_general x1 -> x0, other arithmetic: 7.14 us -> none  [local(): jnp.dot(attended, weight_cols, preferred_element_type=jnp.float32)]
  transfers between devices with their start and end apart: 6 -> 6, of which waited for: 3 -> 5; matrix products, arithmetic and copies ran while one was open for 16% -> 19% of each run, Pallas kernels for 0% -> 0%
where the time goes in v3:
time: 344 us; the launch traced here: 343 us
  waiting for transfers between devices  202 us (59%)
  matrix products  59.3 us (17%)
  local copies, waits for them, and re-layouts  25.5 us (7%)
  other arithmetic  24.9 us (7%)
  between operations  14.4 us (4%)
  starting transfers between devices  8.6 us (2%)
  loops' own time  8.35 us (2%)
    all_gather x1, waiting for transfers between devices, local(): all_packed = lax.all_gather(packed, ('ctx', 'eg'), axis=0, tiled=True)  77.1 us
    all_to_all x1, waiting for transfers between devices, local(): lax.all_to_all(produced.reshape(slot_count, per_slot, -1), ('ctx', 'eg'),...  73.4 us
    all_gather x1, waiting for transfers between devices, local(): gathered = lax.all_gather(both[None], ('ctx', 'eg'), axis=0, tiled=True)  46.2 us
    sub x4, matrix products, attend_pair(): raised = jnp.exp(logits - largest)  15.9 us
    dot_general x4, matrix products, attend_pair(): jnp.einsum('krgn,nkd->rkgd', weights_low, value_rows, preferred_element_t...  10.1 us
    dot_general x3, matrix products, local(): jnp.dot(part, returned_rows, preferred_element_type=jnp.float32)  9.6 us
    another operation x1, loops' own time, attend_rows(): stacked = lax.map(one_pair, jnp.arange(per_group // 2, dtype=jnp.int32))  8.35 us
    dot_general x1, matrix products, local(): jnp.dot(all_packed, jnp.pad(partner[0], pad_rows), preferred_element_type...  8.11 us
  transfers between devices with their start and end apart: 6, of which 5 were waited for; matrix products, arithmetic and copies ran while one was open for 19% of the time, Pallas kernels for 0%

profile of v3, /device:TPU:11, one launch (start us, length us, event | category | flops | bytes accessed | tf_op | source)
XLA Modules:
  0.0 343.0 jit_solution(7842214854649347841)
XLA Ops:
  12.3 46.2 %all-gather.6.cloned.1.call-done = bf16[16,128,512]{2,1,0:T(8,128)(2,1)} async-done(((bf16[1,128,512]{2,1,0:T(8,128)(2,1)}), bf16[16,128,512]{2,1,0:T(8,128)(2,1)}) %all-gather.6.cloned.1.call-update) | async-done | bytes 2097168 | tf_op jit(solution)/shard_map/all_gather | solution.py:101
  66.2 40.3 %while.12 = (s32[]{:T(128)}, bf16[4,128,2,2,128]{1,4,3,0,2:T(8,128)(2,1)}, s32[4]{0:T(128)S(1)}, bf16[128,2,4,2,128]{0,4,3,2,1:T(8,128)(2,1)}, bf16[1536,2,128]{...) while((s32[]{:T(128)}, bf16[4,128,2,2,128]{1,4,3,0,2:T(8,128)(2,1)}, ...), condition=%wide.region_3.4_spmd, body=%wide.region_0.0_spmd.sunk | while | flops 406652416 | bytes 11800759 | solution.py:43
  69.0 4.0 %fusion.82 = (f32[2,128,2]{1,2,0:T(2,128)S(1)}, f32[2,128,2,1536]{3,1,2,0:T(8,128)}) fusion(bf16[1536,2,128]{2,0,1:T(8,128)(2,1)} %get-tuple-element.212, bf16[128,2,4,2,128]{0,4,3,2,1:T(8,128)(2,1)} %get-tuple-element.211, s32[]{:T(128)S(6)} %select_n.203), kind=kOutput, calls=%fused_computation.125.clone.1 | convolution fusion | flops 203687424 | bytes 4065284 | tf_op jit(solution)/shard_map/while/body/eval_jaxpr/sub | solution.py:23
  79.0 4.0 %fusion.82 = (f32[2,128,2]{1,2,0:T(2,128)S(1)}, f32[2,128,2,1536]{3,1,2,0:T(8,128)}) fusion(bf16[1536,2,128]{2,0,1:T(8,128)(2,1)} %get-tuple-element.212, bf16[128,2,4,2,128]{0,4,3,2,1:T(8,128)(2,1)} %get-tuple-element.211, s32[]{:T(128)S(6)} %select_n.203), kind=kOutput, calls=%fused_computation.125.clone.1 | convolution fusion | flops 203687424 | bytes 4065284 | tf_op jit(solution)/shard_map/while/body/eval_jaxpr/sub | solution.py:23
  83.0 2.5 fusion.83
  89.1 4.0 %fusion.82 = (f32[2,128,2]{1,2,0:T(2,128)S(1)}, f32[2,128,2,1536]{3,1,2,0:T(8,128)}) fusion(bf16[1536,2,128]{2,0,1:T(8,128)(2,1)} %get-tuple-element.212, bf16[128,2,4,2,128]{0,4,3,2,1:T(8,128)(2,1)} %get-tuple-element.211, s32[]{:T(128)S(6)} %select_n.203), kind=kOutput, calls=%fused_computation.125.clone.1 | convolution fusion | flops 203687424 | bytes 4065284 | tf_op jit(solution)/shard_map/while/body/eval_jaxpr/sub | solution.py:23
  93.1 2.5 fusion.83
  99.2 4.0 %fusion.82 = (f32[2,128,2]{1,2,0:T(2,128)S(1)}, f32[2,128,2,1536]{3,1,2,0:T(8,128)}) fusion(bf16[1536,2,128]{2,0,1:T(8,128)(2,1)} %get-tuple-element.212, bf16[128,2,4,2,128]{0,4,3,2,1:T(8,128)(2,1)} %get-tuple-element.211, s32[]{:T(128)S(6)} %select_n.203), kind=kOutput, calls=%fused_computation.125.clone.1 | convolution fusion | flops 203687424 | bytes 4065284 | tf_op jit(solution)/shard_map/while/body/eval_jaxpr/sub | solution.py:23
  103.2 2.5 fusion.83
  111.0 3.0 collective-permute-done.1
  114.0 4.4 %fusion.25 = bf16[128,2048]{1,0:T(8,128)(2,1)S(1)} fusion(bf16[128,2048]{0,1:T(8,128)(2,1)} %bitcast.132, bf16[2048,512]{1,0:T(8,128)(2,1)} %collective-permute-done.2, bf16[2048,512]{1,0:T(8,128)(2,1)} %collective-permute-done, bf16[2048,512]{1,0:T(8,128)(2,1)} %collective-permute-done.1, bf16[2048,512]{1,0:T(8,128)(2,1)} %param.21), kind=kOutput, calls=%fused_computation.22 | convolution fusion | flops 1107296256 | bytes 9437184 | tf_op jit(solution)/shard_map/dot_general | solution.py:135
  122.6 77.1 %all-gather.4.cloned.1.call-done = bf16[2048,2176]{0,1:T(8,128)(2,1)} async-done(((bf16[128,2176]{0,1:T(8,128)(2,1)}), bf16[2048,2176]{0,1:T(8,128)(2,1)}) %all-gather.4.cloned.1.call-update) | async-done | bytes 8912912 | tf_op jit(solution)/shard_map/all_gather | solution.py:168
  202.1 8.1 %fusion.35 = f32[2048,384]{1,0:T(8,128)S(1)} fusion(bf16[2048,2176]{0,1:T(8,128)(2,1)} %all-gather.4.cloned.1.call-done, bf16[2048,384]{1,0:T(8,128)(2,1)} %bitcast.130), kind=kOutput, calls=%fused_computation.38 | convolution fusion | flops 3422552064 | bytes 13631488 | tf_op jit(solution)/shard_map/dot_general | solution.py:187
  210.2 5.7 %multiply_convert_fusion = bf16[2048,384]{1,0:T(8,128)(2,1)S(1)} fusion(f32[2048,384]{1,0:T(8,128)S(1)} %fusion.35, bf16[2048,2176]{0,1:T(8,128)(2,1)S(1)} %copy-done.9, bf16[2048,384]{1,0:T(8,128)(2,1)S(1)} %bitcast.131), kind=kOutput, calls=%fused_computation.33 | convolution fusion | flops 3427270656 | bytes 15204352 | tf_op jit(solution)/shard_map/dot_general | solution.py:190
  216.0 5.0 %gather_fusion.2 = bf16[1024,384]{1,0:T(8,128)(2,1)} fusion(bf16[2048,384]{1,0:T(8,128)(2,1)S(1)} %multiply_convert_fusion, s32[1024]{0:T(1024)S(1)} %broadcast_clamp_fusion), kind=kCustom, calls=%fused_computation.2 | custom fusion | bytes 1576960 | tf_op jit(solution)/shard_map/jit(_take)/gather | solution.py:194
  221.0 5.5 %convolution_convert_fusion = bf16[1024,2048]{1,0:T(8,128)(2,1)} fusion(bf16[1,384,2048]{2,1,0:T(8,128)(2,1)S(1)} %copy-done, bf16[1024,384]{1,0:T(8,128)(2,1)} %gather_fusion.2, pred[1024]{0:T(1024)(128)(4,1)S(1)} %compare_and_fusion), kind=kOutput, calls=%fused_computation.32 | convolution fusion | flops 1613103104 | bytes 6554624 | tf_op jit(solution)/shard_map/dot_general | solution.py:195
  226.4 7.7 %all-to-all-start = ((bf16[16,64,2048]{2,1,0:T(8,128)(2,1)}), bf16[16,64,2048]{2,1,0:T(8,128)(2,1)}, u32[]{:S(2)}, u32[]{:S(2)}) async-start(bf16[16,64,2048]{2,1,0:T(8,128)(2,1)} %bitcast.118), calls=%async_computation | async-start | bytes 8388608 | tf_op jit(solution)/shard_map/all_to_all | solution.py:205
  235.3 4.5 %compare_select_fusion.2 = (s32[1024,1]{0,1:T(1,128)S(1)}, s32[1024,1]{0,1:T(1,128)S(1)}) fusion(s32[]{:T(128)} %bitcast.27, s32[]{:T(128)} %bitcast.28, s32[]{:T(128)} %bitcast.29, s32[]{:T(128)} %bitcast.30, s32[]{:T(128)} %bitcast.31, s32[]{:T(128)} %bitcast.33, s32[]{:T(128)} %bitcast.32, s32[1024,1]{0,1:T(1,128)S(1)} %reshape.329), kind=kLoop, calls=%fused_computation.83 | loop fusion | flops 15360 | bytes 12316 | tf_op jit(solution)/shard_map/jit(_take)/gather | solution.py:150
  239.9 5.5 %and_select_fusion = (s32[1024]{0:T(1024)S(1)}, s32[1024]{0:T(1024)S(1)}) fusion(s32[1024]{0:T(1024)S(1)} %reshape.330, pred[1024]{0:T(1024)(128)(4,1)S(1)} %get-tuple-element.110, pred[1024]{0:T(1024)(128)(4,1)S(1)} %get-tuple-element.109, pred[1024]{0:T(1024)(128)(4,1)S(1)} %get-tuple-element.108, pred[1024]{0:T(1024)(128)(4,1)S(1)} %get-tuple-element.107, ...), kind=kLoop, calls=%fused_computation.103 | loop fusion | flops 16384 | bytes 25636 | tf_op jit(solution)/shard_map/jit(_take)/select_n | solution.py:150
  245.6 4.5 %reduce-window.6 = s32[16,8,128]{2,1,0:T(8,128)S(1)} reduce-window(s32[16,8,128]{2,1,0:T(8,128)S(1)} %fusion.51, s32[]{:T(128)} %constant.149.clone.1), window={size=1x1x128 pad=0_0x0_0x127_0}, to_apply=%region_4.5 | reduce-window | flops 2080768 | bytes 131076 | tf_op jit(solution)/shard_map/reduce-window
  253.2 73.4 %all-to-all-done = bf16[16,64,2048]{2,1,0:T(8,128)(2,1)} async-done(((bf16[16,64,2048]{2,1,0:T(8,128)(2,1)}), bf16[16,64,2048]{2,1,0:T(8,128)(2,1)}, u32[]{:S(2)}, u32[]{:S(2)}) %all-to-all-start) | async-done | bytes 4194336 | tf_op jit(solution)/shard_map/all_to_all | solution.py:205
  326.6 2.9 fusion.46
  329.5 2.9 convolution_add_fusion.1
  332.5 3.8 %fusion.33 = bf16[128,2048]{1,0:T(8,128)(2,1)} fusion(f32[128,2048]{1,0:T(8,128)S(1)} %convolution_add_fusion.1, bf16[1024,2048]{1,0:T(8,128)(2,1)} %bitcast.44, f32[128,1024]{1,0:T(8,128)S(1)} %select_reduce_fusion), kind=kOutput, calls=%fused_computation.36 | convolution fusion | flops 538312704 | bytes 6291456 | tf_op jit(solution)/shard_map/dot_general | solution.py:222
  (118 shorter events, 36.6 us)
Async XLA Ops:
  7.2 213.8 %copy-start = (bf16[1,384,2048]{2,1,0:T(8,128)(2,1)S(1)}, bf16[1,384,2048]{2,1,0:T(8,128)(2,1)}, u32[]{:S(2)}) copy-start(bf16[1,384,2048]{2,1,0:T(8,128)(2,1)} %param.29) | copy-start | bytes 4718596
  7.2 51.4 %all-gather.6.cloned.1.call-start = ((), (), s32[]{:S(2)}) async-start(), calls=%async_computation.2 | async-start | bytes 2228224 | tf_op jit(solution)/shard_map/all_gather | solution.py:101
  8.9 190.8 %all-gather.4.cloned.1.call-start = ((), (), s32[]{:S(2)}) async-start(), calls=%async_computation.1 | async-start | bytes 9469952 | tf_op jit(solution)/shard_map/all_gather | solution.py:168
  8.9 97.6 %collective-permute-start = (bf16[2048,512]{1,0:T(8,128)(2,1)}, bf16[2048,512]{1,0:T(8,128)(2,1)}, u32[]{:S(2)}, u32[]{:S(2)}) collective-permute-start(bf16[2048,512]{1,0:T(8,128)(2,1)} %param.21), channel_id=1, source_target_pairs={{0,2},{1,3},{2,0},{3,1},{4,6},{5,7},{6,4},{7,5},{8,10},{9,11},{10,... | collective-permute-start | bytes 6291464 | tf_op jit(solution)/shard_map/ppermute | solution.py:14
  66.2 40.8 %copy-start.4 = (bf16[128,2048]{1,0:T(8,128)(2,1)S(1)}, bf16[128,2048]{1,0:T(8,128)(2,1)}, u32[]{:S(2)}) copy-start(bf16[128,2048]{1,0:T(8,128)(2,1)} %param.22) | copy-start | bytes 1572868
  66.2 41.9 %copy-start.6 = (s32[128,8]{0,1:T(8,128)S(1)}, s32[128,8]{0,1:T(8,128)}, u32[]{:S(2)}) copy-start(s32[128,8]{0,1:T(8,128)} %param.24) | copy-start | bytes 12292
  66.2 6.7 %copy-start.3 = (bf16[1536,2,128]{2,0,1:T(8,128)(2,1)S(1)}, bf16[1536,2,128]{2,0,1:T(8,128)(2,1)}, u32[]{:S(2)}) copy-start(bf16[1536,2,128]{2,0,1:T(8,128)(2,1)} %get-tuple-element.213) | copy-start | bytes 2359300 | tf_op jit(solution)/shard_map/while
  76.3 6.7 %copy-start.3 = (bf16[1536,2,128]{2,0,1:T(8,128)(2,1)S(1)}, bf16[1536,2,128]{2,0,1:T(8,128)(2,1)}, u32[]{:S(2)}) copy-start(bf16[1536,2,128]{2,0,1:T(8,128)(2,1)} %get-tuple-element.213) | copy-start | bytes 2359300 | tf_op jit(solution)/shard_map/while
  86.4 6.7 %copy-start.3 = (bf16[1536,2,128]{2,0,1:T(8,128)(2,1)S(1)}, bf16[1536,2,128]{2,0,1:T(8,128)(2,1)}, u32[]{:S(2)}) copy-start(bf16[1536,2,128]{2,0,1:T(8,128)(2,1)} %get-tuple-element.213) | copy-start | bytes 2359300 | tf_op jit(solution)/shard_map/while
  96.5 6.7 %copy-start.3 = (bf16[1536,2,128]{2,0,1:T(8,128)(2,1)S(1)}, bf16[1536,2,128]{2,0,1:T(8,128)(2,1)}, u32[]{:S(2)}) copy-start(bf16[1536,2,128]{2,0,1:T(8,128)(2,1)} %get-tuple-element.213) | copy-start | bytes 2359300 | tf_op jit(solution)/shard_map/while
  106.5 4.5 %collective-permute-start.2 = (bf16[2048,512]{1,0:T(8,128)(2,1)}, bf16[2048,512]{1,0:T(8,128)(2,1)}, u32[]{:S(2)}, u32[]{:S(2)}) collective-permute-start(bf16[2048,512]{1,0:T(8,128)(2,1)} %collective-permute-done), channel_id=1, source_target_pairs={{0,1},{1,0},{2,3},{3,2},{4,5},{5,4},{6,7},{7,6},{8,9},{9,8},{10,11... | collective-permute-start | bytes 6291464 | tf_op jit(solution)/shard_map/ppermute | solution.py:14
  106.8 7.2 %collective-permute-start.1 = (bf16[2048,512]{1,0:T(8,128)(2,1)}, bf16[2048,512]{1,0:T(8,128)(2,1)}, u32[]{:S(2)}, u32[]{:S(2)}) collective-permute-start(bf16[2048,512]{1,0:T(8,128)(2,1)} %param.21), channel_id=1, source_target_pairs={{0,1},{1,0},{2,3},{3,2},{4,5},{5,4},{6,7},{7,6},{8,9},{9,8},{10,11... | collective-permute-start | bytes 6291464 | tf_op jit(solution)/shard_map/ppermute | solution.py:14
  118.4 2.3 copy-start.7
  119.1 2.9 copy-start.5
  119.9 0.8 copy-start.1
  202.1 8.1 %copy-start.9 = (bf16[2048,2176]{0,1:T(8,128)(2,1)S(1)}, bf16[2048,2176]{0,1:T(8,128)(2,1)}, u32[]{:S(2)}) copy-start(bf16[2048,2176]{0,1:T(8,128)(2,1)} %all-gather.4.cloned.1.call-done) | copy-start | bytes 26738692
  202.1 8.1 %copy-start.10 = (bf16[1,2048,384]{2,1,0:T(8,128)(2,1)S(1)}, bf16[1,2048,384]{2,1,0:T(8,128)(2,1)}, u32[]{:S(2)}) copy-start(bf16[1,2048,384]{2,1,0:T(8,128)(2,1)} %param.28) | copy-start | bytes 4718596
  226.4 8.1 %copy-start.8 = (f32[128,8]{0,1:T(8,128)S(1)}, f32[128,8]{0,1:T(8,128)}, u32[]{:S(2)}) copy-start(f32[128,8]{0,1:T(8,128)} %param.25) | copy-start | bytes 12292
  226.4 25.8 %copy-start.2 = (bf16[128,2048]{0,1:T(8,128)(2,1)S(1)}, bf16[128,2048]{0,1:T(8,128)(2,1)}, u32[]{:S(2)}) copy-start(bf16[128,2048]{0,1:T(8,128)(2,1)} %copy-done.1) | copy-start | bytes 1572868
  226.4 100.2 %all-to-all-start = ((bf16[16,64,2048]{2,1,0:T(8,128)(2,1)}), bf16[16,64,2048]{2,1,0:T(8,128)(2,1)}, u32[]{:S(2)}, u32[]{:S(2)}) async-start(bf16[16,64,2048]{2,1,0:T(8,128)(2,1)} %bitcast.118), calls=%async_computation | async-start | bytes 8388608 | tf_op jit(solution)/shard_map/all_to_all | solution.py:205
Sparse Core Ops, SparseCore 0:
  10.2 48.3 all-gather.5
  122.1 77.5 all-gather.3

commit v4 on v3

--- a/solution.py
+++ b/solution.py
@@ -8,9 +8,24 @@
 HD = 128
 
 
+EG = ("ex", "ec")
+
+
+def size_of(axes):
+    return math.prod(lax.axis_size(axis) for axis in axes)
+
+
+def index_of(axes):
+    index = 0
+    for axis in axes:
+        index = index * lax.axis_size(axis) + lax.axis_index(axis)
+    return index
+
+
 def swapped(value, axis, bit):
     mask = 2**bit
-    pairs = [(source, source ^ mask) for source in range(lax.axis_size(axis))]
+    axes = axis if isinstance(axis, tuple) else (axis,)
+    pairs = [(source, source ^ mask) for source in range(size_of(axes))]
     return lax.ppermute(value, axis, pairs)
 
 
@@ -67,7 +82,9 @@
     w_down,
 ):
     n_ctx = lax.axis_size("ctx")
-    n_eg = lax.axis_size("eg")
+    n_eg = size_of(EG)
+    n_ec = lax.axis_size("ec")
+    n_ex = lax.axis_size("ex")
     n_rep = lax.axis_size("rep")
     my_ctx = lax.axis_index("ctx")
 
@@ -96,12 +113,14 @@
     shard_blocks, slice_rows, kv_width = keys.shape
     pick_count = selected.shape[1]
     block_rows = slice_rows * n_eg
-    my_eg = lax.axis_index("eg")
+    my_eg = index_of(EG)
     both = jnp.concatenate([keys, values], axis=2)
-    gathered = lax.all_gather(both[None], ("ctx", "eg"), axis=0, tiled=True)
+    gathered = lax.all_gather(both[None], ("ctx", "ex"), axis=0, tiled=True)
+    gathered = lax.all_gather(gathered[None], "ec", axis=0, tiled=True)
+    out_weight, gathered = lax.optimization_barrier((out_weight, gathered))
     every_block = (
-        gathered.reshape(n_ctx, n_eg, shard_blocks, slice_rows, 2 * kv_width)
-        .transpose(0, 2, 1, 3, 4)
+        gathered.reshape(n_ec, n_ctx, n_ex, shard_blocks, slice_rows, 2 * kv_width)
+        .transpose(1, 3, 2, 0, 4, 5)
         .reshape(n_ctx * shard_blocks, block_rows, 2 * kv_width)
     )
     query_rows = queries.shape[0]
@@ -128,7 +147,7 @@
             barrier_out = lax.optimization_barrier((tuple(pieces[m] for m in held), attended))
             pieces = dict(zip(held, barrier_out[0]))
             attended = barrier_out[1]
-        fetched = swapped(tuple(pieces[m] for m in held), "eg", bit)
+        fetched = swapped(tuple(pieces[m] for m in held), EG, bit)
         for m, piece in zip(held, fetched):
             pieces[m + stride] = piece
     weight_cols = jnp.concatenate([pieces[m] for m in range(n_eg)], axis=1)
@@ -165,7 +184,8 @@
         id_cols = jnp.full((tok_dev, 128), -1.0, jnp.bfloat16)
         id_cols = id_cols.at[:, :top_count].set(expert_ids.astype(jnp.bfloat16))
         packed = jnp.concatenate([normed, id_cols], axis=1)
-        all_packed = lax.all_gather(packed, ("ctx", "eg"), axis=0, tiled=True)
+        all_packed = lax.all_gather(packed, ("ctx", "ex"), axis=0, tiled=True)
+        all_packed = lax.all_gather(all_packed, "ec", axis=0, tiled=True)
         all_normed = all_packed[:, :width]
         all_ids = all_packed[:, width : width + top_count].astype(jnp.int32)
         expert_count = expert_home.shape[0]
@@ -173,7 +193,12 @@
             jnp.where(expert_home == my_slot, jnp.arange(expert_count, dtype=jnp.int32), 0)
         )
         hits = jnp.any(all_ids == my_expert, axis=1)
-        hits = hits.reshape(slot_count, tok_dev).astype(jnp.int32)
+        hits = (
+            hits.reshape(n_ec, n_ctx * n_ex, tok_dev)
+            .transpose(1, 0, 2)
+            .reshape(slot_count, tok_dev)
+            .astype(jnp.int32)
+        )
         rank = jnp.cumsum(hits, axis=1) - 1
         chosen = jnp.logical_and(
             hits[:, None, :] == 1,
@@ -182,7 +207,9 @@
         local_row = jnp.sum(
             chosen.astype(jnp.int32) * jnp.arange(tok_dev, dtype=jnp.int32)[None, None, :], axis=2
         )
-        src_rows = local_row + jnp.arange(slot_count, dtype=jnp.int32)[:, None] * tok_dev
+        slot_ids = jnp.arange(slot_count, dtype=jnp.int32)
+        row_base = (slot_ids % n_ec) * (n_ctx * n_ex * tok_dev) + (slot_ids // n_ec) * tok_dev
+        src_rows = local_row + row_base[:, None]
         pad_rows = ((0, all_packed.shape[1] - width), (0, 0))
         gate_act = jnp.dot(
             all_packed, jnp.pad(partner[0], pad_rows), preferred_element_type=jnp.float32
@@ -199,12 +226,12 @@
         outbound = jnp.take(normed, source_pair // top_count, axis=0).reshape(
             slot_count, per_slot, -1
         )
-        arrived = lax.all_to_all(outbound, ("ctx", "eg"), split_axis=0, concat_axis=0, tiled=True)
+        arrived = lax.all_to_all(outbound, ("ctx",) + EG, split_axis=0, concat_axis=0, tiled=True)
         flat_rows = arrived.reshape(-1, arrived.shape[2])
         produced = expert_apply(flat_rows, partner[0], partner[1], partner[2])
     returned = lax.all_to_all(
         produced.reshape(slot_count, per_slot, -1),
-        ("ctx", "eg"),
+        ("ctx",) + EG,
         split_axis=0,
         concat_axis=0,
         tiled=True,
@@ -225,27 +252,31 @@
 
 
 def solution(mesh):
+    devices = mesh.devices
+    groups, ctx, eg, rep = devices.shape
+    low = 2 if eg % 2 == 0 else 1
+    split_mesh = jax.sharding.Mesh(
+        devices.reshape(groups, ctx, eg // low, low, rep), ("groups", "ctx") + EG + ("rep",)
+    )
+    rows = ("groups", "ctx") + EG + ("rep",)
     return jax.shard_map(
         local,
-        mesh=mesh,
+        mesh=split_mesh,
         in_specs=(
-            P(("groups", "ctx", "eg"), "rep"),
-            P(("groups", "ctx"), "eg", "rep"),
-            P(("groups", "ctx"), "eg", "rep"),
+            P(("groups", "ctx") + EG, "rep"),
+            P(("groups", "ctx"), EG, "rep"),
+            P(("groups", "ctx"), EG, "rep"),
             P("groups", None),
-            P("rep", "eg"),
-            P(("groups", "ctx", "eg", "rep"), None),
+            P("rep", EG),
+            P(rows, None),
             P(),
-            P(("groups", "ctx", "eg", "rep"), None),
-            P(("groups", "ctx", "eg", "rep"), None),
+            P(rows, None),
+            P(rows, None),
             P(),
-            P(("ctx", "eg"), None, "rep"),
-            P(("ctx", "eg"), None, "rep"),
-            P(("ctx", "eg"), "rep", None),
+            P(("ctx",) + EG, None, "rep"),
+            P(("ctx",) + EG, None, "rep"),
+            P(("ctx",) + EG, "rep", None),
         ),
-        out_specs=(
-            P(("groups", "ctx", "eg", "rep"), None),
-            P(("groups", "ctx", "eg", "rep"), None),
-        ),
+        out_specs=(P(rows, None), P(rows, None)),
         check_vma=False,
     )

time: 344 us -> 373 us (1.084)
  waiting for transfers between devices: 202 us -> 230 us
    all_gather x2 -> x4, waiting for transfers between devices: 123 us -> 151 us  [the longest x1 75.4 us: local(): all_packed = lax.all_gather(packed, ('ctx', 'ex'), axis=0, tiled=True)]
  transfers between devices with their start and end apart: 6 -> 8, of which waited for: 5 -> 7; matrix products, arithmetic and copies ran while one was open for 19% -> 18% of each run, Pallas kernels for 0% -> 0%
where the time goes in v4:
time: 373 us; the launch traced here: 372 us
  waiting for transfers between devices  230 us (62%)
  matrix products  59.1 us (16%)
  local copies, waits for them, and re-layouts  28.6 us (8%)
  other arithmetic  24.8 us (7%)
  between operations  14.2 us (4%)
  loops' own time  8.35 us (2%)
  starting transfers between devices  7.17 us (2%)
    all_gather x1, waiting for transfers between devices, local(): all_packed = lax.all_gather(packed, ('ctx', 'ex'), axis=0, tiled=True)  75.4 us
    all_to_all x1, waiting for transfers between devices, local(): lax.all_to_all(produced.reshape(slot_count, per_slot, -1), ('ctx',) + EG,...  73.4 us
    all_gather x1, waiting for transfers between devices, local(): gathered = lax.all_gather(both[None], ('ctx', 'ex'), axis=0, tiled=True)  40.5 us
    all_gather x1, waiting for transfers between devices, local(): all_packed = lax.all_gather(all_packed, 'ec', axis=0, tiled=True)  24 us
    sub x4, matrix products, attend_pair(): raised = jnp.exp(logits - largest)  15.9 us
    all_gather x1, waiting for transfers between devices, local(): gathered = lax.all_gather(gathered[None], 'ec', axis=0, tiled=True)  11 us
    dot_general x4, matrix products, attend_pair(): jnp.einsum('krgn,nkd->rkgd', weights_low, value_rows, preferred_element_t...  10.1 us
    dot_general x3, matrix products, local(): jnp.dot(part, returned_rows, preferred_element_type=jnp.float32)  9.6 us
  transfers between devices with their start and end apart: 8, of which 7 were waited for; matrix products, arithmetic and copies ran while one was open for 18% of the time, Pallas kernels for 0%

profile of v4, /device:TPU:11, one launch (start us, length us, event | category | flops | bytes accessed | tf_op | source)
XLA Modules:
  0.0 372.1 jit_solution(4858949258210857398)
XLA Ops:
  8.9 40.5 %all-gather.11.cloned.1.call-done = bf16[8,128,512]{2,1,0:T(8,128)(2,1)} async-done(((bf16[1,128,512]{2,1,0:T(8,128)(2,1)}), bf16[8,128,512]{2,1,0:T(8,128)(2,1)}) %all-gather.11.cloned.1.call-update) | async-done | bytes 1048592 | tf_op jit(solution)/shard_map/all_gather | solution.py:118
  52.7 11.0 %all-gather.13.cloned.1.call-done = bf16[16,128,512]{2,1,0:T(8,128)(2,1)} async-done(((bf16[8,128,512]{2,1,0:T(8,128)(2,1)}), bf16[16,128,512]{2,1,0:T(8,128)(2,1)}) %all-gather.13.cloned.1.call-update) | async-done | bytes 2097168 | tf_op jit(solution)/shard_map/all_gather | solution.py:119
  63.9 3.1 copy.106
  74.8 40.3 %while.12 = (s32[]{:T(128)}, bf16[4,128,2,2,128]{1,4,3,0,2:T(8,128)(2,1)}, s32[4]{0:T(128)S(1)}, bf16[128,2,4,2,128]{0,4,3,2,1:T(8,128)(2,1)}, bf16[1536,2,128]{...) while((s32[]{:T(128)}, bf16[4,128,2,2,128]{1,4,3,0,2:T(8,128)(2,1)}, ...), condition=%wide.region_3.4_spmd, body=%wide.region_0.0_spmd.sunk | while | flops 406652416 | bytes 11800759 | solution.py:58
  77.5 4.0 %fusion.85 = (f32[2,128,2]{1,2,0:T(2,128)S(1)}, f32[2,128,2,1536]{3,1,2,0:T(8,128)}) fusion(bf16[1536,2,128]{2,0,1:T(8,128)(2,1)} %get-tuple-element.216, bf16[128,2,4,2,128]{0,4,3,2,1:T(8,128)(2,1)} %get-tuple-element.215, s32[]{:T(128)S(6)} %select_n.234), kind=kOutput, calls=%fused_computation.132.clone.1 | convolution fusion | flops 203687424 | bytes 4065284 | tf_op jit(solution)/shard_map/while/body/eval_jaxpr/sub | solution.py:38
  87.6 4.0 %fusion.85 = (f32[2,128,2]{1,2,0:T(2,128)S(1)}, f32[2,128,2,1536]{3,1,2,0:T(8,128)}) fusion(bf16[1536,2,128]{2,0,1:T(8,128)(2,1)} %get-tuple-element.216, bf16[128,2,4,2,128]{0,4,3,2,1:T(8,128)(2,1)} %get-tuple-element.215, s32[]{:T(128)S(6)} %select_n.234), kind=kOutput, calls=%fused_computation.132.clone.1 | convolution fusion | flops 203687424 | bytes 4065284 | tf_op jit(solution)/shard_map/while/body/eval_jaxpr/sub | solution.py:38
  97.7 4.0 %fusion.85 = (f32[2,128,2]{1,2,0:T(2,128)S(1)}, f32[2,128,2,1536]{3,1,2,0:T(8,128)}) fusion(bf16[1536,2,128]{2,0,1:T(8,128)(2,1)} %get-tuple-element.216, bf16[128,2,4,2,128]{0,4,3,2,1:T(8,128)(2,1)} %get-tuple-element.215, s32[]{:T(128)S(6)} %select_n.234), kind=kOutput, calls=%fused_computation.132.clone.1 | convolution fusion | flops 203687424 | bytes 4065284 | tf_op jit(solution)/shard_map/while/body/eval_jaxpr/sub | solution.py:38
  107.7 4.0 %fusion.85 = (f32[2,128,2]{1,2,0:T(2,128)S(1)}, f32[2,128,2,1536]{3,1,2,0:T(8,128)}) fusion(bf16[1536,2,128]{2,0,1:T(8,128)(2,1)} %get-tuple-element.216, bf16[128,2,4,2,128]{0,4,3,2,1:T(8,128)(2,1)} %get-tuple-element.215, s32[]{:T(128)S(6)} %select_n.234), kind=kOutput, calls=%fused_computation.132.clone.1 | convolution fusion | flops 203687424 | bytes 4065284 | tf_op jit(solution)/shard_map/while/body/eval_jaxpr/sub | solution.py:38
  119.7 3.0 collective-permute-done.1
  122.7 4.4 %fusion.25 = bf16[128,2048]{1,0:T(8,128)(2,1)S(1)} fusion(bf16[128,2048]{0,1:T(8,128)(2,1)} %bitcast.141, bf16[2048,512]{1,0:T(8,128)(2,1)} %collective-permute-done.2, bf16[2048,512]{1,0:T(8,128)(2,1)} %collective-permute-done, bf16[2048,512]{1,0:T(8,128)(2,1)} %collective-permute-done.1, bf16[2048,512]{1,0:T(8,128)(2,1)} %param.21), kind=kOutput, calls=%fused_computation.22 | convolution fusion | flops 1107296256 | bytes 9437184 | tf_op jit(solution)/shard_map/dot_general | solution.py:154
  130.8 75.4 %all-gather.7.cloned.1.call-done = bf16[1024,2176]{0,1:T(8,128)(2,1)} async-done(((bf16[128,2176]{0,1:T(8,128)(2,1)}), bf16[1024,2176]{0,1:T(8,128)(2,1)}) %all-gather.7.cloned.1.call-update) | async-done | bytes 4456464 | tf_op jit(solution)/shard_map/all_gather | solution.py:187
  206.9 24.0 %all-gather.9.cloned.1.call-done = bf16[2048,2176]{0,1:T(8,128)(2,1)} async-done(((bf16[1024,2176]{0,1:T(8,128)(2,1)}), bf16[2048,2176]{0,1:T(8,128)(2,1)}) %all-gather.9.cloned.1.call-update) | async-done | bytes 8912912 | tf_op jit(solution)/shard_map/all_gather | solution.py:188
  233.3 7.9 %fusion.35 = f32[2048,384]{1,0:T(8,128)S(1)} fusion(bf16[2048,2176]{0,1:T(8,128)(2,1)} %all-gather.9.cloned.1.call-done, bf16[2048,384]{1,0:T(8,128)(2,1)} %bitcast.139), kind=kOutput, calls=%fused_computation.38 | convolution fusion | flops 3422552064 | bytes 13631488 | tf_op jit(solution)/shard_map/dot_general | solution.py:214
  241.3 5.7 %multiply_convert_fusion = bf16[2048,384]{1,0:T(8,128)(2,1)S(1)} fusion(f32[2048,384]{1,0:T(8,128)S(1)} %fusion.35, bf16[2048,2176]{0,1:T(8,128)(2,1)S(1)} %copy-done.9, bf16[2048,384]{1,0:T(8,128)(2,1)S(1)} %bitcast.140), kind=kOutput, calls=%fused_computation.33 | convolution fusion | flops 3427270656 | bytes 15204352 | tf_op jit(solution)/shard_map/dot_general | solution.py:217
  247.0 5.0 %gather_fusion.2 = bf16[1024,384]{1,0:T(8,128)(2,1)} fusion(bf16[2048,384]{1,0:T(8,128)(2,1)S(1)} %multiply_convert_fusion, s32[1024]{0:T(1024)S(1)} %broadcast_clamp_fusion), kind=kCustom, calls=%fused_computation.2 | custom fusion | bytes 1576960 | tf_op jit(solution)/shard_map/jit(_take)/gather | solution.py:221
  252.0 5.5 %convolution_convert_fusion = bf16[1024,2048]{1,0:T(8,128)(2,1)} fusion(bf16[1,384,2048]{2,1,0:T(8,128)(2,1)S(1)} %copy-done, bf16[1024,384]{1,0:T(8,128)(2,1)} %gather_fusion.2, pred[1024]{0:T(1024)(128)(4,1)S(1)} %compare_and_fusion), kind=kOutput, calls=%fused_computation.32 | convolution fusion | flops 1613103104 | bytes 6554624 | tf_op jit(solution)/shard_map/dot_general | solution.py:222
  257.5 6.0 %all-to-all-start = ((bf16[16,64,2048]{2,1,0:T(8,128)(2,1)}), bf16[16,64,2048]{2,1,0:T(8,128)(2,1)}, u32[]{:S(2)}, u32[]{:S(2)}) async-start(bf16[16,64,2048]{2,1,0:T(8,128)(2,1)} %bitcast.125), calls=%async_computation | async-start | bytes 8388608 | tf_op jit(solution)/shard_map/all_to_all | solution.py:232
  264.7 4.5 %compare_select_fusion.2 = (s32[1024,1]{0,1:T(1,128)S(1)}, s32[1024,1]{0,1:T(1,128)S(1)}) fusion(s32[]{:T(128)} %bitcast.30, s32[]{:T(128)} %bitcast.31, s32[]{:T(128)} %bitcast.32, s32[]{:T(128)} %bitcast.33, s32[]{:T(128)} %bitcast.34, s32[]{:T(128)} %bitcast.36, s32[]{:T(128)} %bitcast.35, s32[1024,1]{0,1:T(1,128)S(1)} %reshape.358), kind=kLoop, calls=%fused_computation.83 | loop fusion | flops 15360 | bytes 12316 | tf_op jit(solution)/shard_map/jit(_take)/gather | solution.py:169
  269.3 5.5 %and_select_fusion = (s32[1024]{0:T(1024)S(1)}, s32[1024]{0:T(1024)S(1)}) fusion(s32[1024]{0:T(1024)S(1)} %reshape.359, pred[1024]{0:T(1024)(128)(4,1)S(1)} %get-tuple-element.114, pred[1024]{0:T(1024)(128)(4,1)S(1)} %get-tuple-element.113, pred[1024]{0:T(1024)(128)(4,1)S(1)} %get-tuple-element.112, pred[1024]{0:T(1024)(128)(4,1)S(1)} %get-tuple-element.111, ...), kind=kLoop, calls=%fused_computation.103 | loop fusion | flops 16384 | bytes 25636 | tf_op jit(solution)/shard_map/jit(_take)/select_n | solution.py:169
  274.9 4.5 %reduce-window.6 = s32[16,8,128]{2,1,0:T(8,128)S(1)} reduce-window(s32[16,8,128]{2,1,0:T(8,128)S(1)} %fusion.51, s32[]{:T(128)} %constant.179.clone.1), window={size=1x1x128 pad=0_0x0_0x127_0}, to_apply=%region_4.5 | reduce-window | flops 2080768 | bytes 131076 | tf_op jit(solution)/shard_map/reduce-window
  282.6 73.4 %all-to-all-done = bf16[16,64,2048]{2,1,0:T(8,128)(2,1)} async-done(((bf16[16,64,2048]{2,1,0:T(8,128)(2,1)}), bf16[16,64,2048]{2,1,0:T(8,128)(2,1)}, u32[]{:S(2)}, u32[]{:S(2)}) %all-to-all-start) | async-done | bytes 4194336 | tf_op jit(solution)/shard_map/all_to_all | solution.py:232
  356.0 2.9 fusion.46
  358.9 2.9 convolution_add_fusion.1
  361.8 3.8 %fusion.33 = bf16[128,2048]{1,0:T(8,128)(2,1)} fusion(f32[128,2048]{1,0:T(8,128)S(1)} %convolution_add_fusion.1, bf16[1024,2048]{1,0:T(8,128)(2,1)} %bitcast.49, f32[128,1024]{1,0:T(8,128)S(1)} %select_reduce_fusion), kind=kOutput, calls=%fused_computation.36 | convolution fusion | flops 538312704 | bytes 6291456 | tf_op jit(solution)/shard_map/dot_general | solution.py:249
  (126 shorter events, 44.5 us)
Async XLA Ops:
  7.2 244.8 %copy-start = (bf16[1,384,2048]{2,1,0:T(8,128)(2,1)S(1)}, bf16[1,384,2048]{2,1,0:T(8,128)(2,1)}, u32[]{:S(2)}) copy-start(bf16[1,384,2048]{2,1,0:T(8,128)(2,1)} %param.29) | copy-start | bytes 4718596
  7.2 42.3 %all-gather.11.cloned.1.call-start = ((), (), s32[]{:S(2)}) async-start(), calls=%async_computation.3 | async-start | bytes 1179648 | tf_op jit(solution)/shard_map/all_gather | solution.py:118
  8.9 54.8 %all-gather.13.cloned.1.call-start = ((), (), s32[]{:S(2)}) async-start(), calls=%async_computation.4 | async-start | bytes 3145728 | tf_op jit(solution)/shard_map/all_gather | solution.py:119
  49.5 156.7 %all-gather.7.cloned.1.call-start = ((), (), s32[]{:S(2)}) async-start(), calls=%async_computation.1 | async-start | bytes 5013504 | tf_op jit(solution)/shard_map/all_gather | solution.py:187
  63.7 51.4 %collective-permute-start = (bf16[2048,512]{1,0:T(8,128)(2,1)}, bf16[2048,512]{1,0:T(8,128)(2,1)}, u32[]{:S(2)}, u32[]{:S(2)}) collective-permute-start(bf16[2048,512]{1,0:T(8,128)(2,1)} %param.21), channel_id=1, source_target_pairs={{0,2},{1,3},{2,0},{3,1},{4,6},{5,7},{6,4},{7,5},{8,10},{9,11},{10,... | collective-permute-start | bytes 6291464 | tf_op jit(solution)/shard_map/ppermute | solution.py:29
  74.8 40.8 %copy-start.4 = (bf16[128,2048]{1,0:T(8,128)(2,1)S(1)}, bf16[128,2048]{1,0:T(8,128)(2,1)}, u32[]{:S(2)}) copy-start(bf16[128,2048]{1,0:T(8,128)(2,1)} %param.22) | copy-start | bytes 1572868
  74.8 41.9 %copy-start.6 = (s32[128,8]{0,1:T(8,128)S(1)}, s32[128,8]{0,1:T(8,128)}, u32[]{:S(2)}) copy-start(s32[128,8]{0,1:T(8,128)} %param.24) | copy-start | bytes 12292
  74.8 6.7 %copy-start.3 = (bf16[1536,2,128]{2,0,1:T(8,128)(2,1)S(1)}, bf16[1536,2,128]{2,0,1:T(8,128)(2,1)}, u32[]{:S(2)}) copy-start(bf16[1536,2,128]{2,0,1:T(8,128)(2,1)} %get-tuple-element.217) | copy-start | bytes 2359300 | tf_op jit(solution)/shard_map/while
  84.8 6.7 %copy-start.3 = (bf16[1536,2,128]{2,0,1:T(8,128)(2,1)S(1)}, bf16[1536,2,128]{2,0,1:T(8,128)(2,1)}, u32[]{:S(2)}) copy-start(bf16[1536,2,128]{2,0,1:T(8,128)(2,1)} %get-tuple-element.217) | copy-start | bytes 2359300 | tf_op jit(solution)/shard_map/while
  94.9 6.7 %copy-start.3 = (bf16[1536,2,128]{2,0,1:T(8,128)(2,1)S(1)}, bf16[1536,2,128]{2,0,1:T(8,128)(2,1)}, u32[]{:S(2)}) copy-start(bf16[1536,2,128]{2,0,1:T(8,128)(2,1)} %get-tuple-element.217) | copy-start | bytes 2359300 | tf_op jit(solution)/shard_map/while
  105.0 6.7 %copy-start.3 = (bf16[1536,2,128]{2,0,1:T(8,128)(2,1)S(1)}, bf16[1536,2,128]{2,0,1:T(8,128)(2,1)}, u32[]{:S(2)}) copy-start(bf16[1536,2,128]{2,0,1:T(8,128)(2,1)} %get-tuple-element.217) | copy-start | bytes 2359300 | tf_op jit(solution)/shard_map/while
  115.1 4.6 %collective-permute-start.2 = (bf16[2048,512]{1,0:T(8,128)(2,1)}, bf16[2048,512]{1,0:T(8,128)(2,1)}, u32[]{:S(2)}, u32[]{:S(2)}) collective-permute-start(bf16[2048,512]{1,0:T(8,128)(2,1)} %collective-permute-done), channel_id=1, source_target_pairs={{0,1},{1,0},{2,3},{3,2},{4,5},{5,4},{6,7},{7,6},{8,9},{9,8},{10,11... | collective-permute-start | bytes 6291464 | tf_op jit(solution)/shard_map/ppermute | solution.py:29
  115.6 7.1 %collective-permute-start.1 = (bf16[2048,512]{1,0:T(8,128)(2,1)}, bf16[2048,512]{1,0:T(8,128)(2,1)}, u32[]{:S(2)}, u32[]{:S(2)}) collective-permute-start(bf16[2048,512]{1,0:T(8,128)(2,1)} %param.21), channel_id=1, source_target_pairs={{0,1},{1,0},{2,3},{3,2},{4,5},{5,4},{6,7},{7,6},{8,9},{9,8},{10,11... | collective-permute-start | bytes 6291464 | tf_op jit(solution)/shard_map/ppermute | solution.py:29
  127.1 2.2 copy-start.7
  128.5 0.8 copy-start.1
  129.7 76.6 %copy-start.5 = (s32[16]{0:T(128)S(1)}, s32[16]{0:T(128)}, u32[]{:S(2)}) copy-start(s32[16]{0:T(128)} %param.26) | copy-start | bytes 196
  130.6 100.4 %all-gather.9.cloned.1.call-start = ((), (), s32[]{:S(2)}) async-start(), calls=%async_computation.2 | async-start | bytes 13369344 | tf_op jit(solution)/shard_map/all_gather | solution.py:188
  233.3 8.0 %copy-start.9 = (bf16[2048,2176]{0,1:T(8,128)(2,1)S(1)}, bf16[2048,2176]{0,1:T(8,128)(2,1)}, u32[]{:S(2)}) copy-start(bf16[2048,2176]{0,1:T(8,128)(2,1)} %all-gather.9.cloned.1.call-done) | copy-start | bytes 26738692
  233.3 8.0 %copy-start.10 = (bf16[1,2048,384]{2,1,0:T(8,128)(2,1)S(1)}, bf16[1,2048,384]{2,1,0:T(8,128)(2,1)}, u32[]{:S(2)}) copy-start(bf16[1,2048,384]{2,1,0:T(8,128)(2,1)} %param.28) | copy-start | bytes 4718596
  257.5 6.4 %copy-start.8 = (f32[128,8]{0,1:T(8,128)S(1)}, f32[128,8]{0,1:T(8,128)}, u32[]{:S(2)}) copy-start(f32[128,8]{0,1:T(8,128)} %param.25) | copy-start | bytes 12292
  257.5 24.1 %copy-start.2 = (bf16[128,2048]{0,1:T(8,128)(2,1)S(1)}, bf16[128,2048]{0,1:T(8,128)(2,1)}, u32[]{:S(2)}) copy-start(bf16[128,2048]{0,1:T(8,128)(2,1)} %copy-done.1) | copy-start | bytes 1572868
  257.5 98.5 %all-to-all-start = ((bf16[16,64,2048]{2,1,0:T(8,128)(2,1)}), bf16[16,64,2048]{2,1,0:T(8,128)(2,1)}, u32[]{:S(2)}, u32[]{:S(2)}) async-start(bf16[16,64,2048]{2,1,0:T(8,128)(2,1)} %bitcast.125), calls=%async_computation | async-start | bytes 8388608 | tf_op jit(solution)/shard_map/all_to_all | solution.py:232
Sparse Core Ops, SparseCore 0:
  10.7 38.7 all-gather.10
  51.0 12.5 all-gather.12
  130.7 75.4 all-gather.6
  207.6 23.2 all-gather.8

commit v5 on v3

--- a/solution.py
+++ b/solution.py
@@ -14,9 +14,14 @@
     return lax.ppermute(value, axis, pairs)
 
 
-def attend_pair(query_pair, key_rows, value_rows, inverse_root):
+def attend_rows(queries_flat, key_rows, value_rows):
+    row_count = queries_flat.shape[0]
+    kv_heads = key_rows.shape[1]
+    per_group = queries_flat.shape[1] // (kv_heads * HD)
+    inverse_root = 1.0 / math.sqrt(HD)
+    arranged = queries_flat.reshape(row_count, kv_heads, per_group, HD).transpose(1, 2, 0, 3)
     logits = (
-        jnp.einsum("rkgd,nkd->krgn", query_pair, key_rows, preferred_element_type=jnp.float32)
+        jnp.einsum("kgrd,nkd->kgrn", arranged, key_rows, preferred_element_type=jnp.float32)
         * inverse_root
     )
     largest = jnp.max(logits, axis=-1, keepdims=True)
@@ -24,24 +29,9 @@
     denominator = jnp.sum(raised, axis=-1, keepdims=True)
     weights_low = (raised / denominator).astype(jnp.bfloat16)
     blended = jnp.einsum(
-        "krgn,nkd->rkgd", weights_low, value_rows, preferred_element_type=jnp.float32
-    )
-    return blended.astype(jnp.bfloat16)
-
-
-def attend_rows(queries_flat, key_rows, value_rows):
-    row_count = queries_flat.shape[0]
-    kv_heads = key_rows.shape[1]
-    per_group = queries_flat.shape[1] // (kv_heads * HD)
-    arranged = queries_flat.reshape(row_count, kv_heads, per_group // 2, 2, HD)
-    inverse_root = 1.0 / math.sqrt(HD)
-
-    def one_pair(pair_index):
-        query_pair = lax.dynamic_index_in_dim(arranged, pair_index, 2, keepdims=False)
-        return attend_pair(query_pair, key_rows, value_rows, inverse_root)
-
-    stacked = lax.map(one_pair, jnp.arange(per_group // 2, dtype=jnp.int32))
-    return jnp.moveaxis(stacked, 0, 2).reshape(row_count, kv_heads * per_group * HD)
+        "kgrn,nkd->rkgd", weights_low, value_rows, preferred_element_type=jnp.float32
+    )
+    return blended.astype(jnp.bfloat16).reshape(row_count, kv_heads * per_group * HD)
 
 
 def expert_apply(rows_in, gate_full, up_full, down_full):

time: 344 us -> 316 us (0.919)
  matrix products: 59.3 us -> 49.3 us
  local copies, waits for them, and re-layouts: 25.5 us -> 16.7 us
  loops' own time: 8.35 us -> 0 us
    another operation x1 -> x0, loops' own time: 8.35 us -> none  [attend_rows(): stacked = lax.map(one_pair, jnp.arange(per_group // 2, dtype=jnp.int32))]
    sub x4 -> x1, matrix products: 15.9 us -> 9.71 us  [attend_rows(): raised = jnp.exp(logits - largest)]
    dot_general x4 -> x1, matrix products: 10.1 us -> 6.48 us  [attend_rows(): jnp.einsum('kgrn,nkd->rkgd', weights_low, value_rows, preferred_element_t...]
  transfers between devices with their start and end apart: 6 -> 6, of which waited for: 5 -> 5; matrix products, arithmetic and copies ran while one was open for 19% -> 14% of each run, Pallas kernels for 0% -> 0%
where the time goes in v5:
time: 316 us; the launch traced here: 315 us
  waiting for transfers between devices  201 us (64%)
  matrix products  49.3 us (16%)
  other arithmetic  25.1 us (8%)
  local copies, waits for them, and re-layouts  16.7 us (5%)
  between operations  14.4 us (5%)
  starting transfers between devices  8.6 us (3%)
    all_gather x1, waiting for transfers between devices, local(): all_packed = lax.all_gather(packed, ('ctx', 'eg'), axis=0, tiled=True)  77.1 us
    all_to_all x1, waiting for transfers between devices, local(): lax.all_to_all(produced.reshape(slot_count, per_slot, -1), ('ctx', 'eg'),...  73.4 us
    all_gather x1, waiting for transfers between devices, local(): gathered = lax.all_gather(both[None], ('ctx', 'eg'), axis=0, tiled=True)  46.9 us
    sub x1, matrix products, attend_rows(): raised = jnp.exp(logits - largest)  9.71 us
    dot_general x3, matrix products, local(): jnp.dot(part, returned_rows, preferred_element_type=jnp.float32)  9.6 us
    dot_general x1, matrix products, local(): jnp.dot(all_packed, jnp.pad(partner[0], pad_rows), preferred_element_type...  7.93 us
    all_to_all x1, starting transfers between devices, local(): lax.all_to_all(produced.reshape(slot_count, per_slot, -1), ('ctx', 'eg'),...  7.69 us
    dot_general x1, matrix products, attend_rows(): jnp.einsum('kgrn,nkd->rkgd', weights_low, value_rows, preferred_element_t...  6.48 us
  transfers between devices with their start and end apart: 6, of which 5 were waited for; matrix products, arithmetic and copies ran while one was open for 14% of the time, Pallas kernels for 0%

profile of v5, /device:TPU:11, one launch (start us, length us, event | category | flops | bytes accessed | tf_op | source)
XLA Modules:
  0.0 315.5 jit_solution(13828684155489878505)
XLA Ops:
  7.2 1.6 pad_maximum_fusion
  9.3 1.9 copy.122
  12.2 46.9 %all-gather.6.cloned.1.call-done = bf16[16,128,512]{2,1,0:T(8,128)(2,1)} async-done(((bf16[1,128,512]{2,1,0:T(8,128)(2,1)}), bf16[16,128,512]{2,1,0:T(8,128)(2,1)}) %all-gather.6.cloned.1.call-update) | async-done | bytes 2097168 | tf_op jit(solution)/shard_map/all_gather | solution.py:91
  59.1 2.2 gather_fusion
  62.9 9.7 %fusion.66 = (f32[2,8,128]{2,1,0:T(8,128)S(1)}, f32[2,8,128,1536]{2,3,1,0:T(8,128)}) fusion(bf16[1536,2,128,1]{2,1,0,3:T(2,128)(2,1)} %bitcast.106, bf16[128,2,8,128]{3,2,1,0:T(8,128)(2,1)} %bitcast.109), kind=kOutput, calls=%fused_computation.128 | convolution fusion | flops 814745088 | bytes 13901824 | tf_op jit(solution)/shard_map/sub | solution.py:28
  72.7 6.5 %fusion.23 = bf16[2,128,8,128]{3,1,2,0:T(8,128)(2,1)} fusion(f32[2,8,128,1536]{2,3,1,0:T(8,128)} %get-tuple-element.73, f32[2,8,128]{2,1,0:T(8,128)S(1)} %get-tuple-element.72, bf16[1536,2,128,1]{2,1,0,3:T(2,128)(2,1)S(1)} %bitcast.107), kind=kOutput, calls=%fused_computation.33 | convolution fusion | flops 811859968 | bytes 13901824 | tf_op jit(solution)/shard_map/kgrn,nkd->rkgd/dot_general | solution.py:31
  79.7 1.3 copy.111
  83.6 3.0 collective-permute-done.2
  86.6 4.4 %fusion.6 = bf16[128,2048]{1,0:T(8,128)(2,1)S(1)} fusion(bf16[128,2048]{0,1:T(8,128)(2,1)} %bitcast.119, bf16[2048,512]{1,0:T(8,128)(2,1)} %collective-permute-done.2, bf16[2048,512]{1,0:T(8,128)(2,1)} %collective-permute-done, bf16[2048,512]{1,0:T(8,128)(2,1)} %collective-permute-done.1, bf16[2048,512]{1,0:T(8,128)(2,1)} %param.19), kind=kOutput, calls=%fused_computation.10 | convolution fusion | flops 1107296256 | bytes 9437184 | tf_op jit(solution)/shard_map/dot_general | solution.py:125
  95.2 77.1 %all-gather.4.cloned.1.call-done = bf16[2048,2176]{0,1:T(8,128)(2,1)} async-done(((bf16[128,2176]{0,1:T(8,128)(2,1)}), bf16[2048,2176]{0,1:T(8,128)(2,1)}) %all-gather.4.cloned.1.call-update) | async-done | bytes 8912912 | tf_op jit(solution)/shard_map/all_gather | solution.py:158
  172.3 1.4 fusion.54
  174.7 7.9 %fusion.18 = f32[2048,384]{1,0:T(8,128)S(1)} fusion(bf16[2048,2176]{0,1:T(8,128)(2,1)} %all-gather.4.cloned.1.call-done, bf16[2048,384]{1,0:T(8,128)(2,1)} %bitcast.117), kind=kOutput, calls=%fused_computation.28 | convolution fusion | flops 3422552064 | bytes 13631488 | tf_op jit(solution)/shard_map/dot_general | solution.py:177
  182.6 5.7 %multiply_convert_fusion = bf16[2048,384]{1,0:T(8,128)(2,1)S(1)} fusion(f32[2048,384]{1,0:T(8,128)S(1)} %fusion.18, bf16[2048,2176]{0,1:T(8,128)(2,1)S(1)} %copy-done.7, bf16[2048,384]{1,0:T(8,128)(2,1)S(1)} %bitcast.118), kind=kOutput, calls=%fused_computation.23 | convolution fusion | flops 3427270656 | bytes 15204352 | tf_op jit(solution)/shard_map/dot_general | solution.py:180
  188.4 5.0 %gather_fusion.2 = bf16[1024,384]{1,0:T(8,128)(2,1)} fusion(bf16[2048,384]{1,0:T(8,128)(2,1)S(1)} %multiply_convert_fusion, s32[1024]{0:T(1024)S(1)} %broadcast_clamp_fusion), kind=kCustom, calls=%fused_computation.2 | custom fusion | bytes 1576960 | tf_op jit(solution)/shard_map/jit(_take)/gather | solution.py:184
  193.4 5.5 %convolution_convert_fusion = bf16[1024,2048]{1,0:T(8,128)(2,1)} fusion(bf16[1,384,2048]{2,1,0:T(8,128)(2,1)S(1)} %copy-done, bf16[1024,384]{1,0:T(8,128)(2,1)} %gather_fusion.2, pred[1024]{0:T(1024)(128)(4,1)S(1)} %compare_and_fusion), kind=kOutput, calls=%fused_computation.22 | convolution fusion | flops 1613103104 | bytes 6554624 | tf_op jit(solution)/shard_map/dot_general | solution.py:185
  198.8 7.7 %all-to-all-start = ((bf16[16,64,2048]{2,1,0:T(8,128)(2,1)}), bf16[16,64,2048]{2,1,0:T(8,128)(2,1)}, u32[]{:S(2)}, u32[]{:S(2)}) async-start(bf16[16,64,2048]{2,1,0:T(8,128)(2,1)} %bitcast.102), calls=%async_computation | async-start | bytes 8388608 | tf_op jit(solution)/shard_map/all_to_all | solution.py:195
  207.6 4.5 %compare_select_fusion.2 = (s32[1024,1]{0,1:T(1,128)S(1)}, s32[1024,1]{0,1:T(1,128)S(1)}) fusion(s32[]{:T(128)} %bitcast.22, s32[]{:T(128)} %bitcast.23, s32[]{:T(128)} %bitcast.24, s32[]{:T(128)} %bitcast.25, s32[]{:T(128)} %bitcast.26, s32[]{:T(128)} %bitcast.28, s32[]{:T(128)} %bitcast.27, s32[1024,1]{0,1:T(1,128)S(1)} %reshape.329), kind=kLoop, calls=%fused_computation.83 | loop fusion | flops 15360 | bytes 12316 | tf_op jit(solution)/shard_map/jit(_take)/gather | solution.py:140
  212.3 5.5 %and_select_fusion = (s32[1024]{0:T(1024)S(1)}, s32[1024]{0:T(1024)S(1)}) fusion(s32[1024]{0:T(1024)S(1)} %reshape.330, pred[1024]{0:T(1024)(128)(4,1)S(1)} %get-tuple-element.47, pred[1024]{0:T(1024)(128)(4,1)S(1)} %get-tuple-element.46, pred[1024]{0:T(1024)(128)(4,1)S(1)} %get-tuple-element.45, pred[1024]{0:T(1024)(128)(4,1)S(1)} %get-tuple-element.44, ...), kind=kLoop, calls=%fused_computation.103 | loop fusion | flops 16384 | bytes 25636 | tf_op jit(solution)/shard_map/jit(_take)/select_n | solution.py:140
  217.9 4.5 %reduce-window.6 = s32[16,8,128]{2,1,0:T(8,128)S(1)} reduce-window(s32[16,8,128]{2,1,0:T(8,128)S(1)} %fusion.53, s32[]{:T(128)} %constant.132.clone.1), window={size=1x1x128 pad=0_0x0_0x127_0}, to_apply=%region_2.3 | reduce-window | flops 2080768 | bytes 131076 | tf_op jit(solution)/shard_map/reduce-window
  223.3 1.3 select_reduce_fusion
  225.6 73.4 %all-to-all-done = bf16[16,64,2048]{2,1,0:T(8,128)(2,1)} async-done(((bf16[16,64,2048]{2,1,0:T(8,128)(2,1)}), bf16[16,64,2048]{2,1,0:T(8,128)(2,1)}, u32[]{:S(2)}, u32[]{:S(2)}) %all-to-all-start) | async-done | bytes 4194336 | tf_op jit(solution)/shard_map/all_to_all | solution.py:195
  299.0 2.9 fusion.48
  301.9 3.0 convolution_add_fusion.1
  304.9 3.8 %fusion.16 = bf16[128,2048]{1,0:T(8,128)(2,1)} fusion(f32[128,2048]{1,0:T(8,128)S(1)} %convolution_add_fusion.1, bf16[1024,2048]{1,0:T(8,128)(2,1)} %bitcast.39, f32[128,1024]{1,0:T(8,128)S(1)} %select_reduce_fusion), kind=kOutput, calls=%fused_computation.26 | convolution fusion | flops 538312704 | bytes 6291456 | tf_op jit(solution)/shard_map/dot_general | solution.py:212
  (85 shorter events, 14.4 us)
Async XLA Ops:
  7.2 186.2 %copy-start = (bf16[1,384,2048]{2,1,0:T(8,128)(2,1)S(1)}, bf16[1,384,2048]{2,1,0:T(8,128)(2,1)}, u32[]{:S(2)}) copy-start(bf16[1,384,2048]{2,1,0:T(8,128)(2,1)} %param.27) | copy-start | bytes 4718596
  7.2 51.9 %all-gather.6.cloned.1.call-start = ((), (), s32[]{:S(2)}) async-start(), calls=%async_computation.2 | async-start | bytes 2228224 | tf_op jit(solution)/shard_map/all_gather | solution.py:91
  8.9 163.4 %all-gather.4.cloned.1.call-start = ((), (), s32[]{:S(2)}) async-start(), calls=%async_computation.1 | async-start | bytes 9469952 | tf_op jit(solution)/shard_map/all_gather | solution.py:158
  8.9 70.2 %collective-permute-start = (bf16[2048,512]{1,0:T(8,128)(2,1)}, bf16[2048,512]{1,0:T(8,128)(2,1)}, u32[]{:S(2)}, u32[]{:S(2)}) collective-permute-start(bf16[2048,512]{1,0:T(8,128)(2,1)} %param.19), channel_id=1, source_target_pairs={{0,2},{1,3},{2,0},{3,1},{4,6},{5,7},{6,4},{7,5},{8,10},{9,11},{10,... | collective-permute-start | bytes 6291464 | tf_op jit(solution)/shard_map/ppermute | solution.py:14
  72.7 9.3 %copy-start.4 = (s32[128,8]{0,1:T(8,128)S(1)}, s32[128,8]{0,1:T(8,128)}, u32[]{:S(2)}) copy-start(s32[128,8]{0,1:T(8,128)} %param.22) | copy-start | bytes 12292
  79.1 4.5 %collective-permute-start.1 = (bf16[2048,512]{1,0:T(8,128)(2,1)}, bf16[2048,512]{1,0:T(8,128)(2,1)}, u32[]{:S(2)}, u32[]{:S(2)}) collective-permute-start(bf16[2048,512]{1,0:T(8,128)(2,1)} %param.19), channel_id=1, source_target_pairs={{0,1},{1,0},{2,3},{3,2},{4,5},{5,4},{6,7},{7,6},{8,9},{9,8},{10,11... | collective-permute-start | bytes 6291464 | tf_op jit(solution)/shard_map/ppermute | solution.py:14
  79.4 7.2 %collective-permute-start.2 = (bf16[2048,512]{1,0:T(8,128)(2,1)}, bf16[2048,512]{1,0:T(8,128)(2,1)}, u32[]{:S(2)}, u32[]{:S(2)}) collective-permute-start(bf16[2048,512]{1,0:T(8,128)(2,1)} %collective-permute-done), channel_id=1, source_target_pairs={{0,1},{1,0},{2,3},{3,2},{4,5},{5,4},{6,7},{7,6},{8,9},{9,8},{10,11... | collective-permute-start | bytes 6291464 | tf_op jit(solution)/shard_map/ppermute | solution.py:14
  91.0 2.3 copy-start.5
  91.7 2.9 copy-start.3
  92.5 0.8 copy-start.1
  174.7 8.0 %copy-start.7 = (bf16[2048,2176]{0,1:T(8,128)(2,1)S(1)}, bf16[2048,2176]{0,1:T(8,128)(2,1)}, u32[]{:S(2)}) copy-start(bf16[2048,2176]{0,1:T(8,128)(2,1)} %all-gather.4.cloned.1.call-done) | copy-start | bytes 26738692
  174.7 8.0 %copy-start.8 = (bf16[1,2048,384]{2,1,0:T(8,128)(2,1)S(1)}, bf16[1,2048,384]{2,1,0:T(8,128)(2,1)}, u32[]{:S(2)}) copy-start(bf16[1,2048,384]{2,1,0:T(8,128)(2,1)} %param.26) | copy-start | bytes 4718596
  198.8 24.3 %copy-start.6 = (f32[128,8]{0,1:T(8,128)S(1)}, f32[128,8]{0,1:T(8,128)}, u32[]{:S(2)}) copy-start(f32[128,8]{0,1:T(8,128)} %param.23) | copy-start | bytes 12292
  198.8 25.8 %copy-start.2 = (bf16[128,2048]{0,1:T(8,128)(2,1)S(1)}, bf16[128,2048]{0,1:T(8,128)(2,1)}, u32[]{:S(2)}) copy-start(bf16[128,2048]{0,1:T(8,128)(2,1)} %copy-done.1) | copy-start | bytes 1572868
  198.8 100.2 %all-to-all-start = ((bf16[16,64,2048]{2,1,0:T(8,128)(2,1)}), bf16[16,64,2048]{2,1,0:T(8,128)(2,1)}, u32[]{:S(2)}, u32[]{:S(2)}) async-start(bf16[16,64,2048]{2,1,0:T(8,128)(2,1)} %bitcast.102), calls=%async_computation | async-start | bytes 8388608 | tf_op jit(solution)/shard_map/all_to_all | solution.py:195
Sparse Core Ops, SparseCore 0:
  10.8 48.3 all-gather.5
  94.7 77.5 all-gather.3

commit v6 on v5

--- a/solution.py
+++ b/solution.py
@@ -88,7 +88,8 @@
     block_rows = slice_rows * n_eg
     my_eg = lax.axis_index("eg")
     both = jnp.concatenate([keys, values], axis=2)
-    gathered = lax.all_gather(both[None], ("ctx", "eg"), axis=0, tiled=True)
+    copies = jnp.broadcast_to(both[None], (n_ctx * n_eg,) + both.shape)
+    gathered = lax.all_to_all(copies, ("ctx", "eg"), split_axis=0, concat_axis=0, tiled=True)
     every_block = (
         gathered.reshape(n_ctx, n_eg, shard_blocks, slice_rows, 2 * kv_width)
         .transpose(0, 2, 1, 3, 4)

time: 316 us -> 325 us (1.028)
  starting transfers between devices: 8.6 us -> 15.6 us
    all_gather x1 -> x0, waiting for transfers between devices: 46.9 us -> none  [local(): gathered = lax.all_gather(both[None], ('ctx', 'eg'), axis=0, tiled=True)]
    all_to_all x0 -> x1, waiting for transfers between devices: none -> 46.3 us  [local(): lax.all_to_all(copies, ('ctx', 'eg'), split_axis=0, concat_axis=0, tiled=...]
    all_to_all x0 -> x1, starting transfers between devices: none -> 6.69 us  [local(): lax.all_to_all(copies, ('ctx', 'eg'), split_axis=0, concat_axis=0, tiled=...]
  transfers between devices with their start and end apart: 6 -> 6, of which waited for: 5 -> 6; matrix products, arithmetic and copies ran while one was open for 14% -> 14% of each run, Pallas kernels for 0% -> 0%
where the time goes in v6:
time: 325 us; the launch traced here: 324 us
  waiting for transfers between devices  204 us (63%)
  matrix products  49.3 us (15%)
  other arithmetic  23.8 us (7%)
  local copies, waits for them, and re-layouts  17.1 us (5%)
  starting transfers between devices  15.6 us (5%)
  between operations  14.4 us (4%)
    all_gather x1, waiting for transfers between devices, local(): all_packed = lax.all_gather(packed, ('ctx', 'eg'), axis=0, tiled=True)  78.9 us
    all_to_all x1, waiting for transfers between devices, local(): lax.all_to_all(produced.reshape(slot_count, per_slot, -1), ('ctx', 'eg'),...  73.4 us
    all_to_all x1, waiting for transfers between devices, local(): lax.all_to_all(copies, ('ctx', 'eg'), split_axis=0, concat_axis=0, tiled=...  46.3 us
    sub x1, matrix products, attend_rows(): raised = jnp.exp(logits - largest)  9.71 us
    dot_general x3, matrix products, local(): jnp.dot(part, returned_rows, preferred_element_type=jnp.float32)  9.6 us
    dot_general x1, matrix products, local(): jnp.dot(all_packed, jnp.pad(partner[0], pad_rows), preferred_element_type...  7.93 us
    all_to_all x1, starting transfers between devices, local(): lax.all_to_all(produced.reshape(slot_count, per_slot, -1), ('ctx', 'eg'),...  7.69 us
    all_to_all x1, starting transfers between devices, local(): lax.all_to_all(copies, ('ctx', 'eg'), split_axis=0, concat_axis=0, tiled=...  6.69 us
  transfers between devices with their start and end apart: 6, of which 6 were waited for; matrix products, arithmetic and copies ran while one was open for 14% of the time, Pallas kernels for 0%

profile of v6, /device:TPU:11, one launch (start us, length us, event | category | flops | bytes accessed | tf_op | source)
XLA Modules:
  0.0 323.8 jit_solution(3143106892275477453)
XLA Ops:
  8.2 1.5 broadcast_in_dim.98
  9.7 6.7 %all-to-all-start = ((bf16[16,1,128,512]{3,2,1,0:T(8,128)(2,1)}), bf16[16,1,128,512]{3,2,1,0:T(8,128)(2,1)}, u32[]{:S(2)}, u32[]{:S(2)}) async-start(bf16[16,1,128,512]{3,2,1,0:T(8,128)(2,1)} %broadcast_in_dim.98), calls=%async_computation | async-start | bytes 4194304 | tf_op jit(solution)/shard_map/all_to_all | solution.py:92
  18.0 46.3 %all-to-all-done = bf16[16,1,128,512]{3,2,1,0:T(8,128)(2,1)} async-done(((bf16[16,1,128,512]{3,2,1,0:T(8,128)(2,1)}), bf16[16,1,128,512]{3,2,1,0:T(8,128)(2,1)}, u32[]{:S(2)}, u32[]{:S(2)}) %all-to-all-start) | async-done | bytes 2097184 | tf_op jit(solution)/shard_map/all_to_all | solution.py:92
  64.3 2.2 gather_fusion
  68.2 9.7 %fusion.66 = (f32[2,8,128]{2,1,0:T(8,128)S(1)}, f32[2,8,128,1536]{2,3,1,0:T(8,128)}) fusion(bf16[1536,2,128,1]{2,1,0,3:T(2,128)(2,1)} %bitcast.107, bf16[128,2,8,128]{3,2,1,0:T(8,128)(2,1)} %bitcast.110), kind=kOutput, calls=%fused_computation.128 | convolution fusion | flops 814745088 | bytes 13901824 | tf_op jit(solution)/shard_map/sub | solution.py:28
  77.9 6.5 %fusion.23 = bf16[2,128,8,128]{3,1,2,0:T(8,128)(2,1)} fusion(f32[2,8,128,1536]{2,3,1,0:T(8,128)} %get-tuple-element.73, f32[2,8,128]{2,1,0:T(8,128)S(1)} %get-tuple-element.72, bf16[1536,2,128,1]{2,1,0,3:T(2,128)(2,1)S(1)} %bitcast.108), kind=kOutput, calls=%fused_computation.33 | convolution fusion | flops 811859968 | bytes 13901824 | tf_op jit(solution)/shard_map/kgrn,nkd->rkgd/dot_general | solution.py:31
  86.1 1.3 copy.111
  90.2 3.0 collective-permute-done.2
  93.2 4.4 %fusion.6 = bf16[128,2048]{1,0:T(8,128)(2,1)S(1)} fusion(bf16[128,2048]{0,1:T(8,128)(2,1)} %bitcast.120, bf16[2048,512]{1,0:T(8,128)(2,1)} %collective-permute-done.2, bf16[2048,512]{1,0:T(8,128)(2,1)} %collective-permute-done, bf16[2048,512]{1,0:T(8,128)(2,1)} %collective-permute-done.1, bf16[2048,512]{1,0:T(8,128)(2,1)} %param.19), kind=kOutput, calls=%fused_computation.10 | convolution fusion | flops 1107296256 | bytes 9437184 | tf_op jit(solution)/shard_map/dot_general | solution.py:126
  101.7 78.9 %all-gather.2.cloned.1.call-done = bf16[2048,2176]{0,1:T(8,128)(2,1)} async-done(((bf16[128,2176]{0,1:T(8,128)(2,1)}), bf16[2048,2176]{0,1:T(8,128)(2,1)}) %all-gather.2.cloned.1.call-update) | async-done | bytes 8912912 | tf_op jit(solution)/shard_map/all_gather | solution.py:159
  180.6 1.4 fusion.54
  183.0 7.9 %fusion.18 = f32[2048,384]{1,0:T(8,128)S(1)} fusion(bf16[2048,2176]{0,1:T(8,128)(2,1)} %all-gather.2.cloned.1.call-done, bf16[2048,384]{1,0:T(8,128)(2,1)} %bitcast.118), kind=kOutput, calls=%fused_computation.28 | convolution fusion | flops 3422552064 | bytes 13631488 | tf_op jit(solution)/shard_map/dot_general | solution.py:178
  191.0 5.7 %multiply_convert_fusion = bf16[2048,384]{1,0:T(8,128)(2,1)S(1)} fusion(f32[2048,384]{1,0:T(8,128)S(1)} %fusion.18, bf16[2048,2176]{0,1:T(8,128)(2,1)S(1)} %copy-done.9, bf16[2048,384]{1,0:T(8,128)(2,1)S(1)} %bitcast.119), kind=kOutput, calls=%fused_computation.23 | convolution fusion | flops 3427270656 | bytes 15204352 | tf_op jit(solution)/shard_map/dot_general | solution.py:181
  196.7 5.0 %gather_fusion.2 = bf16[1024,384]{1,0:T(8,128)(2,1)} fusion(bf16[2048,384]{1,0:T(8,128)(2,1)S(1)} %multiply_convert_fusion, s32[1024]{0:T(1024)S(1)} %broadcast_clamp_fusion), kind=kCustom, calls=%fused_computation.2 | custom fusion | bytes 1576960 | tf_op jit(solution)/shard_map/jit(_take)/gather | solution.py:185
  201.7 5.5 %convolution_convert_fusion = bf16[1024,2048]{1,0:T(8,128)(2,1)} fusion(bf16[1,384,2048]{2,1,0:T(8,128)(2,1)S(1)} %copy-done, bf16[1024,384]{1,0:T(8,128)(2,1)} %gather_fusion.2, pred[1024]{0:T(1024)(128)(4,1)S(1)} %compare_and_fusion), kind=kOutput, calls=%fused_computation.22 | convolution fusion | flops 1613103104 | bytes 6554624 | tf_op jit(solution)/shard_map/dot_general | solution.py:186
  207.2 7.7 %all-to-all-start.1 = ((bf16[16,64,2048]{2,1,0:T(8,128)(2,1)}), bf16[16,64,2048]{2,1,0:T(8,128)(2,1)}, u32[]{:S(2)}, u32[]{:S(2)}) async-start(bf16[16,64,2048]{2,1,0:T(8,128)(2,1)} %bitcast.104), calls=%async_computation.1 | async-start | bytes 8388608 | tf_op jit(solution)/shard_map/all_to_all | solution.py:196
  215.9 4.5 %compare_select_fusion.2 = (s32[1024,1]{0,1:T(1,128)S(1)}, s32[1024,1]{0,1:T(1,128)S(1)}) fusion(s32[]{:T(128)} %bitcast.23, s32[]{:T(128)} %bitcast.24, s32[]{:T(128)} %bitcast.25, s32[]{:T(128)} %bitcast.26, s32[]{:T(128)} %bitcast.27, s32[]{:T(128)} %bitcast.29, s32[]{:T(128)} %bitcast.28, s32[1024,1]{0,1:T(1,128)S(1)} %reshape.332), kind=kLoop, calls=%fused_computation.83 | loop fusion | flops 15360 | bytes 12316 | tf_op jit(solution)/shard_map/jit(_take)/gather | solution.py:141
  220.6 5.5 %and_select_fusion = (s32[1024]{0:T(1024)S(1)}, s32[1024]{0:T(1024)S(1)}) fusion(s32[1024]{0:T(1024)S(1)} %reshape.333, pred[1024]{0:T(1024)(128)(4,1)S(1)} %get-tuple-element.47, pred[1024]{0:T(1024)(128)(4,1)S(1)} %get-tuple-element.46, pred[1024]{0:T(1024)(128)(4,1)S(1)} %get-tuple-element.45, pred[1024]{0:T(1024)(128)(4,1)S(1)} %get-tuple-element.44, ...), kind=kLoop, calls=%fused_computation.103 | loop fusion | flops 16384 | bytes 25636 | tf_op jit(solution)/shard_map/jit(_take)/select_n | solution.py:141
  226.2 4.5 %reduce-window.6 = s32[16,8,128]{2,1,0:T(8,128)S(1)} reduce-window(s32[16,8,128]{2,1,0:T(8,128)S(1)} %fusion.53, s32[]{:T(128)} %constant.132.clone.1), window={size=1x1x128 pad=0_0x0_0x127_0}, to_apply=%region_2.3 | reduce-window | flops 2080768 | bytes 131076 | tf_op jit(solution)/shard_map/reduce-window
  231.6 1.3 select_reduce_fusion
  234.0 73.4 %all-to-all-done.1 = bf16[16,64,2048]{2,1,0:T(8,128)(2,1)} async-done(((bf16[16,64,2048]{2,1,0:T(8,128)(2,1)}), bf16[16,64,2048]{2,1,0:T(8,128)(2,1)}, u32[]{:S(2)}, u32[]{:S(2)}) %all-to-all-start.1) | async-done | bytes 4194336 | tf_op jit(solution)/shard_map/all_to_all | solution.py:196
  307.3 2.9 fusion.48
  310.2 3.0 convolution_add_fusion.1
  313.2 3.8 %fusion.16 = bf16[128,2048]{1,0:T(8,128)(2,1)} fusion(f32[128,2048]{1,0:T(8,128)S(1)} %convolution_add_fusion.1, bf16[1024,2048]{1,0:T(8,128)(2,1)} %bitcast.40, f32[128,1024]{1,0:T(8,128)S(1)} %select_reduce_fusion), kind=kOutput, calls=%fused_computation.26 | convolution fusion | flops 538312704 | bytes 6291456 | tf_op jit(solution)/shard_map/dot_general | solution.py:213
  (89 shorter events, 16.8 us)
Async XLA Ops:
  7.2 194.5 %copy-start = (bf16[1,384,2048]{2,1,0:T(8,128)(2,1)S(1)}, bf16[1,384,2048]{2,1,0:T(8,128)(2,1)}, u32[]{:S(2)}) copy-start(bf16[1,384,2048]{2,1,0:T(8,128)(2,1)} %param.27) | copy-start | bytes 4718596
  8.2 8.6 %copy-start.3 = (bf16[128,2048]{1,0:T(8,128)(2,1)S(1)}, bf16[128,2048]{1,0:T(8,128)(2,1)}, u32[]{:S(2)}) copy-start(bf16[128,2048]{1,0:T(8,128)(2,1)} %param.15) | copy-start | bytes 1572868
  9.7 8.0 %copy-start.8 = (s32[4,2]{0,1:T(2,128)S(1)}, s32[4,2]{0,1:T(2,128)}, u32[]{:S(2)}) copy-start(s32[4,2]{0,1:T(2,128)} %param.18) | copy-start | bytes 100
  9.7 54.6 %all-to-all-start = ((bf16[16,1,128,512]{3,2,1,0:T(8,128)(2,1)}), bf16[16,1,128,512]{3,2,1,0:T(8,128)(2,1)}, u32[]{:S(2)}, u32[]{:S(2)}) async-start(bf16[16,1,128,512]{3,2,1,0:T(8,128)(2,1)} %broadcast_in_dim.98), calls=%async_computation | async-start | bytes 4194304 | tf_op jit(solution)/shard_map/all_to_all | solution.py:92
  16.4 164.2 %all-gather.2.cloned.1.call-start = ((), (), s32[]{:S(2)}) async-start(), calls=%async_computation.2 | async-start | bytes 9469952 | tf_op jit(solution)/shard_map/all_gather | solution.py:159
  16.4 68.7 %collective-permute-start = (bf16[2048,512]{1,0:T(8,128)(2,1)}, bf16[2048,512]{1,0:T(8,128)(2,1)}, u32[]{:S(2)}, u32[]{:S(2)}) collective-permute-start(bf16[2048,512]{1,0:T(8,128)(2,1)} %param.19), channel_id=1, source_target_pairs={{0,2},{1,3},{2,0},{3,1},{4,6},{5,7},{6,4},{7,5},{8,10},{9,11},{10,... | collective-permute-start | bytes 6291464 | tf_op jit(solution)/shard_map/ppermute | solution.py:14
  77.9 10.4 %copy-start.5 = (s32[128,8]{0,1:T(8,128)S(1)}, s32[128,8]{0,1:T(8,128)}, u32[]{:S(2)}) copy-start(s32[128,8]{0,1:T(8,128)} %param.22) | copy-start | bytes 12292
  85.2 5.0 %collective-permute-start.1 = (bf16[2048,512]{1,0:T(8,128)(2,1)}, bf16[2048,512]{1,0:T(8,128)(2,1)}, u32[]{:S(2)}, u32[]{:S(2)}) collective-permute-start(bf16[2048,512]{1,0:T(8,128)(2,1)} %param.19), channel_id=1, source_target_pairs={{0,1},{1,0},{2,3},{3,2},{4,5},{5,4},{6,7},{7,6},{8,9},{9,8},{10,11... | collective-permute-start | bytes 6291464 | tf_op jit(solution)/shard_map/ppermute | solution.py:14
  86.0 7.1 %collective-permute-start.2 = (bf16[2048,512]{1,0:T(8,128)(2,1)}, bf16[2048,512]{1,0:T(8,128)(2,1)}, u32[]{:S(2)}, u32[]{:S(2)}) collective-permute-start(bf16[2048,512]{1,0:T(8,128)(2,1)} %collective-permute-done), channel_id=1, source_target_pairs={{0,1},{1,0},{2,3},{3,2},{4,5},{5,4},{6,7},{7,6},{8,9},{9,8},{10,11... | collective-permute-start | bytes 6291464 | tf_op jit(solution)/shard_map/ppermute | solution.py:14
  97.5 2.3 copy-start.6
  98.2 2.9 copy-start.4
  99.0 0.8 copy-start.1
  183.0 8.0 %copy-start.9 = (bf16[2048,2176]{0,1:T(8,128)(2,1)S(1)}, bf16[2048,2176]{0,1:T(8,128)(2,1)}, u32[]{:S(2)}) copy-start(bf16[2048,2176]{0,1:T(8,128)(2,1)} %all-gather.2.cloned.1.call-done) | copy-start | bytes 26738692
  183.0 8.0 %copy-start.10 = (bf16[1,2048,384]{2,1,0:T(8,128)(2,1)S(1)}, bf16[1,2048,384]{2,1,0:T(8,128)(2,1)}, u32[]{:S(2)}) copy-start(bf16[1,2048,384]{2,1,0:T(8,128)(2,1)} %param.26) | copy-start | bytes 4718596
  207.2 24.3 %copy-start.7 = (f32[128,8]{0,1:T(8,128)S(1)}, f32[128,8]{0,1:T(8,128)}, u32[]{:S(2)}) copy-start(f32[128,8]{0,1:T(8,128)} %param.23) | copy-start | bytes 12292
  207.2 25.8 %copy-start.2 = (bf16[128,2048]{0,1:T(8,128)(2,1)S(1)}, bf16[128,2048]{0,1:T(8,128)(2,1)}, u32[]{:S(2)}) copy-start(bf16[128,2048]{0,1:T(8,128)(2,1)} %copy-done.1) | copy-start | bytes 1572868
  207.2 100.2 %all-to-all-start.1 = ((bf16[16,64,2048]{2,1,0:T(8,128)(2,1)}), bf16[16,64,2048]{2,1,0:T(8,128)(2,1)}, u32[]{:S(2)}, u32[]{:S(2)}) async-start(bf16[16,64,2048]{2,1,0:T(8,128)(2,1)} %bitcast.104), calls=%async_computation.1 | async-start | bytes 8388608 | tf_op jit(solution)/shard_map/all_to_all | solution.py:196
Sparse Core Ops, SparseCore 0:
  101.2 79.3 all-gather.1

commit v7 on v5

--- a/solution.py
+++ b/solution.py
@@ -154,10 +154,14 @@
         width = normed.shape[1]
         id_cols = jnp.full((tok_dev, 128), -1.0, jnp.bfloat16)
         id_cols = id_cols.at[:, :top_count].set(expert_ids.astype(jnp.bfloat16))
-        packed = jnp.concatenate([normed, id_cols], axis=1)
+        lead = width // 2
+        packed = jnp.concatenate([normed[:, :lead], id_cols], axis=1)
         all_packed = lax.all_gather(packed, ("ctx", "eg"), axis=0, tiled=True)
-        all_normed = all_packed[:, :width]
-        all_ids = all_packed[:, width : width + top_count].astype(jnp.int32)
+        trailing = jnp.take(normed[:, lead:], source_pair // top_count, axis=0).reshape(
+            slot_count, per_slot, width - lead
+        )
+        arrived = lax.all_to_all(trailing, ("ctx", "eg"), split_axis=0, concat_axis=0, tiled=True)
+        all_ids = all_packed[:, lead : lead + top_count].astype(jnp.int32)
         expert_count = expert_home.shape[0]
         my_expert = jnp.sum(
             jnp.where(expert_home == my_slot, jnp.arange(expert_count, dtype=jnp.int32), 0)
@@ -173,18 +177,9 @@
             chosen.astype(jnp.int32) * jnp.arange(tok_dev, dtype=jnp.int32)[None, None, :], axis=2
         )
         src_rows = local_row + jnp.arange(slot_count, dtype=jnp.int32)[:, None] * tok_dev
-        pad_rows = ((0, all_packed.shape[1] - width), (0, 0))
-        gate_act = jnp.dot(
-            all_packed, jnp.pad(partner[0], pad_rows), preferred_element_type=jnp.float32
-        )
-        up_act = jnp.dot(
-            all_packed, jnp.pad(partner[1], pad_rows), preferred_element_type=jnp.float32
-        )
-        activation = (jax.nn.silu(gate_act) * up_act).astype(jnp.bfloat16)
-        picked = jnp.take(activation, src_rows.reshape(-1), axis=0)
-        produced = jnp.dot(picked, partner[2], preferred_element_type=jnp.float32).astype(
-            jnp.bfloat16
-        )
+        leading = jnp.take(all_packed[:, :lead], src_rows.reshape(-1), axis=0)
+        flat_rows = jnp.concatenate([leading, arrived.reshape(pair_count, width - lead)], axis=1)
+        produced = expert_apply(flat_rows, partner[0], partner[1], partner[2])
     else:
         outbound = jnp.take(normed, source_pair // top_count, axis=0).reshape(
             slot_count, per_slot, -1

time: 316 us -> 333 us (1.054)
  local copies, waits for them, and re-layouts: 16.7 us -> 32.8 us
  waiting for transfers between devices: 201 us -> 192 us
  starting transfers between devices: 8.6 us -> 16.4 us
  other arithmetic: 25.1 us -> 31.4 us
  matrix products: 49.3 us -> 45.1 us
    all_gather x1, waiting for transfers between devices: 77.1 us -> 55.2 us  [local(): all_packed = lax.all_gather(packed, ('ctx', 'eg'), axis=0, tiled=True)]
    all_to_all x1, waiting for transfers between devices: 73.4 us -> 90.9 us  [local(): lax.all_to_all(produced.reshape(slot_count, per_slot, -1), ('ctx', 'eg'),...]
    gather x1 -> x2, local copies, waits for them, and re-layouts: 4.99 us -> 14.1 us  [the longest x1 8.76 us: local(): leading = jnp.take(all_packed[:, :lead], src_rows.reshape(-1), axis=0)]
    select_n x1 -> x4, other arithmetic: 0.01 us -> 6.51 us  [the longest x2 3.29 us: local(): leading = jnp.take(all_packed[:, :lead], src_rows.reshape(-1), axis=0)]
    all_to_all x0 -> x1, starting transfers between devices: none -> 4.89 us  [local(): lax.all_to_all(trailing, ('ctx', 'eg'), split_axis=0, concat_axis=0, tile...]
    slice x0 -> x2, local copies, waits for them, and re-layouts: none -> 4.69 us  [the longest x1 4.65 us: local(): leading = jnp.take(all_packed[:, :lead], src_rows.reshape(-1), axis=0)]
    scatter x0 -> x1, local copies, waits for them, and re-layouts: none -> 4.31 us  [local(): source_pair = jnp.zeros((pair_count,), jnp.int32).at[position].set(jnp.ar...]
    ppermute x3, waiting for transfers between devices: 4.08 us -> 0.01 us  [swapped(): return lax.ppermute(value, axis, pairs)]
  transfers between devices with their start and end apart: 6 -> 7, of which waited for: 5 -> 3; matrix products, arithmetic and copies ran while one was open for 14% -> 23% of each run, Pallas kernels for 0% -> 0%
where the time goes in v7:
time: 333 us; the launch traced here: 332 us
  waiting for transfers between devices  192 us (58%)
  matrix products  45.1 us (14%)
  local copies, waits for them, and re-layouts  32.8 us (10%)
  other arithmetic  31.4 us (9%)
  starting transfers between devices  16.4 us (5%)
  between operations  14.4 us (4%)
    all_to_all x1, waiting for transfers between devices, local(): lax.all_to_all(produced.reshape(slot_count, per_slot, -1), ('ctx', 'eg'),...  90.9 us
    all_gather x1, waiting for transfers between devices, local(): all_packed = lax.all_gather(packed, ('ctx', 'eg'), axis=0, tiled=True)  55.2 us
    all_gather x1, waiting for transfers between devices, local(): gathered = lax.all_gather(both[None], ('ctx', 'eg'), axis=0, tiled=True)  45.7 us
    all_to_all x1, starting transfers between devices, local(): lax.all_to_all(produced.reshape(slot_count, per_slot, -1), ('ctx', 'eg'),...  10.6 us
    sub x1, matrix products, attend_rows(): raised = jnp.exp(logits - largest)  9.7 us
    dot_general x3, matrix products, local(): jnp.dot(part, returned_rows, preferred_element_type=jnp.float32)  9.6 us
    dot_general x1, matrix products, expert_apply(): jnp.dot(activation, down_full, preferred_element_type=jnp.float32)  9.57 us
    gather x1, local copies, waits for them, and re-layouts, local(): leading = jnp.take(all_packed[:, :lead], src_rows.reshape(-1), axis=0)  8.76 us
  transfers between devices with their start and end apart: 7, of which 3 were waited for; matrix products, arithmetic and copies ran while one was open for 23% of the time, Pallas kernels for 0%

profile of v7, /device:TPU:11, one launch (start us, length us, event | category | flops | bytes accessed | tf_op | source)
XLA Modules:
  0.0 332.0 jit_solution(822409524649385241)
XLA Ops:
  10.3 2.0 copy.122
  13.4 45.7 %all-gather.6.cloned.1.call-done = bf16[16,128,512]{2,1,0:T(8,128)(2,1)} async-done(((bf16[1,128,512]{2,1,0:T(8,128)(2,1)}), bf16[16,128,512]{2,1,0:T(8,128)(2,1)}) %all-gather.6.cloned.1.call-update) | async-done | bytes 2097168 | tf_op jit(solution)/shard_map/all_gather | solution.py:91
  59.2 2.2 gather_fusion
  63.0 9.7 %fusion.73 = (f32[2,8,128]{2,1,0:T(8,128)S(1)}, f32[2,8,128,1536]{2,3,1,0:T(8,128)}) fusion(bf16[1536,2,128,1]{2,1,0,3:T(2,128)(2,1)} %bitcast.115, bf16[128,2,8,128]{3,2,1,0:T(8,128)(2,1)} %bitcast.118), kind=kOutput, calls=%fused_computation.146 | convolution fusion | flops 814745088 | bytes 13901824 | tf_op jit(solution)/shard_map/sub | solution.py:28
  72.7 5.7 %fusion.26 = bf16[2,128,8,128]{3,1,2,0:T(8,128)(2,1)S(1)} fusion(f32[2,8,128,1536]{2,3,1,0:T(8,128)} %get-tuple-element.69, f32[2,8,128]{2,1,0:T(8,128)S(1)} %get-tuple-element.68, bf16[1536,2,128,1]{2,1,0,3:T(2,128)(2,1)S(1)} %bitcast.116), kind=kOutput, calls=%fused_computation.39 | convolution fusion | flops 811859968 | bytes 13901824 | tf_op jit(solution)/shard_map/kgrn,nkd->rkgd/dot_general | solution.py:31
  79.7 4.3 %compare_select_fusion.3 = (s32[1024,1]{0,1:T(1,128)S(1)}, s32[1024,1]{0,1:T(1,128)S(1)}) fusion(s32[]{:T(128)} %bitcast.22, s32[]{:T(128)} %bitcast.23, s32[]{:T(128)} %bitcast.24, s32[]{:T(128)} %bitcast.25, s32[]{:T(128)} %bitcast.26, s32[]{:T(128)} %bitcast.28, s32[]{:T(128)} %bitcast.27, s32[1024,1]{0,1:T(1,128)S(1)} %reshape.385), kind=kLoop, calls=%fused_computation.88 | loop fusion | flops 15360 | bytes 12316 | tf_op jit(solution)/shard_map/jit(_take)/gather | solution.py:140
  84.1 5.7 %and_select_fusion.1 = (s32[1024]{0:T(1024)S(1)}, s32[1024]{0:T(1024)S(1)}) fusion(s32[1024]{0:T(1024)S(1)} %reshape.386, pred[1024]{0:T(1024)(128)(4,1)S(1)} %get-tuple-element.39, pred[1024]{0:T(1024)(128)(4,1)S(1)} %get-tuple-element.37, pred[1024]{0:T(1024)(128)(4,1)S(1)} %get-tuple-element.38, pred[1024]{0:T(1024)(128)(4,1)S(1)} %get-tuple-element.36, ...), kind=kLoop, calls=%fused_computation.118 | loop fusion | flops 16384 | bytes 25636 | tf_op jit(solution)/shard_map/jit(_take)/select_n | solution.py:140
  89.9 4.5 %reduce-window.6 = s32[16,8,128]{2,1,0:T(8,128)S(1)} reduce-window(s32[16,8,128]{2,1,0:T(8,128)S(1)} %fusion.56, s32[]{:T(128)} %constant.156.clone.1), window={size=1x1x128 pad=0_0x0_0x127_0}, to_apply=%region_2.3 | reduce-window | flops 2080768 | bytes 131076 | tf_op jit(solution)/shard_map/reduce-window
  96.6 4.8 %fusion.6 = bf16[128,2048]{1,0:T(8,128)(2,1)S(1)} fusion(bf16[128,2048]{0,1:T(8,128)(2,1)S(1)} %bitcast.129, bf16[2048,512]{1,0:T(8,128)(2,1)} %collective-permute-done.2, bf16[2048,512]{1,0:T(8,128)(2,1)} %collective-permute-done, bf16[2048,512]{1,0:T(8,128)(2,1)} %collective-permute-done.1, bf16[2048,512]{1,0:T(8,128)(2,1)} %param.19), kind=kOutput, calls=%fused_computation.12 | convolution fusion | flops 1107296256 | bytes 9437184 | tf_op jit(solution)/shard_map/dot_general | solution.py:125
  104.0 4.3 %scatter_custom_fusion = s32[1024]{0:T(1024)S(1)} fusion(s32[1024]{0:T(1024)S(1)} %bitcast.127, s32[1024]{0:T(1024)S(1)} %iota.45, s32[]{:T(128)} %constant.156.clone.1), kind=kCustom, calls=%fused_computation.126 | custom fusion | bytes 4100 | tf_op jit(solution)/shard_map/scatter | solution.py:149
  108.5 5.4 %gather_fusion.3 = bf16[1024,1024]{1,0:T(8,128)(2,1)} fusion(bf16[128,1024]{1,0:T(8,128)(2,1)S(1)} %get-tuple-element.49, s32[1024]{0:T(1024)S(1)} %broadcast_clamp_fusion), kind=kCustom, calls=%fused_computation.3 | custom fusion | bytes 4198400 | tf_op jit(solution)/shard_map/jit(_take)/gather | solution.py:160
  113.8 3.2 broadcast_select_fusion.1
  117.1 4.9 %all-to-all-start = ((bf16[16,64,1024]{2,1,0:T(8,128)(2,1)}), bf16[16,64,1024]{2,1,0:T(8,128)(2,1)}, u32[]{:S(2)}, u32[]{:S(2)}) async-start(bf16[16,64,1024]{2,1,0:T(8,128)(2,1)} %broadcast_select_fusion.1), calls=%async_computation | async-start | bytes 4194304 | tf_op jit(solution)/shard_map/all_to_all | solution.py:163
  122.6 55.2 %all-gather.4.cloned.1.call-done = bf16[2048,1152]{1,0:T(8,128)(2,1)} async-done(((bf16[128,1152]{1,0:T(8,128)(2,1)}), bf16[2048,1152]{1,0:T(8,128)(2,1)}) %all-gather.4.cloned.1.call-update) | async-done | bytes 4718608 | tf_op jit(solution)/shard_map/all_gather | solution.py:159
  180.5 4.7 %slice.86 = bf16[2048,1024]{1,0:T(8,128)(2,1)} slice(bf16[2048,1152]{1,0:T(8,128)(2,1)} %all-gather.4.cloned.1.call-done), slice={[0:2048], [0:1024]} | slice | bytes 8388608 | tf_op jit(solution)/shard_map/slice | solution.py:180
  185.2 8.8 %gather_fusion.2 = bf16[1024,1024]{1,0:T(8,128)(2,1)} fusion(bf16[2048,1024]{1,0:T(8,128)(2,1)} %slice.86, s32[1024]{0:T(1024)S(1)} %broadcast_clamp_fusion.1), kind=kCustom, calls=%fused_computation.2 | custom fusion | bytes 4198400 | tf_op jit(solution)/shard_map/jit(_take)/gather | solution.py:180
  194.0 3.3 broadcast_select_fusion
  197.3 5.7 %fusion.17 = f32[1024,384]{1,0:T(8,128)} fusion(bf16[1024,1024]{1,0:T(8,128)(2,1)} %bitcast.39, bf16[1024,1024]{1,0:T(8,128)(2,1)} %broadcast_select_fusion, bf16[1,2048,384]{2,1,0:T(8,128)(2,1)S(1)} %copy-done.7), kind=kOutput, calls=%fused_computation.27 | convolution fusion | flops 1619001344 | bytes 7340032 | tf_op jit(solution)/shard_map/dot_general | solution.py:38
  202.9 9.6 %convolution_convert_fusion = bf16[1024,2048]{1,0:T(8,128)(2,1)} fusion(bf16[1,384,2048]{2,1,0:T(8,128)(2,1)S(1)} %copy-done, f32[1024,384]{1,0:T(8,128)} %fusion.17, bf16[1,2048,384]{2,1,0:T(8,128)(2,1)} %param.26, bf16[1024,1024]{1,0:T(8,128)(2,1)} %bitcast.39, bf16[1024,1024]{1,0:T(8,128)(2,1)} %broadcast_select_fusion), kind=kOutput, calls=%fused_computation.25 | convolution fusion | flops 3234070528 | bytes 13107200 | tf_op jit(solution)/shard_map/dot_general | solution.py:41
  212.5 10.6 %all-to-all-start.1 = ((bf16[16,64,2048]{2,1,0:T(8,128)(2,1)}), bf16[16,64,2048]{2,1,0:T(8,128)(2,1)}, u32[]{:S(2)}, u32[]{:S(2)}) async-start(bf16[16,64,2048]{2,1,0:T(8,128)(2,1)} %bitcast.110), calls=%async_computation.1 | async-start | bytes 8388608 | tf_op jit(solution)/shard_map/all_to_all | solution.py:190
  224.6 90.9 %all-to-all-done.1 = bf16[16,64,2048]{2,1,0:T(8,128)(2,1)} async-done(((bf16[16,64,2048]{2,1,0:T(8,128)(2,1)}), bf16[16,64,2048]{2,1,0:T(8,128)(2,1)}, u32[]{:S(2)}, u32[]{:S(2)}) %all-to-all-start.1) | async-done | bytes 4194336 | tf_op jit(solution)/shard_map/all_to_all | solution.py:190
  315.5 2.9 fusion.50
  318.4 3.0 convolution_add_fusion.1
  321.4 3.7 %fusion.18 = bf16[128,2048]{1,0:T(8,128)(2,1)} fusion(f32[128,2048]{1,0:T(8,128)S(1)} %convolution_add_fusion.1, bf16[1024,2048]{1,0:T(8,128)(2,1)} %bitcast.44, f32[128,1024]{1,0:T(8,128)S(1)} %select_reduce_fusion), kind=kOutput, calls=%fused_computation.30 | convolution fusion | flops 538312704 | bytes 6291456 | tf_op jit(solution)/shard_map/dot_general | solution.py:207
  (95 shorter events, 17.0 us)
Async XLA Ops:
  7.2 195.8 %copy-start = (bf16[1,384,2048]{2,1,0:T(8,128)(2,1)S(1)}, bf16[1,384,2048]{2,1,0:T(8,128)(2,1)}, u32[]{:S(2)}) copy-start(bf16[1,384,2048]{2,1,0:T(8,128)(2,1)} %param.27) | copy-start | bytes 4718596
  7.2 52.0 %all-gather.6.cloned.1.call-start = ((), (), s32[]{:S(2)}) async-start(), calls=%async_computation.3 | async-start | bytes 2228224 | tf_op jit(solution)/shard_map/all_gather | solution.py:91
  8.9 168.8 %all-gather.4.cloned.1.call-start = ((), (), s32[]{:S(2)}) async-start(), calls=%async_computation.2 | async-start | bytes 5013504 | tf_op jit(solution)/shard_map/all_gather | solution.py:159
  8.9 69.5 %collective-permute-start = (bf16[2048,512]{1,0:T(8,128)(2,1)}, bf16[2048,512]{1,0:T(8,128)(2,1)}, u32[]{:S(2)}, u32[]{:S(2)}) collective-permute-start(bf16[2048,512]{1,0:T(8,128)(2,1)} %param.19), channel_id=1, source_target_pairs={{0,2},{1,3},{2,0},{3,1},{4,6},{5,7},{6,4},{7,5},{8,10},{9,11},{10,... | collective-permute-start | bytes 6291464 | tf_op jit(solution)/shard_map/ppermute | solution.py:14
  72.7 6.3 %copy-start.3 = (s32[16]{0:T(128)S(1)}, s32[16]{0:T(128)}, u32[]{:S(2)}) copy-start(s32[16]{0:T(128)} %param.24) | copy-start | bytes 196
  72.7 22.4 %copy-start.4 = (s32[128,8]{0,1:T(8,128)S(1)}, s32[128,8]{0,1:T(8,128)}, u32[]{:S(2)}) copy-start(s32[128,8]{0,1:T(8,128)} %param.22) | copy-start | bytes 12292
  78.4 18.2 %collective-permute-start.1 = (bf16[2048,512]{1,0:T(8,128)(2,1)}, bf16[2048,512]{1,0:T(8,128)(2,1)}, u32[]{:S(2)}, u32[]{:S(2)}) collective-permute-start(bf16[2048,512]{1,0:T(8,128)(2,1)} %param.19), channel_id=1, source_target_pairs={{0,1},{1,0},{2,3},{3,2},{4,5},{5,4},{6,7},{7,6},{8,9},{9,8},{10,11... | collective-permute-start | bytes 6291464 | tf_op jit(solution)/shard_map/ppermute | solution.py:14
  78.7 17.9 %collective-permute-start.2 = (bf16[2048,512]{1,0:T(8,128)(2,1)}, bf16[2048,512]{1,0:T(8,128)(2,1)}, u32[]{:S(2)}, u32[]{:S(2)}) collective-permute-start(bf16[2048,512]{1,0:T(8,128)(2,1)} %collective-permute-done), channel_id=1, source_target_pairs={{0,1},{1,0},{2,3},{3,2},{4,5},{5,4},{6,7},{7,6},{8,9},{9,8},{10,11... | collective-permute-start | bytes 6291464 | tf_op jit(solution)/shard_map/ppermute | solution.py:14
  101.5 1.2 copy-start.1
  102.1 0.9 copy-start.5
  102.9 10.9 %copy-start.2 = (bf16[128,2048]{1,0:T(8,128)(2,1)}, bf16[128,2048]{1,0:T(8,128)(2,1)S(1)}, u32[]{:S(2)}) copy-start(bf16[128,2048]{1,0:T(8,128)(2,1)S(1)} %get-tuple-element.45) | copy-start | bytes 1572868
  117.1 80.2 %all-to-all-start = ((bf16[16,64,1024]{2,1,0:T(8,128)(2,1)}), bf16[16,64,1024]{2,1,0:T(8,128)(2,1)}, u32[]{:S(2)}, u32[]{:S(2)}) async-start(bf16[16,64,1024]{2,1,0:T(8,128)(2,1)} %broadcast_select_fusion.1), calls=%async_computation | async-start | bytes 4194304 | tf_op jit(solution)/shard_map/all_to_all | solution.py:163
  194.0 3.3 copy-start.7
  212.5 10.7 %copy-start.6 = (f32[128,8]{0,1:T(8,128)S(1)}, f32[128,8]{0,1:T(8,128)}, u32[]{:S(2)}) copy-start(f32[128,8]{0,1:T(8,128)} %param.23) | copy-start | bytes 12292
  212.5 103.0 %all-to-all-start.1 = ((bf16[16,64,2048]{2,1,0:T(8,128)(2,1)}), bf16[16,64,2048]{2,1,0:T(8,128)(2,1)}, u32[]{:S(2)}, u32[]{:S(2)}) async-start(bf16[16,64,2048]{2,1,0:T(8,128)(2,1)} %bitcast.110), calls=%async_computation.1 | async-start | bytes 8388608 | tf_op jit(solution)/shard_map/all_to_all | solution.py:190
Sparse Core Ops, SparseCore 0:
  10.8 48.3 all-gather.5
  104.1 73.5 all-gather.3

commit v8 on v5

--- a/solution.py
+++ b/solution.py
@@ -88,18 +88,42 @@
     block_rows = slice_rows * n_eg
     my_eg = lax.axis_index("eg")
     both = jnp.concatenate([keys, values], axis=2)
-    gathered = lax.all_gather(both[None], ("ctx", "eg"), axis=0, tiled=True)
-    every_block = (
-        gathered.reshape(n_ctx, n_eg, shard_blocks, slice_rows, 2 * kv_width)
-        .transpose(0, 2, 1, 3, 4)
-        .reshape(n_ctx * shard_blocks, block_rows, 2 * kv_width)
-    )
     query_rows = queries.shape[0]
     my_block = (my_ctx * n_eg + my_eg) * query_rows // block_rows
     chosen_blocks = jnp.concatenate(
         [my_block[None].astype(jnp.int32), jnp.take(selected, my_block, axis=0)]
     )
-    context = jnp.take(every_block, chosen_blocks, axis=0)
+    if n_ctx * n_eg <= 16:
+        received = []
+        for ctx_step in range(n_ctx):
+            for eg_flip in range(n_eg):
+                if ctx_step == 0 and eg_flip == 0:
+                    received.append(both)
+                    continue
+                pairs = [
+                    (c * n_eg + e, ((c + ctx_step) % n_ctx) * n_eg + (e ^ eg_flip))
+                    for c in range(n_ctx)
+                    for e in range(n_eg)
+                ]
+                received.append(lax.ppermute(both, ("ctx", "eg"), pairs))
+        stacked = jnp.stack(received).reshape(
+            n_ctx, n_eg, shard_blocks, slice_rows, 2 * kv_width
+        )
+        source_ctx = chosen_blocks // shard_blocks
+        by_block = jnp.take(stacked, (my_ctx - source_ctx) % n_ctx, axis=0)
+        by_block = jnp.take(by_block, jnp.arange(n_eg, dtype=jnp.int32) ^ my_eg, axis=1)
+        inner = chosen_blocks % shard_blocks
+        context = jnp.take_along_axis(
+            by_block, inner[:, None, None, None, None], axis=2
+        ).reshape(1 + pick_count, block_rows, 2 * kv_width)
+    else:
+        gathered = lax.all_gather(both[None], ("ctx", "eg"), axis=0, tiled=True)
+        every_block = (
+            gathered.reshape(n_ctx, n_eg, shard_blocks, slice_rows, 2 * kv_width)
+            .transpose(0, 2, 1, 3, 4)
+            .reshape(n_ctx * shard_blocks, block_rows, 2 * kv_width)
+        )
+        context = jnp.take(every_block, chosen_blocks, axis=0)
     context_keys = context[:, :, :kv_width]
     context_values = context[:, :, kv_width:]
     span = (1 + pick_count) * block_rows
@@ -181,7 +205,13 @@
             all_packed, jnp.pad(partner[1], pad_rows), preferred_element_type=jnp.float32
         )
         activation = (jax.nn.silu(gate_act) * up_act).astype(jnp.bfloat16)
-        picked = jnp.take(activation, src_rows.reshape(-1), axis=0)
+        pick_matrix = (
+            src_rows.reshape(-1)[:, None]
+            == jnp.arange(activation.shape[0], dtype=jnp.int32)[None, :]
+        ).astype(jnp.bfloat16)
+        picked = jnp.dot(pick_matrix, activation, preferred_element_type=jnp.float32).astype(
+            jnp.bfloat16
+        )
         produced = jnp.dot(picked, partner[2], preferred_element_type=jnp.float32).astype(
             jnp.bfloat16
         )

time: 316 us -> 349 us (1.10)
  starting transfers between devices: 8.6 us -> 30.3 us
  local copies, waits for them, and re-layouts: 16.7 us -> 31.1 us
  waiting for transfers between devices: 201 us -> 191 us
  matrix products: 49.3 us -> 55.3 us
    all_gather x1 -> x0, waiting for transfers between devices: 46.9 us -> none  [local(): gathered = lax.all_gather(both[None], ('ctx', 'eg'), axis=0, tiled=True)]
    ppermute x0 -> x15, starting transfers between devices: none -> 21.2 us  [local(): received.append(lax.ppermute(both, ('ctx', 'eg'), pairs))]
    ppermute x0 -> x15, waiting for transfers between devices: none -> 17.8 us  [local(): received.append(lax.ppermute(both, ('ctx', 'eg'), pairs))]
    ppermute x3, waiting for transfers between devices: 4.08 us -> 20.1 us  [swapped(): return lax.ppermute(value, axis, pairs)]
    unnamed x25 -> x39, local copies, waits for them, and re-layouts: 5.37 us -> 14.4 us
    dot_general x1, matrix products: 5.73 us -> 12 us  [local(): jnp.dot(pick_matrix, activation, preferred_element_type=jnp.float32)]
    gather x2 -> x4, local copies, waits for them, and re-layouts: 7.23 us -> 6.35 us  [the longest x1 2.24 us: local(): by_block = jnp.take(stacked, (my_ctx - source_ctx) % n_ctx, axis=0)]
  transfers between devices with their start and end apart: 6 -> 20, of which waited for: 5 -> 10; matrix products, arithmetic and copies ran while one was open for 14% -> 19% of each run, Pallas kernels for 0% -> 0%
where the time goes in v8:
time: 349 us; the launch traced here: 348 us
  waiting for transfers between devices  191 us (55%)
  matrix products  55.3 us (16%)
  local copies, waits for them, and re-layouts  31.1 us (9%)
  starting transfers between devices  30.3 us (9%)
  other arithmetic  25.8 us (7%)
  between operations  14.4 us (4%)
    all_gather x1, waiting for transfers between devices, local(): all_packed = lax.all_gather(packed, ('ctx', 'eg'), axis=0, tiled=True)  79.5 us
    all_to_all x1, waiting for transfers between devices, local(): lax.all_to_all(produced.reshape(slot_count, per_slot, -1), ('ctx', 'eg'),...  73.3 us
    ppermute x15, starting transfers between devices, local(): received.append(lax.ppermute(both, ('ctx', 'eg'), pairs))  21.2 us
    ppermute x3, waiting for transfers between devices, swapped(): return lax.ppermute(value, axis, pairs)  20.1 us
    ppermute x15, waiting for transfers between devices, local(): received.append(lax.ppermute(both, ('ctx', 'eg'), pairs))  17.8 us
    unnamed x39, local copies, waits for them, and re-layouts  14.4 us
    dot_general x1, matrix products, local(): jnp.dot(pick_matrix, activation, preferred_element_type=jnp.float32)  12 us
    dot_general x3, matrix products, local(): jnp.dot(part, returned_rows, preferred_element_type=jnp.float32)  9.6 us
  transfers between devices with their start and end apart: 20, of which 10 were waited for; matrix products, arithmetic and copies ran while one was open for 19% of the time, Pallas kernels for 0%

profile of v8, /device:TPU:11, one launch (start us, length us, event | category | flops | bytes accessed | tf_op | source)
XLA Modules:
  0.0 347.7 jit_solution(15837346812360561656)
XLA Ops:
  18.7 2.3 collective-permute-start.7
  21.7 2.3 collective-permute-start.8
  25.8 2.3 collective-permute-start.10
  31.5 9.3 %collective-permute-done.8 = bf16[1,128,512]{2,1,0:T(8,128)(2,1)S(1)} collective-permute-done((bf16[1,128,512]{2,1,0:T(8,128)(2,1)S(1)}, bf16[1,128,512]{2,1,0:T(8,128)(2,1)S(1)}, u32[]{:S(2)}, u32[]{:S(2)}) %collective-permute-start.8) | collective-permute-done | bytes 131104 | tf_op jit(solution)/shard_map/ppermute | solution.py:108
  43.7 3.9 %collective-permute-start.14 = (bf16[1,128,512]{2,1,0:T(8,128)(2,1)S(1)}, bf16[1,128,512]{2,1,0:T(8,128)(2,1)S(1)}, u32[]{:S(2)}, u32[]{:S(2)}) collective-permute-start(bf16[1,128,512]{2,1,0:T(8,128)(2,1)S(1)} %constant_dynamic-update-slice_fusion), channel_id=1, source_target_pairs={{0,14},{1,15},{2,12},{3,13},{4,2},{5,3},{6,0},{7,1},{8,6},{9,7},{1... | collective-permute-start | bytes 393224 | tf_op jit(solution)/shard_map/ppermute | solution.py:108
  50.7 4.2 %collective-permute-done.11 = bf16[1,128,512]{2,1,0:T(8,128)(2,1)S(1)} collective-permute-done((bf16[1,128,512]{2,1,0:T(8,128)(2,1)S(1)}, bf16[1,128,512]{2,1,0:T(8,128)(2,1)S(1)}, u32[]{:S(2)}, u32[]{:S(2)}) %collective-permute-start.11) | collective-permute-done | bytes 131104 | tf_op jit(solution)/shard_map/ppermute | solution.py:108
  76.0 9.5 %fusion.75 = (f32[2,8,128]{2,1,0:T(8,128)S(1)}, f32[2,8,128,1536]{2,3,1,0:T(8,128)}) fusion(bf16[1536,2,128,1]{2,1,0,3:T(2,128)(2,1)S(1)} %bitcast.150, bf16[128,2,8,128]{3,2,1,0:T(8,128)(2,1)} %bitcast.153), kind=kOutput, calls=%fused_computation.156 | convolution fusion | flops 814745088 | bytes 13901824 | tf_op jit(solution)/shard_map/sub | solution.py:28
  85.6 6.5 %fusion.32 = bf16[2,128,8,128]{3,1,2,0:T(8,128)(2,1)} fusion(f32[2,8,128,1536]{2,3,1,0:T(8,128)} %get-tuple-element.71, f32[2,8,128]{2,1,0:T(8,128)S(1)} %get-tuple-element.70, bf16[1536,2,128,1]{2,1,0,3:T(2,128)(2,1)S(1)} %bitcast.151), kind=kOutput, calls=%fused_computation.41 | convolution fusion | flops 811859968 | bytes 13901824 | tf_op jit(solution)/shard_map/kgrn,nkd->rkgd/dot_general | solution.py:31
  92.1 14.7 %collective-permute-done = bf16[2048,512]{1,0:T(8,128)(2,1)} collective-permute-done((bf16[2048,512]{1,0:T(8,128)(2,1)}, bf16[2048,512]{1,0:T(8,128)(2,1)}, u32[]{:S(2)}, u32[]{:S(2)}) %collective-permute-start) | collective-permute-done | bytes 2097184 | tf_op jit(solution)/shard_map/ppermute | solution.py:14
  108.9 2.4 collective-permute-done.16
  111.4 3.0 collective-permute-done.17
  114.4 4.4 %fusion.6 = bf16[128,2048]{1,0:T(8,128)(2,1)S(1)} fusion(bf16[128,2048]{0,1:T(8,128)(2,1)} %bitcast.162, bf16[2048,512]{1,0:T(8,128)(2,1)} %collective-permute-done.17, bf16[2048,512]{1,0:T(8,128)(2,1)} %collective-permute-done, bf16[2048,512]{1,0:T(8,128)(2,1)} %collective-permute-done.16, bf16[2048,512]{1,0:T(8,128)(2,1)} %param.19), kind=kOutput, calls=%fused_computation.11 | convolution fusion | flops 1107296256 | bytes 9437184 | tf_op jit(solution)/shard_map/dot_general | solution.py:149
  124.0 79.5 %all-gather.2.cloned.1.call-done = bf16[2048,2176]{0,1:T(8,128)(2,1)} async-done(((bf16[128,2176]{0,1:T(8,128)(2,1)}), bf16[2048,2176]{0,1:T(8,128)(2,1)}) %all-gather.2.cloned.1.call-update) | async-done | bytes 8912912 | tf_op jit(solution)/shard_map/all_gather | solution.py:182
  205.8 8.9 %fusion.22 = f32[2048,384]{1,0:T(8,128)} fusion(bf16[2048,2176]{0,1:T(8,128)(2,1)} %all-gather.2.cloned.1.call-done, bf16[2048,384]{1,0:T(8,128)(2,1)} %bitcast.160), kind=kOutput, calls=%fused_computation.32 | convolution fusion | flops 3422552064 | bytes 13631488 | tf_op jit(solution)/shard_map/dot_general | solution.py:201
  214.7 12.0 %fusion.29 = bf16[1024,384]{1,0:T(8,128)(2,1)S(1)} fusion(f32[2048,384]{1,0:T(8,128)} %fusion.22, bf16[2048,2176]{0,1:T(8,128)(2,1)} %all-gather.2.cloned.1.call-done, bf16[2048,384]{1,0:T(8,128)(2,1)} %bitcast.161, s32[1024]{0:T(1024)S(1)} %add.207), kind=kOutput, calls=%fused_computation.40 | convolution fusion | flops 5040373760 | bytes 14422016 | tf_op jit(solution)/shard_map/dot_general | solution.py:212
  226.7 4.3 %convolution_convert_fusion = bf16[1024,2048]{1,0:T(8,128)(2,1)} fusion(bf16[1024,384]{1,0:T(8,128)(2,1)S(1)} %fusion.29, bf16[1,384,2048]{2,1,0:T(8,128)(2,1)S(1)} %copy-done), kind=kOutput, calls=%fused_computation.26 | convolution fusion | flops 1612709888 | bytes 6553600 | tf_op jit(solution)/shard_map/dot_general | solution.py:215
  231.1 7.7 %all-to-all-start = ((bf16[16,64,2048]{2,1,0:T(8,128)(2,1)}), bf16[16,64,2048]{2,1,0:T(8,128)(2,1)}, u32[]{:S(2)}, u32[]{:S(2)}) async-start(bf16[16,64,2048]{2,1,0:T(8,128)(2,1)} %bitcast.146), calls=%async_computation | async-start | bytes 8388608 | tf_op jit(solution)/shard_map/all_to_all | solution.py:225
  239.9 4.4 %compare_select_fusion.1 = (s32[1024,1]{0,1:T(1,128)S(1)}, s32[1024,1]{0,1:T(1,128)S(1)}) fusion(s32[]{:T(128)} %bitcast.43, s32[]{:T(128)} %bitcast.44, s32[]{:T(128)} %bitcast.45, s32[]{:T(128)} %bitcast.46, s32[]{:T(128)} %bitcast.47, s32[]{:T(128)} %bitcast.49, s32[]{:T(128)} %bitcast.48, s32[1024,1]{0,1:T(1,128)S(1)} %reshape.377), kind=kLoop, calls=%fused_computation.104 | loop fusion | flops 15360 | bytes 12316 | tf_op jit(solution)/shard_map/jit(_take)/gather | solution.py:164
  244.4 5.6 %and_select_fusion = (s32[1024]{0:T(1024)S(1)}, s32[1024]{0:T(1024)S(1)}) fusion(s32[1024]{0:T(1024)S(1)} %reshape.378, pred[1024]{0:T(1024)(128)(4,1)S(1)} %get-tuple-element.45, pred[1024]{0:T(1024)(128)(4,1)S(1)} %get-tuple-element.44, pred[1024]{0:T(1024)(128)(4,1)S(1)} %get-tuple-element.43, pred[1024]{0:T(1024)(128)(4,1)S(1)} %get-tuple-element.42, ...), kind=kLoop, calls=%fused_computation.122 | loop fusion | flops 16384 | bytes 25636 | tf_op jit(solution)/shard_map/jit(_take)/select_n | solution.py:164
  250.1 4.5 %reduce-window.6 = s32[16,8,128]{2,1,0:T(8,128)S(1)} reduce-window(s32[16,8,128]{2,1,0:T(8,128)S(1)} %fusion.59, s32[]{:T(128)} %constant.184.clone.1), window={size=1x1x128 pad=0_0x0_0x127_0}, to_apply=%region_2.3 | reduce-window | flops 2080768 | bytes 131076 | tf_op jit(solution)/shard_map/reduce-window
  257.9 73.3 %all-to-all-done = bf16[16,64,2048]{2,1,0:T(8,128)(2,1)} async-done(((bf16[16,64,2048]{2,1,0:T(8,128)(2,1)}), bf16[16,64,2048]{2,1,0:T(8,128)(2,1)}, u32[]{:S(2)}, u32[]{:S(2)}) %all-to-all-start) | async-done | bytes 4194336 | tf_op jit(solution)/shard_map/all_to_all | solution.py:225
  331.2 2.9 fusion.54
  334.2 2.9 convolution_add_fusion.1
  337.1 3.8 %fusion.18 = bf16[128,2048]{1,0:T(8,128)(2,1)} fusion(f32[128,2048]{1,0:T(8,128)S(1)} %convolution_add_fusion.1, bf16[1024,2048]{1,0:T(8,128)(2,1)} %bitcast.59, f32[128,1024]{1,0:T(8,128)S(1)} %select_reduce_fusion), kind=kOutput, calls=%fused_computation.30 | convolution fusion | flops 538312704 | bytes 6291456 | tf_op jit(solution)/shard_map/dot_general | solution.py:242
  (126 shorter events, 58.5 us)
Async XLA Ops:
  7.2 219.6 %copy-start = (bf16[1,384,2048]{2,1,0:T(8,128)(2,1)S(1)}, bf16[1,384,2048]{2,1,0:T(8,128)(2,1)}, u32[]{:S(2)}) copy-start(bf16[1,384,2048]{2,1,0:T(8,128)(2,1)} %param.27) | copy-start | bytes 4718596
  7.2 196.4 %all-gather.2.cloned.1.call-start = ((), (), s32[]{:S(2)}) async-start(), calls=%async_computation.1 | async-start | bytes 9469952 | tf_op jit(solution)/shard_map/all_gather | solution.py:182
  9.0 9.0 %collective-permute-start.1 = (bf16[1,128,512]{2,1,0:T(8,128)(2,1)S(1)}, bf16[1,128,512]{2,1,0:T(8,128)(2,1)S(1)}, u32[]{:S(2)}, u32[]{:S(2)}) collective-permute-start(bf16[1,128,512]{2,1,0:T(8,128)(2,1)S(1)} %constant_dynamic-update-slice_fusion), channel_id=1, source_target_pairs={{0,1},{1,0},{2,3},{3,2},{4,5},{5,4},{6,7},{7,6},{8,9},{9,8},{10,11... | collective-permute-start | bytes 393224 | tf_op jit(solution)/shard_map/ppermute | solution.py:108
  9.7 9.0 %collective-permute-start.2 = (bf16[1,128,512]{2,1,0:T(8,128)(2,1)S(1)}, bf16[1,128,512]{2,1,0:T(8,128)(2,1)S(1)}, u32[]{:S(2)}, u32[]{:S(2)}) collective-permute-start(bf16[1,128,512]{2,1,0:T(8,128)(2,1)S(1)} %constant_dynamic-update-slice_fusion), channel_id=1, source_target_pairs={{0,2},{1,3},{2,0},{3,1},{4,6},{5,7},{6,4},{7,5},{8,10},{9,11},{10,... | collective-permute-start | bytes 393224 | tf_op jit(solution)/shard_map/ppermute | solution.py:108
  10.0 11.7 %collective-permute-start.3 = (bf16[1,128,512]{2,1,0:T(8,128)(2,1)S(1)}, bf16[1,128,512]{2,1,0:T(8,128)(2,1)S(1)}, u32[]{:S(2)}, u32[]{:S(2)}) collective-permute-start(bf16[1,128,512]{2,1,0:T(8,128)(2,1)S(1)} %constant_dynamic-update-slice_fusion), channel_id=1, source_target_pairs={{0,3},{1,2},{2,1},{3,0},{4,7},{5,6},{6,5},{7,4},{8,11},{9,10},{10,... | collective-permute-start | bytes 393224 | tf_op jit(solution)/shard_map/ppermute | solution.py:108
  11.3 13.3 %collective-permute-start.4 = (bf16[1,128,512]{2,1,0:T(8,128)(2,1)S(1)}, bf16[1,128,512]{2,1,0:T(8,128)(2,1)S(1)}, u32[]{:S(2)}, u32[]{:S(2)}) collective-permute-start(bf16[1,128,512]{2,1,0:T(8,128)(2,1)S(1)} %constant_dynamic-update-slice_fusion), channel_id=1, source_target_pairs={{0,4},{1,5},{2,6},{3,7},{4,8},{5,9},{6,10},{7,11},{8,12},{9,13},{1... | collective-permute-start | bytes 393224 | tf_op jit(solution)/shard_map/ppermute | solution.py:108
  12.6 13.2 %collective-permute-start.5 = (bf16[1,128,512]{2,1,0:T(8,128)(2,1)S(1)}, bf16[1,128,512]{2,1,0:T(8,128)(2,1)S(1)}, u32[]{:S(2)}, u32[]{:S(2)}) collective-permute-start(bf16[1,128,512]{2,1,0:T(8,128)(2,1)S(1)} %constant_dynamic-update-slice_fusion), channel_id=1, source_target_pairs={{0,5},{1,4},{2,7},{3,6},{4,9},{5,8},{6,11},{7,10},{8,13},{9,12},{1... | collective-permute-start | bytes 393224 | tf_op jit(solution)/shard_map/ppermute | solution.py:108
  18.0 10.7 %collective-permute-start.6 = (bf16[1,128,512]{2,1,0:T(8,128)(2,1)S(1)}, bf16[1,128,512]{2,1,0:T(8,128)(2,1)S(1)}, u32[]{:S(2)}, u32[]{:S(2)}) collective-permute-start(bf16[1,128,512]{2,1,0:T(8,128)(2,1)S(1)} %constant_dynamic-update-slice_fusion), channel_id=1, source_target_pairs={{0,6},{1,7},{2,4},{3,5},{4,10},{5,11},{6,8},{7,9},{8,14},{9,15},{1... | collective-permute-start | bytes 393224 | tf_op jit(solution)/shard_map/ppermute | solution.py:108
  18.7 11.9 %collective-permute-start.7 = (bf16[1,128,512]{2,1,0:T(8,128)(2,1)S(1)}, bf16[1,128,512]{2,1,0:T(8,128)(2,1)S(1)}, u32[]{:S(2)}, u32[]{:S(2)}) collective-permute-start(bf16[1,128,512]{2,1,0:T(8,128)(2,1)S(1)} %constant_dynamic-update-slice_fusion), channel_id=1, source_target_pairs={{0,7},{1,6},{2,5},{3,4},{4,11},{5,10},{6,9},{7,8},{8,15},{9,14},{1... | collective-permute-start | bytes 393224 | tf_op jit(solution)/shard_map/ppermute | solution.py:108
  21.7 19.1 %collective-permute-start.8 = (bf16[1,128,512]{2,1,0:T(8,128)(2,1)S(1)}, bf16[1,128,512]{2,1,0:T(8,128)(2,1)S(1)}, u32[]{:S(2)}, u32[]{:S(2)}) collective-permute-start(bf16[1,128,512]{2,1,0:T(8,128)(2,1)S(1)} %constant_dynamic-update-slice_fusion), channel_id=1, source_target_pairs={{0,8},{1,9},{2,10},{3,11},{4,12},{5,13},{6,14},{7,15},{8,0},{9,1},... | collective-permute-start | bytes 393224 | tf_op jit(solution)/shard_map/ppermute | solution.py:108
  24.7 19.0 %collective-permute-start.9 = (bf16[1,128,512]{2,1,0:T(8,128)(2,1)S(1)}, bf16[1,128,512]{2,1,0:T(8,128)(2,1)S(1)}, u32[]{:S(2)}, u32[]{:S(2)}) collective-permute-start(bf16[1,128,512]{2,1,0:T(8,128)(2,1)S(1)} %constant_dynamic-update-slice_fusion), channel_id=1, source_target_pairs={{0,9},{1,8},{2,11},{3,10},{4,13},{5,12},{6,15},{7,14},{8,1},{9,0},... | collective-permute-start | bytes 393224 | tf_op jit(solution)/shard_map/ppermute | solution.py:108
  25.8 23.3 %collective-permute-start.10 = (bf16[1,128,512]{2,1,0:T(8,128)(2,1)S(1)}, bf16[1,128,512]{2,1,0:T(8,128)(2,1)S(1)}, u32[]{:S(2)}, u32[]{:S(2)}) collective-permute-start(bf16[1,128,512]{2,1,0:T(8,128)(2,1)S(1)} %constant_dynamic-update-slice_fusion), channel_id=1, source_target_pairs={{0,10},{1,11},{2,8},{3,9},{4,14},{5,15},{6,12},{7,13},{8,2},{9,3},... | collective-permute-start | bytes 393224 | tf_op jit(solution)/shard_map/ppermute | solution.py:108
  28.7 26.2 %collective-permute-start.11 = (bf16[1,128,512]{2,1,0:T(8,128)(2,1)S(1)}, bf16[1,128,512]{2,1,0:T(8,128)(2,1)S(1)}, u32[]{:S(2)}, u32[]{:S(2)}) collective-permute-start(bf16[1,128,512]{2,1,0:T(8,128)(2,1)S(1)} %constant_dynamic-update-slice_fusion), channel_id=1, source_target_pairs={{0,11},{1,10},{2,9},{3,8},{4,15},{5,14},{6,13},{7,12},{8,3},{9,2},... | collective-permute-start | bytes 393224 | tf_op jit(solution)/shard_map/ppermute | solution.py:108
  30.6 25.8 %collective-permute-start.12 = (bf16[1,128,512]{2,1,0:T(8,128)(2,1)S(1)}, bf16[1,128,512]{2,1,0:T(8,128)(2,1)S(1)}, u32[]{:S(2)}, u32[]{:S(2)}) collective-permute-start(bf16[1,128,512]{2,1,0:T(8,128)(2,1)S(1)} %constant_dynamic-update-slice_fusion), channel_id=1, source_target_pairs={{0,12},{1,13},{2,14},{3,15},{4,0},{5,1},{6,2},{7,3},{8,4},{9,5},{1... | collective-permute-start | bytes 393224 | tf_op jit(solution)/shard_map/ppermute | solution.py:108
  40.8 16.2 %collective-permute-start.13 = (bf16[1,128,512]{2,1,0:T(8,128)(2,1)S(1)}, bf16[1,128,512]{2,1,0:T(8,128)(2,1)S(1)}, u32[]{:S(2)}, u32[]{:S(2)}) collective-permute-start(bf16[1,128,512]{2,1,0:T(8,128)(2,1)S(1)} %constant_dynamic-update-slice_fusion), channel_id=1, source_target_pairs={{0,13},{1,12},{2,15},{3,14},{4,1},{5,0},{6,3},{7,2},{8,5},{9,4},{1... | collective-permute-start | bytes 393224 | tf_op jit(solution)/shard_map/ppermute | solution.py:108
  43.7 15.3 %collective-permute-start.14 = (bf16[1,128,512]{2,1,0:T(8,128)(2,1)S(1)}, bf16[1,128,512]{2,1,0:T(8,128)(2,1)S(1)}, u32[]{:S(2)}, u32[]{:S(2)}) collective-permute-start(bf16[1,128,512]{2,1,0:T(8,128)(2,1)S(1)} %constant_dynamic-update-slice_fusion), channel_id=1, source_target_pairs={{0,14},{1,15},{2,12},{3,13},{4,2},{5,3},{6,0},{7,1},{8,6},{9,7},{1... | collective-permute-start | bytes 393224 | tf_op jit(solution)/shard_map/ppermute | solution.py:108
  49.1 12.7 %collective-permute-start.15 = (bf16[1,128,512]{2,1,0:T(8,128)(2,1)S(1)}, bf16[1,128,512]{2,1,0:T(8,128)(2,1)S(1)}, u32[]{:S(2)}, u32[]{:S(2)}) collective-permute-start(bf16[1,128,512]{2,1,0:T(8,128)(2,1)S(1)} %constant_dynamic-update-slice_fusion), channel_id=1, source_target_pairs={{0,15},{1,14},{2,13},{3,12},{4,3},{5,2},{6,1},{7,0},{8,7},{9,6},{1... | collective-permute-start | bytes 393224 | tf_op jit(solution)/shard_map/ppermute | solution.py:108
  54.9 51.9 %collective-permute-start = (bf16[2048,512]{1,0:T(8,128)(2,1)}, bf16[2048,512]{1,0:T(8,128)(2,1)}, u32[]{:S(2)}, u32[]{:S(2)}) collective-permute-start(bf16[2048,512]{1,0:T(8,128)(2,1)} %param.19), channel_id=1, source_target_pairs={{0,2},{1,3},{2,0},{3,1},{4,6},{5,7},{6,4},{7,5},{8,10},{9,11},{10,... | collective-permute-start | bytes 6291464 | tf_op jit(solution)/shard_map/ppermute | solution.py:14
  85.6 21.8 %copy-start.3 = (bf16[128,2048]{1,0:T(8,128)(2,1)S(1)}, bf16[128,2048]{1,0:T(8,128)(2,1)}, u32[]{:S(2)}) copy-start(bf16[128,2048]{1,0:T(8,128)(2,1)} %param.20) | copy-start | bytes 1572868
  85.6 22.7 %copy-start.5 = (s32[128,8]{0,1:T(8,128)S(1)}, s32[128,8]{0,1:T(8,128)}, u32[]{:S(2)}) copy-start(s32[128,8]{0,1:T(8,128)} %param.22) | copy-start | bytes 12292
  106.8 4.6 %collective-permute-start.16 = (bf16[2048,512]{1,0:T(8,128)(2,1)}, bf16[2048,512]{1,0:T(8,128)(2,1)}, u32[]{:S(2)}, u32[]{:S(2)}) collective-permute-start(bf16[2048,512]{1,0:T(8,128)(2,1)} %param.19), channel_id=1, source_target_pairs={{0,1},{1,0},{2,3},{3,2},{4,5},{5,4},{6,7},{7,6},{8,9},{9,8},{10,11... | collective-permute-start | bytes 6291464 | tf_op jit(solution)/shard_map/ppermute | solution.py:14
  107.3 7.1 %collective-permute-start.17 = (bf16[2048,512]{1,0:T(8,128)(2,1)}, bf16[2048,512]{1,0:T(8,128)(2,1)}, u32[]{:S(2)}, u32[]{:S(2)}) collective-permute-start(bf16[2048,512]{1,0:T(8,128)(2,1)} %collective-permute-done), channel_id=1, source_target_pairs={{0,1},{1,0},{2,3},{3,2},{4,5},{5,4},{6,7},{7,6},{8,9},{9,8},{10,11... | collective-permute-start | bytes 6291464 | tf_op jit(solution)/shard_map/ppermute | solution.py:14
  231.1 24.4 %copy-start.7 = (f32[128,8]{0,1:T(8,128)S(1)}, f32[128,8]{0,1:T(8,128)}, u32[]{:S(2)}) copy-start(f32[128,8]{0,1:T(8,128)} %param.23) | copy-start | bytes 12292
  231.1 100.2 %all-to-all-start = ((bf16[16,64,2048]{2,1,0:T(8,128)(2,1)}), bf16[16,64,2048]{2,1,0:T(8,128)(2,1)}, u32[]{:S(2)}, u32[]{:S(2)}) async-start(bf16[16,64,2048]{2,1,0:T(8,128)(2,1)} %bitcast.146), calls=%async_computation | async-start | bytes 8388608 | tf_op jit(solution)/shard_map/all_to_all | solution.py:225
  (4 other events, 16.7 us)
Sparse Core Ops, SparseCore 0:
  123.5 80.0 all-gather.1

commit v9 on v5

--- a/solution.py
+++ b/solution.py
@@ -89,6 +89,25 @@
     my_eg = lax.axis_index("eg")
     both = jnp.concatenate([keys, values], axis=2)
     gathered = lax.all_gather(both[None], ("ctx", "eg"), axis=0, tiled=True)
+    tok_dev = residual.shape[0]
+    top_count = expert_ids.shape[1]
+    slot_count = n_ctx * n_eg
+    pair_count = tok_dev * top_count
+    per_slot = pair_count // slot_count
+    home_slot = jnp.take(expert_home, expert_ids.reshape(-1), axis=0)
+    indicator = (home_slot[:, None] == jnp.arange(slot_count, dtype=jnp.int32)[None, :]).astype(
+        jnp.int32
+    )
+    rank_in_slot = jnp.sum((jnp.cumsum(indicator, axis=0) - 1) * indicator, axis=1)
+    position = home_slot * per_slot + rank_in_slot
+    source_pair = (
+        jnp.zeros((pair_count,), jnp.int32)
+        .at[position]
+        .set(jnp.arange(pair_count, dtype=jnp.int32))
+    )
+    (source_pair, position), gathered = lax.optimization_barrier(
+        ((source_pair, position), gathered)
+    )
     every_block = (
         gathered.reshape(n_ctx, n_eg, shard_blocks, slice_rows, 2 * kv_width)
         .transpose(0, 2, 1, 3, 4)
@@ -133,23 +152,8 @@
     stream = residual.astype(jnp.float32) + attn_out.astype(jnp.float32)
     meansq = jnp.mean(stream * stream, axis=1, keepdims=True)
     normed = (stream * lax.rsqrt(meansq + 1e-06) * norm_gain).astype(jnp.bfloat16)
-    top_count = expert_ids.shape[1]
-    slot_count = n_ctx * n_eg
-    pair_count = tok_dev * top_count
-    per_slot = pair_count // slot_count
-    home_slot = jnp.take(expert_home, expert_ids.reshape(-1), axis=0)
-    indicator = (home_slot[:, None] == jnp.arange(slot_count, dtype=jnp.int32)[None, :]).astype(
-        jnp.int32
-    )
-    rank_in_slot = jnp.sum((jnp.cumsum(indicator, axis=0) - 1) * indicator, axis=1)
-    position = home_slot * per_slot + rank_in_slot
-    source_pair = (
-        jnp.zeros((pair_count,), jnp.int32)
-        .at[position]
-        .set(jnp.arange(pair_count, dtype=jnp.int32))
-    )
     partner = fetch_panels()
-    if slot_count <= 4 * top_count:
+    if slot_count < 0:
         my_slot = my_ctx * n_eg + my_eg
         width = normed.shape[1]
         id_cols = jnp.full((tok_dev, 128), -1.0, jnp.bfloat16)

time: 316 us -> 326 us (1.032)
  blocking collectives: 0 us -> 96.5 us
  waiting for transfers between devices: 201 us -> 122 us
  matrix products: 49.3 us -> 41.1 us
  local copies, waits for them, and re-layouts: 16.7 us -> 22.6 us
    all_to_all x0 -> x1, blocking collectives: none -> 96.5 us  [local(): lax.all_to_all(outbound, ('ctx', 'eg'), split_axis=0, concat_axis=0, tile...]
    all_gather x1 -> x0, waiting for transfers between devices: 77.1 us -> none  [local(): all_packed = lax.all_gather(packed, ('ctx', 'eg'), axis=0, tiled=True)]
    all_gather x1, waiting for transfers between devices: 46.9 us -> 24.4 us  [local(): gathered = lax.all_gather(both[None], ('ctx', 'eg'), axis=0, tiled=True)]
    all_to_all x1, waiting for transfers between devices: 73.4 us -> 90.9 us  [local(): lax.all_to_all(produced.reshape(slot_count, per_slot, -1), ('ctx', 'eg'),...]
    dot_general x3 -> x2, matrix products: 19.1 us -> 11.3 us  [the longest x1 7.77 us: expert_apply(): jnp.dot(activation, down_full, preferred_element_type=jnp.float32)]
    scatter x0 -> x1, local copies, waits for them, and re-layouts: none -> 4.31 us  [local(): source_pair = jnp.zeros((pair_count,), jnp.int32).at[position].set(jnp.ar...]
  transfers between devices with their start and end apart: 6 -> 5, of which waited for: 5 -> 4; matrix products, arithmetic and copies ran while one was open for 14% -> 14% of each run, Pallas kernels for 0% -> 0%
where the time goes in v9:
time: 326 us; the launch traced here: 325 us
  waiting for transfers between devices  122 us (37%)
  blocking collectives  96.5 us (30%)
  matrix products  41.1 us (13%)
  local copies, waits for them, and re-layouts  22.6 us (7%)
  other arithmetic  22.2 us (7%)
  between operations  14.4 us (4%)
  starting transfers between devices  6.38 us (2%)
    all_to_all x1, blocking collectives, local(): lax.all_to_all(outbound, ('ctx', 'eg'), split_axis=0, concat_axis=0, tile...  96.5 us
    all_to_all x1, waiting for transfers between devices, local(): lax.all_to_all(produced.reshape(slot_count, per_slot, -1), ('ctx', 'eg'),...  90.9 us
    all_gather x1, waiting for transfers between devices, local(): gathered = lax.all_gather(both[None], ('ctx', 'eg'), axis=0, tiled=True)  24.4 us
    sub x1, matrix products, attend_rows(): raised = jnp.exp(logits - largest)  9.71 us
    dot_general x3, matrix products, local(): jnp.dot(part, returned_rows, preferred_element_type=jnp.float32)  9.6 us
    dot_general x1, matrix products, expert_apply(): jnp.dot(activation, down_full, preferred_element_type=jnp.float32)  7.77 us
    ppermute x3, waiting for transfers between devices, swapped(): return lax.ppermute(value, axis, pairs)  6.77 us
  transfers between devices with their start and end apart: 5, of which 4 were waited for; matrix products, arithmetic and copies ran while one was open for 14% of the time, Pallas kernels for 0%

profile of v9, /device:TPU:11, one launch (start us, length us, event | category | flops | bytes accessed | tf_op | source)
XLA Modules:
  0.0 325.3 jit_solution(15016640591027610316)
XLA Ops:
  10.3 1.9 fusion.62
  12.3 4.5 %compare_select_fusion.2 = (s32[1024,1]{0,1:T(1,128)S(1)}, s32[1024,1]{0,1:T(1,128)S(1)}) fusion(s32[]{:T(128)} %bitcast.10, s32[]{:T(128)} %bitcast.11, s32[]{:T(128)} %bitcast.12, s32[]{:T(128)} %bitcast.13, s32[]{:T(128)} %bitcast.14, s32[]{:T(128)} %bitcast.16, s32[]{:T(128)} %bitcast.15, s32[1024,1]{0,1:T(1,128)S(1)} %reshape.275), kind=kLoop, calls=%fused_computation.74 | loop fusion | flops 15360 | bytes 12316 | tf_op jit(solution)/shard_map/jit(_take)/gather | solution.py:97
  16.9 5.5 %and_select_fusion.1 = (s32[1024]{0:T(1024)S(1)}, s32[1024]{0:T(1024)S(1)}) fusion(s32[1024]{0:T(1024)S(1)} %reshape.276, pred[1024]{0:T(1024)(128)(4,1)S(1)} %get-tuple-element.32, pred[1024]{0:T(1024)(128)(4,1)S(1)} %get-tuple-element.31, pred[1024]{0:T(1024)(128)(4,1)S(1)} %get-tuple-element.33, pred[1024]{0:T(1024)(128)(4,1)S(1)} %get-tuple-element.30, ...), kind=kLoop, calls=%fused_computation.97 | loop fusion | flops 16384 | bytes 25636 | tf_op jit(solution)/shard_map/jit(_take)/select_n | solution.py:97
  22.4 4.5 %reduce-window.6 = s32[16,8,128]{2,1,0:T(8,128)S(1)} reduce-window(s32[16,8,128]{2,1,0:T(8,128)S(1)} %fusion.51, s32[]{:T(128)} %constant.108.clone.1), window={size=1x1x128 pad=0_0x0_0x127_0}, to_apply=%region_0.1 | reduce-window | flops 2080768 | bytes 131076 | tf_op jit(solution)/shard_map/reduce-window
  27.2 2.0 copy.80
  29.3 4.3 %scatter_custom_fusion = s32[1024]{0:T(1024)S(1)} fusion(s32[1024]{0:T(1024)S(1)} %bitcast.126, s32[1024]{0:T(1024)S(1)} %iota.22, s32[]{:T(128)} %constant.108.clone.1), kind=kCustom, calls=%fused_computation.104 | custom fusion | bytes 4100 | tf_op jit(solution)/shard_map/scatter | solution.py:106
  34.7 24.4 %all-gather.3.cloned.1.call-done = bf16[16,128,512]{2,1,0:T(8,128)(2,1)} async-done(((bf16[1,128,512]{2,1,0:T(8,128)(2,1)}), bf16[16,128,512]{2,1,0:T(8,128)(2,1)}) %all-gather.3.cloned.1.call-update) | async-done | bytes 2097168 | tf_op jit(solution)/shard_map/all_gather | solution.py:91
  59.1 2.2 gather_fusion
  63.0 9.7 %fusion.63 = (f32[2,8,128]{2,1,0:T(8,128)S(1)}, f32[2,8,128,1536]{2,3,1,0:T(8,128)}) fusion(bf16[1536,2,128,1]{2,1,0,3:T(2,128)(2,1)} %bitcast.115, bf16[128,2,8,128]{3,2,1,0:T(8,128)(2,1)} %bitcast.118), kind=kOutput, calls=%fused_computation.117 | convolution fusion | flops 814745088 | bytes 13901824 | tf_op jit(solution)/shard_map/sub | solution.py:28
  72.7 5.7 %fusion.26 = bf16[2,128,8,128]{3,1,2,0:T(8,128)(2,1)S(1)} fusion(f32[2,8,128,1536]{2,3,1,0:T(8,128)} %get-tuple-element.59, f32[2,8,128]{2,1,0:T(8,128)S(1)} %get-tuple-element.58, bf16[1536,2,128,1]{2,1,0,3:T(2,128)(2,1)S(1)} %bitcast.116), kind=kOutput, calls=%fused_computation.36 | convolution fusion | flops 811859968 | bytes 13901824 | tf_op jit(solution)/shard_map/kgrn,nkd->rkgd/dot_general | solution.py:31
  79.2 3.8 %collective-permute-done.1 = bf16[2048,512]{1,0:T(8,128)(2,1)} collective-permute-done((bf16[2048,512]{1,0:T(8,128)(2,1)}, bf16[2048,512]{1,0:T(8,128)(2,1)}, u32[]{:S(2)}, u32[]{:S(2)}) %collective-permute-start.1) | collective-permute-done | bytes 2097184 | tf_op jit(solution)/shard_map/ppermute | solution.py:14
  82.9 3.0 collective-permute-done.2
  85.9 4.8 %fusion.6 = bf16[128,2048]{1,0:T(8,128)(2,1)S(1)} fusion(bf16[128,2048]{0,1:T(8,128)(2,1)S(1)} %bitcast.128, bf16[2048,512]{1,0:T(8,128)(2,1)} %collective-permute-done.2, bf16[2048,512]{1,0:T(8,128)(2,1)} %collective-permute-done, bf16[2048,512]{1,0:T(8,128)(2,1)} %collective-permute-done.1, bf16[2048,512]{1,0:T(8,128)(2,1)} %param.17), kind=kOutput, calls=%fused_computation.11 | convolution fusion | flops 1107296256 | bytes 9437184 | tf_op jit(solution)/shard_map/dot_general | solution.py:144
  92.5 6.0 %gather_fusion.2 = bf16[1024,2048]{1,0:T(8,128)(2,1)} fusion(bf16[128,2048]{1,0:T(8,128)(2,1)S(1)} %multiply_convert_fusion.1, s32[1024]{0:T(1024)S(1)} %broadcast_clamp_fusion), kind=kCustom, calls=%fused_computation.2 | custom fusion | bytes 8392704 | tf_op jit(solution)/shard_map/jit(_take)/gather | solution.py:193
  98.5 2.6 broadcast_select_fusion
  101.2 96.5 %all_to_all.10 = bf16[16,64,2048]{2,1,0:T(8,128)(2,1)S(1)} all-to-all(bf16[16,64,2048]{2,1,0:T(8,128)(2,1)S(1)} %broadcast_select_fusion), channel_id=1, replica_groups=mesh['groups'=2,'ctx'=4,'eg'=4,'rep'=1] {'ctx','eg'}, dimensions={0} | all-to-all | bytes 8388608 | tf_op jit(solution)/shard_map/all_to_all | solution.py:196
  197.6 2.0 copy-done.1
  199.6 3.6 %fusion.20 = f32[1024,384]{1,0:T(8,128)} fusion(bf16[1024,2048]{1,0:T(8,128)(2,1)S(1)} %bitcast.109, bf16[1,2048,384]{2,1,0:T(8,128)(2,1)S(1)} %copy-done.6), kind=kOutput, calls=%fused_computation.31 | convolution fusion | flops 1610612736 | bytes 7340032 | tf_op jit(solution)/shard_map/dot_general | solution.py:38
  203.2 7.8 %convolution_convert_fusion = bf16[1024,2048]{1,0:T(8,128)(2,1)} fusion(bf16[1,384,2048]{2,1,0:T(8,128)(2,1)S(1)} %copy-done, f32[1024,384]{1,0:T(8,128)} %fusion.20, bf16[1024,2048]{1,0:T(8,128)(2,1)} %bitcast.110, bf16[1,2048,384]{2,1,0:T(8,128)(2,1)S(1)} %copy-done.7), kind=kOutput, calls=%fused_computation.24 | convolution fusion | flops 3225681920 | bytes 13107200 | tf_op jit(solution)/shard_map/dot_general | solution.py:41
  210.9 5.4 %all-to-all-start.1 = ((bf16[16,64,2048]{2,1,0:T(8,128)(2,1)}), bf16[16,64,2048]{2,1,0:T(8,128)(2,1)}, u32[]{:S(2)}, u32[]{:S(2)}) async-start(bf16[16,64,2048]{2,1,0:T(8,128)(2,1)} %bitcast.108), calls=%async_computation.1 | async-start | bytes 8388608 | tf_op jit(solution)/shard_map/all_to_all | solution.py:199
  217.9 90.9 %all-to-all-done.1 = bf16[16,64,2048]{2,1,0:T(8,128)(2,1)} async-done(((bf16[16,64,2048]{2,1,0:T(8,128)(2,1)}), bf16[16,64,2048]{2,1,0:T(8,128)(2,1)}, u32[]{:S(2)}, u32[]{:S(2)}) %all-to-all-start.1) | async-done | bytes 4194336 | tf_op jit(solution)/shard_map/all_to_all | solution.py:199
  308.9 2.9 fusion.46
  311.8 3.0 convolution_add_fusion.1
  314.7 3.7 %fusion.16 = bf16[128,2048]{1,0:T(8,128)(2,1)} fusion(f32[128,2048]{1,0:T(8,128)S(1)} %convolution_add_fusion.1, bf16[1024,2048]{1,0:T(8,128)(2,1)} %bitcast.43, f32[128,1024]{1,0:T(8,128)S(1)} %select_reduce_fusion), kind=kOutput, calls=%fused_computation.27 | convolution fusion | flops 538312704 | bytes 6291456 | tf_op jit(solution)/shard_map/dot_general | solution.py:216
  (65 shorter events, 10.2 us)
Async XLA Ops:
  7.2 196.0 %copy-start = (bf16[1,384,2048]{2,1,0:T(8,128)(2,1)S(1)}, bf16[1,384,2048]{2,1,0:T(8,128)(2,1)}, u32[]{:S(2)}) copy-start(bf16[1,384,2048]{2,1,0:T(8,128)(2,1)} %param.25) | copy-start | bytes 4718596
  7.2 51.9 %all-gather.3.cloned.1.call-start = ((), (), s32[]{:S(2)}) async-start(), calls=%async_computation.2 | async-start | bytes 2228224 | tf_op jit(solution)/shard_map/all_gather | solution.py:91
  8.9 69.5 %collective-permute-start = (bf16[2048,512]{1,0:T(8,128)(2,1)}, bf16[2048,512]{1,0:T(8,128)(2,1)}, u32[]{:S(2)}, u32[]{:S(2)}) collective-permute-start(bf16[2048,512]{1,0:T(8,128)(2,1)} %param.17), channel_id=1, source_target_pairs={{0,2},{1,3},{2,0},{3,1},{4,6},{5,7},{6,4},{7,5},{8,10},{9,11},{10,... | collective-permute-start | bytes 6291464 | tf_op jit(solution)/shard_map/ppermute | solution.py:14
  78.4 4.6 %collective-permute-start.1 = (bf16[2048,512]{1,0:T(8,128)(2,1)}, bf16[2048,512]{1,0:T(8,128)(2,1)}, u32[]{:S(2)}, u32[]{:S(2)}) collective-permute-start(bf16[2048,512]{1,0:T(8,128)(2,1)} %param.17), channel_id=1, source_target_pairs={{0,1},{1,0},{2,3},{3,2},{4,5},{5,4},{6,7},{7,6},{8,9},{9,8},{10,11... | collective-permute-start | bytes 6291464 | tf_op jit(solution)/shard_map/ppermute | solution.py:14
  78.7 7.2 %collective-permute-start.2 = (bf16[2048,512]{1,0:T(8,128)(2,1)}, bf16[2048,512]{1,0:T(8,128)(2,1)}, u32[]{:S(2)}, u32[]{:S(2)}) collective-permute-start(bf16[2048,512]{1,0:T(8,128)(2,1)} %collective-permute-done), channel_id=1, source_target_pairs={{0,1},{1,0},{2,3},{3,2},{4,5},{5,4},{6,7},{7,6},{8,9},{9,8},{10,11... | collective-permute-start | bytes 6291464 | tf_op jit(solution)/shard_map/ppermute | solution.py:14
  90.8 1.2 copy-start.2
  90.8 1.5 copy-start.4
  92.2 6.3 %copy-start.3 = (bf16[128,2048]{1,0:T(8,128)(2,1)}, bf16[128,2048]{1,0:T(8,128)(2,1)S(1)}, u32[]{:S(2)}) copy-start(bf16[128,2048]{1,0:T(8,128)(2,1)S(1)} %get-tuple-element.35) | copy-start | bytes 1572868
  101.2 98.4 %copy-start.6 = (bf16[1,2048,384]{2,1,0:T(8,128)(2,1)S(1)}, bf16[1,2048,384]{2,1,0:T(8,128)(2,1)}, u32[]{:S(2)}) copy-start(bf16[1,2048,384]{2,1,0:T(8,128)(2,1)} %param.23) | copy-start | bytes 4718596
  197.6 2.0 copy-start.1
  199.6 3.6 %copy-start.7 = (bf16[1,2048,384]{2,1,0:T(8,128)(2,1)S(1)}, bf16[1,2048,384]{2,1,0:T(8,128)(2,1)}, u32[]{:S(2)}) copy-start(bf16[1,2048,384]{2,1,0:T(8,128)(2,1)} %param.24) | copy-start | bytes 4718596
  210.9 5.5 %copy-start.5 = (f32[128,8]{0,1:T(8,128)S(1)}, f32[128,8]{0,1:T(8,128)}, u32[]{:S(2)}) copy-start(f32[128,8]{0,1:T(8,128)} %param.21) | copy-start | bytes 12292
  210.9 97.9 %all-to-all-start.1 = ((bf16[16,64,2048]{2,1,0:T(8,128)(2,1)}), bf16[16,64,2048]{2,1,0:T(8,128)(2,1)}, u32[]{:S(2)}, u32[]{:S(2)}) async-start(bf16[16,64,2048]{2,1,0:T(8,128)(2,1)} %bitcast.108), calls=%async_computation.1 | async-start | bytes 8388608 | tf_op jit(solution)/shard_map/all_to_all | solution.py:199
Sparse Core Ops, SparseCore 0:
  10.8 48.3 all-gather.2

commit v10 on v5

--- a/solution.py
+++ b/solution.py
@@ -174,14 +174,19 @@
         )
         src_rows = local_row + jnp.arange(slot_count, dtype=jnp.int32)[:, None] * tok_dev
         pad_rows = ((0, all_packed.shape[1] - width), (0, 0))
-        gate_act = jnp.dot(
-            all_packed, jnp.pad(partner[0], pad_rows), preferred_element_type=jnp.float32
-        )
-        up_act = jnp.dot(
-            all_packed, jnp.pad(partner[1], pad_rows), preferred_element_type=jnp.float32
-        )
+        hidden = partner[0].shape[1]
+        gate_up = jnp.pad(jnp.concatenate([partner[0], partner[1]], axis=1), pad_rows)
+        both_act = jnp.dot(all_packed, gate_up, preferred_element_type=jnp.float32)
+        gate_act = both_act[:, :hidden]
+        up_act = both_act[:, hidden:]
         activation = (jax.nn.silu(gate_act) * up_act).astype(jnp.bfloat16)
-        picked = jnp.take(activation, src_rows.reshape(-1), axis=0)
+        pick_matrix = (
+            src_rows.reshape(-1)[:, None]
+            == jnp.arange(activation.shape[0], dtype=jnp.int32)[None, :]
+        ).astype(jnp.bfloat16)
+        picked = jnp.dot(pick_matrix, activation, preferred_element_type=jnp.float32).astype(
+            jnp.bfloat16
+        )
         produced = jnp.dot(picked, partner[2], preferred_element_type=jnp.float32).astype(
             jnp.bfloat16
         )

time: 316 us -> 315 us (level)
  local copies, waits for them, and re-layouts: 16.7 us -> 11.6 us
    gather x1 -> x0, local copies, waits for them, and re-layouts: 4.99 us -> none  [local(): picked = jnp.take(activation, src_rows.reshape(-1), axis=0)]
    dot_general x1, matrix products: 5.45 us -> 9.36 us  [local(): jnp.dot(picked, partner[2], preferred_element_type=jnp.float32)]
    dot_general x2 -> x1, matrix products: 13.7 us -> 12.3 us  [local(): both_act = jnp.dot(all_packed, gate_up, preferred_element_type=jnp.float32)]
where the time goes in v10:
time: 315 us; the launch traced here: 314 us
  waiting for transfers between devices  202 us (64%)
  matrix products  51.9 us (16%)
  other arithmetic  25.1 us (8%)
  between operations  14.3 us (5%)
  local copies, waits for them, and re-layouts  11.6 us (4%)
  starting transfers between devices  8.6 us (3%)
    all_gather x1, waiting for transfers between devices, local(): all_packed = lax.all_gather(packed, ('ctx', 'eg'), axis=0, tiled=True)  77.1 us
    all_to_all x1, waiting for transfers between devices, local(): lax.all_to_all(produced.reshape(slot_count, per_slot, -1), ('ctx', 'eg'),...  73.3 us
    all_gather x1, waiting for transfers between devices, local(): gathered = lax.all_gather(both[None], ('ctx', 'eg'), axis=0, tiled=True)  46.9 us
    dot_general x1, matrix products, local(): both_act = jnp.dot(all_packed, gate_up, preferred_element_type=jnp.float32)  12.3 us
    sub x1, matrix products, attend_rows(): raised = jnp.exp(logits - largest)  9.71 us
    dot_general x3, matrix products, local(): jnp.dot(part, returned_rows, preferred_element_type=jnp.float32)  9.6 us
    dot_general x1, matrix products, local(): jnp.dot(picked, partner[2], preferred_element_type=jnp.float32)  9.36 us
    all_to_all x1, starting transfers between devices, local(): lax.all_to_all(produced.reshape(slot_count, per_slot, -1), ('ctx', 'eg'),...  7.69 us
  transfers between devices with their start and end apart: 6, of which 5 were waited for; matrix products, arithmetic and copies ran while one was open for 14% of the time, Pallas kernels for 0%

profile of v10, /device:TPU:11, one launch (start us, length us, event | category | flops | bytes accessed | tf_op | source)
XLA Modules:
  0.0 314.0 jit_solution(8959990437383679681)
XLA Ops:
  7.2 1.6 pad_maximum_fusion
  9.3 1.9 copy.122
  12.2 46.9 %all-gather.6.cloned.1.call-done = bf16[16,128,512]{2,1,0:T(8,128)(2,1)} async-done(((bf16[1,128,512]{2,1,0:T(8,128)(2,1)}), bf16[16,128,512]{2,1,0:T(8,128)(2,1)}) %all-gather.6.cloned.1.call-update) | async-done | bytes 2097168 | tf_op jit(solution)/shard_map/all_gather | solution.py:91
  59.1 2.2 gather_fusion
  62.9 9.7 %fusion.81 = (f32[2,8,128]{2,1,0:T(8,128)S(1)}, f32[2,8,128,1536]{2,3,1,0:T(8,128)}) fusion(bf16[1536,2,128,1]{2,1,0,3:T(2,128)(2,1)} %bitcast.104, bf16[128,2,8,128]{3,2,1,0:T(8,128)(2,1)} %bitcast.107), kind=kOutput, calls=%fused_computation.132 | convolution fusion | flops 814745088 | bytes 13901824 | tf_op jit(solution)/shard_map/sub | solution.py:28
  72.7 6.5 %fusion.37 = bf16[2,128,8,128]{3,1,2,0:T(8,128)(2,1)} fusion(f32[2,8,128,1536]{2,3,1,0:T(8,128)} %get-tuple-element.73, f32[2,8,128]{2,1,0:T(8,128)S(1)} %get-tuple-element.72, bf16[1536,2,128,1]{2,1,0,3:T(2,128)(2,1)S(1)} %bitcast.105), kind=kOutput, calls=%fused_computation.43 | convolution fusion | flops 811859968 | bytes 13901824 | tf_op jit(solution)/shard_map/kgrn,nkd->rkgd/dot_general | solution.py:31
  81.6 2.1 collective-permute-done.1
  83.7 3.0 collective-permute-done.2
  86.7 4.4 %fusion.6 = bf16[128,2048]{1,0:T(8,128)(2,1)S(1)} fusion(bf16[128,2048]{0,1:T(8,128)(2,1)} %bitcast.116, bf16[2048,512]{1,0:T(8,128)(2,1)} %collective-permute-done.2, bf16[2048,512]{1,0:T(8,128)(2,1)} %collective-permute-done, bf16[2048,512]{1,0:T(8,128)(2,1)} %collective-permute-done.1, bf16[2048,512]{1,0:T(8,128)(2,1)} %param.19), kind=kOutput, calls=%fused_computation.9 | convolution fusion | flops 1107296256 | bytes 9437184 | tf_op jit(solution)/shard_map/dot_general | solution.py:125
  91.1 1.4 gather_fusion.1
  92.5 1.3 copy.101
  96.3 77.1 %all-gather.4.cloned.1.call-done = bf16[2048,2176]{0,1:T(8,128)(2,1)} async-done(((bf16[128,2176]{0,1:T(8,128)(2,1)}), bf16[2048,2176]{0,1:T(8,128)(2,1)}) %all-gather.4.cloned.1.call-update) | async-done | bytes 8912912 | tf_op jit(solution)/shard_map/all_gather | solution.py:158
  173.4 1.4 fusion.67
  175.7 12.3 %fusion.21 = f32[2048,768]{1,0:T(8,128)} fusion(bf16[2048,2176]{0,1:T(8,128)(2,1)} %all-gather.4.cloned.1.call-done, bf16[2048,384]{1,0:T(8,128)(2,1)} %bitcast.114, bf16[2048,384]{1,0:T(8,128)(2,1)} %bitcast.115), kind=kOutput, calls=%fused_computation.29 | convolution fusion | flops 6856802304 | bytes 18350080 | tf_op jit(solution)/shard_map/dot_general | solution.py:179
  188.0 9.4 %convolution_convert_fusion = bf16[1024,2048]{1,0:T(8,128)(2,1)} fusion(bf16[1,384,2048]{2,1,0:T(8,128)(2,1)S(1)} %copy-done, f32[2048,768]{1,0:T(8,128)} %fusion.21, s32[1024]{0:T(1024)S(1)} %add.153), kind=kOutput, calls=%fused_computation.27 | convolution fusion | flops 3230531584 | bytes 12062720 | tf_op jit(solution)/shard_map/dot_general | solution.py:190
  197.3 7.7 %all-to-all-start = ((bf16[16,64,2048]{2,1,0:T(8,128)(2,1)}), bf16[16,64,2048]{2,1,0:T(8,128)(2,1)}, u32[]{:S(2)}, u32[]{:S(2)}) async-start(bf16[16,64,2048]{2,1,0:T(8,128)(2,1)} %bitcast.100), calls=%async_computation | async-start | bytes 8388608 | tf_op jit(solution)/shard_map/all_to_all | solution.py:200
  206.1 4.4 %compare_select_fusion.1 = (s32[1024,1]{0,1:T(1,128)S(1)}, s32[1024,1]{0,1:T(1,128)S(1)}) fusion(s32[]{:T(128)} %bitcast.22, s32[]{:T(128)} %bitcast.23, s32[]{:T(128)} %bitcast.24, s32[]{:T(128)} %bitcast.25, s32[]{:T(128)} %bitcast.26, s32[]{:T(128)} %bitcast.28, s32[]{:T(128)} %bitcast.27, s32[1024,1]{0,1:T(1,128)S(1)} %reshape.302), kind=kLoop, calls=%fused_computation.89 | loop fusion | flops 15360 | bytes 12316 | tf_op jit(solution)/shard_map/jit(_take)/gather | solution.py:140
  210.7 5.6 %and_select_fusion = (s32[1024]{0:T(1024)S(1)}, s32[1024]{0:T(1024)S(1)}) fusion(s32[1024]{0:T(1024)S(1)} %reshape.303, pred[1024]{0:T(1024)(128)(4,1)S(1)} %get-tuple-element.47, pred[1024]{0:T(1024)(128)(4,1)S(1)} %get-tuple-element.46, pred[1024]{0:T(1024)(128)(4,1)S(1)} %get-tuple-element.45, pred[1024]{0:T(1024)(128)(4,1)S(1)} %get-tuple-element.44, ...), kind=kLoop, calls=%fused_computation.107 | loop fusion | flops 16384 | bytes 25636 | tf_op jit(solution)/shard_map/jit(_take)/select_n | solution.py:140
  216.4 4.5 %reduce-window.6 = s32[16,8,128]{2,1,0:T(8,128)S(1)} reduce-window(s32[16,8,128]{2,1,0:T(8,128)S(1)} %fusion.66, s32[]{:T(128)} %constant.120.clone.1), window={size=1x1x128 pad=0_0x0_0x127_0}, to_apply=%region_2.3 | reduce-window | flops 2080768 | bytes 131076 | tf_op jit(solution)/shard_map/reduce-window
  221.8 1.3 select_reduce_fusion
  224.2 73.3 %all-to-all-done = bf16[16,64,2048]{2,1,0:T(8,128)(2,1)} async-done(((bf16[16,64,2048]{2,1,0:T(8,128)(2,1)}), bf16[16,64,2048]{2,1,0:T(8,128)(2,1)}, u32[]{:S(2)}, u32[]{:S(2)}) %all-to-all-start) | async-done | bytes 4194336 | tf_op jit(solution)/shard_map/all_to_all | solution.py:200
  297.5 2.9 fusion.61
  300.4 2.9 convolution_add_fusion.1
  303.4 3.8 %fusion.28 = bf16[128,2048]{1,0:T(8,128)(2,1)} fusion(f32[128,2048]{1,0:T(8,128)S(1)} %convolution_add_fusion.1, bf16[1024,2048]{1,0:T(8,128)(2,1)} %bitcast.38, f32[128,1024]{1,0:T(8,128)S(1)} %select_reduce_fusion), kind=kOutput, calls=%fused_computation.37 | convolution fusion | flops 538312704 | bytes 6291456 | tf_op jit(solution)/shard_map/dot_general | solution.py:217
  (73 shorter events, 11.8 us)
Async XLA Ops:
  7.2 180.8 %copy-start = (bf16[1,384,2048]{2,1,0:T(8,128)(2,1)S(1)}, bf16[1,384,2048]{2,1,0:T(8,128)(2,1)}, u32[]{:S(2)}) copy-start(bf16[1,384,2048]{2,1,0:T(8,128)(2,1)} %param.27) | copy-start | bytes 4718596
  7.2 51.9 %all-gather.6.cloned.1.call-start = ((), (), s32[]{:S(2)}) async-start(), calls=%async_computation.2 | async-start | bytes 2228224 | tf_op jit(solution)/shard_map/all_gather | solution.py:91
  8.9 164.5 %all-gather.4.cloned.1.call-start = ((), (), s32[]{:S(2)}) async-start(), calls=%async_computation.1 | async-start | bytes 9469952 | tf_op jit(solution)/shard_map/all_gather | solution.py:158
  8.9 70.2 %collective-permute-start = (bf16[2048,512]{1,0:T(8,128)(2,1)}, bf16[2048,512]{1,0:T(8,128)(2,1)}, u32[]{:S(2)}, u32[]{:S(2)}) collective-permute-start(bf16[2048,512]{1,0:T(8,128)(2,1)} %param.19), channel_id=1, source_target_pairs={{0,2},{1,3},{2,0},{3,1},{4,6},{5,7},{6,4},{7,5},{8,10},{9,11},{10,... | collective-permute-start | bytes 6291464 | tf_op jit(solution)/shard_map/ppermute | solution.py:14
  72.7 7.1 %copy-start.1 = (bf16[128,2048]{1,0:T(8,128)(2,1)S(1)}, bf16[128,2048]{1,0:T(8,128)(2,1)}, u32[]{:S(2)}) copy-start(bf16[128,2048]{1,0:T(8,128)(2,1)} %param.20) | copy-start | bytes 1572868
  72.7 8.3 %copy-start.3 = (s32[128,8]{0,1:T(8,128)S(1)}, s32[128,8]{0,1:T(8,128)}, u32[]{:S(2)}) copy-start(s32[128,8]{0,1:T(8,128)} %param.22) | copy-start | bytes 12292
  79.2 4.5 %collective-permute-start.1 = (bf16[2048,512]{1,0:T(8,128)(2,1)}, bf16[2048,512]{1,0:T(8,128)(2,1)}, u32[]{:S(2)}, u32[]{:S(2)}) collective-permute-start(bf16[2048,512]{1,0:T(8,128)(2,1)} %param.19), channel_id=1, source_target_pairs={{0,1},{1,0},{2,3},{3,2},{4,5},{5,4},{6,7},{7,6},{8,9},{9,8},{10,11... | collective-permute-start | bytes 6291464 | tf_op jit(solution)/shard_map/ppermute | solution.py:14
  79.5 7.2 %collective-permute-start.2 = (bf16[2048,512]{1,0:T(8,128)(2,1)}, bf16[2048,512]{1,0:T(8,128)(2,1)}, u32[]{:S(2)}, u32[]{:S(2)}) collective-permute-start(bf16[2048,512]{1,0:T(8,128)(2,1)} %collective-permute-done), channel_id=1, source_target_pairs={{0,1},{1,0},{2,3},{3,2},{4,5},{5,4},{6,7},{7,6},{8,9},{9,8},{10,11... | collective-permute-start | bytes 6291464 | tf_op jit(solution)/shard_map/ppermute | solution.py:14
  91.1 3.3 %copy-start.4 = (f32[2048]{0:T(1024)S(1)}, f32[2048]{0:T(1024)}, u32[]{:S(2)}) copy-start(f32[2048]{0:T(1024)} %param.21) | copy-start | bytes 24580
  91.1 4.6 %copy-start.2 = (s32[16]{0:T(128)S(1)}, s32[16]{0:T(128)}, u32[]{:S(2)}) copy-start(s32[16]{0:T(128)} %param.24) | copy-start | bytes 196
  197.3 24.4 %copy-start.5 = (f32[128,8]{0,1:T(8,128)S(1)}, f32[128,8]{0,1:T(8,128)}, u32[]{:S(2)}) copy-start(f32[128,8]{0,1:T(8,128)} %param.23) | copy-start | bytes 12292
  197.3 100.2 %all-to-all-start = ((bf16[16,64,2048]{2,1,0:T(8,128)(2,1)}), bf16[16,64,2048]{2,1,0:T(8,128)(2,1)}, u32[]{:S(2)}, u32[]{:S(2)}) async-start(bf16[16,64,2048]{2,1,0:T(8,128)(2,1)} %bitcast.100), calls=%async_computation | async-start | bytes 8388608 | tf_op jit(solution)/shard_map/all_to_all | solution.py:200
Sparse Core Ops, SparseCore 0:
  10.8 48.3 all-gather.5
  95.8 77.5 all-gather.3

commit v11 on v10

--- a/solution.py
+++ b/solution.py
@@ -3,6 +3,7 @@
 import jax
 import jax.numpy as jnp
 from jax import lax
+from jax.experimental import pallas as pl
 from jax.sharding import PartitionSpec as P
 
 HD = 128
@@ -14,24 +15,45 @@
     return lax.ppermute(value, axis, pairs)
 
 
-def attend_rows(queries_flat, key_rows, value_rows):
+def attention_kernel(query_ref, key_ref, value_ref, out_ref):
+    inverse_root = 1.0 / math.sqrt(HD)
+    key_block = key_ref[...]
+    value_block = value_ref[...]
+    for head in range(query_ref.shape[1] // HD):
+        query_head = query_ref[:, head * HD : (head + 1) * HD]
+        logits = (
+            lax.dot_general(
+                query_head,
+                key_block,
+                (((1,), (1,)), ((), ())),
+                preferred_element_type=jnp.float32,
+            )
+            * inverse_root
+        )
+        largest = jnp.max(logits, axis=-1, keepdims=True)
+        raised = jnp.exp(logits - largest)
+        denominator = jnp.sum(raised, axis=-1, keepdims=True)
+        weights_low = (raised / denominator).astype(jnp.bfloat16)
+        blended = jnp.dot(weights_low, value_block, preferred_element_type=jnp.float32)
+        out_ref[:, head * HD : (head + 1) * HD] = blended.astype(out_ref.dtype)
+
+
+def attend_rows(queries_flat, key_rows, value_rows, interpret=False):
     row_count = queries_flat.shape[0]
-    kv_heads = key_rows.shape[1]
-    per_group = queries_flat.shape[1] // (kv_heads * HD)
-    inverse_root = 1.0 / math.sqrt(HD)
-    arranged = queries_flat.reshape(row_count, kv_heads, per_group, HD).transpose(1, 2, 0, 3)
-    logits = (
-        jnp.einsum("kgrd,nkd->kgrn", arranged, key_rows, preferred_element_type=jnp.float32)
-        * inverse_root
-    )
-    largest = jnp.max(logits, axis=-1, keepdims=True)
-    raised = jnp.exp(logits - largest)
-    denominator = jnp.sum(raised, axis=-1, keepdims=True)
-    weights_low = (raised / denominator).astype(jnp.bfloat16)
-    blended = jnp.einsum(
-        "kgrn,nkd->rkgd", weights_low, value_rows, preferred_element_type=jnp.float32
-    )
-    return blended.astype(jnp.bfloat16).reshape(row_count, kv_heads * per_group * HD)
+    span, kv_heads, _ = key_rows.shape
+    group_width = queries_flat.shape[1] // kv_heads
+    return pl.pallas_call(
+        attention_kernel,
+        grid=(kv_heads,),
+        in_specs=[
+            pl.BlockSpec((row_count, group_width), lambda k: (0, k)),
+            pl.BlockSpec((span, HD), lambda k: (0, k)),
+            pl.BlockSpec((span, HD), lambda k: (0, k)),
+        ],
+        out_specs=pl.BlockSpec((row_count, group_width), lambda k: (0, k)),
+        out_shape=jax.ShapeDtypeStruct(queries_flat.shape, jnp.bfloat16),
+        interpret=interpret,
+    )(queries_flat, key_rows.reshape(span, -1), value_rows.reshape(span, -1))
 
 
 def expert_apply(rows_in, gate_full, up_full, down_full):

time: 315 us -> 310 us (0.984)
  matrix products: 51.9 us -> 35.7 us
  Pallas kernels: 0 us -> 11.5 us
    pallas_call x0 -> x1, Pallas kernels: none -> 11.5 us  [attend_rows(): pl.pallas_call(attention_kernel, grid=(kv_heads,), in_specs=[pl.BlockSpec...]
    sub x1 -> x0, matrix products: 9.71 us -> none  [attend_rows(): raised = jnp.exp(logits - largest)]
    dot_general x1 -> x0, matrix products: 6.53 us -> none  [attend_rows(): jnp.einsum('kgrn,nkd->rkgd', weights_low, value_rows, preferred_element_t...]
  transfers between devices with their start and end apart: 6 -> 6, of which waited for: 5 -> 5; matrix products, arithmetic and copies ran while one was open for 14% -> 8% of each run, Pallas kernels for 0% -> 4%
where the time goes in v11:
time: 310 us; the launch traced here: 309 us
  waiting for transfers between devices  205 us (66%)
  matrix products  35.7 us (12%)
  other arithmetic  24.9 us (8%)
  between operations  14.3 us (5%)
  Pallas kernels  11.5 us (4%)
  local copies, waits for them, and re-layouts  9.58 us (3%)
  starting transfers between devices  8.6 us (3%)
    all_gather x1, waiting for transfers between devices, local(): all_packed = lax.all_gather(packed, ('ctx', 'eg'), axis=0, tiled=True)  77.1 us
    all_to_all x1, waiting for transfers between devices, local(): lax.all_to_all(produced.reshape(slot_count, per_slot, -1), ('ctx', 'eg'),...  73.3 us
    all_gather x1, waiting for transfers between devices, local(): gathered = lax.all_gather(both[None], ('ctx', 'eg'), axis=0, tiled=True)  48.8 us
    dot_general x1, matrix products, local(): both_act = jnp.dot(all_packed, gate_up, preferred_element_type=jnp.float32)  12.3 us
    pallas_call x1, Pallas kernels, attend_rows(): pl.pallas_call(attention_kernel, grid=(kv_heads,), in_specs=[pl.BlockSpec...  11.5 us
    dot_general x3, matrix products, local(): jnp.dot(part, returned_rows, preferred_element_type=jnp.float32)  9.64 us
    dot_general x1, matrix products, local(): jnp.dot(picked, partner[2], preferred_element_type=jnp.float32)  9.36 us
    all_to_all x1, starting transfers between devices, local(): lax.all_to_all(produced.reshape(slot_count, per_slot, -1), ('ctx', 'eg'),...  7.69 us
  transfers between devices with their start and end apart: 6, of which 5 were waited for; matrix products, arithmetic and copies ran while one was open for 8% of the time, Pallas kernels for 4%

profile of v11, /device:TPU:11, one launch (start us, length us, event | category | flops | bytes accessed | tf_op | source)
XLA Modules:
  0.0 309.1 jit_solution(16699165032221048077)
XLA Ops:
  7.2 1.6 pad_maximum_fusion
  10.3 48.8 %all-gather.6.cloned.1.call-done = bf16[16,128,512]{2,1,0:T(8,128)(2,1)} async-done(((bf16[1,128,512]{2,1,0:T(8,128)(2,1)}), bf16[16,128,512]{2,1,0:T(8,128)(2,1)}) %all-gather.6.cloned.1.call-update) | async-done | bytes 2097168 | tf_op jit(solution)/shard_map/all_gather | solution.py:113
  59.1 2.2 gather_fusion
  61.6 1.3 fusion.51
  62.8 11.5 %shard_map.140 = bf16[128,2048]{1,0:T(8,128)(2,1)} custom-call(bf16[128,2048]{1,0:T(8,128)(2,1)} %query_ref.1, bf16[1536,256]{1,0:T(8,128)(2,1)} %bitcast.74, bf16[1536,256]{1,0:T(8,128)(2,1)} %bitcast.73), custom_call_target="tpu_custom_call" | custom-call | tf_op jit(solution)/shard_map/pallas_call | solution.py:45
  76.5 2.3 collective-permute-done.2
  78.8 3.0 collective-permute-done.1
  81.8 4.4 %fusion = bf16[128,2048]{1,0:T(8,128)(2,1)S(1)} fusion(bf16[128,2048]{1,0:T(8,128)(2,1)} %shard_map.140, bf16[2048,512]{1,0:T(8,128)(2,1)} %collective-permute-done.2, bf16[2048,512]{1,0:T(8,128)(2,1)} %collective-permute-done, bf16[2048,512]{1,0:T(8,128)(2,1)} %collective-permute-done.1, bf16[2048,512]{1,0:T(8,128)(2,1)} %param.19), kind=kOutput, calls=%fused_computation.2 | convolution fusion | flops 1107296256 | bytes 9437184 | tf_op jit(solution)/shard_map/dot_general | solution.py:147
  86.3 1.4 gather_fusion.1
  87.6 1.3 copy.79
  91.4 77.1 %all-gather.4.cloned.1.call-done = bf16[2048,2176]{0,1:T(8,128)(2,1)} async-done(((bf16[128,2176]{0,1:T(8,128)(2,1)}), bf16[2048,2176]{0,1:T(8,128)(2,1)}) %all-gather.4.cloned.1.call-update) | async-done | bytes 8912912 | tf_op jit(solution)/shard_map/all_gather | solution.py:180
  168.5 1.4 fusion.40
  170.8 12.3 %fusion.13 = f32[2048,768]{1,0:T(8,128)} fusion(bf16[2048,2176]{0,1:T(8,128)(2,1)} %all-gather.4.cloned.1.call-done, bf16[2048,384]{1,0:T(8,128)(2,1)} %bitcast.84, bf16[2048,384]{1,0:T(8,128)(2,1)} %bitcast.85), kind=kOutput, calls=%fused_computation.20 | convolution fusion | flops 6856802304 | bytes 18350080 | tf_op jit(solution)/shard_map/dot_general | solution.py:201
  183.1 9.4 %convolution_convert_fusion = bf16[1024,2048]{1,0:T(8,128)(2,1)} fusion(bf16[1,384,2048]{2,1,0:T(8,128)(2,1)S(1)} %copy-done, f32[2048,768]{1,0:T(8,128)} %fusion.13, s32[1024]{0:T(1024)S(1)} %add.153), kind=kOutput, calls=%fused_computation.18 | convolution fusion | flops 3230531584 | bytes 12062720 | tf_op jit(solution)/shard_map/dot_general | solution.py:212
  192.5 7.7 %all-to-all-start = ((bf16[16,64,2048]{2,1,0:T(8,128)(2,1)}), bf16[16,64,2048]{2,1,0:T(8,128)(2,1)}, u32[]{:S(2)}, u32[]{:S(2)}) async-start(bf16[16,64,2048]{2,1,0:T(8,128)(2,1)} %bitcast.72), calls=%async_computation | async-start | bytes 8388608 | tf_op jit(solution)/shard_map/all_to_all | solution.py:222
  201.4 4.4 %compare_select_fusion.1 = (s32[1024,1]{0,1:T(1,128)S(1)}, s32[1024,1]{0,1:T(1,128)S(1)}) fusion(s32[]{:T(128)} %bitcast.18, s32[]{:T(128)} %bitcast.19, s32[]{:T(128)} %bitcast.20, s32[]{:T(128)} %bitcast.21, s32[]{:T(128)} %bitcast.22, s32[]{:T(128)} %bitcast.24, s32[]{:T(128)} %bitcast.23, s32[1024,1]{0,1:T(1,128)S(1)} %reshape.284), kind=kLoop, calls=%fused_computation.70 | loop fusion | flops 15360 | bytes 12316 | tf_op jit(solution)/shard_map/jit(_take)/gather | solution.py:162
  205.9 5.6 %and_select_fusion = (s32[1024]{0:T(1024)S(1)}, s32[1024]{0:T(1024)S(1)}) fusion(s32[1024]{0:T(1024)S(1)} %reshape.285, pred[1024]{0:T(1024)(128)(4,1)S(1)} %get-tuple-element.47, pred[1024]{0:T(1024)(128)(4,1)S(1)} %get-tuple-element.46, pred[1024]{0:T(1024)(128)(4,1)S(1)} %get-tuple-element.45, pred[1024]{0:T(1024)(128)(4,1)S(1)} %get-tuple-element.44, ...), kind=kLoop, calls=%fused_computation.88 | loop fusion | flops 16384 | bytes 25636 | tf_op jit(solution)/shard_map/jit(_take)/select_n | solution.py:162
  211.7 4.5 %reduce-window.6 = s32[16,8,128]{2,1,0:T(8,128)S(1)} reduce-window(s32[16,8,128]{2,1,0:T(8,128)S(1)} %fusion.39, s32[]{:T(128)} %constant.118.clone.1), window={size=1x1x128 pad=0_0x0_0x127_0}, to_apply=%region_0.1 | reduce-window | flops 2080768 | bytes 131076 | tf_op jit(solution)/shard_map/reduce-window
  217.0 1.3 select_reduce_fusion
  218.3 1.0 copy.90
  219.3 73.3 %all-to-all-done = bf16[16,64,2048]{2,1,0:T(8,128)(2,1)} async-done(((bf16[16,64,2048]{2,1,0:T(8,128)(2,1)}), bf16[16,64,2048]{2,1,0:T(8,128)(2,1)}, u32[]{:S(2)}, u32[]{:S(2)}) %all-to-all-start) | async-done | bytes 4194336 | tf_op jit(solution)/shard_map/all_to_all | solution.py:222
  292.6 2.9 fusion.34
  295.6 2.9 convolution_add_fusion.1
  298.6 3.7 %fusion.20 = bf16[128,2048]{1,0:T(8,128)(2,1)} fusion(f32[128,2048]{1,0:T(8,128)S(1)} %convolution_add_fusion.1, bf16[1024,2048]{1,0:T(8,128)(2,1)} %bitcast.34, f32[128,1024]{1,0:T(8,128)S(1)} %select_reduce_fusion), kind=kOutput, calls=%fused_computation.28 | convolution fusion | flops 538312704 | bytes 6291456 | tf_op jit(solution)/shard_map/dot_general | solution.py:239
  (69 shorter events, 9.3 us)
Async XLA Ops:
  7.2 175.9 %copy-start = (bf16[1,384,2048]{2,1,0:T(8,128)(2,1)S(1)}, bf16[1,384,2048]{2,1,0:T(8,128)(2,1)}, u32[]{:S(2)}) copy-start(bf16[1,384,2048]{2,1,0:T(8,128)(2,1)} %param.27) | copy-start | bytes 4718596
  7.2 51.9 %all-gather.6.cloned.1.call-start = ((), (), s32[]{:S(2)}) async-start(), calls=%async_computation.2 | async-start | bytes 2228224 | tf_op jit(solution)/shard_map/all_gather | solution.py:113
  8.9 159.6 %all-gather.4.cloned.1.call-start = ((), (), s32[]{:S(2)}) async-start(), calls=%async_computation.1 | async-start | bytes 9469952 | tf_op jit(solution)/shard_map/all_gather | solution.py:180
  8.9 65.4 %collective-permute-start = (bf16[2048,512]{1,0:T(8,128)(2,1)}, bf16[2048,512]{1,0:T(8,128)(2,1)}, u32[]{:S(2)}, u32[]{:S(2)}) collective-permute-start(bf16[2048,512]{1,0:T(8,128)(2,1)} %param.19), channel_id=1, source_target_pairs={{0,2},{1,3},{2,0},{3,1},{4,6},{5,7},{6,4},{7,5},{8,10},{9,11},{10,... | collective-permute-start | bytes 6291464 | tf_op jit(solution)/shard_map/ppermute | solution.py:15
  61.6 13.3 %copy-start.1 = (bf16[128,2048]{1,0:T(8,128)(2,1)S(1)}, bf16[128,2048]{1,0:T(8,128)(2,1)}, u32[]{:S(2)}) copy-start(bf16[128,2048]{1,0:T(8,128)(2,1)} %param.20) | copy-start | bytes 1572868
  61.6 14.3 %copy-start.3 = (s32[128,8]{0,1:T(8,128)S(1)}, s32[128,8]{0,1:T(8,128)}, u32[]{:S(2)}) copy-start(s32[128,8]{0,1:T(8,128)} %param.22) | copy-start | bytes 12292
  74.3 4.5 %collective-permute-start.2 = (bf16[2048,512]{1,0:T(8,128)(2,1)}, bf16[2048,512]{1,0:T(8,128)(2,1)}, u32[]{:S(2)}, u32[]{:S(2)}) collective-permute-start(bf16[2048,512]{1,0:T(8,128)(2,1)} %collective-permute-done), channel_id=1, source_target_pairs={{0,1},{1,0},{2,3},{3,2},{4,5},{5,4},{6,7},{7,6},{8,9},{9,8},{10,11... | collective-permute-start | bytes 6291464 | tf_op jit(solution)/shard_map/ppermute | solution.py:15
  74.6 7.2 %collective-permute-start.1 = (bf16[2048,512]{1,0:T(8,128)(2,1)}, bf16[2048,512]{1,0:T(8,128)(2,1)}, u32[]{:S(2)}, u32[]{:S(2)}) collective-permute-start(bf16[2048,512]{1,0:T(8,128)(2,1)} %param.19), channel_id=1, source_target_pairs={{0,1},{1,0},{2,3},{3,2},{4,5},{5,4},{6,7},{7,6},{8,9},{9,8},{10,11... | collective-permute-start | bytes 6291464 | tf_op jit(solution)/shard_map/ppermute | solution.py:15
  86.2 3.3 %copy-start.4 = (f32[2048]{0:T(1024)S(1)}, f32[2048]{0:T(1024)}, u32[]{:S(2)}) copy-start(f32[2048]{0:T(1024)} %param.21) | copy-start | bytes 24580
  86.2 4.5 %copy-start.2 = (s32[16]{0:T(128)S(1)}, s32[16]{0:T(128)}, u32[]{:S(2)}) copy-start(s32[16]{0:T(128)} %param.24) | copy-start | bytes 196
  192.5 8.1 %copy-start.5 = (f32[128,8]{0,1:T(8,128)S(1)}, f32[128,8]{0,1:T(8,128)}, u32[]{:S(2)}) copy-start(f32[128,8]{0,1:T(8,128)} %param.23) | copy-start | bytes 12292
  192.5 100.2 %all-to-all-start = ((bf16[16,64,2048]{2,1,0:T(8,128)(2,1)}), bf16[16,64,2048]{2,1,0:T(8,128)(2,1)}, u32[]{:S(2)}, u32[]{:S(2)}) async-start(bf16[16,64,2048]{2,1,0:T(8,128)(2,1)} %bitcast.72), calls=%async_computation | async-start | bytes 8388608 | tf_op jit(solution)/shard_map/all_to_all | solution.py:222
Sparse Core Ops, SparseCore 0:
  10.7 48.3 all-gather.5
  90.9 77.5 all-gather.3

commit v12 on v11

--- a/solution.py
+++ b/solution.py
@@ -22,18 +22,12 @@
     for head in range(query_ref.shape[1] // HD):
         query_head = query_ref[:, head * HD : (head + 1) * HD]
         logits = (
-            lax.dot_general(
-                query_head,
-                key_block,
-                (((1,), (1,)), ((), ())),
-                preferred_element_type=jnp.float32,
-            )
-            * inverse_root
+            jnp.dot(query_head, key_block, preferred_element_type=jnp.float32) * inverse_root
         )
         largest = jnp.max(logits, axis=-1, keepdims=True)
         raised = jnp.exp(logits - largest)
         denominator = jnp.sum(raised, axis=-1, keepdims=True)
-        weights_low = (raised / denominator).astype(jnp.bfloat16)
+        weights_low = (raised * (1.0 / denominator)).astype(jnp.bfloat16)
         blended = jnp.dot(weights_low, value_block, preferred_element_type=jnp.float32)
         out_ref[:, head * HD : (head + 1) * HD] = blended.astype(out_ref.dtype)
 
@@ -47,13 +41,13 @@
         grid=(kv_heads,),
         in_specs=[
             pl.BlockSpec((row_count, group_width), lambda k: (0, k)),
-            pl.BlockSpec((span, HD), lambda k: (0, k)),
+            pl.BlockSpec((HD, span), lambda k: (k, 0)),
             pl.BlockSpec((span, HD), lambda k: (0, k)),
         ],
         out_specs=pl.BlockSpec((row_count, group_width), lambda k: (0, k)),
         out_shape=jax.ShapeDtypeStruct(queries_flat.shape, jnp.bfloat16),
         interpret=interpret,
-    )(queries_flat, key_rows.reshape(span, -1), value_rows.reshape(span, -1))
+    )(queries_flat, key_rows.reshape(span, -1).T, value_rows.reshape(span, -1))
 
 
 def expert_apply(rows_in, gate_full, up_full, down_full):

time: 310 us -> 311 us (level)
  transfers between devices with their start and end apart: 6 -> 6, of which waited for: 5 -> 5; matrix products, arithmetic and copies ran while one was open for 8% -> 9% of each run, Pallas kernels for 4% -> 4%
where the time goes in v12:
time: 311 us; the launch traced here: 310 us
  waiting for transfers between devices  205 us (66%)
  matrix products  35.7 us (11%)
  other arithmetic  24.9 us (8%)
  between operations  14.3 us (5%)
  Pallas kernels  11.4 us (4%)
  local copies, waits for them, and re-layouts  10.5 us (3%)
  starting transfers between devices  8.6 us (3%)
    all_gather x1, waiting for transfers between devices, local(): all_packed = lax.all_gather(packed, ('ctx', 'eg'), axis=0, tiled=True)  77.1 us
    all_to_all x1, waiting for transfers between devices, local(): lax.all_to_all(produced.reshape(slot_count, per_slot, -1), ('ctx', 'eg'),...  73.3 us
    all_gather x1, waiting for transfers between devices, local(): gathered = lax.all_gather(both[None], ('ctx', 'eg'), axis=0, tiled=True)  48.8 us
    dot_general x1, matrix products, local(): both_act = jnp.dot(all_packed, gate_up, preferred_element_type=jnp.float32)  12.3 us
    pallas_call x1, Pallas kernels, attend_rows(): pl.pallas_call(attention_kernel, grid=(kv_heads,), in_specs=[pl.BlockSpec...  11.4 us
    dot_general x3, matrix products, local(): jnp.dot(part, returned_rows, preferred_element_type=jnp.float32)  9.63 us
    dot_general x1, matrix products, local(): jnp.dot(picked, partner[2], preferred_element_type=jnp.float32)  9.36 us
    all_to_all x1, starting transfers between devices, local(): lax.all_to_all(produced.reshape(slot_count, per_slot, -1), ('ctx', 'eg'),...  7.69 us
  transfers between devices with their start and end apart: 6, of which 5 were waited for; matrix products, arithmetic and copies ran while one was open for 9% of the time, Pallas kernels for 4%

profile of v12, /device:TPU:11, one launch (start us, length us, event | category | flops | bytes accessed | tf_op | source)
XLA Modules:
  0.0 310.0 jit_solution(7609896020451926795)
XLA Ops:
  7.2 1.6 pad_maximum_fusion
  10.3 48.8 %all-gather.6.cloned.1.call-done = bf16[16,128,512]{2,1,0:T(8,128)(2,1)} async-done(((bf16[1,128,512]{2,1,0:T(8,128)(2,1)}), bf16[16,128,512]{2,1,0:T(8,128)(2,1)}) %all-gather.6.cloned.1.call-update) | async-done | bytes 2097168 | tf_op jit(solution)/shard_map/all_gather | solution.py:107
  59.1 2.2 gather_fusion
  62.6 1.2 copy.83
  63.8 11.4 %shard_map.140 = bf16[128,2048]{1,0:T(8,128)(2,1)} custom-call(bf16[128,2048]{1,0:T(8,128)(2,1)} %query_ref.1, bf16[256,1536]{1,0:T(8,128)(2,1)} %bitcast.75, bf16[1536,256]{1,0:T(8,128)(2,1)} %bitcast.76), custom_call_target="tpu_custom_call" | custom-call | tf_op jit(solution)/shard_map/pallas_call | solution.py:39
  77.4 2.3 collective-permute-done.2
  79.7 3.0 collective-permute-done.1
  82.7 4.4 %fusion = bf16[128,2048]{1,0:T(8,128)(2,1)S(1)} fusion(bf16[128,2048]{1,0:T(8,128)(2,1)} %shard_map.140, bf16[2048,512]{1,0:T(8,128)(2,1)} %collective-permute-done.2, bf16[2048,512]{1,0:T(8,128)(2,1)} %collective-permute-done, bf16[2048,512]{1,0:T(8,128)(2,1)} %collective-permute-done.1, bf16[2048,512]{1,0:T(8,128)(2,1)} %param.19), kind=kOutput, calls=%fused_computation.2 | convolution fusion | flops 1107296256 | bytes 9437184 | tf_op jit(solution)/shard_map/dot_general | solution.py:141
  87.1 1.4 gather_fusion.1
  88.5 1.3 copy.85
  92.3 77.1 %all-gather.4.cloned.1.call-done = bf16[2048,2176]{0,1:T(8,128)(2,1)} async-done(((bf16[128,2176]{0,1:T(8,128)(2,1)}), bf16[2048,2176]{0,1:T(8,128)(2,1)}) %all-gather.4.cloned.1.call-update) | async-done | bytes 8912912 | tf_op jit(solution)/shard_map/all_gather | solution.py:174
  169.4 1.4 fusion.40
  171.7 12.3 %fusion.13 = f32[2048,768]{1,0:T(8,128)} fusion(bf16[2048,2176]{0,1:T(8,128)(2,1)} %all-gather.4.cloned.1.call-done, bf16[2048,384]{1,0:T(8,128)(2,1)} %bitcast.86, bf16[2048,384]{1,0:T(8,128)(2,1)} %bitcast.87), kind=kOutput, calls=%fused_computation.20 | convolution fusion | flops 6856802304 | bytes 18350080 | tf_op jit(solution)/shard_map/dot_general | solution.py:195
  184.0 9.4 %convolution_convert_fusion = bf16[1024,2048]{1,0:T(8,128)(2,1)} fusion(bf16[1,384,2048]{2,1,0:T(8,128)(2,1)S(1)} %copy-done, f32[2048,768]{1,0:T(8,128)} %fusion.13, s32[1024]{0:T(1024)S(1)} %add.153), kind=kOutput, calls=%fused_computation.18 | convolution fusion | flops 3230531584 | bytes 12062720 | tf_op jit(solution)/shard_map/dot_general | solution.py:206
  193.4 7.7 %all-to-all-start = ((bf16[16,64,2048]{2,1,0:T(8,128)(2,1)}), bf16[16,64,2048]{2,1,0:T(8,128)(2,1)}, u32[]{:S(2)}, u32[]{:S(2)}) async-start(bf16[16,64,2048]{2,1,0:T(8,128)(2,1)} %bitcast.73), calls=%async_computation | async-start | bytes 8388608 | tf_op jit(solution)/shard_map/all_to_all | solution.py:216
  202.3 4.4 %compare_select_fusion.1 = (s32[1024,1]{0,1:T(1,128)S(1)}, s32[1024,1]{0,1:T(1,128)S(1)}) fusion(s32[]{:T(128)} %bitcast.19, s32[]{:T(128)} %bitcast.20, s32[]{:T(128)} %bitcast.21, s32[]{:T(128)} %bitcast.22, s32[]{:T(128)} %bitcast.23, s32[]{:T(128)} %bitcast.25, s32[]{:T(128)} %bitcast.24, s32[1024,1]{0,1:T(1,128)S(1)} %reshape.284), kind=kLoop, calls=%fused_computation.70 | loop fusion | flops 15360 | bytes 12316 | tf_op jit(solution)/shard_map/jit(_take)/gather | solution.py:156
  206.8 5.6 %and_select_fusion = (s32[1024]{0:T(1024)S(1)}, s32[1024]{0:T(1024)S(1)}) fusion(s32[1024]{0:T(1024)S(1)} %reshape.285, pred[1024]{0:T(1024)(128)(4,1)S(1)} %get-tuple-element.47, pred[1024]{0:T(1024)(128)(4,1)S(1)} %get-tuple-element.46, pred[1024]{0:T(1024)(128)(4,1)S(1)} %get-tuple-element.45, pred[1024]{0:T(1024)(128)(4,1)S(1)} %get-tuple-element.44, ...), kind=kLoop, calls=%fused_computation.88 | loop fusion | flops 16384 | bytes 25636 | tf_op jit(solution)/shard_map/jit(_take)/select_n | solution.py:156
  212.5 4.5 %reduce-window.6 = s32[16,8,128]{2,1,0:T(8,128)S(1)} reduce-window(s32[16,8,128]{2,1,0:T(8,128)S(1)} %fusion.39, s32[]{:T(128)} %constant.118.clone.1), window={size=1x1x128 pad=0_0x0_0x127_0}, to_apply=%region_0.1 | reduce-window | flops 2080768 | bytes 131076 | tf_op jit(solution)/shard_map/reduce-window
  217.8 1.3 select_reduce_fusion
  219.2 1.0 copy.96
  220.2 73.3 %all-to-all-done = bf16[16,64,2048]{2,1,0:T(8,128)(2,1)} async-done(((bf16[16,64,2048]{2,1,0:T(8,128)(2,1)}), bf16[16,64,2048]{2,1,0:T(8,128)(2,1)}, u32[]{:S(2)}, u32[]{:S(2)}) %all-to-all-start) | async-done | bytes 4194336 | tf_op jit(solution)/shard_map/all_to_all | solution.py:216
  293.5 2.9 fusion.34
  296.5 2.9 convolution_add_fusion.1
  299.4 3.7 %fusion.20 = bf16[128,2048]{1,0:T(8,128)(2,1)} fusion(f32[128,2048]{1,0:T(8,128)S(1)} %convolution_add_fusion.1, bf16[1024,2048]{1,0:T(8,128)(2,1)} %bitcast.35, f32[128,1024]{1,0:T(8,128)S(1)} %select_reduce_fusion), kind=kOutput, calls=%fused_computation.28 | convolution fusion | flops 538312704 | bytes 6291456 | tf_op jit(solution)/shard_map/dot_general | solution.py:233
  (70 shorter events, 10.3 us)
Async XLA Ops:
  7.2 176.8 %copy-start = (bf16[1,384,2048]{2,1,0:T(8,128)(2,1)S(1)}, bf16[1,384,2048]{2,1,0:T(8,128)(2,1)}, u32[]{:S(2)}) copy-start(bf16[1,384,2048]{2,1,0:T(8,128)(2,1)} %param.27) | copy-start | bytes 4718596
  7.2 51.9 %all-gather.6.cloned.1.call-start = ((), (), s32[]{:S(2)}) async-start(), calls=%async_computation.2 | async-start | bytes 2228224 | tf_op jit(solution)/shard_map/all_gather | solution.py:107
  8.9 160.5 %all-gather.4.cloned.1.call-start = ((), (), s32[]{:S(2)}) async-start(), calls=%async_computation.1 | async-start | bytes 9469952 | tf_op jit(solution)/shard_map/all_gather | solution.py:174
  8.9 66.2 %collective-permute-start = (bf16[2048,512]{1,0:T(8,128)(2,1)}, bf16[2048,512]{1,0:T(8,128)(2,1)}, u32[]{:S(2)}, u32[]{:S(2)}) collective-permute-start(bf16[2048,512]{1,0:T(8,128)(2,1)} %param.19), channel_id=1, source_target_pairs={{0,2},{1,3},{2,0},{3,1},{4,6},{5,7},{6,4},{7,5},{8,10},{9,11},{10,... | collective-permute-start | bytes 6291464 | tf_op jit(solution)/shard_map/ppermute | solution.py:15
  61.6 14.1 %copy-start.1 = (bf16[128,2048]{1,0:T(8,128)(2,1)S(1)}, bf16[128,2048]{1,0:T(8,128)(2,1)}, u32[]{:S(2)}) copy-start(bf16[128,2048]{1,0:T(8,128)(2,1)} %param.20) | copy-start | bytes 1572868
  62.6 14.1 %copy-start.3 = (s32[128,8]{0,1:T(8,128)S(1)}, s32[128,8]{0,1:T(8,128)}, u32[]{:S(2)}) copy-start(s32[128,8]{0,1:T(8,128)} %param.22) | copy-start | bytes 12292
  75.2 4.5 %collective-permute-start.2 = (bf16[2048,512]{1,0:T(8,128)(2,1)}, bf16[2048,512]{1,0:T(8,128)(2,1)}, u32[]{:S(2)}, u32[]{:S(2)}) collective-permute-start(bf16[2048,512]{1,0:T(8,128)(2,1)} %collective-permute-done), channel_id=1, source_target_pairs={{0,1},{1,0},{2,3},{3,2},{4,5},{5,4},{6,7},{7,6},{8,9},{9,8},{10,11... | collective-permute-start | bytes 6291464 | tf_op jit(solution)/shard_map/ppermute | solution.py:15
  75.4 7.3 %collective-permute-start.1 = (bf16[2048,512]{1,0:T(8,128)(2,1)}, bf16[2048,512]{1,0:T(8,128)(2,1)}, u32[]{:S(2)}, u32[]{:S(2)}) collective-permute-start(bf16[2048,512]{1,0:T(8,128)(2,1)} %param.19), channel_id=1, source_target_pairs={{0,1},{1,0},{2,3},{3,2},{4,5},{5,4},{6,7},{7,6},{8,9},{9,8},{10,11... | collective-permute-start | bytes 6291464 | tf_op jit(solution)/shard_map/ppermute | solution.py:15
  87.1 3.3 %copy-start.4 = (f32[2048]{0:T(1024)S(1)}, f32[2048]{0:T(1024)}, u32[]{:S(2)}) copy-start(f32[2048]{0:T(1024)} %param.21) | copy-start | bytes 24580
  87.1 4.5 %copy-start.2 = (s32[16]{0:T(128)S(1)}, s32[16]{0:T(128)}, u32[]{:S(2)}) copy-start(s32[16]{0:T(128)} %param.24) | copy-start | bytes 196
  193.4 8.1 %copy-start.5 = (f32[128,8]{0,1:T(8,128)S(1)}, f32[128,8]{0,1:T(8,128)}, u32[]{:S(2)}) copy-start(f32[128,8]{0,1:T(8,128)} %param.23) | copy-start | bytes 12292
  193.4 100.2 %all-to-all-start = ((bf16[16,64,2048]{2,1,0:T(8,128)(2,1)}), bf16[16,64,2048]{2,1,0:T(8,128)(2,1)}, u32[]{:S(2)}, u32[]{:S(2)}) async-start(bf16[16,64,2048]{2,1,0:T(8,128)(2,1)} %bitcast.73), calls=%async_computation | async-start | bytes 8388608 | tf_op jit(solution)/shard_map/all_to_all | solution.py:216
Sparse Core Ops, SparseCore 0:
  10.7 48.3 all-gather.5
  91.8 77.5 all-gather.3

commit v13 on v11

--- a/solution.py
+++ b/solution.py
@@ -233,7 +233,7 @@
     mixing = jnp.sum(jnp.where(placed, gate_weights[:, :, None], 0.0), axis=1)
     combined = jnp.zeros((tok_dev, returned_rows.shape[1]), jnp.float32)
     remainder = mixing
-    for _ in range(3):
+    for _ in range(2):
         part = remainder.astype(jnp.bfloat16)
         remainder = remainder - part.astype(jnp.float32)
         combined = combined + jnp.dot(part, returned_rows, preferred_element_type=jnp.float32)

time: 310 us -> 307 us (level)
    dot_general x3 -> x2, matrix products: 9.64 us -> 6.65 us  [local(): jnp.dot(part, returned_rows, preferred_element_type=jnp.float32)]
  transfers between devices with their start and end apart: 6 -> 6, of which waited for: 5 -> 5; matrix products, arithmetic and copies ran while one was open for 8% -> 9% of each run, Pallas kernels for 4% -> 4%
where the time goes in v13:
time: 307 us; the launch traced here: 306 us
  waiting for transfers between devices  205 us (67%)
  matrix products  32.7 us (11%)
  other arithmetic  24.9 us (8%)
  between operations  14.3 us (5%)
  Pallas kernels  11.5 us (4%)
  local copies, waits for them, and re-layouts  9.57 us (3%)
  starting transfers between devices  8.6 us (3%)
    all_gather x1, waiting for transfers between devices, local(): all_packed = lax.all_gather(packed, ('ctx', 'eg'), axis=0, tiled=True)  77.1 us
    all_to_all x1, waiting for transfers between devices, local(): lax.all_to_all(produced.reshape(slot_count, per_slot, -1), ('ctx', 'eg'),...  73.3 us
    all_gather x1, waiting for transfers between devices, local(): gathered = lax.all_gather(both[None], ('ctx', 'eg'), axis=0, tiled=True)  48.8 us
    dot_general x1, matrix products, local(): both_act = jnp.dot(all_packed, gate_up, preferred_element_type=jnp.float32)  12.3 us
    pallas_call x1, Pallas kernels, attend_rows(): pl.pallas_call(attention_kernel, grid=(kv_heads,), in_specs=[pl.BlockSpec...  11.5 us
    dot_general x1, matrix products, local(): jnp.dot(picked, partner[2], preferred_element_type=jnp.float32)  9.36 us
    all_to_all x1, starting transfers between devices, local(): lax.all_to_all(produced.reshape(slot_count, per_slot, -1), ('ctx', 'eg'),...  7.69 us
    dot_general x2, matrix products, local(): jnp.dot(part, returned_rows, preferred_element_type=jnp.float32)  6.65 us
  transfers between devices with their start and end apart: 6, of which 5 were waited for; matrix products, arithmetic and copies ran while one was open for 9% of the time, Pallas kernels for 4%

profile of v13, /device:TPU:11, one launch (start us, length us, event | category | flops | bytes accessed | tf_op | source)
XLA Modules:
  0.0 306.1 jit_solution(4161844745827866863)
XLA Ops:
  7.2 1.6 pad_maximum_fusion
  10.3 48.8 %all-gather.6.cloned.1.call-done = bf16[16,128,512]{2,1,0:T(8,128)(2,1)} async-done(((bf16[1,128,512]{2,1,0:T(8,128)(2,1)}), bf16[16,128,512]{2,1,0:T(8,128)(2,1)}) %all-gather.6.cloned.1.call-update) | async-done | bytes 2097168 | tf_op jit(solution)/shard_map/all_gather | solution.py:113
  59.1 2.2 gather_fusion
  61.6 1.3 fusion.50
  62.8 11.5 %shard_map.140 = bf16[128,2048]{1,0:T(8,128)(2,1)} custom-call(bf16[128,2048]{1,0:T(8,128)(2,1)} %query_ref.1, bf16[1536,256]{1,0:T(8,128)(2,1)} %bitcast.73, bf16[1536,256]{1,0:T(8,128)(2,1)} %bitcast.72), custom_call_target="tpu_custom_call" | custom-call | tf_op jit(solution)/shard_map/pallas_call | solution.py:45
  76.5 2.3 collective-permute-done.2
  78.8 3.0 collective-permute-done.1
  81.8 4.4 %fusion = bf16[128,2048]{1,0:T(8,128)(2,1)S(1)} fusion(bf16[128,2048]{1,0:T(8,128)(2,1)} %shard_map.140, bf16[2048,512]{1,0:T(8,128)(2,1)} %collective-permute-done.2, bf16[2048,512]{1,0:T(8,128)(2,1)} %collective-permute-done, bf16[2048,512]{1,0:T(8,128)(2,1)} %collective-permute-done.1, bf16[2048,512]{1,0:T(8,128)(2,1)} %param.19), kind=kOutput, calls=%fused_computation.2 | convolution fusion | flops 1107296256 | bytes 9437184 | tf_op jit(solution)/shard_map/dot_general | solution.py:147
  86.2 1.4 gather_fusion.1
  87.6 1.3 copy.79
  89.8 0.9 fusion.31
  91.4 77.1 %all-gather.4.cloned.1.call-done = bf16[2048,2176]{0,1:T(8,128)(2,1)} async-done(((bf16[128,2176]{0,1:T(8,128)(2,1)}), bf16[2048,2176]{0,1:T(8,128)(2,1)}) %all-gather.4.cloned.1.call-update) | async-done | bytes 8912912 | tf_op jit(solution)/shard_map/all_gather | solution.py:180
  168.5 1.4 fusion.39
  170.8 12.3 %fusion.13 = f32[2048,768]{1,0:T(8,128)} fusion(bf16[2048,2176]{0,1:T(8,128)(2,1)} %all-gather.4.cloned.1.call-done, bf16[2048,384]{1,0:T(8,128)(2,1)} %bitcast.83, bf16[2048,384]{1,0:T(8,128)(2,1)} %bitcast.84), kind=kOutput, calls=%fused_computation.20 | convolution fusion | flops 6856802304 | bytes 18350080 | tf_op jit(solution)/shard_map/dot_general | solution.py:201
  183.1 9.4 %convolution_convert_fusion = bf16[1024,2048]{1,0:T(8,128)(2,1)} fusion(bf16[1,384,2048]{2,1,0:T(8,128)(2,1)S(1)} %copy-done, f32[2048,768]{1,0:T(8,128)} %fusion.13, s32[1024]{0:T(1024)S(1)} %add.150), kind=kOutput, calls=%fused_computation.18 | convolution fusion | flops 3230531584 | bytes 12062720 | tf_op jit(solution)/shard_map/dot_general | solution.py:212
  192.5 7.7 %all-to-all-start = ((bf16[16,64,2048]{2,1,0:T(8,128)(2,1)}), bf16[16,64,2048]{2,1,0:T(8,128)(2,1)}, u32[]{:S(2)}, u32[]{:S(2)}) async-start(bf16[16,64,2048]{2,1,0:T(8,128)(2,1)} %bitcast.71), calls=%async_computation | async-start | bytes 8388608 | tf_op jit(solution)/shard_map/all_to_all | solution.py:222
  201.4 4.4 %compare_select_fusion.1 = (s32[1024,1]{0,1:T(1,128)S(1)}, s32[1024,1]{0,1:T(1,128)S(1)}) fusion(s32[]{:T(128)} %bitcast.18, s32[]{:T(128)} %bitcast.19, s32[]{:T(128)} %bitcast.20, s32[]{:T(128)} %bitcast.21, s32[]{:T(128)} %bitcast.22, s32[]{:T(128)} %bitcast.24, s32[]{:T(128)} %bitcast.23, s32[1024,1]{0,1:T(1,128)S(1)} %reshape.284), kind=kLoop, calls=%fused_computation.68 | loop fusion | flops 15360 | bytes 12316 | tf_op jit(solution)/shard_map/jit(_take)/gather | solution.py:162
  205.9 5.6 %and_select_fusion = (s32[1024]{0:T(1024)S(1)}, s32[1024]{0:T(1024)S(1)}) fusion(s32[1024]{0:T(1024)S(1)} %reshape.285, pred[1024]{0:T(1024)(128)(4,1)S(1)} %get-tuple-element.47, pred[1024]{0:T(1024)(128)(4,1)S(1)} %get-tuple-element.46, pred[1024]{0:T(1024)(128)(4,1)S(1)} %get-tuple-element.45, pred[1024]{0:T(1024)(128)(4,1)S(1)} %get-tuple-element.44, ...), kind=kLoop, calls=%fused_computation.86 | loop fusion | flops 16384 | bytes 25636 | tf_op jit(solution)/shard_map/jit(_take)/select_n | solution.py:162
  211.7 4.5 %reduce-window.6 = s32[16,8,128]{2,1,0:T(8,128)S(1)} reduce-window(s32[16,8,128]{2,1,0:T(8,128)S(1)} %fusion.38, s32[]{:T(128)} %constant.118.clone.1), window={size=1x1x128 pad=0_0x0_0x127_0}, to_apply=%region_0.1 | reduce-window | flops 2080768 | bytes 131076 | tf_op jit(solution)/shard_map/reduce-window
  217.0 1.3 select_reduce_fusion
  218.3 1.0 copy.90
  219.3 73.3 %all-to-all-done = bf16[16,64,2048]{2,1,0:T(8,128)(2,1)} async-done(((bf16[16,64,2048]{2,1,0:T(8,128)(2,1)}), bf16[16,64,2048]{2,1,0:T(8,128)(2,1)}, u32[]{:S(2)}, u32[]{:S(2)}) %all-to-all-start) | async-done | bytes 4194336 | tf_op jit(solution)/shard_map/all_to_all | solution.py:222
  292.6 2.9 fusion.34
  295.6 3.8 %fusion.20 = bf16[128,2048]{1,0:T(8,128)(2,1)} fusion(f32[128,2048]{1,0:T(8,128)S(1)} %fusion.34, bf16[1024,2048]{1,0:T(8,128)(2,1)} %bitcast.34, f32[128,1024]{1,0:T(8,128)S(1)} %select_reduce_fusion), kind=kOutput, calls=%fused_computation.27 | convolution fusion | flops 537919488 | bytes 6291456 | tf_op jit(solution)/shard_map/dot_general | solution.py:239
  (68 shorter events, 8.4 us)
Async XLA Ops:
  7.2 175.9 %copy-start = (bf16[1,384,2048]{2,1,0:T(8,128)(2,1)S(1)}, bf16[1,384,2048]{2,1,0:T(8,128)(2,1)}, u32[]{:S(2)}) copy-start(bf16[1,384,2048]{2,1,0:T(8,128)(2,1)} %param.27) | copy-start | bytes 4718596
  7.2 51.9 %all-gather.6.cloned.1.call-start = ((), (), s32[]{:S(2)}) async-start(), calls=%async_computation.2 | async-start | bytes 2228224 | tf_op jit(solution)/shard_map/all_gather | solution.py:113
  8.9 159.6 %all-gather.4.cloned.1.call-start = ((), (), s32[]{:S(2)}) async-start(), calls=%async_computation.1 | async-start | bytes 9469952 | tf_op jit(solution)/shard_map/all_gather | solution.py:180
  8.9 65.4 %collective-permute-start = (bf16[2048,512]{1,0:T(8,128)(2,1)}, bf16[2048,512]{1,0:T(8,128)(2,1)}, u32[]{:S(2)}, u32[]{:S(2)}) collective-permute-start(bf16[2048,512]{1,0:T(8,128)(2,1)} %param.19), channel_id=1, source_target_pairs={{0,2},{1,3},{2,0},{3,1},{4,6},{5,7},{6,4},{7,5},{8,10},{9,11},{10,... | collective-permute-start | bytes 6291464 | tf_op jit(solution)/shard_map/ppermute | solution.py:15
  61.6 13.3 %copy-start.1 = (bf16[128,2048]{1,0:T(8,128)(2,1)S(1)}, bf16[128,2048]{1,0:T(8,128)(2,1)}, u32[]{:S(2)}) copy-start(bf16[128,2048]{1,0:T(8,128)(2,1)} %param.20) | copy-start | bytes 1572868
  61.6 14.3 %copy-start.3 = (s32[128,8]{0,1:T(8,128)S(1)}, s32[128,8]{0,1:T(8,128)}, u32[]{:S(2)}) copy-start(s32[128,8]{0,1:T(8,128)} %param.22) | copy-start | bytes 12292
  74.3 4.5 %collective-permute-start.2 = (bf16[2048,512]{1,0:T(8,128)(2,1)}, bf16[2048,512]{1,0:T(8,128)(2,1)}, u32[]{:S(2)}, u32[]{:S(2)}) collective-permute-start(bf16[2048,512]{1,0:T(8,128)(2,1)} %collective-permute-done), channel_id=1, source_target_pairs={{0,1},{1,0},{2,3},{3,2},{4,5},{5,4},{6,7},{7,6},{8,9},{9,8},{10,11... | collective-permute-start | bytes 6291464 | tf_op jit(solution)/shard_map/ppermute | solution.py:15
  74.6 7.2 %collective-permute-start.1 = (bf16[2048,512]{1,0:T(8,128)(2,1)}, bf16[2048,512]{1,0:T(8,128)(2,1)}, u32[]{:S(2)}, u32[]{:S(2)}) collective-permute-start(bf16[2048,512]{1,0:T(8,128)(2,1)} %param.19), channel_id=1, source_target_pairs={{0,1},{1,0},{2,3},{3,2},{4,5},{5,4},{6,7},{7,6},{8,9},{9,8},{10,11... | collective-permute-start | bytes 6291464 | tf_op jit(solution)/shard_map/ppermute | solution.py:15
  86.2 3.3 %copy-start.4 = (f32[2048]{0:T(1024)S(1)}, f32[2048]{0:T(1024)}, u32[]{:S(2)}) copy-start(f32[2048]{0:T(1024)} %param.21) | copy-start | bytes 24580
  87.6 3.2 %copy-start.2 = (s32[16]{0:T(128)S(1)}, s32[16]{0:T(128)}, u32[]{:S(2)}) copy-start(s32[16]{0:T(128)} %param.24) | copy-start | bytes 196
  192.5 8.1 %copy-start.5 = (f32[128,8]{0,1:T(8,128)S(1)}, f32[128,8]{0,1:T(8,128)}, u32[]{:S(2)}) copy-start(f32[128,8]{0,1:T(8,128)} %param.23) | copy-start | bytes 12292
  192.5 100.2 %all-to-all-start = ((bf16[16,64,2048]{2,1,0:T(8,128)(2,1)}), bf16[16,64,2048]{2,1,0:T(8,128)(2,1)}, u32[]{:S(2)}, u32[]{:S(2)}) async-start(bf16[16,64,2048]{2,1,0:T(8,128)(2,1)} %bitcast.71), calls=%async_computation | async-start | bytes 8388608 | tf_op jit(solution)/shard_map/all_to_all | solution.py:222
Sparse Core Ops, SparseCore 0:
  10.7 48.3 all-gather.5
  90.9 77.5 all-gather.3

commit v14 on v13

--- a/solution.py
+++ b/solution.py
@@ -231,12 +231,11 @@
         pair_count, dtype=jnp.int32
     )[None, None, :]
     mixing = jnp.sum(jnp.where(placed, gate_weights[:, :, None], 0.0), axis=1)
-    combined = jnp.zeros((tok_dev, returned_rows.shape[1]), jnp.float32)
-    remainder = mixing
-    for _ in range(2):
-        part = remainder.astype(jnp.bfloat16)
-        remainder = remainder - part.astype(jnp.float32)
-        combined = combined + jnp.dot(part, returned_rows, preferred_element_type=jnp.float32)
+    high_part = mixing.astype(jnp.bfloat16)
+    low_part = (mixing - high_part.astype(jnp.float32)).astype(jnp.bfloat16)
+    both_parts = jnp.concatenate([high_part, low_part], axis=0)
+    stacked_out = jnp.dot(both_parts, returned_rows, preferred_element_type=jnp.float32)
+    combined = stacked_out[:tok_dev] + stacked_out[tok_dev:]
     moe_out = combined.astype(jnp.bfloat16)
     return (attn_out, moe_out)
 

time: 307 us -> 304 us (level)
  matrix products: 32.7 us -> 29.5 us
    dot_general x2 -> x1, matrix products: 6.65 us -> 3.46 us  [local(): jnp.dot(both_parts, returned_rows, preferred_element_type=jnp.float32)]
where the time goes in v14:
time: 304 us
  waiting for transfers between devices  204 us (67%)
  matrix products  29.5 us (10%)
  other arithmetic  25.9 us (9%)
  between operations  14.3 us (5%)
  Pallas kernels  11.5 us (4%)
  local copies, waits for them, and re-layouts  9.59 us (3%)
  starting transfers between devices  8.6 us (3%)
    all_gather x1, waiting for transfers between devices, local(): all_packed = lax.all_gather(packed, ('ctx', 'eg'), axis=0, tiled=True)  77.1 us
    all_to_all x1, waiting for transfers between devices, local(): lax.all_to_all(produced.reshape(slot_count, per_slot, -1), ('ctx', 'eg'),...  73.2 us
    all_gather x1, waiting for transfers between devices, local(): gathered = lax.all_gather(both[None], ('ctx', 'eg'), axis=0, tiled=True)  48.8 us
    dot_general x1, matrix products, local(): both_act = jnp.dot(all_packed, gate_up, preferred_element_type=jnp.float32)  12.3 us
    pallas_call x1, Pallas kernels, attend_rows(): pl.pallas_call(attention_kernel, grid=(kv_heads,), in_specs=[pl.BlockSpec...  11.5 us
    dot_general x1, matrix products, local(): jnp.dot(picked, partner[2], preferred_element_type=jnp.float32)  9.36 us
    all_to_all x1, starting transfers between devices, local(): lax.all_to_all(produced.reshape(slot_count, per_slot, -1), ('ctx', 'eg'),...  7.69 us
  transfers between devices with their start and end apart: 6, of which 5 were waited for; matrix products, arithmetic and copies ran while one was open for 9% of the time, Pallas kernels for 4%

profile of v14, /device:TPU:11, one launch (start us, length us, event | category | flops | bytes accessed | tf_op | source)
XLA Modules:
  0.0 303.9 jit_solution(3774069757874039173)
XLA Ops:
  7.2 1.6 pad_maximum_fusion
  10.3 48.8 %all-gather.6.cloned.1.call-done = bf16[16,128,512]{2,1,0:T(8,128)(2,1)} async-done(((bf16[1,128,512]{2,1,0:T(8,128)(2,1)}), bf16[16,128,512]{2,1,0:T(8,128)(2,1)}) %all-gather.6.cloned.1.call-update) | async-done | bytes 2097168 | tf_op jit(solution)/shard_map/all_gather | solution.py:113
  59.1 2.2 gather_fusion
  61.6 1.3 fusion.52
  62.8 11.5 %shard_map.140 = bf16[128,2048]{1,0:T(8,128)(2,1)} custom-call(bf16[128,2048]{1,0:T(8,128)(2,1)} %query_ref.1, bf16[1536,256]{1,0:T(8,128)(2,1)} %bitcast.72, bf16[1536,256]{1,0:T(8,128)(2,1)} %bitcast.71), custom_call_target="tpu_custom_call" | custom-call | tf_op jit(solution)/shard_map/pallas_call | solution.py:45
  76.5 2.3 collective-permute-done.2
  78.8 3.0 collective-permute-done.1
  81.8 4.4 %fusion = bf16[128,2048]{1,0:T(8,128)(2,1)S(1)} fusion(bf16[128,2048]{1,0:T(8,128)(2,1)} %shard_map.140, bf16[2048,512]{1,0:T(8,128)(2,1)} %collective-permute-done.2, bf16[2048,512]{1,0:T(8,128)(2,1)} %collective-permute-done, bf16[2048,512]{1,0:T(8,128)(2,1)} %collective-permute-done.1, bf16[2048,512]{1,0:T(8,128)(2,1)} %param.19), kind=kOutput, calls=%fused_computation.2 | convolution fusion | flops 1107296256 | bytes 9437184 | tf_op jit(solution)/shard_map/dot_general | solution.py:147
  86.2 1.4 gather_fusion.1
  87.6 1.3 copy.79
  89.8 0.9 fusion.31
  91.4 77.1 %all-gather.4.cloned.1.call-done = bf16[2048,2176]{0,1:T(8,128)(2,1)} async-done(((bf16[128,2176]{0,1:T(8,128)(2,1)}), bf16[2048,2176]{0,1:T(8,128)(2,1)}) %all-gather.4.cloned.1.call-update) | async-done | bytes 8912912 | tf_op jit(solution)/shard_map/all_gather | solution.py:180
  168.5 1.4 fusion.40
  170.8 12.3 %fusion.13 = f32[2048,768]{1,0:T(8,128)} fusion(bf16[2048,2176]{0,1:T(8,128)(2,1)} %all-gather.4.cloned.1.call-done, bf16[2048,384]{1,0:T(8,128)(2,1)} %bitcast.82, bf16[2048,384]{1,0:T(8,128)(2,1)} %bitcast.83), kind=kOutput, calls=%fused_computation.20 | convolution fusion | flops 6856802304 | bytes 18350080 | tf_op jit(solution)/shard_map/dot_general | solution.py:201
  183.1 9.4 %convolution_convert_fusion = bf16[1024,2048]{1,0:T(8,128)(2,1)} fusion(bf16[1,384,2048]{2,1,0:T(8,128)(2,1)S(1)} %copy-done, f32[2048,768]{1,0:T(8,128)} %fusion.13, s32[1024]{0:T(1024)S(1)} %add.150), kind=kOutput, calls=%fused_computation.18 | convolution fusion | flops 3230531584 | bytes 12062720 | tf_op jit(solution)/shard_map/dot_general | solution.py:212
  192.5 7.7 %all-to-all-start = ((bf16[16,64,2048]{2,1,0:T(8,128)(2,1)}), bf16[16,64,2048]{2,1,0:T(8,128)(2,1)}, u32[]{:S(2)}, u32[]{:S(2)}) async-start(bf16[16,64,2048]{2,1,0:T(8,128)(2,1)} %bitcast.70), calls=%async_computation | async-start | bytes 8388608 | tf_op jit(solution)/shard_map/all_to_all | solution.py:222
  201.4 4.4 %compare_select_fusion.1 = (s32[1024,1]{0,1:T(1,128)S(1)}, s32[1024,1]{0,1:T(1,128)S(1)}) fusion(s32[]{:T(128)} %bitcast.18, s32[]{:T(128)} %bitcast.19, s32[]{:T(128)} %bitcast.20, s32[]{:T(128)} %bitcast.21, s32[]{:T(128)} %bitcast.22, s32[]{:T(128)} %bitcast.24, s32[]{:T(128)} %bitcast.23, s32[1024,1]{0,1:T(1,128)S(1)} %reshape.284), kind=kLoop, calls=%fused_computation.69 | loop fusion | flops 15360 | bytes 12316 | tf_op jit(solution)/shard_map/jit(_take)/gather | solution.py:162
  205.9 5.6 %and_select_fusion = (s32[1024]{0:T(1024)S(1)}, s32[1024]{0:T(1024)S(1)}) fusion(s32[1024]{0:T(1024)S(1)} %reshape.285, pred[1024]{0:T(1024)(128)(4,1)S(1)} %get-tuple-element.47, pred[1024]{0:T(1024)(128)(4,1)S(1)} %get-tuple-element.46, pred[1024]{0:T(1024)(128)(4,1)S(1)} %get-tuple-element.45, pred[1024]{0:T(1024)(128)(4,1)S(1)} %get-tuple-element.44, ...), kind=kLoop, calls=%fused_computation.87 | loop fusion | flops 16384 | bytes 25636 | tf_op jit(solution)/shard_map/jit(_take)/select_n | solution.py:162
  211.7 4.5 %reduce-window.6 = s32[16,8,128]{2,1,0:T(8,128)S(1)} reduce-window(s32[16,8,128]{2,1,0:T(8,128)S(1)} %fusion.39, s32[]{:T(128)} %constant.118.clone.1), window={size=1x1x128 pad=0_0x0_0x127_0}, to_apply=%region_0.1 | reduce-window | flops 2080768 | bytes 131076 | tf_op jit(solution)/shard_map/reduce-window
  217.0 1.3 select_reduce_fusion
  218.4 1.0 copy.90
  219.4 73.2 %all-to-all-done = bf16[16,64,2048]{2,1,0:T(8,128)(2,1)} async-done(((bf16[16,64,2048]{2,1,0:T(8,128)(2,1)}), bf16[16,64,2048]{2,1,0:T(8,128)(2,1)}, u32[]{:S(2)}, u32[]{:S(2)}) %all-to-all-start) | async-done | bytes 4194336 | tf_op jit(solution)/shard_map/all_to_all | solution.py:222
  292.6 3.5 %fusion.32 = f32[256,2048]{1,0:T(8,128)S(1)} fusion(bf16[1024,2048]{1,0:T(8,128)(2,1)} %bitcast.34, bf16[128,1024]{1,0:T(8,128)(2,1)S(1)} %get-tuple-element.48, bf16[128,1024]{1,0:T(8,128)(2,1)S(1)} %get-tuple-element.49), kind=kOutput, calls=%fused_computation.41 | convolution fusion | flops 1074790400 | bytes 6815744 | tf_op jit(solution)/shard_map/dot_general | solution.py:237
  296.1 0.9 fusion.27
  (69 shorter events, 8.4 us)
Async XLA Ops:
  7.2 175.9 %copy-start = (bf16[1,384,2048]{2,1,0:T(8,128)(2,1)S(1)}, bf16[1,384,2048]{2,1,0:T(8,128)(2,1)}, u32[]{:S(2)}) copy-start(bf16[1,384,2048]{2,1,0:T(8,128)(2,1)} %param.27) | copy-start | bytes 4718596
  7.2 51.9 %all-gather.6.cloned.1.call-start = ((), (), s32[]{:S(2)}) async-start(), calls=%async_computation.2 | async-start | bytes 2228224 | tf_op jit(solution)/shard_map/all_gather | solution.py:113
  8.9 159.6 %all-gather.4.cloned.1.call-start = ((), (), s32[]{:S(2)}) async-start(), calls=%async_computation.1 | async-start | bytes 9469952 | tf_op jit(solution)/shard_map/all_gather | solution.py:180
  8.9 65.4 %collective-permute-start = (bf16[2048,512]{1,0:T(8,128)(2,1)}, bf16[2048,512]{1,0:T(8,128)(2,1)}, u32[]{:S(2)}, u32[]{:S(2)}) collective-permute-start(bf16[2048,512]{1,0:T(8,128)(2,1)} %param.19), channel_id=1, source_target_pairs={{0,2},{1,3},{2,0},{3,1},{4,6},{5,7},{6,4},{7,5},{8,10},{9,11},{10,... | collective-permute-start | bytes 6291464 | tf_op jit(solution)/shard_map/ppermute | solution.py:15
  61.6 13.3 %copy-start.1 = (bf16[128,2048]{1,0:T(8,128)(2,1)S(1)}, bf16[128,2048]{1,0:T(8,128)(2,1)}, u32[]{:S(2)}) copy-start(bf16[128,2048]{1,0:T(8,128)(2,1)} %param.20) | copy-start | bytes 1572868
  61.6 14.3 %copy-start.3 = (s32[128,8]{0,1:T(8,128)S(1)}, s32[128,8]{0,1:T(8,128)}, u32[]{:S(2)}) copy-start(s32[128,8]{0,1:T(8,128)} %param.22) | copy-start | bytes 12292
  74.3 4.5 %collective-permute-start.2 = (bf16[2048,512]{1,0:T(8,128)(2,1)}, bf16[2048,512]{1,0:T(8,128)(2,1)}, u32[]{:S(2)}, u32[]{:S(2)}) collective-permute-start(bf16[2048,512]{1,0:T(8,128)(2,1)} %collective-permute-done), channel_id=1, source_target_pairs={{0,1},{1,0},{2,3},{3,2},{4,5},{5,4},{6,7},{7,6},{8,9},{9,8},{10,11... | collective-permute-start | bytes 6291464 | tf_op jit(solution)/shard_map/ppermute | solution.py:15
  74.6 7.2 %collective-permute-start.1 = (bf16[2048,512]{1,0:T(8,128)(2,1)}, bf16[2048,512]{1,0:T(8,128)(2,1)}, u32[]{:S(2)}, u32[]{:S(2)}) collective-permute-start(bf16[2048,512]{1,0:T(8,128)(2,1)} %param.19), channel_id=1, source_target_pairs={{0,1},{1,0},{2,3},{3,2},{4,5},{5,4},{6,7},{7,6},{8,9},{9,8},{10,11... | collective-permute-start | bytes 6291464 | tf_op jit(solution)/shard_map/ppermute | solution.py:15
  86.2 3.3 %copy-start.4 = (f32[2048]{0:T(1024)S(1)}, f32[2048]{0:T(1024)}, u32[]{:S(2)}) copy-start(f32[2048]{0:T(1024)} %param.21) | copy-start | bytes 24580
  87.6 3.2 %copy-start.2 = (s32[16]{0:T(128)S(1)}, s32[16]{0:T(128)}, u32[]{:S(2)}) copy-start(s32[16]{0:T(128)} %param.24) | copy-start | bytes 196
  192.5 8.1 %copy-start.5 = (f32[128,8]{0,1:T(8,128)S(1)}, f32[128,8]{0,1:T(8,128)}, u32[]{:S(2)}) copy-start(f32[128,8]{0,1:T(8,128)} %param.23) | copy-start | bytes 12292
  192.5 100.2 %all-to-all-start = ((bf16[16,64,2048]{2,1,0:T(8,128)(2,1)}), bf16[16,64,2048]{2,1,0:T(8,128)(2,1)}, u32[]{:S(2)}, u32[]{:S(2)}) async-start(bf16[16,64,2048]{2,1,0:T(8,128)(2,1)} %bitcast.70), calls=%async_computation | async-start | bytes 8388608 | tf_op jit(solution)/shard_map/all_to_all | solution.py:222
Sparse Core Ops, SparseCore 0:
  10.7 48.3 all-gather.5
  90.9 77.5 all-gather.3

commit v15 on v14

--- a/solution.py
+++ b/solution.py
@@ -110,7 +110,26 @@
     block_rows = slice_rows * n_eg
     my_eg = lax.axis_index("eg")
     both = jnp.concatenate([keys, values], axis=2)
+    top_count = expert_ids.shape[1]
+    use_gather = n_ctx * n_eg <= 4 * top_count
+    if use_gather:
+        flat_ids = expert_ids.reshape(-1).astype(jnp.bfloat16)
+        id_count = flat_ids.shape[0]
+        lane = shard_blocks * 2 * kv_width
+        id_rows = -(-(-(-id_count // lane)) // 8) * 8
+        id_slab = jnp.pad(flat_ids, (0, id_rows * lane - id_count)).reshape(
+            shard_blocks, id_rows, 2 * kv_width
+        )
+        both = jnp.concatenate([both, id_slab], axis=1)
     gathered = lax.all_gather(both[None], ("ctx", "eg"), axis=0, tiled=True)
+    if use_gather:
+        all_ids = (
+            gathered[:, :, slice_rows:, :]
+            .reshape(n_ctx * n_eg, -1)[:, :id_count]
+            .reshape(-1, top_count)
+            .astype(jnp.int32)
+        )
+        gathered = gathered[:, :, :slice_rows, :]
     every_block = (
         gathered.reshape(n_ctx, n_eg, shard_blocks, slice_rows, 2 * kv_width)
         .transpose(0, 2, 1, 3, 4)
@@ -171,15 +190,9 @@
         .set(jnp.arange(pair_count, dtype=jnp.int32))
     )
     partner = fetch_panels()
-    if slot_count <= 4 * top_count:
+    if use_gather:
         my_slot = my_ctx * n_eg + my_eg
-        width = normed.shape[1]
-        id_cols = jnp.full((tok_dev, 128), -1.0, jnp.bfloat16)
-        id_cols = id_cols.at[:, :top_count].set(expert_ids.astype(jnp.bfloat16))
-        packed = jnp.concatenate([normed, id_cols], axis=1)
-        all_packed = lax.all_gather(packed, ("ctx", "eg"), axis=0, tiled=True)
-        all_normed = all_packed[:, :width]
-        all_ids = all_packed[:, width : width + top_count].astype(jnp.int32)
+        all_packed = lax.all_gather(normed, ("ctx", "eg"), axis=0, tiled=True)
         expert_count = expert_home.shape[0]
         my_expert = jnp.sum(
             jnp.where(expert_home == my_slot, jnp.arange(expert_count, dtype=jnp.int32), 0)
@@ -195,9 +208,8 @@
             chosen.astype(jnp.int32) * jnp.arange(tok_dev, dtype=jnp.int32)[None, None, :], axis=2
         )
         src_rows = local_row + jnp.arange(slot_count, dtype=jnp.int32)[:, None] * tok_dev
-        pad_rows = ((0, all_packed.shape[1] - width), (0, 0))
         hidden = partner[0].shape[1]
-        gate_up = jnp.pad(jnp.concatenate([partner[0], partner[1]], axis=1), pad_rows)
+        gate_up = jnp.concatenate([partner[0], partner[1]], axis=1)
         both_act = jnp.dot(all_packed, gate_up, preferred_element_type=jnp.float32)
         gate_act = both_act[:, :hidden]
         up_act = both_act[:, hidden:]

time: 304 us -> 303 us (level)
  local copies, waits for them, and re-layouts: 9.59 us -> 15 us
  waiting for transfers between devices: 204 us -> 200 us
    all_gather x1, waiting for transfers between devices: 77.1 us -> 70.5 us  [local(): all_packed = lax.all_gather(normed, ('ctx', 'eg'), axis=0, tiled=True)]
    slice x0 -> x4, local copies, waits for them, and re-layouts: none -> 4.19 us  [the longest x1 3.07 us: local(): gathered = gathered[:, :, :slice_rows, :]]
  transfers between devices with their start and end apart: 6 -> 6, of which waited for: 5 -> 5; matrix products, arithmetic and copies ran while one was open for 9% -> 10% of each run, Pallas kernels for 4% -> 4%
where the time goes in v15:
time: 303 us; the launch traced here: 302 us
  waiting for transfers between devices  200 us (66%)
  matrix products  29.1 us (10%)
  other arithmetic  24 us (8%)
  local copies, waits for them, and re-layouts  15 us (5%)
  between operations  14.3 us (5%)
  Pallas kernels  11.5 us (4%)
  starting transfers between devices  8.6 us (3%)
    all_to_all x1, waiting for transfers between devices, local(): lax.all_to_all(produced.reshape(slot_count, per_slot, -1), ('ctx', 'eg'),...  73.5 us
    all_gather x1, waiting for transfers between devices, local(): all_packed = lax.all_gather(normed, ('ctx', 'eg'), axis=0, tiled=True)  70.5 us
    all_gather x1, waiting for transfers between devices, local(): gathered = lax.all_gather(both[None], ('ctx', 'eg'), axis=0, tiled=True)  49.1 us
    dot_general x1, matrix products, local(): both_act = jnp.dot(all_packed, gate_up, preferred_element_type=jnp.float32)  11.9 us
    pallas_call x1, Pallas kernels, attend_rows(): pl.pallas_call(attention_kernel, grid=(kv_heads,), in_specs=[pl.BlockSpec...  11.5 us
    dot_general x1, matrix products, local(): jnp.dot(picked, partner[2], preferred_element_type=jnp.float32)  9.36 us
    all_to_all x1, starting transfers between devices, local(): lax.all_to_all(produced.reshape(slot_count, per_slot, -1), ('ctx', 'eg'),...  7.69 us
    ppermute x3, waiting for transfers between devices, swapped(): return lax.ppermute(value, axis, pairs)  6.59 us
  transfers between devices with their start and end apart: 6, of which 5 were waited for; matrix products, arithmetic and copies ran while one was open for 10% of the time, Pallas kernels for 4%

profile of v15, /device:TPU:11, one launch (start us, length us, event | category | flops | bytes accessed | tf_op | source)
XLA Modules:
  0.0 302.2 jit_solution(17820750807836154525)
XLA Ops:
  8.3 1.5 pad_maximum_fusion
  11.2 49.1 %all-gather.6.cloned.1.call-done = bf16[16,136,512]{2,1,0:T(8,128)(2,1)} async-done(((bf16[1,136,512]{2,1,0:T(8,128)(2,1)}), bf16[16,136,512]{2,1,0:T(8,128)(2,1)}) %all-gather.6.cloned.1.call-update) | async-done | bytes 2228240 | tf_op jit(solution)/shard_map/all_gather | solution.py:124
  60.3 3.1 %slice.72 = bf16[16,1,128,512]{3,2,0,1:T(8,128)(2,1)} slice(bf16[16,1,136,512]{3,2,0,1:T(8,128)(2,1)} %bitcast.79), slice={[0:16], [0:1], [0:128], [0:512]} | slice | bytes 4194304 | tf_op jit(solution)/shard_map/slice | solution.py:132
  63.4 2.2 gather_fusion
  65.8 1.3 fusion.41
  67.1 11.5 %shard_map.140 = bf16[128,2048]{1,0:T(8,128)(2,1)} custom-call(bf16[128,2048]{1,0:T(8,128)(2,1)} %query_ref.1, bf16[1536,256]{1,0:T(8,128)(2,1)} %bitcast.78, bf16[1536,256]{1,0:T(8,128)(2,1)} %bitcast.77), custom_call_target="tpu_custom_call" | custom-call | tf_op jit(solution)/shard_map/pallas_call | solution.py:45
  79.5 3.6 %collective-permute-done.1 = bf16[2048,512]{1,0:T(8,128)(2,1)} collective-permute-done((bf16[2048,512]{1,0:T(8,128)(2,1)}, bf16[2048,512]{1,0:T(8,128)(2,1)}, u32[]{:S(2)}, u32[]{:S(2)}) %collective-permute-start.1) | collective-permute-done | bytes 2097184 | tf_op jit(solution)/shard_map/ppermute | solution.py:15
  83.1 3.0 collective-permute-done.2
  86.1 4.4 %fusion = bf16[128,2048]{1,0:T(8,128)(2,1)S(1)} fusion(bf16[128,2048]{1,0:T(8,128)(2,1)} %shard_map.140, bf16[2048,512]{1,0:T(8,128)(2,1)} %collective-permute-done.2, bf16[2048,512]{1,0:T(8,128)(2,1)} %collective-permute-done, bf16[2048,512]{1,0:T(8,128)(2,1)} %collective-permute-done.1, bf16[2048,512]{1,0:T(8,128)(2,1)} %param.17), kind=kOutput, calls=%fused_computation.2 | convolution fusion | flops 1107296256 | bytes 9437184 | tf_op jit(solution)/shard_map/dot_general | solution.py:166
  90.5 1.4 gather_fusion.1
  91.9 1.3 copy.78
  93.7 1.1 multiply_convert_fusion
  95.5 0.9 slice.77
  99.0 70.5 %all-gather.4.cloned.1.call-done = bf16[2048,2048]{0,1:T(8,128)(2,1)} async-done(((bf16[128,2048]{0,1:T(8,128)(2,1)}), bf16[2048,2048]{0,1:T(8,128)(2,1)}) %all-gather.4.cloned.1.call-update) | async-done | bytes 8388624 | tf_op jit(solution)/shard_map/all_gather | solution.py:195
  169.6 11.9 %fusion.11 = f32[2048,768]{1,0:T(8,128)} fusion(bf16[2048,2048]{0,1:T(8,128)(2,1)} %all-gather.4.cloned.1.call-done, bf16[2048,384]{1,0:T(8,128)(2,1)} %bitcast.91, bf16[2048,384]{1,0:T(8,128)(2,1)} %bitcast.92), kind=kOutput, calls=%fused_computation.18 | convolution fusion | flops 6448742400 | bytes 17825792 | tf_op jit(solution)/shard_map/dot_general | solution.py:213
  181.5 9.4 %convolution_convert_fusion = bf16[1024,2048]{1,0:T(8,128)(2,1)} fusion(bf16[1,384,2048]{2,1,0:T(8,128)(2,1)S(1)} %copy-done, f32[2048,768]{1,0:T(8,128)} %fusion.11, s32[1024]{0:T(1024)S(1)} %add.143), kind=kOutput, calls=%fused_computation.15 | convolution fusion | flops 3230531584 | bytes 12062720 | tf_op jit(solution)/shard_map/dot_general | solution.py:224
  190.9 7.7 %all-to-all-start = ((bf16[16,64,2048]{2,1,0:T(8,128)(2,1)}), bf16[16,64,2048]{2,1,0:T(8,128)(2,1)}, u32[]{:S(2)}, u32[]{:S(2)}) async-start(bf16[16,64,2048]{2,1,0:T(8,128)(2,1)} %bitcast.76), calls=%async_computation | async-start | bytes 8388608 | tf_op jit(solution)/shard_map/all_to_all | solution.py:234
  199.5 4.4 %compare_select_fusion.1 = (s32[1024,1]{0,1:T(1,128)S(1)}, s32[1024,1]{0,1:T(1,128)S(1)}) fusion(s32[]{:T(128)} %bitcast.19, s32[]{:T(128)} %bitcast.20, s32[]{:T(128)} %bitcast.21, s32[]{:T(128)} %bitcast.22, s32[]{:T(128)} %bitcast.23, s32[]{:T(128)} %bitcast.25, s32[]{:T(128)} %bitcast.24, s32[1024,1]{0,1:T(1,128)S(1)} %reshape.271), kind=kLoop, calls=%fused_computation.60 | loop fusion | flops 15360 | bytes 12316 | tf_op jit(solution)/shard_map/jit(_take)/gather | solution.py:181
  204.0 5.6 %and_select_fusion = (s32[1024]{0:T(1024)S(1)}, s32[1024]{0:T(1024)S(1)}) fusion(s32[1024]{0:T(1024)S(1)} %reshape.268, pred[1024]{0:T(1024)(128)(4,1)S(1)} %get-tuple-element.35, pred[1024]{0:T(1024)(128)(4,1)S(1)} %get-tuple-element.34, pred[1024]{0:T(1024)(128)(4,1)S(1)} %get-tuple-element.33, pred[1024]{0:T(1024)(128)(4,1)S(1)} %get-tuple-element.32, ...), kind=kLoop, calls=%fused_computation.78 | loop fusion | flops 16384 | bytes 25636 | tf_op jit(solution)/shard_map/jit(_take)/select_n | solution.py:181
  209.8 4.5 %reduce-window.6 = s32[16,8,128]{2,1,0:T(8,128)S(1)} reduce-window(s32[16,8,128]{2,1,0:T(8,128)S(1)} %fusion.31, s32[]{:T(128)} %constant.91.clone.1), window={size=1x1x128 pad=0_0x0_0x127_0}, to_apply=%region_0.1 | reduce-window | flops 2080768 | bytes 131076 | tf_op jit(solution)/shard_map/reduce-window
  215.1 1.3 select_reduce_fusion
  216.5 1.0 copy.88
  217.6 73.5 %all-to-all-done = bf16[16,64,2048]{2,1,0:T(8,128)(2,1)} async-done(((bf16[16,64,2048]{2,1,0:T(8,128)(2,1)}), bf16[16,64,2048]{2,1,0:T(8,128)(2,1)}, u32[]{:S(2)}, u32[]{:S(2)}) %all-to-all-start) | async-done | bytes 4194336 | tf_op jit(solution)/shard_map/all_to_all | solution.py:234
  291.0 3.4 %fusion.24 = f32[256,2048]{1,0:T(8,128)S(1)} fusion(bf16[1024,2048]{1,0:T(8,128)(2,1)} %bitcast.35, bf16[128,1024]{1,0:T(8,128)(2,1)S(1)} %get-tuple-element.36, bf16[128,1024]{1,0:T(8,128)(2,1)S(1)} %get-tuple-element.37), kind=kOutput, calls=%fused_computation.33 | convolution fusion | flops 1074790400 | bytes 6815744 | tf_op jit(solution)/shard_map/dot_general | solution.py:249
  (74 shorter events, 10.3 us)
Async XLA Ops:
  7.2 174.3 %copy-start = (bf16[1,384,2048]{2,1,0:T(8,128)(2,1)S(1)}, bf16[1,384,2048]{2,1,0:T(8,128)(2,1)}, u32[]{:S(2)}) copy-start(bf16[1,384,2048]{2,1,0:T(8,128)(2,1)} %param.25) | copy-start | bytes 4718596
  7.2 53.1 %all-gather.6.cloned.1.call-start = ((), (), s32[]{:S(2)}) async-start(), calls=%async_computation.2 | async-start | bytes 2367488 | tf_op jit(solution)/shard_map/all_gather | solution.py:124
  9.8 159.7 %all-gather.4.cloned.1.call-start = ((), (), s32[]{:S(2)}) async-start(), calls=%async_computation.1 | async-start | bytes 8912896 | tf_op jit(solution)/shard_map/all_gather | solution.py:195
  9.9 68.7 %collective-permute-start = (bf16[2048,512]{1,0:T(8,128)(2,1)}, bf16[2048,512]{1,0:T(8,128)(2,1)}, u32[]{:S(2)}, u32[]{:S(2)}) collective-permute-start(bf16[2048,512]{1,0:T(8,128)(2,1)} %param.17), channel_id=1, source_target_pairs={{0,2},{1,3},{2,0},{3,1},{4,6},{5,7},{6,4},{7,5},{8,10},{9,11},{10,... | collective-permute-start | bytes 6291464 | tf_op jit(solution)/shard_map/ppermute | solution.py:15
  65.8 13.3 %copy-start.1 = (bf16[128,2048]{1,0:T(8,128)(2,1)S(1)}, bf16[128,2048]{1,0:T(8,128)(2,1)}, u32[]{:S(2)}) copy-start(bf16[128,2048]{1,0:T(8,128)(2,1)} %param.18) | copy-start | bytes 1572868
  78.6 4.5 %collective-permute-start.1 = (bf16[2048,512]{1,0:T(8,128)(2,1)}, bf16[2048,512]{1,0:T(8,128)(2,1)}, u32[]{:S(2)}, u32[]{:S(2)}) collective-permute-start(bf16[2048,512]{1,0:T(8,128)(2,1)} %param.17), channel_id=1, source_target_pairs={{0,1},{1,0},{2,3},{3,2},{4,5},{5,4},{6,7},{7,6},{8,9},{9,8},{10,11... | collective-permute-start | bytes 6291464 | tf_op jit(solution)/shard_map/ppermute | solution.py:15
  78.8 7.2 %collective-permute-start.2 = (bf16[2048,512]{1,0:T(8,128)(2,1)}, bf16[2048,512]{1,0:T(8,128)(2,1)}, u32[]{:S(2)}, u32[]{:S(2)}) collective-permute-start(bf16[2048,512]{1,0:T(8,128)(2,1)} %collective-permute-done), channel_id=1, source_target_pairs={{0,1},{1,0},{2,3},{3,2},{4,5},{5,4},{6,7},{7,6},{8,9},{9,8},{10,11... | collective-permute-start | bytes 6291464 | tf_op jit(solution)/shard_map/ppermute | solution.py:15
  90.4 3.3 %copy-start.4 = (f32[2048]{0:T(1024)S(1)}, f32[2048]{0:T(1024)}, u32[]{:S(2)}) copy-start(f32[2048]{0:T(1024)} %param.19) | copy-start | bytes 24580
  90.5 4.4 %copy-start.2 = (s32[16]{0:T(128)S(1)}, s32[16]{0:T(128)}, u32[]{:S(2)}) copy-start(s32[16]{0:T(128)} %param.22) | copy-start | bytes 196
  190.9 24.1 %copy-start.3 = (s32[128,8]{0,1:T(8,128)S(1)}, s32[128,8]{0,1:T(8,128)}, u32[]{:S(2)}) copy-start(s32[128,8]{0,1:T(8,128)} %param.20) | copy-start | bytes 12292
  190.9 24.2 %copy-start.5 = (f32[128,8]{0,1:T(8,128)S(1)}, f32[128,8]{0,1:T(8,128)}, u32[]{:S(2)}) copy-start(f32[128,8]{0,1:T(8,128)} %param.21) | copy-start | bytes 12292
  190.9 100.2 %all-to-all-start = ((bf16[16,64,2048]{2,1,0:T(8,128)(2,1)}), bf16[16,64,2048]{2,1,0:T(8,128)(2,1)}, u32[]{:S(2)}, u32[]{:S(2)}) async-start(bf16[16,64,2048]{2,1,0:T(8,128)(2,1)} %bitcast.76), calls=%async_computation | async-start | bytes 8388608 | tf_op jit(solution)/shard_map/all_to_all | solution.py:234
Sparse Core Ops, SparseCore 0:
  10.9 49.3 all-gather.5
  95.0 74.4 all-gather.3

commit v16 on v15

--- a/solution.py
+++ b/solution.py
@@ -141,27 +141,27 @@
         [my_block[None].astype(jnp.int32), jnp.take(selected, my_block, axis=0)]
     )
     context = jnp.take(every_block, chosen_blocks, axis=0)
-    context_keys = context[:, :, :kv_width]
-    context_values = context[:, :, kv_width:]
     span = (1 + pick_count) * block_rows
     kv_heads = kv_width // HD
-    attended = attend_rows(
-        queries,
-        context_keys.reshape(span, kv_heads, HD),
-        context_values.reshape(span, kv_heads, HD),
-    )
     tok_dev = residual.shape[0]
     pieces = {0: out_weight}
     for bit in reversed(range(n_eg.bit_length() - 1)):
         stride = 2**bit
         held = sorted(pieces)
         if len(held) > 1:
-            barrier_out = lax.optimization_barrier((tuple(pieces[m] for m in held), attended))
+            barrier_out = lax.optimization_barrier((tuple(pieces[m] for m in held), context))
             pieces = dict(zip(held, barrier_out[0]))
-            attended = barrier_out[1]
+            context = barrier_out[1]
         fetched = swapped(tuple(pieces[m] for m in held), "eg", bit)
         for m, piece in zip(held, fetched):
             pieces[m + stride] = piece
+    context_keys = context[:, :, :kv_width]
+    context_values = context[:, :, kv_width:]
+    attended = attend_rows(
+        queries,
+        context_keys.reshape(span, kv_heads, HD),
+        context_values.reshape(span, kv_heads, HD),
+    )
     weight_cols = jnp.concatenate([pieces[m] for m in range(n_eg)], axis=1)
     out_by_piece = jnp.dot(attended, weight_cols, preferred_element_type=jnp.float32).reshape(
         query_rows, n_eg, -1

time: 303 us -> 301 us (level)
  waiting for transfers between devices: 200 us -> 193 us
    ppermute x3, waiting for transfers between devices: 6.59 us -> 0.01 us  [swapped(): return lax.ppermute(value, axis, pairs)]
  transfers between devices with their start and end apart: 6 -> 6, of which waited for: 5 -> 3; matrix products, arithmetic and copies ran while one was open for 10% -> 12% of each run, Pallas kernels for 4% -> 4%
where the time goes in v16:
time: 301 us; the launch traced here: 300 us
  waiting for transfers between devices  193 us (64%)
  matrix products  29.1 us (10%)
  other arithmetic  25.4 us (8%)
  local copies, waits for them, and re-layouts  18 us (6%)
  between operations  14.3 us (5%)
  Pallas kernels  11.5 us (4%)
  starting transfers between devices  8.67 us (3%)
    all_to_all x1, waiting for transfers between devices, local(): lax.all_to_all(produced.reshape(slot_count, per_slot, -1), ('ctx', 'eg'),...  73.5 us
    all_gather x1, waiting for transfers between devices, local(): all_packed = lax.all_gather(normed, ('ctx', 'eg'), axis=0, tiled=True)  70.5 us
    all_gather x1, waiting for transfers between devices, local(): gathered = lax.all_gather(both[None], ('ctx', 'eg'), axis=0, tiled=True)  49.1 us
    dot_general x1, matrix products, local(): both_act = jnp.dot(all_packed, gate_up, preferred_element_type=jnp.float32)  11.9 us
    pallas_call x1, Pallas kernels, attend_rows(): pl.pallas_call(attention_kernel, grid=(kv_heads,), in_specs=[pl.BlockSpec...  11.5 us
    dot_general x1, matrix products, local(): jnp.dot(picked, partner[2], preferred_element_type=jnp.float32)  9.36 us
    all_to_all x1, starting transfers between devices, local(): lax.all_to_all(produced.reshape(slot_count, per_slot, -1), ('ctx', 'eg'),...  7.69 us
  transfers between devices with their start and end apart: 6, of which 3 were waited for; matrix products, arithmetic and copies ran while one was open for 12% of the time, Pallas kernels for 4%

profile of v16, /device:TPU:11, one launch (start us, length us, event | category | flops | bytes accessed | tf_op | source)
XLA Modules:
  0.0 300.1 jit_solution(14539015851226997184)
XLA Ops:
  8.3 1.5 pad_maximum_fusion
  11.2 49.1 %all-gather.6.cloned.1.call-done = bf16[16,136,512]{2,1,0:T(8,128)(2,1)} async-done(((bf16[1,136,512]{2,1,0:T(8,128)(2,1)}), bf16[16,136,512]{2,1,0:T(8,128)(2,1)}) %all-gather.6.cloned.1.call-update) | async-done | bytes 2228240 | tf_op jit(solution)/shard_map/all_gather | solution.py:124
  60.3 3.1 %slice.72 = bf16[16,1,128,512]{3,2,0,1:T(8,128)(2,1)} slice(bf16[16,1,136,512]{3,2,0,1:T(8,128)(2,1)} %bitcast.79), slice={[0:16], [0:1], [0:128], [0:512]} | slice | bytes 4194304 | tf_op jit(solution)/shard_map/slice | solution.py:132
  63.4 3.5 %gather_fusion = bf16[3,512,512]{2,1,0:T(8,128)(2,1)} fusion(bf16[4,512,512]{2,1,0:T(8,128)(2,1)} %bitcast.75, s32[1024]{0:T(1024)S(1)} %pad_clamp_fusion.1), kind=kCustom, calls=%fused_computation | custom fusion | bytes 3145740 | tf_op jit(solution)/shard_map/jit(_take)/gather | solution.py:143
  66.8 1.6 broadcast_select_fusion
  69.1 2.0 copy.87
  71.2 1.2 fusion.41
  72.4 11.5 %shard_map.140 = bf16[128,2048]{1,0:T(8,128)(2,1)} custom-call(bf16[128,2048]{1,0:T(8,128)(2,1)} %query_ref.1, bf16[1536,256]{1,0:T(8,128)(2,1)} %bitcast.78, bf16[1536,256]{1,0:T(8,128)(2,1)} %bitcast.77), custom_call_target="tpu_custom_call" | custom-call | tf_op jit(solution)/shard_map/pallas_call | solution.py:45
  83.9 4.4 %fusion = bf16[128,2048]{1,0:T(8,128)(2,1)S(1)} fusion(bf16[128,2048]{1,0:T(8,128)(2,1)} %shard_map.140, bf16[2048,512]{1,0:T(8,128)(2,1)} %collective-permute-done.2, bf16[2048,512]{1,0:T(8,128)(2,1)} %collective-permute-done, bf16[2048,512]{1,0:T(8,128)(2,1)} %collective-permute-done.1, bf16[2048,512]{1,0:T(8,128)(2,1)} %param.17), kind=kOutput, calls=%fused_computation.2 | convolution fusion | flops 1107296256 | bytes 9437184 | tf_op jit(solution)/shard_map/dot_general | solution.py:166
  88.4 1.4 gather_fusion.1
  89.7 1.3 copy.78
  91.6 1.1 multiply_convert_fusion
  93.4 0.9 slice.75
  96.9 70.5 %all-gather.4.cloned.1.call-done = bf16[2048,2048]{0,1:T(8,128)(2,1)} async-done(((bf16[128,2048]{0,1:T(8,128)(2,1)}), bf16[2048,2048]{0,1:T(8,128)(2,1)}) %all-gather.4.cloned.1.call-update) | async-done | bytes 8388624 | tf_op jit(solution)/shard_map/all_gather | solution.py:195
  167.4 11.9 %fusion.11 = f32[2048,768]{1,0:T(8,128)} fusion(bf16[2048,2048]{0,1:T(8,128)(2,1)} %all-gather.4.cloned.1.call-done, bf16[2048,384]{1,0:T(8,128)(2,1)} %bitcast.91, bf16[2048,384]{1,0:T(8,128)(2,1)} %bitcast.92), kind=kOutput, calls=%fused_computation.18 | convolution fusion | flops 6448742400 | bytes 17825792 | tf_op jit(solution)/shard_map/dot_general | solution.py:213
  179.4 9.4 %convolution_convert_fusion = bf16[1024,2048]{1,0:T(8,128)(2,1)} fusion(bf16[1,384,2048]{2,1,0:T(8,128)(2,1)S(1)} %copy-done, f32[2048,768]{1,0:T(8,128)} %fusion.11, s32[1024]{0:T(1024)S(1)} %add.143), kind=kOutput, calls=%fused_computation.15 | convolution fusion | flops 3230531584 | bytes 12062720 | tf_op jit(solution)/shard_map/dot_general | solution.py:224
  188.7 7.7 %all-to-all-start = ((bf16[16,64,2048]{2,1,0:T(8,128)(2,1)}), bf16[16,64,2048]{2,1,0:T(8,128)(2,1)}, u32[]{:S(2)}, u32[]{:S(2)}) async-start(bf16[16,64,2048]{2,1,0:T(8,128)(2,1)} %bitcast.76), calls=%async_computation | async-start | bytes 8388608 | tf_op jit(solution)/shard_map/all_to_all | solution.py:234
  197.3 4.4 %compare_select_fusion.1 = (s32[1024,1]{0,1:T(1,128)S(1)}, s32[1024,1]{0,1:T(1,128)S(1)}) fusion(s32[]{:T(128)} %bitcast.19, s32[]{:T(128)} %bitcast.20, s32[]{:T(128)} %bitcast.21, s32[]{:T(128)} %bitcast.22, s32[]{:T(128)} %bitcast.23, s32[]{:T(128)} %bitcast.25, s32[]{:T(128)} %bitcast.24, s32[1024,1]{0,1:T(1,128)S(1)} %reshape.271), kind=kLoop, calls=%fused_computation.60 | loop fusion | flops 15360 | bytes 12316 | tf_op jit(solution)/shard_map/jit(_take)/gather | solution.py:181
  201.9 5.6 %and_select_fusion = (s32[1024]{0:T(1024)S(1)}, s32[1024]{0:T(1024)S(1)}) fusion(s32[1024]{0:T(1024)S(1)} %reshape.268, pred[1024]{0:T(1024)(128)(4,1)S(1)} %get-tuple-element.35, pred[1024]{0:T(1024)(128)(4,1)S(1)} %get-tuple-element.34, pred[1024]{0:T(1024)(128)(4,1)S(1)} %get-tuple-element.33, pred[1024]{0:T(1024)(128)(4,1)S(1)} %get-tuple-element.32, ...), kind=kLoop, calls=%fused_computation.78 | loop fusion | flops 16384 | bytes 25636 | tf_op jit(solution)/shard_map/jit(_take)/select_n | solution.py:181
  207.7 4.5 %reduce-window.6 = s32[16,8,128]{2,1,0:T(8,128)S(1)} reduce-window(s32[16,8,128]{2,1,0:T(8,128)S(1)} %fusion.31, s32[]{:T(128)} %constant.91.clone.1), window={size=1x1x128 pad=0_0x0_0x127_0}, to_apply=%region_0.1 | reduce-window | flops 2080768 | bytes 131076 | tf_op jit(solution)/shard_map/reduce-window
  213.0 1.3 select_reduce_fusion
  214.4 1.0 copy.88
  215.4 73.5 %all-to-all-done = bf16[16,64,2048]{2,1,0:T(8,128)(2,1)} async-done(((bf16[16,64,2048]{2,1,0:T(8,128)(2,1)}), bf16[16,64,2048]{2,1,0:T(8,128)(2,1)}, u32[]{:S(2)}, u32[]{:S(2)}) %all-to-all-start) | async-done | bytes 4194336 | tf_op jit(solution)/shard_map/all_to_all | solution.py:234
  288.9 3.4 %fusion.24 = f32[256,2048]{1,0:T(8,128)S(1)} fusion(bf16[1024,2048]{1,0:T(8,128)(2,1)} %bitcast.35, bf16[128,1024]{1,0:T(8,128)(2,1)S(1)} %get-tuple-element.36, bf16[128,1024]{1,0:T(8,128)(2,1)S(1)} %get-tuple-element.37), kind=kOutput, calls=%fused_computation.33 | convolution fusion | flops 1074790400 | bytes 6815744 | tf_op jit(solution)/shard_map/dot_general | solution.py:249
  (74 shorter events, 9.9 us)
Async XLA Ops:
  7.2 172.2 %copy-start = (bf16[1,384,2048]{2,1,0:T(8,128)(2,1)S(1)}, bf16[1,384,2048]{2,1,0:T(8,128)(2,1)}, u32[]{:S(2)}) copy-start(bf16[1,384,2048]{2,1,0:T(8,128)(2,1)} %param.25) | copy-start | bytes 4718596
  7.2 53.1 %all-gather.6.cloned.1.call-start = ((), (), s32[]{:S(2)}) async-start(), calls=%async_computation.2 | async-start | bytes 2367488 | tf_op jit(solution)/shard_map/all_gather | solution.py:124
  9.8 157.6 %all-gather.4.cloned.1.call-start = ((), (), s32[]{:S(2)}) async-start(), calls=%async_computation.1 | async-start | bytes 8912896 | tf_op jit(solution)/shard_map/all_gather | solution.py:195
  9.9 58.6 %collective-permute-start = (bf16[2048,512]{1,0:T(8,128)(2,1)}, bf16[2048,512]{1,0:T(8,128)(2,1)}, u32[]{:S(2)}, u32[]{:S(2)}) collective-permute-start(bf16[2048,512]{1,0:T(8,128)(2,1)} %param.17), channel_id=1, source_target_pairs={{0,2},{1,3},{2,0},{3,1},{4,6},{5,7},{6,4},{7,5},{8,10},{9,11},{10,... | collective-permute-start | bytes 6291464 | tf_op jit(solution)/shard_map/ppermute | solution.py:15
  68.5 15.4 %collective-permute-start.1 = (bf16[2048,512]{1,0:T(8,128)(2,1)}, bf16[2048,512]{1,0:T(8,128)(2,1)}, u32[]{:S(2)}, u32[]{:S(2)}) collective-permute-start(bf16[2048,512]{1,0:T(8,128)(2,1)} %param.17), channel_id=1, source_target_pairs={{0,1},{1,0},{2,3},{3,2},{4,5},{5,4},{6,7},{7,6},{8,9},{9,8},{10,11... | collective-permute-start | bytes 6291464 | tf_op jit(solution)/shard_map/ppermute | solution.py:15
  68.8 15.1 %collective-permute-start.2 = (bf16[2048,512]{1,0:T(8,128)(2,1)}, bf16[2048,512]{1,0:T(8,128)(2,1)}, u32[]{:S(2)}, u32[]{:S(2)}) collective-permute-start(bf16[2048,512]{1,0:T(8,128)(2,1)} %collective-permute-done), channel_id=1, source_target_pairs={{0,1},{1,0},{2,3},{3,2},{4,5},{5,4},{6,7},{7,6},{8,9},{9,8},{10,11... | collective-permute-start | bytes 6291464 | tf_op jit(solution)/shard_map/ppermute | solution.py:15
  88.3 2.8 copy-start.1
  88.3 3.3 %copy-start.4 = (f32[2048]{0:T(1024)S(1)}, f32[2048]{0:T(1024)}, u32[]{:S(2)}) copy-start(f32[2048]{0:T(1024)} %param.19) | copy-start | bytes 24580
  88.4 4.4 %copy-start.2 = (s32[16]{0:T(128)S(1)}, s32[16]{0:T(128)}, u32[]{:S(2)}) copy-start(s32[16]{0:T(128)} %param.22) | copy-start | bytes 196
  188.7 24.1 %copy-start.3 = (s32[128,8]{0,1:T(8,128)S(1)}, s32[128,8]{0,1:T(8,128)}, u32[]{:S(2)}) copy-start(s32[128,8]{0,1:T(8,128)} %param.20) | copy-start | bytes 12292
  188.7 24.2 %copy-start.5 = (f32[128,8]{0,1:T(8,128)S(1)}, f32[128,8]{0,1:T(8,128)}, u32[]{:S(2)}) copy-start(f32[128,8]{0,1:T(8,128)} %param.21) | copy-start | bytes 12292
  188.7 100.2 %all-to-all-start = ((bf16[16,64,2048]{2,1,0:T(8,128)(2,1)}), bf16[16,64,2048]{2,1,0:T(8,128)(2,1)}, u32[]{:S(2)}, u32[]{:S(2)}) async-start(bf16[16,64,2048]{2,1,0:T(8,128)(2,1)} %bitcast.76), calls=%async_computation | async-start | bytes 8388608 | tf_op jit(solution)/shard_map/all_to_all | solution.py:234
Sparse Core Ops, SparseCore 0:
  10.9 49.3 all-gather.5
  92.9 74.4 all-gather.3

commit v17 on v16

--- a/solution.py
+++ b/solution.py
@@ -38,9 +38,9 @@
         out_ref[:, head * HD : (head + 1) * HD] = blended.astype(out_ref.dtype)
 
 
-def attend_rows(queries_flat, key_rows, value_rows, interpret=False):
+def attend_rows(queries_flat, context, kv_heads, interpret=False):
     row_count = queries_flat.shape[0]
-    span, kv_heads, _ = key_rows.shape
+    span = context.shape[0]
     group_width = queries_flat.shape[1] // kv_heads
     return pl.pallas_call(
         attention_kernel,
@@ -48,12 +48,12 @@
         in_specs=[
             pl.BlockSpec((row_count, group_width), lambda k: (0, k)),
             pl.BlockSpec((span, HD), lambda k: (0, k)),
-            pl.BlockSpec((span, HD), lambda k: (0, k)),
+            pl.BlockSpec((span, HD), lambda k: (0, kv_heads + k)),
         ],
         out_specs=pl.BlockSpec((row_count, group_width), lambda k: (0, k)),
         out_shape=jax.ShapeDtypeStruct(queries_flat.shape, jnp.bfloat16),
         interpret=interpret,
-    )(queries_flat, key_rows.reshape(span, -1), value_rows.reshape(span, -1))
+    )(queries_flat, context, context)
 
 
 def expert_apply(rows_in, gate_full, up_full, down_full):
@@ -129,18 +129,18 @@
             .reshape(-1, top_count)
             .astype(jnp.int32)
         )
-        gathered = gathered[:, :, :slice_rows, :]
-    every_block = (
-        gathered.reshape(n_ctx, n_eg, shard_blocks, slice_rows, 2 * kv_width)
-        .transpose(0, 2, 1, 3, 4)
-        .reshape(n_ctx * shard_blocks, block_rows, 2 * kv_width)
-    )
+    held_rows = gathered.shape[2]
+    by_shard = gathered.reshape(n_ctx, n_eg, shard_blocks, held_rows, 2 * kv_width)
     query_rows = queries.shape[0]
     my_block = (my_ctx * n_eg + my_eg) * query_rows // block_rows
     chosen_blocks = jnp.concatenate(
         [my_block[None].astype(jnp.int32), jnp.take(selected, my_block, axis=0)]
     )
-    context = jnp.take(every_block, chosen_blocks, axis=0)
+    picked_shards = jnp.take(by_shard, chosen_blocks // shard_blocks, axis=0)
+    picked_shards = jnp.take_along_axis(
+        picked_shards, (chosen_blocks % shard_blocks)[:, None, None, None, None], axis=2
+    )
+    context = picked_shards[:, :, 0, :slice_rows, :].reshape(-1, 2 * kv_width)
     span = (1 + pick_count) * block_rows
     kv_heads = kv_width // HD
     tok_dev = residual.shape[0]
@@ -155,13 +155,7 @@
         fetched = swapped(tuple(pieces[m] for m in held), "eg", bit)
         for m, piece in zip(held, fetched):
             pieces[m + stride] = piece
-    context_keys = context[:, :, :kv_width]
-    context_values = context[:, :, kv_width:]
-    attended = attend_rows(
-        queries,
-        context_keys.reshape(span, kv_heads, HD),
-        context_values.reshape(span, kv_heads, HD),
-    )
+    attended = attend_rows(queries, context, kv_heads)
     weight_cols = jnp.concatenate([pieces[m] for m in range(n_eg)], axis=1)
     out_by_piece = jnp.dot(attended, weight_cols, preferred_element_type=jnp.float32).reshape(
         query_rows, n_eg, -1

time: 301 us -> 299 us (level)
  transfers between devices with their start and end apart: 6 -> 6, of which waited for: 3 -> 3; matrix products, arithmetic and copies ran while one was open for 12% -> 11% of each run, Pallas kernels for 4% -> 4%
where the time goes in v17:
time: 299 us
  waiting for transfers between devices  193 us (65%)
  matrix products  29.1 us (10%)
  other arithmetic  25.4 us (8%)
  local copies, waits for them, and re-layouts  16.6 us (6%)
  between operations  14.3 us (5%)
  Pallas kernels  11.5 us (4%)
  starting transfers between devices  8.59 us (3%)
    all_to_all x1, waiting for transfers between devices, local(): lax.all_to_all(produced.reshape(slot_count, per_slot, -1), ('ctx', 'eg'),...  73.5 us
    all_gather x1, waiting for transfers between devices, local(): all_packed = lax.all_gather(normed, ('ctx', 'eg'), axis=0, tiled=True)  70.5 us
    all_gather x1, waiting for transfers between devices, local(): gathered = lax.all_gather(both[None], ('ctx', 'eg'), axis=0, tiled=True)  49.1 us
    dot_general x1, matrix products, local(): both_act = jnp.dot(all_packed, gate_up, preferred_element_type=jnp.float32)  11.9 us
    pallas_call x1, Pallas kernels, attend_rows(): pl.pallas_call(attention_kernel, grid=(kv_heads,), in_specs=[pl.BlockSpec...  11.5 us
    dot_general x1, matrix products, local(): jnp.dot(picked, partner[2], preferred_element_type=jnp.float32)  9.36 us
    all_to_all x1, starting transfers between devices, local(): lax.all_to_all(produced.reshape(slot_count, per_slot, -1), ('ctx', 'eg'),...  7.68 us
  transfers between devices with their start and end apart: 6, of which 3 were waited for; matrix products, arithmetic and copies ran while one was open for 11% of the time, Pallas kernels for 4%

profile of v17, /device:TPU:11, one launch (start us, length us, event | category | flops | bytes accessed | tf_op | source)
XLA Modules:
  0.0 298.6 jit_solution(4597286416019639724)
XLA Ops:
  8.3 1.5 pad_maximum_fusion
  11.2 49.1 %all-gather.6.cloned.1.call-done = bf16[16,136,512]{2,1,0:T(8,128)(2,1)} async-done(((bf16[1,136,512]{2,1,0:T(8,128)(2,1)}), bf16[16,136,512]{2,1,0:T(8,128)(2,1)}) %all-gather.6.cloned.1.call-update) | async-done | bytes 2228240 | tf_op jit(solution)/shard_map/all_gather | solution.py:124
  60.3 3.5 %gather_fusion = bf16[3,4,136,512]{3,2,1,0:T(8,128)(2,1)} fusion(bf16[4,4,136,512]{3,2,1,0:T(8,128)(2,1)} %bitcast.83, s32[1024]{0:T(1024)S(1)} %pad_clamp_fusion.1), kind=kCustom, calls=%fused_computation | custom fusion | bytes 3342348 | tf_op jit(solution)/shard_map/jit(_take)/gather | solution.py:139
  63.8 1.7 bitcast_select_fusion
  65.5 1.9 gather_fusion.2
  67.4 2.7 slice.66
  71.0 11.5 %shard_map.140 = bf16[128,2048]{1,0:T(8,128)(2,1)} custom-call(bf16[128,2048]{1,0:T(8,128)(2,1)} %query_ref.1, bf16[1536,512]{1,0:T(8,128)(2,1)} %bitcast.77, bf16[1536,512]{1,0:T(8,128)(2,1)} %bitcast.78), custom_call_target="tpu_custom_call" | custom-call | tf_op jit(solution)/shard_map/pallas_call | solution.py:45
  82.5 4.4 %fusion = bf16[128,2048]{1,0:T(8,128)(2,1)S(1)} fusion(bf16[128,2048]{1,0:T(8,128)(2,1)} %shard_map.140, bf16[2048,512]{1,0:T(8,128)(2,1)} %collective-permute-done.2, bf16[2048,512]{1,0:T(8,128)(2,1)} %collective-permute-done, bf16[2048,512]{1,0:T(8,128)(2,1)} %collective-permute-done.1, bf16[2048,512]{1,0:T(8,128)(2,1)} %param.17), kind=kOutput, calls=%fused_computation.3 | convolution fusion | flops 1107296256 | bytes 9437184 | tf_op jit(solution)/shard_map/dot_general | solution.py:160
  86.9 1.4 gather_fusion.1
  88.3 1.3 copy.78
  90.2 1.1 multiply_convert_fusion
  92.0 0.9 slice.69
  95.4 70.5 %all-gather.4.cloned.1.call-done = bf16[2048,2048]{0,1:T(8,128)(2,1)} async-done(((bf16[128,2048]{0,1:T(8,128)(2,1)}), bf16[2048,2048]{0,1:T(8,128)(2,1)}) %all-gather.4.cloned.1.call-update) | async-done | bytes 8388624 | tf_op jit(solution)/shard_map/all_gather | solution.py:189
  166.0 11.9 %fusion.11 = f32[2048,768]{1,0:T(8,128)} fusion(bf16[2048,2048]{0,1:T(8,128)(2,1)} %all-gather.4.cloned.1.call-done, bf16[2048,384]{1,0:T(8,128)(2,1)} %bitcast.93, bf16[2048,384]{1,0:T(8,128)(2,1)} %bitcast.94), kind=kOutput, calls=%fused_computation.19 | convolution fusion | flops 6448742400 | bytes 17825792 | tf_op jit(solution)/shard_map/dot_general | solution.py:207
  177.9 9.4 %convolution_convert_fusion = bf16[1024,2048]{1,0:T(8,128)(2,1)} fusion(bf16[1,384,2048]{2,1,0:T(8,128)(2,1)S(1)} %copy-done, f32[2048,768]{1,0:T(8,128)} %fusion.11, s32[1024]{0:T(1024)S(1)} %add.176), kind=kOutput, calls=%fused_computation.16 | convolution fusion | flops 3230531584 | bytes 12062720 | tf_op jit(solution)/shard_map/dot_general | solution.py:218
  187.3 7.7 %all-to-all-start = ((bf16[16,64,2048]{2,1,0:T(8,128)(2,1)}), bf16[16,64,2048]{2,1,0:T(8,128)(2,1)}, u32[]{:S(2)}, u32[]{:S(2)}) async-start(bf16[16,64,2048]{2,1,0:T(8,128)(2,1)} %bitcast.80), calls=%async_computation | async-start | bytes 8388608 | tf_op jit(solution)/shard_map/all_to_all | solution.py:228
  195.9 4.4 %compare_select_fusion.1 = (s32[1024,1]{0,1:T(1,128)S(1)}, s32[1024,1]{0,1:T(1,128)S(1)}) fusion(s32[]{:T(128)} %bitcast.19, s32[]{:T(128)} %bitcast.20, s32[]{:T(128)} %bitcast.21, s32[]{:T(128)} %bitcast.22, s32[]{:T(128)} %bitcast.23, s32[]{:T(128)} %bitcast.25, s32[]{:T(128)} %bitcast.24, s32[1024,1]{0,1:T(1,128)S(1)} %reshape.336), kind=kLoop, calls=%fused_computation.61 | loop fusion | flops 15360 | bytes 12316 | tf_op jit(solution)/shard_map/jit(_take)/gather | solution.py:175
  200.4 5.6 %and_select_fusion = (s32[1024]{0:T(1024)S(1)}, s32[1024]{0:T(1024)S(1)}) fusion(s32[1024]{0:T(1024)S(1)} %reshape.332, pred[1024]{0:T(1024)(128)(4,1)S(1)} %get-tuple-element.35, pred[1024]{0:T(1024)(128)(4,1)S(1)} %get-tuple-element.34, pred[1024]{0:T(1024)(128)(4,1)S(1)} %get-tuple-element.33, pred[1024]{0:T(1024)(128)(4,1)S(1)} %get-tuple-element.32, ...), kind=kLoop, calls=%fused_computation.79 | loop fusion | flops 16384 | bytes 25636 | tf_op jit(solution)/shard_map/jit(_take)/select_n | solution.py:175
  206.2 4.5 %reduce-window.6 = s32[16,8,128]{2,1,0:T(8,128)S(1)} reduce-window(s32[16,8,128]{2,1,0:T(8,128)S(1)} %fusion.31, s32[]{:T(128)} %constant.133.clone.1), window={size=1x1x128 pad=0_0x0_0x127_0}, to_apply=%region_0.1 | reduce-window | flops 2080768 | bytes 131076 | tf_op jit(solution)/shard_map/reduce-window
  211.6 1.3 select_reduce_fusion
  213.0 1.0 copy.88
  214.0 73.5 %all-to-all-done = bf16[16,64,2048]{2,1,0:T(8,128)(2,1)} async-done(((bf16[16,64,2048]{2,1,0:T(8,128)(2,1)}), bf16[16,64,2048]{2,1,0:T(8,128)(2,1)}, u32[]{:S(2)}, u32[]{:S(2)}) %all-to-all-start) | async-done | bytes 4194336 | tf_op jit(solution)/shard_map/all_to_all | solution.py:228
  287.4 3.4 %fusion.24 = f32[256,2048]{1,0:T(8,128)S(1)} fusion(bf16[1024,2048]{1,0:T(8,128)(2,1)} %bitcast.36, bf16[128,1024]{1,0:T(8,128)(2,1)S(1)} %get-tuple-element.36, bf16[128,1024]{1,0:T(8,128)(2,1)S(1)} %get-tuple-element.37), kind=kOutput, calls=%fused_computation.34 | convolution fusion | flops 1074790400 | bytes 6815744 | tf_op jit(solution)/shard_map/dot_general | solution.py:243
  290.9 0.9 fusion.20
  (75 shorter events, 9.1 us)
Async XLA Ops:
  7.2 170.7 %copy-start = (bf16[1,384,2048]{2,1,0:T(8,128)(2,1)S(1)}, bf16[1,384,2048]{2,1,0:T(8,128)(2,1)}, u32[]{:S(2)}) copy-start(bf16[1,384,2048]{2,1,0:T(8,128)(2,1)} %param.25) | copy-start | bytes 4718596
  7.2 53.1 %all-gather.6.cloned.1.call-start = ((), (), s32[]{:S(2)}) async-start(), calls=%async_computation.2 | async-start | bytes 2367488 | tf_op jit(solution)/shard_map/all_gather | solution.py:124
  9.8 156.1 %all-gather.4.cloned.1.call-start = ((), (), s32[]{:S(2)}) async-start(), calls=%async_computation.1 | async-start | bytes 8912896 | tf_op jit(solution)/shard_map/all_gather | solution.py:189
  9.9 60.2 %collective-permute-start = (bf16[2048,512]{1,0:T(8,128)(2,1)}, bf16[2048,512]{1,0:T(8,128)(2,1)}, u32[]{:S(2)}, u32[]{:S(2)}) collective-permute-start(bf16[2048,512]{1,0:T(8,128)(2,1)} %param.17), channel_id=1, source_target_pairs={{0,2},{1,3},{2,0},{3,1},{4,6},{5,7},{6,4},{7,5},{8,10},{9,11},{10,... | collective-permute-start | bytes 6291464 | tf_op jit(solution)/shard_map/ppermute | solution.py:15
  67.4 3.3 %copy-start.1 = (bf16[128,2048]{1,0:T(8,128)(2,1)S(1)}, bf16[128,2048]{1,0:T(8,128)(2,1)}, u32[]{:S(2)}) copy-start(bf16[128,2048]{1,0:T(8,128)(2,1)} %param.18) | copy-start | bytes 1572868
  70.1 12.4 %collective-permute-start.1 = (bf16[2048,512]{1,0:T(8,128)(2,1)}, bf16[2048,512]{1,0:T(8,128)(2,1)}, u32[]{:S(2)}, u32[]{:S(2)}) collective-permute-start(bf16[2048,512]{1,0:T(8,128)(2,1)} %param.17), channel_id=1, source_target_pairs={{0,1},{1,0},{2,3},{3,2},{4,5},{5,4},{6,7},{7,6},{8,9},{9,8},{10,11... | collective-permute-start | bytes 6291464 | tf_op jit(solution)/shard_map/ppermute | solution.py:15
  70.3 12.1 %collective-permute-start.2 = (bf16[2048,512]{1,0:T(8,128)(2,1)}, bf16[2048,512]{1,0:T(8,128)(2,1)}, u32[]{:S(2)}, u32[]{:S(2)}) collective-permute-start(bf16[2048,512]{1,0:T(8,128)(2,1)} %collective-permute-done), channel_id=1, source_target_pairs={{0,1},{1,0},{2,3},{3,2},{4,5},{5,4},{6,7},{7,6},{8,9},{9,8},{10,11... | collective-permute-start | bytes 6291464 | tf_op jit(solution)/shard_map/ppermute | solution.py:15
  86.9 3.3 %copy-start.4 = (f32[2048]{0:T(1024)S(1)}, f32[2048]{0:T(1024)}, u32[]{:S(2)}) copy-start(f32[2048]{0:T(1024)} %param.19) | copy-start | bytes 24580
  86.9 4.4 %copy-start.2 = (s32[16]{0:T(128)S(1)}, s32[16]{0:T(128)}, u32[]{:S(2)}) copy-start(s32[16]{0:T(128)} %param.22) | copy-start | bytes 196
  187.3 24.0 %copy-start.3 = (s32[128,8]{0,1:T(8,128)S(1)}, s32[128,8]{0,1:T(8,128)}, u32[]{:S(2)}) copy-start(s32[128,8]{0,1:T(8,128)} %param.20) | copy-start | bytes 12292
  187.3 24.2 %copy-start.5 = (f32[128,8]{0,1:T(8,128)S(1)}, f32[128,8]{0,1:T(8,128)}, u32[]{:S(2)}) copy-start(f32[128,8]{0,1:T(8,128)} %param.21) | copy-start | bytes 12292
  187.3 100.2 %all-to-all-start = ((bf16[16,64,2048]{2,1,0:T(8,128)(2,1)}), bf16[16,64,2048]{2,1,0:T(8,128)(2,1)}, u32[]{:S(2)}, u32[]{:S(2)}) async-start(bf16[16,64,2048]{2,1,0:T(8,128)(2,1)} %bitcast.80), calls=%async_computation | async-start | bytes 8388608 | tf_op jit(solution)/shard_map/all_to_all | solution.py:228
Sparse Core Ops, SparseCore 0:
  10.9 49.3 all-gather.5
  91.4 74.4 all-gather.3

commit v18 on v17

--- a/solution.py
+++ b/solution.py
@@ -130,17 +130,18 @@
             .astype(jnp.int32)
         )
     held_rows = gathered.shape[2]
-    by_shard = gathered.reshape(n_ctx, n_eg, shard_blocks, held_rows, 2 * kv_width)
+    by_slice = gathered.reshape(n_ctx * n_eg * shard_blocks, held_rows, 2 * kv_width)
     query_rows = queries.shape[0]
     my_block = (my_ctx * n_eg + my_eg) * query_rows // block_rows
     chosen_blocks = jnp.concatenate(
         [my_block[None].astype(jnp.int32), jnp.take(selected, my_block, axis=0)]
     )
-    picked_shards = jnp.take(by_shard, chosen_blocks // shard_blocks, axis=0)
-    picked_shards = jnp.take_along_axis(
-        picked_shards, (chosen_blocks % shard_blocks)[:, None, None, None, None], axis=2
-    )
-    context = picked_shards[:, :, 0, :slice_rows, :].reshape(-1, 2 * kv_width)
+    slice_index = (
+        (chosen_blocks // shard_blocks)[:, None] * n_eg + jnp.arange(n_eg, dtype=jnp.int32)[None, :]
+    ) * shard_blocks + (chosen_blocks % shard_blocks)[:, None]
+    context = jnp.take(by_slice[:, :slice_rows], slice_index.reshape(-1), axis=0).reshape(
+        -1, 2 * kv_width
+    )
     span = (1 + pick_count) * block_rows
     kv_heads = kv_width // HD
     tok_dev = residual.shape[0]

time: 299 us -> 298 us (level)
    gather x3 -> x1, local copies, waits for them, and re-layouts: 5.4 us -> 2.24 us  [local(): jnp.take(by_slice[:, :slice_rows], slice_index.reshape(-1), axis=0)]
where the time goes in v18:
time: 298 us; the launch traced here: 297 us
  waiting for transfers between devices  193 us (65%)
  matrix products  29.1 us (10%)
  other arithmetic  25.2 us (8%)
  local copies, waits for them, and re-layouts  15.1 us (5%)
  between operations  14.3 us (5%)
  Pallas kernels  11.5 us (4%)
  starting transfers between devices  8.6 us (3%)
    all_to_all x1, waiting for transfers between devices, local(): lax.all_to_all(produced.reshape(slot_count, per_slot, -1), ('ctx', 'eg'),...  73.5 us
    all_gather x1, waiting for transfers between devices, local(): all_packed = lax.all_gather(normed, ('ctx', 'eg'), axis=0, tiled=True)  70.9 us
    all_gather x1, waiting for transfers between devices, local(): gathered = lax.all_gather(both[None], ('ctx', 'eg'), axis=0, tiled=True)  48.8 us
    dot_general x1, matrix products, local(): both_act = jnp.dot(all_packed, gate_up, preferred_element_type=jnp.float32)  11.9 us
    pallas_call x1, Pallas kernels, attend_rows(): pl.pallas_call(attention_kernel, grid=(kv_heads,), in_specs=[pl.BlockSpec...  11.5 us
    dot_general x1, matrix products, local(): jnp.dot(picked, partner[2], preferred_element_type=jnp.float32)  9.36 us
    all_to_all x1, starting transfers between devices, local(): lax.all_to_all(produced.reshape(slot_count, per_slot, -1), ('ctx', 'eg'),...  7.69 us
  transfers between devices with their start and end apart: 6, of which 3 were waited for; matrix products, arithmetic and copies ran while one was open for 11% of the time, Pallas kernels for 4%

profile of v18, /device:TPU:11, one launch (start us, length us, event | category | flops | bytes accessed | tf_op | source)
XLA Modules:
  0.0 297.0 jit_solution(8420758789985749092)
XLA Ops:
  8.3 1.5 pad_maximum_fusion
  11.5 48.8 %all-gather.6.cloned.1.call-done = bf16[16,136,512]{2,1,0:T(8,128)(2,1)} async-done(((bf16[1,136,512]{2,1,0:T(8,128)(2,1)}), bf16[16,136,512]{2,1,0:T(8,128)(2,1)}) %all-gather.6.cloned.1.call-update) | async-done | bytes 2228240 | tf_op jit(solution)/shard_map/all_gather | solution.py:124
  60.3 3.1 %slice.64 = bf16[16,128,512]{2,1,0:T(8,128)(2,1)} slice(bf16[16,136,512]{2,1,0:T(8,128)(2,1)} %all-gather.6.cloned.1.call-done), slice={[0:16], [0:128], [0:512]} | slice | bytes 4194304 | tf_op jit(solution)/shard_map/slice | solution.py:142
  63.4 2.2 gather_fusion
  65.6 1.5 bitcast_select_fusion.key_ref.value_ref
  67.7 1.3 copy.87
  69.0 11.5 %shard_map.140 = bf16[128,2048]{1,0:T(8,128)(2,1)} custom-call(bf16[128,2048]{1,0:T(8,128)(2,1)} %query_ref.1, bf16[1536,512]{1,0:T(8,128)(2,1)} %bitcast_select_fusion.key_ref.value_ref, bf16[1536,512]{1,0:T(8,128)(2,1)} %bitcast_select_fusion.key_ref.value_ref), custom_call_target="tpu_custom_call" | custom-call | tf_op jit(solution)/shard_map/pallas_call | solution.py:45
  80.5 4.4 %fusion = bf16[128,2048]{1,0:T(8,128)(2,1)S(1)} fusion(bf16[128,2048]{1,0:T(8,128)(2,1)} %shard_map.140, bf16[2048,512]{1,0:T(8,128)(2,1)} %collective-permute-done.2, bf16[2048,512]{1,0:T(8,128)(2,1)} %collective-permute-done, bf16[2048,512]{1,0:T(8,128)(2,1)} %collective-permute-done.1, bf16[2048,512]{1,0:T(8,128)(2,1)} %param.17), kind=kOutput, calls=%fused_computation.2 | convolution fusion | flops 1107296256 | bytes 9437184 | tf_op jit(solution)/shard_map/dot_general | solution.py:161
  85.0 1.4 gather_fusion.1
  86.3 1.3 copy.78
  88.2 1.1 multiply_convert_fusion
  90.0 0.9 slice.67
  93.5 70.9 %all-gather.4.cloned.1.call-done = bf16[2048,2048]{0,1:T(8,128)(2,1)} async-done(((bf16[128,2048]{0,1:T(8,128)(2,1)}), bf16[2048,2048]{0,1:T(8,128)(2,1)}) %all-gather.4.cloned.1.call-update) | async-done | bytes 8388624 | tf_op jit(solution)/shard_map/all_gather | solution.py:190
  164.3 11.9 %fusion.11 = f32[2048,768]{1,0:T(8,128)} fusion(bf16[2048,2048]{0,1:T(8,128)(2,1)} %all-gather.4.cloned.1.call-done, bf16[2048,384]{1,0:T(8,128)(2,1)} %bitcast.85, bf16[2048,384]{1,0:T(8,128)(2,1)} %bitcast.86), kind=kOutput, calls=%fused_computation.18 | convolution fusion | flops 6448742400 | bytes 17825792 | tf_op jit(solution)/shard_map/dot_general | solution.py:208
  176.3 9.4 %convolution_convert_fusion = bf16[1024,2048]{1,0:T(8,128)(2,1)} fusion(bf16[1,384,2048]{2,1,0:T(8,128)(2,1)S(1)} %copy-done, f32[2048,768]{1,0:T(8,128)} %fusion.11, s32[1024]{0:T(1024)S(1)} %add.194), kind=kOutput, calls=%fused_computation.15 | convolution fusion | flops 3230531584 | bytes 12062720 | tf_op jit(solution)/shard_map/dot_general | solution.py:219
  185.6 7.7 %all-to-all-start = ((bf16[16,64,2048]{2,1,0:T(8,128)(2,1)}), bf16[16,64,2048]{2,1,0:T(8,128)(2,1)}, u32[]{:S(2)}, u32[]{:S(2)}) async-start(bf16[16,64,2048]{2,1,0:T(8,128)(2,1)} %bitcast.74), calls=%async_computation | async-start | bytes 8388608 | tf_op jit(solution)/shard_map/all_to_all | solution.py:229
  194.2 4.4 %compare_select_fusion.1 = (s32[1024,1]{0,1:T(1,128)S(1)}, s32[1024,1]{0,1:T(1,128)S(1)}) fusion(s32[]{:T(128)} %bitcast.16, s32[]{:T(128)} %bitcast.17, s32[]{:T(128)} %bitcast.18, s32[]{:T(128)} %bitcast.19, s32[]{:T(128)} %bitcast.20, s32[]{:T(128)} %bitcast.22, s32[]{:T(128)} %bitcast.21, s32[1024,1]{0,1:T(1,128)S(1)} %reshape.264), kind=kLoop, calls=%fused_computation.60 | loop fusion | flops 15360 | bytes 12316 | tf_op jit(solution)/shard_map/jit(_take)/gather | solution.py:176
  198.8 5.6 %and_select_fusion = (s32[1024]{0:T(1024)S(1)}, s32[1024]{0:T(1024)S(1)}) fusion(s32[1024]{0:T(1024)S(1)} %reshape.260, pred[1024]{0:T(1024)(128)(4,1)S(1)} %get-tuple-element.35, pred[1024]{0:T(1024)(128)(4,1)S(1)} %get-tuple-element.34, pred[1024]{0:T(1024)(128)(4,1)S(1)} %get-tuple-element.33, pred[1024]{0:T(1024)(128)(4,1)S(1)} %get-tuple-element.32, ...), kind=kLoop, calls=%fused_computation.78 | loop fusion | flops 16384 | bytes 25636 | tf_op jit(solution)/shard_map/jit(_take)/select_n | solution.py:176
  204.6 4.5 %reduce-window.6 = s32[16,8,128]{2,1,0:T(8,128)S(1)} reduce-window(s32[16,8,128]{2,1,0:T(8,128)S(1)} %fusion.31, s32[]{:T(128)} %constant.114.clone.1), window={size=1x1x128 pad=0_0x0_0x127_0}, to_apply=%region_0.1 | reduce-window | flops 2080768 | bytes 131076 | tf_op jit(solution)/shard_map/reduce-window
  209.9 1.3 select_reduce_fusion
  211.3 1.0 copy.88
  212.3 73.5 %all-to-all-done = bf16[16,64,2048]{2,1,0:T(8,128)(2,1)} async-done(((bf16[16,64,2048]{2,1,0:T(8,128)(2,1)}), bf16[16,64,2048]{2,1,0:T(8,128)(2,1)}, u32[]{:S(2)}, u32[]{:S(2)}) %all-to-all-start) | async-done | bytes 4194336 | tf_op jit(solution)/shard_map/all_to_all | solution.py:229
  285.8 3.4 %fusion.24 = f32[256,2048]{1,0:T(8,128)S(1)} fusion(bf16[1024,2048]{1,0:T(8,128)(2,1)} %bitcast.33, bf16[128,1024]{1,0:T(8,128)(2,1)S(1)} %get-tuple-element.36, bf16[128,1024]{1,0:T(8,128)(2,1)S(1)} %get-tuple-element.37), kind=kOutput, calls=%fused_computation.33 | convolution fusion | flops 1074790400 | bytes 6815744 | tf_op jit(solution)/shard_map/dot_general | solution.py:244
  289.2 0.9 fusion.20
  (76 shorter events, 9.1 us)
Async XLA Ops:
  7.2 169.1 %copy-start = (bf16[1,384,2048]{2,1,0:T(8,128)(2,1)S(1)}, bf16[1,384,2048]{2,1,0:T(8,128)(2,1)}, u32[]{:S(2)}) copy-start(bf16[1,384,2048]{2,1,0:T(8,128)(2,1)} %param.25) | copy-start | bytes 4718596
  7.2 53.1 %all-gather.6.cloned.1.call-start = ((), (), s32[]{:S(2)}) async-start(), calls=%async_computation.2 | async-start | bytes 2367488 | tf_op jit(solution)/shard_map/all_gather | solution.py:124
  9.8 154.5 %all-gather.4.cloned.1.call-start = ((), (), s32[]{:S(2)}) async-start(), calls=%async_computation.1 | async-start | bytes 8912896 | tf_op jit(solution)/shard_map/all_gather | solution.py:190
  9.9 57.2 %collective-permute-start = (bf16[2048,512]{1,0:T(8,128)(2,1)}, bf16[2048,512]{1,0:T(8,128)(2,1)}, u32[]{:S(2)}, u32[]{:S(2)}) collective-permute-start(bf16[2048,512]{1,0:T(8,128)(2,1)} %param.17), channel_id=1, source_target_pairs={{0,2},{1,3},{2,0},{3,1},{4,6},{5,7},{6,4},{7,5},{8,10},{9,11},{10,... | collective-permute-start | bytes 6291464 | tf_op jit(solution)/shard_map/ppermute | solution.py:15
  67.1 13.4 %collective-permute-start.1 = (bf16[2048,512]{1,0:T(8,128)(2,1)}, bf16[2048,512]{1,0:T(8,128)(2,1)}, u32[]{:S(2)}, u32[]{:S(2)}) collective-permute-start(bf16[2048,512]{1,0:T(8,128)(2,1)} %param.17), channel_id=1, source_target_pairs={{0,1},{1,0},{2,3},{3,2},{4,5},{5,4},{6,7},{7,6},{8,9},{9,8},{10,11... | collective-permute-start | bytes 6291464 | tf_op jit(solution)/shard_map/ppermute | solution.py:15
  67.3 13.2 %collective-permute-start.2 = (bf16[2048,512]{1,0:T(8,128)(2,1)}, bf16[2048,512]{1,0:T(8,128)(2,1)}, u32[]{:S(2)}, u32[]{:S(2)}) collective-permute-start(bf16[2048,512]{1,0:T(8,128)(2,1)} %collective-permute-done), channel_id=1, source_target_pairs={{0,1},{1,0},{2,3},{3,2},{4,5},{5,4},{6,7},{7,6},{8,9},{9,8},{10,11... | collective-permute-start | bytes 6291464 | tf_op jit(solution)/shard_map/ppermute | solution.py:15
  84.9 3.3 %copy-start.3 = (f32[2048]{0:T(1024)S(1)}, f32[2048]{0:T(1024)}, u32[]{:S(2)}) copy-start(f32[2048]{0:T(1024)} %param.19) | copy-start | bytes 24580
  84.9 4.4 %copy-start.1 = (s32[16]{0:T(128)S(1)}, s32[16]{0:T(128)}, u32[]{:S(2)}) copy-start(s32[16]{0:T(128)} %param.22) | copy-start | bytes 196
  185.6 24.1 %copy-start.2 = (s32[128,8]{0,1:T(8,128)S(1)}, s32[128,8]{0,1:T(8,128)}, u32[]{:S(2)}) copy-start(s32[128,8]{0,1:T(8,128)} %param.20) | copy-start | bytes 12292
  185.6 24.2 %copy-start.4 = (f32[128,8]{0,1:T(8,128)S(1)}, f32[128,8]{0,1:T(8,128)}, u32[]{:S(2)}) copy-start(f32[128,8]{0,1:T(8,128)} %param.21) | copy-start | bytes 12292
  185.6 100.2 %all-to-all-start = ((bf16[16,64,2048]{2,1,0:T(8,128)(2,1)}), bf16[16,64,2048]{2,1,0:T(8,128)(2,1)}, u32[]{:S(2)}, u32[]{:S(2)}) async-start(bf16[16,64,2048]{2,1,0:T(8,128)(2,1)} %bitcast.74), calls=%async_computation | async-start | bytes 8388608 | tf_op jit(solution)/shard_map/all_to_all | solution.py:229
Sparse Core Ops, SparseCore 0:
  10.9 49.3 all-gather.5
  89.5 74.8 all-gather.3

commit v19 on v18

--- a/solution.py
+++ b/solution.py
@@ -115,22 +115,22 @@
     if use_gather:
         flat_ids = expert_ids.reshape(-1).astype(jnp.bfloat16)
         id_count = flat_ids.shape[0]
-        lane = shard_blocks * 2 * kv_width
-        id_rows = -(-(-(-id_count // lane)) // 8) * 8
-        id_slab = jnp.pad(flat_ids, (0, id_rows * lane - id_count)).reshape(
-            shard_blocks, id_rows, 2 * kv_width
-        )
-        both = jnp.concatenate([both, id_slab], axis=1)
+        cells = shard_blocks * slice_rows
+        id_cols = -(-(-(-id_count // cells)) // 128) * 128
+        id_slab = jnp.pad(flat_ids, (0, id_cols * cells - id_count)).reshape(
+            shard_blocks, slice_rows, id_cols
+        )
+        both = jnp.concatenate([both, id_slab], axis=2)
     gathered = lax.all_gather(both[None], ("ctx", "eg"), axis=0, tiled=True)
     if use_gather:
         all_ids = (
-            gathered[:, :, slice_rows:, :]
+            gathered[:, :, :, 2 * kv_width :]
             .reshape(n_ctx * n_eg, -1)[:, :id_count]
             .reshape(-1, top_count)
             .astype(jnp.int32)
         )
-    held_rows = gathered.shape[2]
-    by_slice = gathered.reshape(n_ctx * n_eg * shard_blocks, held_rows, 2 * kv_width)
+    held_width = gathered.shape[3]
+    by_slice = gathered.reshape(n_ctx * n_eg * shard_blocks, slice_rows, held_width)
     query_rows = queries.shape[0]
     my_block = (my_ctx * n_eg + my_eg) * query_rows // block_rows
     chosen_blocks = jnp.concatenate(
@@ -139,9 +139,7 @@
     slice_index = (
         (chosen_blocks // shard_blocks)[:, None] * n_eg + jnp.arange(n_eg, dtype=jnp.int32)[None, :]
     ) * shard_blocks + (chosen_blocks % shard_blocks)[:, None]
-    context = jnp.take(by_slice[:, :slice_rows], slice_index.reshape(-1), axis=0).reshape(
-        -1, 2 * kv_width
-    )
+    context = jnp.take(by_slice, slice_index.reshape(-1), axis=0).reshape(-1, held_width)
     span = (1 + pick_count) * block_rows
     kv_heads = kv_width // HD
     tok_dev = residual.shape[0]

time: 298 us -> 299 us (level)
  waiting for transfers between devices: 193 us -> 197 us
    all_gather x1, waiting for transfers between devices: 48.8 us -> 52 us  [local(): gathered = lax.all_gather(both[None], ('ctx', 'eg'), axis=0, tiled=True)]
  transfers between devices with their start and end apart: 6 -> 6, of which waited for: 3 -> 3; matrix products, arithmetic and copies ran while one was open for 11% -> 10% of each run, Pallas kernels for 4% -> 4%
where the time goes in v19:
time: 299 us; the launch traced here: 298 us
  waiting for transfers between devices  197 us (66%)
  matrix products  29.1 us (10%)
  other arithmetic  25.4 us (8%)
  between operations  14.3 us (5%)
  local copies, waits for them, and re-layouts  12.9 us (4%)
  Pallas kernels  11.5 us (4%)
  starting transfers between devices  8.6 us (3%)
    all_to_all x1, waiting for transfers between devices, local(): lax.all_to_all(produced.reshape(slot_count, per_slot, -1), ('ctx', 'eg'),...  73.5 us
    all_gather x1, waiting for transfers between devices, local(): all_packed = lax.all_gather(normed, ('ctx', 'eg'), axis=0, tiled=True)  71 us
    all_gather x1, waiting for transfers between devices, local(): gathered = lax.all_gather(both[None], ('ctx', 'eg'), axis=0, tiled=True)  52 us
    dot_general x1, matrix products, local(): both_act = jnp.dot(all_packed, gate_up, preferred_element_type=jnp.float32)  11.9 us
    pallas_call x1, Pallas kernels, attend_rows(): pl.pallas_call(attention_kernel, grid=(kv_heads,), in_specs=[pl.BlockSpec...  11.5 us
    dot_general x1, matrix products, local(): jnp.dot(picked, partner[2], preferred_element_type=jnp.float32)  9.36 us
    all_to_all x1, starting transfers between devices, local(): lax.all_to_all(produced.reshape(slot_count, per_slot, -1), ('ctx', 'eg'),...  7.69 us
  transfers between devices with their start and end apart: 6, of which 3 were waited for; matrix products, arithmetic and copies ran while one was open for 10% of the time, Pallas kernels for 4%

profile of v19, /device:TPU:11, one launch (start us, length us, event | category | flops | bytes accessed | tf_op | source)
XLA Modules:
  0.0 298.3 jit_solution(11128264326256756038)
XLA Ops:
  7.2 0.9 copy.76
  8.2 1.6 pad_maximum_fusion
  11.5 52.0 %all-gather.6.cloned.1.call-done = bf16[16,128,640]{2,1,0:T(8,128)(2,1)} async-done(((bf16[1,128,640]{2,1,0:T(8,128)(2,1)}), bf16[16,128,640]{2,1,0:T(8,128)(2,1)}) %all-gather.6.cloned.1.call-update) | async-done | bytes 2621456 | tf_op jit(solution)/shard_map/all_gather | solution.py:124
  63.5 2.7 gather_fusion
  66.1 1.8 bitcast_select_fusion.key_ref.value_ref
  68.5 1.3 copy.87
  69.8 11.5 %shard_map.140 = bf16[128,2048]{1,0:T(8,128)(2,1)} custom-call(bf16[128,2048]{1,0:T(8,128)(2,1)} %query_ref.1, bf16[1536,640]{1,0:T(8,128)(2,1)} %bitcast_select_fusion.key_ref.value_ref, bf16[1536,640]{1,0:T(8,128)(2,1)} %bitcast_select_fusion.key_ref.value_ref), custom_call_target="tpu_custom_call" | custom-call | tf_op jit(solution)/shard_map/pallas_call | solution.py:45
  81.3 4.4 %fusion = bf16[128,2048]{1,0:T(8,128)(2,1)S(1)} fusion(bf16[128,2048]{1,0:T(8,128)(2,1)} %shard_map.140, bf16[2048,512]{1,0:T(8,128)(2,1)} %collective-permute-done.2, bf16[2048,512]{1,0:T(8,128)(2,1)} %collective-permute-done, bf16[2048,512]{1,0:T(8,128)(2,1)} %collective-permute-done.1, bf16[2048,512]{1,0:T(8,128)(2,1)} %param.17), kind=kOutput, calls=%fused_computation.2 | convolution fusion | flops 1107296256 | bytes 9437184 | tf_op jit(solution)/shard_map/dot_general | solution.py:159
  85.8 1.4 gather_fusion.1
  87.1 1.3 copy.78
  89.0 1.1 multiply_convert_fusion
  90.8 1.1 slice.62
  94.6 71.0 %all-gather.4.cloned.1.call-done = bf16[2048,2048]{0,1:T(8,128)(2,1)} async-done(((bf16[128,2048]{0,1:T(8,128)(2,1)}), bf16[2048,2048]{0,1:T(8,128)(2,1)}) %all-gather.4.cloned.1.call-update) | async-done | bytes 8388624 | tf_op jit(solution)/shard_map/all_gather | solution.py:188
  165.6 11.9 %fusion.11 = f32[2048,768]{1,0:T(8,128)} fusion(bf16[2048,2048]{0,1:T(8,128)(2,1)} %all-gather.4.cloned.1.call-done, bf16[2048,384]{1,0:T(8,128)(2,1)} %bitcast.89, bf16[2048,384]{1,0:T(8,128)(2,1)} %bitcast.90), kind=kOutput, calls=%fused_computation.18 | convolution fusion | flops 6448742400 | bytes 17825792 | tf_op jit(solution)/shard_map/dot_general | solution.py:206
  177.6 9.4 %convolution_convert_fusion = bf16[1024,2048]{1,0:T(8,128)(2,1)} fusion(bf16[1,384,2048]{2,1,0:T(8,128)(2,1)S(1)} %copy-done, f32[2048,768]{1,0:T(8,128)} %fusion.11, s32[1024]{0:T(1024)S(1)} %add.194), kind=kOutput, calls=%fused_computation.15 | convolution fusion | flops 3230531584 | bytes 12062720 | tf_op jit(solution)/shard_map/dot_general | solution.py:217
  186.9 7.7 %all-to-all-start = ((bf16[16,64,2048]{2,1,0:T(8,128)(2,1)}), bf16[16,64,2048]{2,1,0:T(8,128)(2,1)}, u32[]{:S(2)}, u32[]{:S(2)}) async-start(bf16[16,64,2048]{2,1,0:T(8,128)(2,1)} %bitcast.78), calls=%async_computation | async-start | bytes 8388608 | tf_op jit(solution)/shard_map/all_to_all | solution.py:227
  195.6 4.4 %compare_select_fusion.1 = (s32[1024,1]{0,1:T(1,128)S(1)}, s32[1024,1]{0,1:T(1,128)S(1)}) fusion(s32[]{:T(128)} %bitcast.17, s32[]{:T(128)} %bitcast.18, s32[]{:T(128)} %bitcast.19, s32[]{:T(128)} %bitcast.20, s32[]{:T(128)} %bitcast.21, s32[]{:T(128)} %bitcast.23, s32[]{:T(128)} %bitcast.22, s32[1024,1]{0,1:T(1,128)S(1)} %reshape.264), kind=kLoop, calls=%fused_computation.62 | loop fusion | flops 15360 | bytes 12316 | tf_op jit(solution)/shard_map/jit(_take)/gather | solution.py:174
  200.1 5.6 %and_select_fusion = (s32[1024]{0:T(1024)S(1)}, s32[1024]{0:T(1024)S(1)}) fusion(s32[1024]{0:T(1024)S(1)} %reshape.260, pred[1024]{0:T(1024)(128)(4,1)S(1)} %get-tuple-element.35, pred[1024]{0:T(1024)(128)(4,1)S(1)} %get-tuple-element.34, pred[1024]{0:T(1024)(128)(4,1)S(1)} %get-tuple-element.33, pred[1024]{0:T(1024)(128)(4,1)S(1)} %get-tuple-element.32, ...), kind=kLoop, calls=%fused_computation.80 | loop fusion | flops 16384 | bytes 25636 | tf_op jit(solution)/shard_map/jit(_take)/select_n | solution.py:174
  205.9 4.5 %reduce-window.6 = s32[16,8,128]{2,1,0:T(8,128)S(1)} reduce-window(s32[16,8,128]{2,1,0:T(8,128)S(1)} %fusion.31, s32[]{:T(128)} %constant.114.clone.1), window={size=1x1x128 pad=0_0x0_0x127_0}, to_apply=%region_0.1 | reduce-window | flops 2080768 | bytes 131076 | tf_op jit(solution)/shard_map/reduce-window
  211.2 1.3 select_reduce_fusion
  212.6 1.0 copy.88
  213.6 73.5 %all-to-all-done = bf16[16,64,2048]{2,1,0:T(8,128)(2,1)} async-done(((bf16[16,64,2048]{2,1,0:T(8,128)(2,1)}), bf16[16,64,2048]{2,1,0:T(8,128)(2,1)}, u32[]{:S(2)}, u32[]{:S(2)}) %all-to-all-start) | async-done | bytes 4194336 | tf_op jit(solution)/shard_map/all_to_all | solution.py:227
  287.1 3.4 %fusion.24 = f32[256,2048]{1,0:T(8,128)S(1)} fusion(bf16[1024,2048]{1,0:T(8,128)(2,1)} %bitcast.34, bf16[128,1024]{1,0:T(8,128)(2,1)S(1)} %get-tuple-element.36, bf16[128,1024]{1,0:T(8,128)(2,1)S(1)} %get-tuple-element.37), kind=kOutput, calls=%fused_computation.34 | convolution fusion | flops 1074790400 | bytes 6815744 | tf_op jit(solution)/shard_map/dot_general | solution.py:242
  290.6 0.9 fusion.20
  (78 shorter events, 8.4 us)
Async XLA Ops:
  7.2 170.4 %copy-start = (bf16[1,384,2048]{2,1,0:T(8,128)(2,1)S(1)}, bf16[1,384,2048]{2,1,0:T(8,128)(2,1)}, u32[]{:S(2)}) copy-start(bf16[1,384,2048]{2,1,0:T(8,128)(2,1)} %param.25) | copy-start | bytes 4718596
  7.2 56.3 %all-gather.6.cloned.1.call-start = ((), (), s32[]{:S(2)}) async-start(), calls=%async_computation.2 | async-start | bytes 2785280 | tf_op jit(solution)/shard_map/all_gather | solution.py:124
  8.1 3.4 %copy-start.1 = (s32[128,8]{1,0:T(8,128)}, s32[128,8]{1,0:T(8,128)S(1)}, u32[]{:S(2)}) copy-start(s32[128,8]{1,0:T(8,128)S(1)} %copy.76) | copy-start | bytes 12292
  9.8 155.8 %all-gather.4.cloned.1.call-start = ((), (), s32[]{:S(2)}) async-start(), calls=%async_computation.1 | async-start | bytes 8912896 | tf_op jit(solution)/shard_map/all_gather | solution.py:188
  9.9 58.0 %collective-permute-start = (bf16[2048,512]{1,0:T(8,128)(2,1)}, bf16[2048,512]{1,0:T(8,128)(2,1)}, u32[]{:S(2)}, u32[]{:S(2)}) collective-permute-start(bf16[2048,512]{1,0:T(8,128)(2,1)} %param.17), channel_id=1, source_target_pairs={{0,2},{1,3},{2,0},{3,1},{4,6},{5,7},{6,4},{7,5},{8,10},{9,11},{10,... | collective-permute-start | bytes 6291464 | tf_op jit(solution)/shard_map/ppermute | solution.py:15
  67.9 13.4 %collective-permute-start.1 = (bf16[2048,512]{1,0:T(8,128)(2,1)}, bf16[2048,512]{1,0:T(8,128)(2,1)}, u32[]{:S(2)}, u32[]{:S(2)}) collective-permute-start(bf16[2048,512]{1,0:T(8,128)(2,1)} %param.17), channel_id=1, source_target_pairs={{0,1},{1,0},{2,3},{3,2},{4,5},{5,4},{6,7},{7,6},{8,9},{9,8},{10,11... | collective-permute-start | bytes 6291464 | tf_op jit(solution)/shard_map/ppermute | solution.py:15
  68.1 13.2 %collective-permute-start.2 = (bf16[2048,512]{1,0:T(8,128)(2,1)}, bf16[2048,512]{1,0:T(8,128)(2,1)}, u32[]{:S(2)}, u32[]{:S(2)}) collective-permute-start(bf16[2048,512]{1,0:T(8,128)(2,1)} %collective-permute-done), channel_id=1, source_target_pairs={{0,1},{1,0},{2,3},{3,2},{4,5},{5,4},{6,7},{7,6},{8,9},{9,8},{10,11... | collective-permute-start | bytes 6291464 | tf_op jit(solution)/shard_map/ppermute | solution.py:15
  85.7 3.3 %copy-start.5 = (f32[2048]{0:T(1024)S(1)}, f32[2048]{0:T(1024)}, u32[]{:S(2)}) copy-start(f32[2048]{0:T(1024)} %param.19) | copy-start | bytes 24580
  85.8 4.4 %copy-start.3 = (s32[16]{0:T(128)S(1)}, s32[16]{0:T(128)}, u32[]{:S(2)}) copy-start(s32[16]{0:T(128)} %param.22) | copy-start | bytes 196
  186.9 7.7 %copy-start.2 = (s32[128,8]{1,0:T(8,128)S(1)}, s32[128,8]{1,0:T(8,128)}, u32[]{:S(2)}) copy-start(s32[128,8]{1,0:T(8,128)} %copy-done.1) | copy-start | bytes 12292
  186.9 24.1 %copy-start.4 = (s32[128,8]{0,1:T(8,128)S(1)}, s32[128,8]{0,1:T(8,128)}, u32[]{:S(2)}) copy-start(s32[128,8]{0,1:T(8,128)} %param.20) | copy-start | bytes 12292
  186.9 24.2 %copy-start.6 = (f32[128,8]{0,1:T(8,128)S(1)}, f32[128,8]{0,1:T(8,128)}, u32[]{:S(2)}) copy-start(f32[128,8]{0,1:T(8,128)} %param.21) | copy-start | bytes 12292
  186.9 100.2 %all-to-all-start = ((bf16[16,64,2048]{2,1,0:T(8,128)(2,1)}), bf16[16,64,2048]{2,1,0:T(8,128)(2,1)}, u32[]{:S(2)}, u32[]{:S(2)}) async-start(bf16[16,64,2048]{2,1,0:T(8,128)(2,1)} %bitcast.78), calls=%async_computation | async-start | bytes 8388608 | tf_op jit(solution)/shard_map/all_to_all | solution.py:227
Sparse Core Ops, SparseCore 0:
  10.9 52.5 all-gather.5
  90.3 75.3 all-gather.3

commit v20 on v18

--- a/solution.py
+++ b/solution.py
@@ -139,7 +139,7 @@
     slice_index = (
         (chosen_blocks // shard_blocks)[:, None] * n_eg + jnp.arange(n_eg, dtype=jnp.int32)[None, :]
     ) * shard_blocks + (chosen_blocks % shard_blocks)[:, None]
-    context = jnp.take(by_slice[:, :slice_rows], slice_index.reshape(-1), axis=0).reshape(
+    context = jnp.take(by_slice, slice_index.reshape(-1), axis=0)[:, :slice_rows].reshape(
         -1, 2 * kv_width
     )
     span = (1 + pick_count) * block_rows

time: 298 us -> 298 us (level)
  local copies, waits for them, and re-layouts: 15.1 us -> 12 us
    slice x3 -> x2, local copies, waits for them, and re-layouts: 3.28 us -> 0.21 us  [the longest x1 3.07 us: local(): by_slice[:, :slice_rows]]
  transfers between devices with their start and end apart: 6 -> 6, of which waited for: 3 -> 4; matrix products, arithmetic and copies ran while one was open for 11% -> 10% of each run, Pallas kernels for 4% -> 4%
where the time goes in v20:
time: 298 us; the launch traced here: 297 us
  waiting for transfers between devices  195 us (65%)
  matrix products  29.1 us (10%)
  other arithmetic  25.1 us (8%)
  between operations  14.3 us (5%)
  local copies, waits for them, and re-layouts  12 us (4%)
  Pallas kernels  11.5 us (4%)
  starting transfers between devices  9.64 us (3%)
    all_to_all x1, waiting for transfers between devices, local(): lax.all_to_all(produced.reshape(slot_count, per_slot, -1), ('ctx', 'eg'),...  73.5 us
    all_gather x1, waiting for transfers between devices, local(): all_packed = lax.all_gather(normed, ('ctx', 'eg'), axis=0, tiled=True)  72.7 us
    all_gather x1, waiting for transfers between devices, local(): gathered = lax.all_gather(both[None], ('ctx', 'eg'), axis=0, tiled=True)  48.9 us
    dot_general x1, matrix products, local(): both_act = jnp.dot(all_packed, gate_up, preferred_element_type=jnp.float32)  11.9 us
    pallas_call x1, Pallas kernels, attend_rows(): pl.pallas_call(attention_kernel, grid=(kv_heads,), in_specs=[pl.BlockSpec...  11.5 us
    dot_general x1, matrix products, local(): jnp.dot(picked, partner[2], preferred_element_type=jnp.float32)  9.36 us
    all_to_all x1, starting transfers between devices, local(): lax.all_to_all(produced.reshape(slot_count, per_slot, -1), ('ctx', 'eg'),...  7.69 us
  transfers between devices with their start and end apart: 6, of which 4 were waited for; matrix products, arithmetic and copies ran while one was open for 10% of the time, Pallas kernels for 4%

profile of v20, /device:TPU:11, one launch (start us, length us, event | category | flops | bytes accessed | tf_op | source)
XLA Modules:
  0.0 297.0 jit_solution(8024199601587717807)
XLA Ops:
  8.3 1.5 pad_maximum_fusion
  11.4 48.9 %all-gather.6.cloned.1.call-done = bf16[16,136,512]{2,1,0:T(8,128)(2,1)} async-done(((bf16[1,136,512]{2,1,0:T(8,128)(2,1)}), bf16[16,136,512]{2,1,0:T(8,128)(2,1)}) %all-gather.6.cloned.1.call-update) | async-done | bytes 2228240 | tf_op jit(solution)/shard_map/all_gather | solution.py:124
  60.3 2.3 gather_fusion
  62.6 1.4 slice_select_fusion
  64.2 1.5 collective-permute-start.1
  65.9 1.3 copy.87
  67.2 11.5 %shard_map.140 = bf16[128,2048]{1,0:T(8,128)(2,1)} custom-call(bf16[128,2048]{1,0:T(8,128)(2,1)} %query_ref.1, bf16[1536,512]{1,0:T(8,128)(2,1)} %bitcast.71, bf16[1536,512]{1,0:T(8,128)(2,1)} %bitcast.72), custom_call_target="tpu_custom_call" | custom-call | tf_op jit(solution)/shard_map/pallas_call | solution.py:45
  78.7 4.4 %fusion = bf16[128,2048]{1,0:T(8,128)(2,1)S(1)} fusion(bf16[128,2048]{1,0:T(8,128)(2,1)} %shard_map.140, bf16[2048,512]{1,0:T(8,128)(2,1)} %collective-permute-done.2, bf16[2048,512]{1,0:T(8,128)(2,1)} %collective-permute-done, bf16[2048,512]{1,0:T(8,128)(2,1)} %collective-permute-done.1, bf16[2048,512]{1,0:T(8,128)(2,1)} %param.17), kind=kOutput, calls=%fused_computation.2 | convolution fusion | flops 1107296256 | bytes 9437184 | tf_op jit(solution)/shard_map/dot_general | solution.py:161
  83.1 1.4 gather_fusion.1
  84.5 1.3 copy.78
  86.4 1.1 multiply_convert_fusion
  88.2 0.9 slice.67
  91.7 72.7 %all-gather.4.cloned.1.call-done = bf16[2048,2048]{0,1:T(8,128)(2,1)} async-done(((bf16[128,2048]{0,1:T(8,128)(2,1)}), bf16[2048,2048]{0,1:T(8,128)(2,1)}) %all-gather.4.cloned.1.call-update) | async-done | bytes 8388624 | tf_op jit(solution)/shard_map/all_gather | solution.py:190
  164.3 11.9 %fusion.11 = f32[2048,768]{1,0:T(8,128)} fusion(bf16[2048,2048]{0,1:T(8,128)(2,1)} %all-gather.4.cloned.1.call-done, bf16[2048,384]{1,0:T(8,128)(2,1)} %bitcast.84, bf16[2048,384]{1,0:T(8,128)(2,1)} %bitcast.85), kind=kOutput, calls=%fused_computation.18 | convolution fusion | flops 6448742400 | bytes 17825792 | tf_op jit(solution)/shard_map/dot_general | solution.py:208
  176.3 9.4 %convolution_convert_fusion = bf16[1024,2048]{1,0:T(8,128)(2,1)} fusion(bf16[1,384,2048]{2,1,0:T(8,128)(2,1)S(1)} %copy-done, f32[2048,768]{1,0:T(8,128)} %fusion.11, s32[1024]{0:T(1024)S(1)} %add.194), kind=kOutput, calls=%fused_computation.15 | convolution fusion | flops 3230531584 | bytes 12062720 | tf_op jit(solution)/shard_map/dot_general | solution.py:219
  185.6 7.7 %all-to-all-start = ((bf16[16,64,2048]{2,1,0:T(8,128)(2,1)}), bf16[16,64,2048]{2,1,0:T(8,128)(2,1)}, u32[]{:S(2)}, u32[]{:S(2)}) async-start(bf16[16,64,2048]{2,1,0:T(8,128)(2,1)} %bitcast.73), calls=%async_computation | async-start | bytes 8388608 | tf_op jit(solution)/shard_map/all_to_all | solution.py:229
  194.2 4.4 %compare_select_fusion.1 = (s32[1024,1]{0,1:T(1,128)S(1)}, s32[1024,1]{0,1:T(1,128)S(1)}) fusion(s32[]{:T(128)} %bitcast.15, s32[]{:T(128)} %bitcast.16, s32[]{:T(128)} %bitcast.17, s32[]{:T(128)} %bitcast.18, s32[]{:T(128)} %bitcast.19, s32[]{:T(128)} %bitcast.21, s32[]{:T(128)} %bitcast.20, s32[1024,1]{0,1:T(1,128)S(1)} %reshape.265), kind=kLoop, calls=%fused_computation.60 | loop fusion | flops 15360 | bytes 12316 | tf_op jit(solution)/shard_map/jit(_take)/gather | solution.py:176
  198.8 5.6 %and_select_fusion = (s32[1024]{0:T(1024)S(1)}, s32[1024]{0:T(1024)S(1)}) fusion(s32[1024]{0:T(1024)S(1)} %reshape.260, pred[1024]{0:T(1024)(128)(4,1)S(1)} %get-tuple-element.35, pred[1024]{0:T(1024)(128)(4,1)S(1)} %get-tuple-element.34, pred[1024]{0:T(1024)(128)(4,1)S(1)} %get-tuple-element.33, pred[1024]{0:T(1024)(128)(4,1)S(1)} %get-tuple-element.32, ...), kind=kLoop, calls=%fused_computation.78 | loop fusion | flops 16384 | bytes 25636 | tf_op jit(solution)/shard_map/jit(_take)/select_n | solution.py:176
  204.6 4.5 %reduce-window.6 = s32[16,8,128]{2,1,0:T(8,128)S(1)} reduce-window(s32[16,8,128]{2,1,0:T(8,128)S(1)} %fusion.31, s32[]{:T(128)} %constant.114.clone.1), window={size=1x1x128 pad=0_0x0_0x127_0}, to_apply=%region_0.1 | reduce-window | flops 2080768 | bytes 131076 | tf_op jit(solution)/shard_map/reduce-window
  209.9 1.3 select_reduce_fusion
  211.3 1.0 copy.88
  212.3 73.5 %all-to-all-done = bf16[16,64,2048]{2,1,0:T(8,128)(2,1)} async-done(((bf16[16,64,2048]{2,1,0:T(8,128)(2,1)}), bf16[16,64,2048]{2,1,0:T(8,128)(2,1)}, u32[]{:S(2)}, u32[]{:S(2)}) %all-to-all-start) | async-done | bytes 4194336 | tf_op jit(solution)/shard_map/all_to_all | solution.py:229
  285.8 3.4 %fusion.24 = f32[256,2048]{1,0:T(8,128)S(1)} fusion(bf16[1024,2048]{1,0:T(8,128)(2,1)} %bitcast.32, bf16[128,1024]{1,0:T(8,128)(2,1)S(1)} %get-tuple-element.36, bf16[128,1024]{1,0:T(8,128)(2,1)S(1)} %get-tuple-element.37), kind=kOutput, calls=%fused_computation.33 | convolution fusion | flops 1074790400 | bytes 6815744 | tf_op jit(solution)/shard_map/dot_general | solution.py:244
  289.2 0.9 fusion.20
  (74 shorter events, 8.8 us)
Async XLA Ops:
  7.2 169.1 %copy-start = (bf16[1,384,2048]{2,1,0:T(8,128)(2,1)S(1)}, bf16[1,384,2048]{2,1,0:T(8,128)(2,1)}, u32[]{:S(2)}) copy-start(bf16[1,384,2048]{2,1,0:T(8,128)(2,1)} %param.25) | copy-start | bytes 4718596
  7.2 53.1 %all-gather.6.cloned.1.call-start = ((), (), s32[]{:S(2)}) async-start(), calls=%async_computation.2 | async-start | bytes 2367488 | tf_op jit(solution)/shard_map/all_gather | solution.py:124
  9.8 154.5 %all-gather.4.cloned.1.call-start = ((), (), s32[]{:S(2)}) async-start(), calls=%async_computation.1 | async-start | bytes 8912896 | tf_op jit(solution)/shard_map/all_gather | solution.py:190
  9.9 54.3 %collective-permute-start = (bf16[2048,512]{1,0:T(8,128)(2,1)}, bf16[2048,512]{1,0:T(8,128)(2,1)}, u32[]{:S(2)}, u32[]{:S(2)}) collective-permute-start(bf16[2048,512]{1,0:T(8,128)(2,1)} %param.17), channel_id=1, source_target_pairs={{0,2},{1,3},{2,0},{3,1},{4,6},{5,7},{6,4},{7,5},{8,10},{9,11},{10,... | collective-permute-start | bytes 6291464 | tf_op jit(solution)/shard_map/ppermute | solution.py:15
  64.2 14.5 %collective-permute-start.1 = (bf16[2048,512]{1,0:T(8,128)(2,1)}, bf16[2048,512]{1,0:T(8,128)(2,1)}, u32[]{:S(2)}, u32[]{:S(2)}) collective-permute-start(bf16[2048,512]{1,0:T(8,128)(2,1)} %param.17), channel_id=1, source_target_pairs={{0,1},{1,0},{2,3},{3,2},{4,5},{5,4},{6,7},{7,6},{8,9},{9,8},{10,11... | collective-permute-start | bytes 6291464 | tf_op jit(solution)/shard_map/ppermute | solution.py:15
  65.8 12.9 %collective-permute-start.2 = (bf16[2048,512]{1,0:T(8,128)(2,1)}, bf16[2048,512]{1,0:T(8,128)(2,1)}, u32[]{:S(2)}, u32[]{:S(2)}) collective-permute-start(bf16[2048,512]{1,0:T(8,128)(2,1)} %collective-permute-done), channel_id=1, source_target_pairs={{0,1},{1,0},{2,3},{3,2},{4,5},{5,4},{6,7},{7,6},{8,9},{9,8},{10,11... | collective-permute-start | bytes 6291464 | tf_op jit(solution)/shard_map/ppermute | solution.py:15
  83.1 3.3 %copy-start.3 = (f32[2048]{0:T(1024)S(1)}, f32[2048]{0:T(1024)}, u32[]{:S(2)}) copy-start(f32[2048]{0:T(1024)} %param.19) | copy-start | bytes 24580
  83.1 4.4 %copy-start.1 = (s32[16]{0:T(128)S(1)}, s32[16]{0:T(128)}, u32[]{:S(2)}) copy-start(s32[16]{0:T(128)} %param.22) | copy-start | bytes 196
  185.6 24.1 %copy-start.2 = (s32[128,8]{0,1:T(8,128)S(1)}, s32[128,8]{0,1:T(8,128)}, u32[]{:S(2)}) copy-start(s32[128,8]{0,1:T(8,128)} %param.20) | copy-start | bytes 12292
  185.6 24.2 %copy-start.4 = (f32[128,8]{0,1:T(8,128)S(1)}, f32[128,8]{0,1:T(8,128)}, u32[]{:S(2)}) copy-start(f32[128,8]{0,1:T(8,128)} %param.21) | copy-start | bytes 12292
  185.6 100.2 %all-to-all-start = ((bf16[16,64,2048]{2,1,0:T(8,128)(2,1)}), bf16[16,64,2048]{2,1,0:T(8,128)(2,1)}, u32[]{:S(2)}, u32[]{:S(2)}) async-start(bf16[16,64,2048]{2,1,0:T(8,128)(2,1)} %bitcast.73), calls=%async_computation | async-start | bytes 8388608 | tf_op jit(solution)/shard_map/all_to_all | solution.py:229
Sparse Core Ops, SparseCore 0:
  10.9 49.3 all-gather.5
  87.7 76.6 all-gather.3

commit v21 on v20

--- a/solution.py
+++ b/solution.py
@@ -158,14 +158,14 @@
             pieces[m + stride] = piece
     attended = attend_rows(queries, context, kv_heads)
     weight_cols = jnp.concatenate([pieces[m] for m in range(n_eg)], axis=1)
-    out_by_piece = jnp.dot(attended, weight_cols, preferred_element_type=jnp.float32).reshape(
-        query_rows, n_eg, -1
+    out_by_piece = (
+        jnp.dot(attended, weight_cols, preferred_element_type=jnp.float32)
+        .astype(jnp.bfloat16)
+        .reshape(query_rows, n_eg, -1)
     )
     piece_of_col = jnp.arange(n_eg, dtype=jnp.int32) ^ my_eg
     partial_out = jnp.take(out_by_piece, piece_of_col, axis=1).reshape(query_rows, -1)
-    attn_out = lax.psum_scatter(
-        partial_out.astype(jnp.bfloat16), "rep", scatter_dimension=0, tiled=True
-    )
+    attn_out = lax.psum_scatter(partial_out, "rep", scatter_dimension=0, tiled=True)
     stream = residual.astype(jnp.float32) + attn_out.astype(jnp.float32)
     meansq = jnp.mean(stream * stream, axis=1, keepdims=True)
     normed = (stream * lax.rsqrt(meansq + 1e-06) * norm_gain).astype(jnp.bfloat16)

time: 298 us -> 298 us (level)
  no operation moved by 1% of the time
where the time goes in v21:
time: 298 us; the launch traced here: 297 us
  waiting for transfers between devices  195 us (65%)
  matrix products  29.1 us (10%)
  other arithmetic  25.1 us (8%)
  between operations  14.3 us (5%)
  local copies, waits for them, and re-layouts  12 us (4%)
  Pallas kernels  11.5 us (4%)
  starting transfers between devices  9.64 us (3%)
    all_to_all x1, waiting for transfers between devices, local(): lax.all_to_all(produced.reshape(slot_count, per_slot, -1), ('ctx', 'eg'),...  73.5 us
    all_gather x1, waiting for transfers between devices, local(): all_packed = lax.all_gather(normed, ('ctx', 'eg'), axis=0, tiled=True)  72.7 us
    all_gather x1, waiting for transfers between devices, local(): gathered = lax.all_gather(both[None], ('ctx', 'eg'), axis=0, tiled=True)  48.9 us
    dot_general x1, matrix products, local(): both_act = jnp.dot(all_packed, gate_up, preferred_element_type=jnp.float32)  11.9 us
    pallas_call x1, Pallas kernels, attend_rows(): pl.pallas_call(attention_kernel, grid=(kv_heads,), in_specs=[pl.BlockSpec...  11.5 us
    dot_general x1, matrix products, local(): jnp.dot(picked, partner[2], preferred_element_type=jnp.float32)  9.36 us
    all_to_all x1, starting transfers between devices, local(): lax.all_to_all(produced.reshape(slot_count, per_slot, -1), ('ctx', 'eg'),...  7.69 us
  transfers between devices with their start and end apart: 6, of which 4 were waited for; matrix products, arithmetic and copies ran while one was open for 10% of the time, Pallas kernels for 4%

profile of v21, /device:TPU:11, one launch (start us, length us, event | category | flops | bytes accessed | tf_op | source)
XLA Modules:
  0.0 297.0 jit_solution(8024199601587717807)
XLA Ops:
  8.3 1.5 pad_maximum_fusion
  11.4 48.9 %all-gather.6.cloned.1.call-done = bf16[16,136,512]{2,1,0:T(8,128)(2,1)} async-done(((bf16[1,136,512]{2,1,0:T(8,128)(2,1)}), bf16[16,136,512]{2,1,0:T(8,128)(2,1)}) %all-gather.6.cloned.1.call-update) | async-done | bytes 2228240 | tf_op jit(solution)/shard_map/all_gather | solution.py:124
  60.3 2.3 gather_fusion
  62.6 1.4 slice_select_fusion
  64.2 1.5 collective-permute-start.1
  65.9 1.3 copy.87
  67.2 11.5 %shard_map.140 = bf16[128,2048]{1,0:T(8,128)(2,1)} custom-call(bf16[128,2048]{1,0:T(8,128)(2,1)} %query_ref.1, bf16[1536,512]{1,0:T(8,128)(2,1)} %bitcast.69, bf16[1536,512]{1,0:T(8,128)(2,1)} %bitcast.70), custom_call_target="tpu_custom_call" | custom-call | tf_op jit(solution)/shard_map/pallas_call | solution.py:45
  78.7 4.4 %fusion.15 = bf16[128,2048]{1,0:T(8,128)(2,1)S(1)} fusion(bf16[128,2048]{1,0:T(8,128)(2,1)} %shard_map.140, bf16[2048,512]{1,0:T(8,128)(2,1)} %collective-permute-done.2, bf16[2048,512]{1,0:T(8,128)(2,1)} %collective-permute-done, bf16[2048,512]{1,0:T(8,128)(2,1)} %collective-permute-done.1, bf16[2048,512]{1,0:T(8,128)(2,1)} %param.17), kind=kOutput, calls=%fused_computation.22 | convolution fusion | flops 1107558400 | bytes 9437184 | tf_op jit(solution)/shard_map/dot_general | solution.py:162
  83.1 1.4 gather_fusion.1
  84.5 1.3 copy.78
  86.4 1.1 multiply_convert_fusion
  88.2 0.9 slice.67
  91.7 72.7 %all-gather.4.cloned.1.call-done = bf16[2048,2048]{0,1:T(8,128)(2,1)} async-done(((bf16[128,2048]{0,1:T(8,128)(2,1)}), bf16[2048,2048]{0,1:T(8,128)(2,1)}) %all-gather.4.cloned.1.call-update) | async-done | bytes 8388624 | tf_op jit(solution)/shard_map/all_gather | solution.py:190
  164.3 11.9 %fusion.11 = f32[2048,768]{1,0:T(8,128)} fusion(bf16[2048,2048]{0,1:T(8,128)(2,1)} %all-gather.4.cloned.1.call-done, bf16[2048,384]{1,0:T(8,128)(2,1)} %bitcast.82, bf16[2048,384]{1,0:T(8,128)(2,1)} %bitcast.83), kind=kOutput, calls=%fused_computation.18 | convolution fusion | flops 6448742400 | bytes 17825792 | tf_op jit(solution)/shard_map/dot_general | solution.py:208
  176.3 9.4 %convolution_convert_fusion = bf16[1024,2048]{1,0:T(8,128)(2,1)} fusion(bf16[1,384,2048]{2,1,0:T(8,128)(2,1)S(1)} %copy-done, f32[2048,768]{1,0:T(8,128)} %fusion.11, s32[1024]{0:T(1024)S(1)} %add.194), kind=kOutput, calls=%fused_computation.15 | convolution fusion | flops 3230531584 | bytes 12062720 | tf_op jit(solution)/shard_map/dot_general | solution.py:219
  185.6 7.7 %all-to-all-start = ((bf16[16,64,2048]{2,1,0:T(8,128)(2,1)}), bf16[16,64,2048]{2,1,0:T(8,128)(2,1)}, u32[]{:S(2)}, u32[]{:S(2)}) async-start(bf16[16,64,2048]{2,1,0:T(8,128)(2,1)} %bitcast.71), calls=%async_computation | async-start | bytes 8388608 | tf_op jit(solution)/shard_map/all_to_all | solution.py:229
  194.2 4.4 %compare_select_fusion.1 = (s32[1024,1]{0,1:T(1,128)S(1)}, s32[1024,1]{0,1:T(1,128)S(1)}) fusion(s32[]{:T(128)} %bitcast.15, s32[]{:T(128)} %bitcast.16, s32[]{:T(128)} %bitcast.17, s32[]{:T(128)} %bitcast.18, s32[]{:T(128)} %bitcast.19, s32[]{:T(128)} %bitcast.21, s32[]{:T(128)} %bitcast.20, s32[1024,1]{0,1:T(1,128)S(1)} %reshape.265), kind=kLoop, calls=%fused_computation.60 | loop fusion | flops 15360 | bytes 12316 | tf_op jit(solution)/shard_map/jit(_take)/gather | solution.py:176
  198.8 5.6 %and_select_fusion = (s32[1024]{0:T(1024)S(1)}, s32[1024]{0:T(1024)S(1)}) fusion(s32[1024]{0:T(1024)S(1)} %reshape.260, pred[1024]{0:T(1024)(128)(4,1)S(1)} %get-tuple-element.35, pred[1024]{0:T(1024)(128)(4,1)S(1)} %get-tuple-element.34, pred[1024]{0:T(1024)(128)(4,1)S(1)} %get-tuple-element.33, pred[1024]{0:T(1024)(128)(4,1)S(1)} %get-tuple-element.32, ...), kind=kLoop, calls=%fused_computation.78 | loop fusion | flops 16384 | bytes 25636 | tf_op jit(solution)/shard_map/jit(_take)/select_n | solution.py:176
  204.6 4.5 %reduce-window.6 = s32[16,8,128]{2,1,0:T(8,128)S(1)} reduce-window(s32[16,8,128]{2,1,0:T(8,128)S(1)} %fusion.33, s32[]{:T(128)} %constant.114.clone.1), window={size=1x1x128 pad=0_0x0_0x127_0}, to_apply=%region_0.1 | reduce-window | flops 2080768 | bytes 131076 | tf_op jit(solution)/shard_map/reduce-window
  209.9 1.3 select_reduce_fusion
  211.3 1.0 copy.88
  212.3 73.5 %all-to-all-done = bf16[16,64,2048]{2,1,0:T(8,128)(2,1)} async-done(((bf16[16,64,2048]{2,1,0:T(8,128)(2,1)}), bf16[16,64,2048]{2,1,0:T(8,128)(2,1)}, u32[]{:S(2)}, u32[]{:S(2)}) %all-to-all-start) | async-done | bytes 4194336 | tf_op jit(solution)/shard_map/all_to_all | solution.py:229
  285.8 3.4 %fusion.26 = f32[256,2048]{1,0:T(8,128)S(1)} fusion(bf16[1024,2048]{1,0:T(8,128)(2,1)} %bitcast.32, bf16[128,1024]{1,0:T(8,128)(2,1)S(1)} %get-tuple-element.36, bf16[128,1024]{1,0:T(8,128)(2,1)S(1)} %get-tuple-element.37), kind=kOutput, calls=%fused_computation.32 | convolution fusion | flops 1074790400 | bytes 6815744 | tf_op jit(solution)/shard_map/dot_general | solution.py:244
  289.2 0.9 fusion.23
  (74 shorter events, 8.8 us)
Async XLA Ops:
  7.2 169.1 %copy-start = (bf16[1,384,2048]{2,1,0:T(8,128)(2,1)S(1)}, bf16[1,384,2048]{2,1,0:T(8,128)(2,1)}, u32[]{:S(2)}) copy-start(bf16[1,384,2048]{2,1,0:T(8,128)(2,1)} %param.25) | copy-start | bytes 4718596
  7.2 53.1 %all-gather.6.cloned.1.call-start = ((), (), s32[]{:S(2)}) async-start(), calls=%async_computation.2 | async-start | bytes 2367488 | tf_op jit(solution)/shard_map/all_gather | solution.py:124
  9.8 154.5 %all-gather.4.cloned.1.call-start = ((), (), s32[]{:S(2)}) async-start(), calls=%async_computation.1 | async-start | bytes 8912896 | tf_op jit(solution)/shard_map/all_gather | solution.py:190
  9.9 54.3 %collective-permute-start = (bf16[2048,512]{1,0:T(8,128)(2,1)}, bf16[2048,512]{1,0:T(8,128)(2,1)}, u32[]{:S(2)}, u32[]{:S(2)}) collective-permute-start(bf16[2048,512]{1,0:T(8,128)(2,1)} %param.17), channel_id=1, source_target_pairs={{0,2},{1,3},{2,0},{3,1},{4,6},{5,7},{6,4},{7,5},{8,10},{9,11},{10,... | collective-permute-start | bytes 6291464 | tf_op jit(solution)/shard_map/ppermute | solution.py:15
  64.2 14.5 %collective-permute-start.1 = (bf16[2048,512]{1,0:T(8,128)(2,1)}, bf16[2048,512]{1,0:T(8,128)(2,1)}, u32[]{:S(2)}, u32[]{:S(2)}) collective-permute-start(bf16[2048,512]{1,0:T(8,128)(2,1)} %param.17), channel_id=1, source_target_pairs={{0,1},{1,0},{2,3},{3,2},{4,5},{5,4},{6,7},{7,6},{8,9},{9,8},{10,11... | collective-permute-start | bytes 6291464 | tf_op jit(solution)/shard_map/ppermute | solution.py:15
  65.8 12.9 %collective-permute-start.2 = (bf16[2048,512]{1,0:T(8,128)(2,1)}, bf16[2048,512]{1,0:T(8,128)(2,1)}, u32[]{:S(2)}, u32[]{:S(2)}) collective-permute-start(bf16[2048,512]{1,0:T(8,128)(2,1)} %collective-permute-done), channel_id=1, source_target_pairs={{0,1},{1,0},{2,3},{3,2},{4,5},{5,4},{6,7},{7,6},{8,9},{9,8},{10,11... | collective-permute-start | bytes 6291464 | tf_op jit(solution)/shard_map/ppermute | solution.py:15
  83.1 3.3 %copy-start.3 = (f32[2048]{0:T(1024)S(1)}, f32[2048]{0:T(1024)}, u32[]{:S(2)}) copy-start(f32[2048]{0:T(1024)} %param.19) | copy-start | bytes 24580
  83.1 4.4 %copy-start.1 = (s32[16]{0:T(128)S(1)}, s32[16]{0:T(128)}, u32[]{:S(2)}) copy-start(s32[16]{0:T(128)} %param.22) | copy-start | bytes 196
  185.6 24.1 %copy-start.2 = (s32[128,8]{0,1:T(8,128)S(1)}, s32[128,8]{0,1:T(8,128)}, u32[]{:S(2)}) copy-start(s32[128,8]{0,1:T(8,128)} %param.20) | copy-start | bytes 12292
  185.6 24.2 %copy-start.4 = (f32[128,8]{0,1:T(8,128)S(1)}, f32[128,8]{0,1:T(8,128)}, u32[]{:S(2)}) copy-start(f32[128,8]{0,1:T(8,128)} %param.21) | copy-start | bytes 12292
  185.6 100.2 %all-to-all-start = ((bf16[16,64,2048]{2,1,0:T(8,128)(2,1)}), bf16[16,64,2048]{2,1,0:T(8,128)(2,1)}, u32[]{:S(2)}, u32[]{:S(2)}) async-start(bf16[16,64,2048]{2,1,0:T(8,128)(2,1)} %bitcast.71), calls=%async_computation | async-start | bytes 8388608 | tf_op jit(solution)/shard_map/all_to_all | solution.py:229
Sparse Core Ops, SparseCore 0:
  10.9 49.3 all-gather.5
  87.7 76.6 all-gather.3
